TPU v7x, 128 devices: a whole 4x4x4 slice. The times are simulated.
128 devices in a mesh: space: 8 (over z, core), vel: 16 (over x, y).
Axes of the slice: x: 4, y: 4, z: 4, core: 2. Of those that a mesh axis runs over, the one named last changes fastest.
Arguments:
- dist: bfloat16 [7168, 16, 16, 128], P('vel', 'space'), may hold values from 0.25 to 4
- vel_map: int32 [7168], P('vel'), may hold values from 0 to 13823, as said below
- cell_mask: int32 [16, 16, 128], P('space'), may hold values from 0 to 2, as said below
- w_modes: bfloat16 [512, 7168], replicated, may hold values from -0.0625 to 0.0625
- e_modes: bfloat16 [7168, 512], replicated, may hold values from -0.25 to 0.25
- rates: float32 [512], replicated, may hold values from 0.1 to 1
Outputs:
- dist_out: bfloat16 [7168, 16, 16, 128], P('vel', 'space')
Inputs may be any that keep to these rules, and one draw needn't show every extreme that they name: `vel_map`: distinct lattice indices: the 7168 points of the 24^3 cube nearest its centre, in a random order. `cell_mask`: cells with x index 0 are fluid.
All inputs are finite; a program needn't handle non-finite values.
Results may differ from a plain program's by a relative error of at most 0.0054.
Values may be sent and summed in bfloat16 or wider, within the bound.
No kernel may reach another device: no remote copies, remote signals or barrier semaphores. Data moves between devices by JAX's collectives and lax.ppermute only.
A program may use at most 192 MiB of HBM per device.

v0:
```python
import jax
import jax.numpy as jnp
from jax import lax
from jax.sharding import PartitionSpec as P

VGRID = 24
STEPS = 2


def extended(cells, sides, width):
    for axis, dim in sides:
        count = lax.axis_size(axis)
        ends = count - 1
        head = lax.slice_in_dim(cells, 0, width, axis=dim)
        tail = lax.slice_in_dim(cells, cells.shape[dim] - width, cells.shape[dim], axis=dim)
        cells = jnp.concatenate(
            [
                lax.ppermute(tail, axis, [(i, (i + 1) % count) for i in range(ends)]),
                cells,
                lax.ppermute(head, axis, [((i + 1) % count, i) for i in range(ends)]),
            ],
            axis=dim,
        )
    return cells


def components(vel_map):
    side = VGRID
    first = (vel_map // (side * side)).astype(jnp.float32)
    second = (vel_map // side % side).astype(jnp.float32)
    third = (vel_map % side).astype(jnp.float32)
    centre = (side - 1) / 2.0
    half_side = side / 2.0
    return (
        0.3 * (first - centre) / half_side,
        0.3 * (second - centre) / half_side,
        0.3 * (third - centre) / half_side,
    )


def transport(field, ax, ay, az, tmask):
    padded = extended(field, (("space", 1),), 1)
    whole = padded.astype(jnp.float32)
    center = whole[:, 1:-1]
    edge_x = jnp.zeros_like(center[..., :1])
    edge_y = jnp.zeros_like(center[:, :, :1])
    x_low = jnp.concatenate([edge_x, center[..., :-1]], axis=3)
    x_high = jnp.concatenate([center[..., 1:], edge_x], axis=3)
    y_low = jnp.concatenate([edge_y, center[:, :, :-1]], axis=2)
    y_high = jnp.concatenate([center[:, :, 1:], edge_y], axis=2)
    flux = jnp.maximum(ax, 0.0) * (center - x_low) + jnp.minimum(ax, 0.0) * (x_high - center)
    flux = flux + jnp.maximum(ay, 0.0) * (center - y_low) + jnp.minimum(ay, 0.0) * (y_high - center)
    flux = (
        flux
        + jnp.maximum(az, 0.0) * (center - whole[:, :-2])
        + jnp.minimum(az, 0.0) * (whole[:, 2:] - center)
    )
    return (center - tmask[None] * flux).astype(jnp.bfloat16)


def per_device(dist, vel_map, cell_mask, w_modes, e_modes, rates):
    vblock, layers, rows_y, rows_x = dist.shape
    cells = layers * rows_y * rows_x
    groups = lax.axis_size("vel")
    device_portion = cells // groups
    starting_cell = lax.axis_index("vel") * device_portion
    comp_x, comp_y, comp_z = components(vel_map)
    ax = comp_x[:, None, None, None]
    ay = comp_y[:, None, None, None]
    az = comp_z[:, None, None, None]
    tmask = (cell_mask != 1).astype(jnp.float32)
    cmask = jnp.where(cell_mask == 0, 1.0, jnp.where(cell_mask == 2, 0.5, 0.0)).astype(jnp.float32)
    flattened_cell_mask = cmask.reshape(cells)
    collision_portion = lax.dynamic_slice_in_dim(
        flattened_cell_mask, starting_cell, device_portion, 0
    )
    field = dist
    for step in range(STEPS):
        half = transport(field, ax, ay, az, tmask)
        flat = half.reshape(vblock, cells)
        local_values = lax.all_to_all(flat, "vel", split_axis=1, concat_axis=0, tiled=True)
        moments = jnp.dot(w_modes, local_values, preferred_element_type=jnp.float32)
        delta = (rates[:, None] * moments).astype(jnp.bfloat16)
        adjustment_term = jnp.dot(e_modes, delta, preferred_element_type=jnp.float32)
        post_collision = (
            local_values.astype(jnp.float32) - collision_portion[None, :] * adjustment_term
        ).astype(jnp.bfloat16)
        flat_new = lax.all_to_all(post_collision, "vel", split_axis=0, concat_axis=1, tiled=True)
        field = flat_new.reshape(vblock, layers, rows_y, rows_x)
    return field


def solution(mesh):
    placed = (P("vel", "space", None, None), P("vel"), P("space", None, None), P(), P(), P())
    return jax.shard_map(
        per_device,
        mesh=mesh,
        in_specs=placed,
        out_specs=P("vel", "space", None, None),
        check_vma=False,
    )
```

profile of v0, /device:TPU:32, one launch (start us, length us, event | category | flops | bytes accessed | tf_op | source)
XLA Modules:
  0.0 466.5 jit_solution(17593386465886846523)
XLA Ops:
  0.0 0.0 copy-start.1
  0.0 0.0 copy-start.4
  0.0 0.0 copy-start.3
  0.0 2.8 fusion.36
  2.8 1.9 collective-permute-start
  4.8 3.6 collective-permute-start.1
  8.4 0.0 copy-done.4
  8.5 0.0 copy-done.3
  8.5 18.9 %collective-permute-done = bf16[448,1,16,128]{3,2,1,0:T(8,128)(2,1)S(1)} collective-permute-done((bf16[448,1,16,128]{3,2,1,0:T(8,128)(2,1)S(1)}, bf16[448,1,16,128]{3,2,1,0:T(8,128)(2,1)S(1)}, u32[]{:S(2)}, u32[]{:S(2)}) %collective-permute-start) | collective-permute-done | bytes 1835040 | tf_op jit(solution)/shard_map/ppermute | solution.py:18
  27.4 1.8 collective-permute-done.1
  29.1 0.0 copy-done.1
  29.2 5.5 %maximum_convert_fusion = f32[448,4,16,128]{3,2,1,0:T(8,128)} fusion(bf16[448,1,16,128]{3,2,1,0:T(8,128)(2,1)S(1)} %collective-permute-done.1, bf16[448,2,16,128]{3,2,1,0:T(8,128)(2,1)S(1)} %copy-done.1, bf16[448,1,16,128]{3,2,1,0:T(8,128)(2,1)S(1)} %collective-permute-done), kind=kLoop, calls=%fused_computation.26 | loop fusion | flops 11010048 | bytes 22020096 | tf_op jit(solution)/shard_map/convert_element_type | solution.py:43
  34.6 12.2 %fusion.34 = (f32[448,2,15,128]{3,2,1,0:T(8,128)}, f32[448,2,15,128]{3,2,1,0:T(8,128)}) fusion(f32[448,4,16,128]{3,2,1,0:T(8,128)} %maximum_convert_fusion), kind=kLoop, calls=%fused_computation.59 | loop fusion | bytes 27525120 | tf_op jit(solution)/shard_map/slice | solution.py:49
  46.8 12.4 %fusion.33 = (f32[448,2,16,127]{3,2,1,0:T(8,128)}, f32[448,2,16,127]{3,2,1,0:T(8,128)}) fusion(f32[448,4,16,128]{3,2,1,0:T(8,128)} %maximum_convert_fusion), kind=kLoop, calls=%fused_computation.58 | loop fusion | bytes 29130752 | tf_op jit(solution)/shard_map/slice | solution.py:47
  59.3 20.3 %fusion.17 = bf16[448,2,16,128]{3,2,1,0:T(8,128)(2,1)} fusion(f32[448,4,16,128]{3,2,1,0:T(8,128)} %maximum_convert_fusion, f32[448,2,15,128]{3,2,1,0:T(8,128)} %get-tuple-element.16, f32[448,2,15,128]{3,2,1,0:T(8,128)} %get-tuple-element.15, f32[448,2,16,127]{3,2,1,0:T(8,128)} %get-tuple-element.14, f32[448,2,16,127]{3,2,1,0:T(8,128)} %get-tuple-element.13, ...), kind=kLoop, calls=%fused_computation.22 | loop fusion | flops 36700160 | bytes 54045184 | tf_op jit(solution)/shard_map/convert_element_type | solution.py:58
  79.5 6.5 %all_to_all.52 = bf16[448,16,256]{2,1,0:T(8,128)(2,1)} reshape(bf16[448,2,16,128]{3,2,1,0:T(8,128)(2,1)} %fusion.17) | data formatting | bytes 7340032 | tf_op jit(solution)/shard_map/all_to_all | solution.py:81
  86.0 5.2 %copy.23 = bf16[448,16,256]{2,0,1:T(8,128)(2,1)} copy(bf16[448,16,256]{2,1,0:T(8,128)(2,1)} %all_to_all.52) | data formatting | bytes 7340032 | tf_op jit(solution)/shard_map/all_to_all | solution.py:81
  91.1 0.0 copy-start.2
  91.1 7.2 %all-to-all-start = ((bf16[448,16,256]{2,0,1:T(8,128)(2,1)}), bf16[448,16,256]{2,0,1:T(8,128)(2,1)}, u32[]{:S(2)}, u32[]{:S(2)}) async-start(bf16[448,16,256]{2,0,1:T(8,128)(2,1)} %copy.23), calls=%async_computation | async-start | bytes 7340032 | tf_op jit(solution)/shard_map/all_to_all | solution.py:81
  98.4 0.1 dynamic_slice.3
  98.5 48.4 %all-to-all-done = bf16[448,16,256]{2,0,1:T(8,128)(2,1)} async-done(((bf16[448,16,256]{2,0,1:T(8,128)(2,1)}), bf16[448,16,256]{2,0,1:T(8,128)(2,1)}, u32[]{:S(2)}, u32[]{:S(2)}) %all-to-all-start) | async-done | bytes 3670048 | tf_op jit(solution)/shard_map/all_to_all | solution.py:81
  146.9 5.9 %copy.24 = bf16[7168,256]{0,1:T(8,128)(2,1)} copy(bf16[7168,256]{1,0:T(8,128)(2,1)} %bitcast.1) | data formatting | bytes 7340032 | tf_op jit(solution)/shard_map/all_to_all | solution.py:81
  152.8 0.0 copy-done.2
  152.8 13.3 %fusion.4 = bf16[7168,256]{0,1:T(8,128)(2,1)} fusion(bf16[7168,512]{1,0:T(8,128)(2,1)} %param.10, bf16[7168,256]{0,1:T(8,128)(2,1)} %copy.24, f32[256]{0:T(256)S(1)} %dynamic_slice.3, bf16[7168,256]{1,0:T(8,128)(2,1)} %bitcast.1, bf16[512,7168]{1,0:T(8,128)(2,1)} %param.9, f32[512]{0:T(512)S(1)} %copy-done.2), kind=kOutput, calls=%fused_computation.6 | convolution fusion | flops 3765698560 | bytes 25693184 | tf_op jit(solution)/shard_map/dot_general | solution.py:84
  166.1 5.9 %copy.25 = bf16[7168,256]{1,0:T(8,128)(2,1)} copy(bf16[7168,256]{0,1:T(8,128)(2,1)} %fusion.4) | data formatting | bytes 7340032 | tf_op jit(solution)/shard_map/convert_element_type | solution.py:87
  172.0 59.8 %all_to_all.70 = bf16[16,448,256]{2,1,0:T(8,128)(2,1)S(1)} all-to-all(bf16[16,448,256]{2,1,0:T(8,128)(2,1)} %bitcast.35), channel_id=1, replica_groups=mesh['space'=8,'vel'=16] {'vel'}, dimensions={0} | all-to-all | bytes 7340032 | tf_op jit(solution)/shard_map/all_to_all | solution.py:88
  231.8 4.0 copy.26
  235.8 6.5 %reshape.43 = bf16[448,2,16,128]{3,2,1,0:T(8,128)(2,1)} reshape(bf16[448,16,256]{2,1,0:T(8,128)(2,1)} %copy.26) | data formatting | bytes 7340032 | tf_op jit(solution)/shard_map/reshape | solution.py:89
  242.3 0.0 copy-start
  242.3 2.8 fusion.35
  245.1 1.9 collective-permute-start.2
  247.0 3.9 collective-permute-start.3
  250.9 18.7 %collective-permute-done.2 = bf16[448,1,16,128]{3,2,1,0:T(8,128)(2,1)S(1)} collective-permute-done((bf16[448,1,16,128]{3,2,1,0:T(8,128)(2,1)S(1)}, bf16[448,1,16,128]{3,2,1,0:T(8,128)(2,1)S(1)}, u32[]{:S(2)}, u32[]{:S(2)}) %collective-permute-start.2) | collective-permute-done | bytes 1835040 | tf_op jit(solution)/shard_map/ppermute | solution.py:18
  269.7 1.8 collective-permute-done.3
  271.4 0.0 copy-done
  271.4 5.5 %maximum_convert_fusion.1 = f32[448,4,16,128]{3,2,1,0:T(8,128)} fusion(bf16[448,1,16,128]{3,2,1,0:T(8,128)(2,1)S(1)} %collective-permute-done.3, bf16[448,2,16,128]{3,2,1,0:T(8,128)(2,1)S(1)} %copy-done, bf16[448,1,16,128]{3,2,1,0:T(8,128)(2,1)S(1)} %collective-permute-done.2), kind=kLoop, calls=%fused_computation.27 | loop fusion | flops 11010048 | bytes 22020096 | tf_op jit(solution)/shard_map/convert_element_type | solution.py:43
  276.9 12.2 %fusion.32 = (f32[448,2,15,128]{3,2,1,0:T(8,128)}, f32[448,2,15,128]{3,2,1,0:T(8,128)}) fusion(f32[448,4,16,128]{3,2,1,0:T(8,128)} %maximum_convert_fusion.1), kind=kLoop, calls=%fused_computation.57 | loop fusion | bytes 27525120 | tf_op jit(solution)/shard_map/slice | solution.py:49
  289.1 12.4 %fusion.31 = (f32[448,2,16,127]{3,2,1,0:T(8,128)}, f32[448,2,16,127]{3,2,1,0:T(8,128)}) fusion(f32[448,4,16,128]{3,2,1,0:T(8,128)} %maximum_convert_fusion.1), kind=kLoop, calls=%fused_computation.56 | loop fusion | bytes 29130752 | tf_op jit(solution)/shard_map/slice | solution.py:47
  301.5 20.3 %fusion.10 = bf16[448,2,16,128]{3,2,1,0:T(8,128)(2,1)} fusion(f32[448,4,16,128]{3,2,1,0:T(8,128)} %maximum_convert_fusion.1, f32[448,2,15,128]{3,2,1,0:T(8,128)} %get-tuple-element.12, f32[448,2,15,128]{3,2,1,0:T(8,128)} %get-tuple-element.11, f32[448,2,16,127]{3,2,1,0:T(8,128)} %get-tuple-element.10, f32[448,2,16,127]{3,2,1,0:T(8,128)} %get-tuple-element.9, ...), kind=kLoop, calls=%fused_computation.13 | loop fusion | flops 36700160 | bytes 54045184 | tf_op jit(solution)/shard_map/convert_element_type | solution.py:58
  321.8 6.5 %all_to_all.59 = bf16[448,16,256]{2,1,0:T(8,128)(2,1)} reshape(bf16[448,2,16,128]{3,2,1,0:T(8,128)(2,1)} %fusion.10) | data formatting | bytes 7340032 | tf_op jit(solution)/shard_map/all_to_all | solution.py:81
  328.2 3.3 copy.27
  331.6 49.7 %all_to_all.71 = bf16[448,16,256]{2,0,1:T(8,128)(2,1)} all-to-all(bf16[448,16,256]{2,0,1:T(8,128)(2,1)S(1)} %copy.27), channel_id=1, replica_groups=mesh['space'=8,'vel'=16] {'vel'}, dimensions={1} | all-to-all | bytes 7340032 | tf_op jit(solution)/shard_map/all_to_all | solution.py:81
  381.3 5.9 %copy.28 = bf16[7168,256]{0,1:T(8,128)(2,1)} copy(bf16[7168,256]{1,0:T(8,128)(2,1)} %bitcast.33) | data formatting | bytes 7340032 | tf_op jit(solution)/shard_map/all_to_all | solution.py:81
  387.2 13.3 %fusion.5 = bf16[7168,256]{0,1:T(8,128)(2,1)} fusion(bf16[7168,512]{1,0:T(8,128)(2,1)} %param.10, bf16[7168,256]{0,1:T(8,128)(2,1)} %copy.28, f32[256]{0:T(256)S(1)} %dynamic_slice.3, bf16[7168,256]{1,0:T(8,128)(2,1)} %bitcast.34, bf16[512,7168]{1,0:T(8,128)(2,1)} %param.9, f32[512]{0:T(512)S(1)} %copy-done.2), kind=kOutput, calls=%fused_computation.7 | convolution fusion | flops 3765698560 | bytes 25693184 | tf_op jit(solution)/shard_map/dot_general | solution.py:84
  400.5 5.9 %copy.29 = bf16[7168,256]{1,0:T(8,128)(2,1)} copy(bf16[7168,256]{0,1:T(8,128)(2,1)} %fusion.5) | data formatting | bytes 7340032 | tf_op jit(solution)/shard_map/convert_element_type | solution.py:87
  406.4 49.7 %all_to_all.72 = bf16[16,448,256]{2,1,0:T(8,128)(2,1)S(1)} all-to-all(bf16[16,448,256]{2,1,0:T(8,128)(2,1)} %bitcast.37), channel_id=1, replica_groups=mesh['space'=8,'vel'=16] {'vel'}, dimensions={0} | all-to-all | bytes 7340032 | tf_op jit(solution)/shard_map/all_to_all | solution.py:88
  456.1 3.9 copy.30
  460.0 6.5 %reshape.44 = bf16[448,2,16,128]{3,2,1,0:T(8,128)(2,1)} reshape(bf16[448,16,256]{2,1,0:T(8,128)(2,1)} %copy.30) | data formatting | bytes 7340032 | tf_op jit(solution)/shard_map/reshape | solution.py:89
  (4 shorter events, 0.0 us)
Async XLA Ops:
  0.0 29.2 %copy-start.1 = (bf16[448,2,16,128]{3,2,1,0:T(8,128)(2,1)S(1)}, bf16[448,2,16,128]{3,2,1,0:T(8,128)(2,1)}, u32[]{:S(2)}) copy-start(bf16[448,2,16,128]{3,2,1,0:T(8,128)(2,1)} %param.6) | copy-start | bytes 11010052
  0.0 8.4 %copy-start.4 = (s32[448]{0:T(512)S(1)}, s32[448]{0:T(512)}, u32[]{:S(2)}) copy-start(s32[448]{0:T(512)} %param.7) | copy-start | bytes 5380
  0.0 8.5 %copy-start.3 = (s32[2,16,128]{2,1,0:T(8,128)S(1)}, s32[2,16,128]{2,1,0:T(8,128)}, u32[]{:S(2)}) copy-start(s32[2,16,128]{2,1,0:T(8,128)} %param.8) | copy-start | bytes 49156
  2.8 24.5 %collective-permute-start = (bf16[448,1,16,128]{3,2,1,0:T(8,128)(2,1)S(1)}, bf16[448,1,16,128]{3,2,1,0:T(8,128)(2,1)S(1)}, u32[]{:S(2)}, u32[]{:S(2)}) collective-permute-start(bf16[448,1,16,128]{3,2,1,0:T(8,128)(2,1)S(1)} %get-tuple-element.19), channel_id=1, source_target_pairs={{0,16},{16,32},{32,48},{48,64},{64,80},{80,96},{96,112},{1,17},{17... | collective-permute-start | bytes 5505032 | tf_op jit(solution)/shard_map/ppermute | solution.py:18
  4.8 24.4 %collective-permute-start.1 = (bf16[448,1,16,128]{3,2,1,0:T(8,128)(2,1)S(1)}, bf16[448,1,16,128]{3,2,1,0:T(8,128)(2,1)S(1)}, u32[]{:S(2)}, u32[]{:S(2)}) collective-permute-start(bf16[448,1,16,128]{3,2,1,0:T(8,128)(2,1)S(1)} %get-tuple-element.20), channel_id=1, source_target_pairs={{16,0},{32,16},{48,32},{64,48},{80,64},{96,80},{112,96},{17,1},{33... | collective-permute-start | bytes 5505032 | tf_op jit(solution)/shard_map/ppermute | solution.py:20
  91.1 61.7 %copy-start.2 = (f32[512]{0:T(512)S(1)}, f32[512]{0:T(512)}, u32[]{:S(2)}) copy-start(f32[512]{0:T(512)} %param.11) | copy-start | bytes 6148
  91.1 55.8 %all-to-all-start = ((bf16[448,16,256]{2,0,1:T(8,128)(2,1)}), bf16[448,16,256]{2,0,1:T(8,128)(2,1)}, u32[]{:S(2)}, u32[]{:S(2)}) async-start(bf16[448,16,256]{2,0,1:T(8,128)(2,1)} %copy.23), calls=%async_computation | async-start | bytes 7340032 | tf_op jit(solution)/shard_map/all_to_all | solution.py:81
  242.3 29.1 %copy-start = (bf16[448,2,16,128]{3,2,1,0:T(8,128)(2,1)S(1)}, bf16[448,2,16,128]{3,2,1,0:T(8,128)(2,1)}, u32[]{:S(2)}) copy-start(bf16[448,2,16,128]{3,2,1,0:T(8,128)(2,1)} %reshape.43) | copy-start | bytes 11010052
  245.1 24.5 %collective-permute-start.2 = (bf16[448,1,16,128]{3,2,1,0:T(8,128)(2,1)S(1)}, bf16[448,1,16,128]{3,2,1,0:T(8,128)(2,1)S(1)}, u32[]{:S(2)}, u32[]{:S(2)}) collective-permute-start(bf16[448,1,16,128]{3,2,1,0:T(8,128)(2,1)S(1)} %get-tuple-element.17), channel_id=1, source_target_pairs={{0,16},{16,32},{32,48},{48,64},{64,80},{80,96},{96,112},{1,17},{17... | collective-permute-start | bytes 5505032 | tf_op jit(solution)/shard_map/ppermute | solution.py:18
  247.0 24.4 %collective-permute-start.3 = (bf16[448,1,16,128]{3,2,1,0:T(8,128)(2,1)S(1)}, bf16[448,1,16,128]{3,2,1,0:T(8,128)(2,1)S(1)}, u32[]{:S(2)}, u32[]{:S(2)}) collective-permute-start(bf16[448,1,16,128]{3,2,1,0:T(8,128)(2,1)S(1)} %get-tuple-element.18), channel_id=1, source_target_pairs={{16,0},{32,16},{48,32},{64,48},{80,64},{96,80},{112,96},{17,1},{33... | collective-permute-start | bytes 5505032 | tf_op jit(solution)/shard_map/ppermute | solution.py:20
where the time goes:
time: 468 us; the launch traced here: 467 us
  blocking collectives  159 us (34%)
  local copies, waits for them, and re-layouts  121 us (26%)
  waiting for transfers between devices  89.6 us (19%)
  other arithmetic  51.5 us (11%)
  matrix products  26.6 us (6%)
  starting transfers between devices  18.6 us (4%)
    all_to_all x2, blocking collectives, per_device(): lax.all_to_all(post_collision, 'vel', split_axis=0, concat_axis=1, tiled=...  110 us
    all_to_all x1, blocking collectives, per_device(): lax.all_to_all(flat, 'vel', split_axis=1, concat_axis=0, tiled=True)  49.7 us
    all_to_all x1, waiting for transfers between devices, per_device(): lax.all_to_all(flat, 'vel', split_axis=1, concat_axis=0, tiled=True)  48.4 us
    convert_element_type x2, other arithmetic, transport(): return (center - tmask[None] * flux).astype(jnp.bfloat16)  40.5 us
    ppermute x2, waiting for transfers between devices, extended(): lax.ppermute(tail, axis, [(i, (i + 1) % count) for i in range(ends)])  37.6 us
    all_to_all x6, local copies, waits for them, and re-layouts, per_device(): lax.all_to_all(flat, 'vel', split_axis=1, concat_axis=0, tiled=True)  33.2 us
    dot_general x2, matrix products, per_device(): jnp.dot(e_modes, delta, preferred_element_type=jnp.float32)  26.6 us
    slice x2, local copies, waits for them, and re-layouts, transport(): x_low = jnp.concatenate([edge_x, center[..., :-1]], axis=3)  24.8 us
  transfers between devices with their start and end apart: 5, of which 5 were waited for; matrix products, arithmetic and copies ran while one was open for 0% of the time, Pallas kernels for 0%

commit v1 on v0

v1 whole, which is shorter than its diff:
```python
import functools

import jax
import jax.numpy as jnp
from jax import lax
from jax.experimental import pallas as pl
from jax.experimental.pallas import tpu as pltpu
from jax.sharding import PartitionSpec as P

VGRID = 24
STEPS = 2
VBLOCK = 64


def components(vel_map):
    side = VGRID
    first = (vel_map // (side * side)).astype(jnp.float32)
    second = (vel_map // side % side).astype(jnp.float32)
    third = (vel_map % side).astype(jnp.float32)
    centre = (side - 1) / 2.0
    half_side = side / 2.0
    return (
        0.3 * (first - centre) / half_side,
        0.3 * (second - centre) / half_side,
        0.3 * (third - centre) / half_side,
    )


def transport_kernel(ny, f_ref, lo_ref, hi_ref, coef_ref, tm_ref, out_ref):
    rows, tv, nx = f_ref.shape
    nzl = rows // ny
    ax = coef_ref[0]
    ay = coef_ref[1]
    az = coef_ref[2]
    zero = jnp.zeros((tv, nx), jnp.float32)
    px, mx = jnp.maximum(ax, 0.0), jnp.minimum(ax, 0.0)
    py, my = jnp.maximum(ay, 0.0), jnp.minimum(ay, 0.0)
    pz, mz = jnp.maximum(az, 0.0), jnp.minimum(az, 0.0)
    lane = lax.broadcasted_iota(jnp.int32, (tv, nx), 1)

    def load(ref, i):
        return ref[i].astype(jnp.float32)

    for w in range(rows):
        z, y = divmod(w, ny)
        c = load(f_ref, w)
        x_low = jnp.where(lane == 0, 0.0, pltpu.roll(c, 1, 1))
        x_high = jnp.where(lane == nx - 1, 0.0, pltpu.roll(c, nx - 1, 1))
        y_low = load(f_ref, w - 1) if y > 0 else zero
        y_high = load(f_ref, w + 1) if y < ny - 1 else zero
        z_low = load(f_ref, w - ny) if z > 0 else load(lo_ref, y)
        z_high = load(f_ref, w + ny) if z < nzl - 1 else load(hi_ref, y)
        flux = px * (c - x_low) + mx * (x_high - c)
        flux = flux + py * (c - y_low) + my * (y_high - c)
        flux = flux + pz * (c - z_low) + mz * (z_high - c)
        out_ref[w] = (c - tm_ref[w : w + 1, :] * flux).astype(out_ref.dtype)


def transport(f, lo, hi, coef, tm, ny):
    rows, vb, nx = f.shape
    tv = VBLOCK
    return pl.pallas_call(
        functools.partial(transport_kernel, ny),
        out_shape=jax.ShapeDtypeStruct(f.shape, f.dtype),
        grid=(vb // tv,),
        in_specs=[
            pl.BlockSpec((rows, tv, nx), lambda i: (0, i, 0)),
            pl.BlockSpec((ny, tv, nx), lambda i: (0, i, 0)),
            pl.BlockSpec((ny, tv, nx), lambda i: (0, i, 0)),
            pl.BlockSpec((3, tv, nx), lambda i: (0, i, 0)),
            pl.BlockSpec((rows, nx), lambda i: (0, 0)),
        ],
        out_specs=pl.BlockSpec((rows, tv, nx), lambda i: (0, i, 0)),
        cost_estimate=pl.CostEstimate(
            flops=30 * rows * vb * nx, transcendentals=0, bytes_accessed=4 * rows * vb * nx
        ),
    )(f, lo, hi, coef, tm)


def per_device(dist, vel_map, cell_mask, w_modes, e_modes, rates):
    vb, nzl, ny, nx = dist.shape
    rows = nzl * ny
    groups = lax.axis_size("vel")
    spaces = lax.axis_size("space")
    chunk = rows // groups
    kmodes = w_modes.shape[0]
    comp_x, comp_y, comp_z = components(vel_map)
    coef = jnp.broadcast_to(jnp.stack([comp_x, comp_y, comp_z])[:, :, None], (3, vb, nx))
    tm = (cell_mask != 1).astype(jnp.float32).reshape(rows, nx)
    cmask = jnp.where(cell_mask == 0, 1.0, jnp.where(cell_mask == 2, 0.5, 0.0)).astype(jnp.float32)
    cm = lax.dynamic_slice_in_dim(cmask.reshape(rows, nx), lax.axis_index("vel") * chunk, chunk, 0)
    w3 = w_modes.reshape(kmodes, groups, vb)
    e3 = e_modes.reshape(groups, vb, kmodes)
    up = [(i, i + 1) for i in range(spaces - 1)]
    down = [(i + 1, i) for i in range(spaces - 1)]

    f = jnp.transpose(dist, (1, 2, 0, 3)).reshape(rows, vb, nx)
    for step in range(STEPS):
        lo = lax.ppermute(f[rows - ny :], "space", up)
        hi = lax.ppermute(f[:ny], "space", down)
        half = transport(f, lo, hi, coef, tm, ny)
        send = half.reshape(groups, chunk, vb, nx)
        recv = lax.all_to_all(send, "vel", 0, 0, tiled=True)
        moments = jnp.einsum("ksv,srvx->krx", w3, recv, preferred_element_type=jnp.float32)
        delta = (rates[:, None, None] * moments).astype(jnp.bfloat16)
        adjustment = jnp.einsum("svk,krx->srvx", e3, delta, preferred_element_type=jnp.float32)
        post = (recv.astype(jnp.float32) - cm[None, :, None, :] * adjustment).astype(jnp.bfloat16)
        back = lax.all_to_all(post, "vel", 0, 0, tiled=True)
        f = back.reshape(rows, vb, nx)
    return jnp.transpose(f.reshape(nzl, ny, vb, nx), (2, 0, 1, 3))


def solution(mesh):
    placed = (P("vel", "space", None, None), P("vel"), P("space", None, None), P(), P(), P())
    return jax.shard_map(
        per_device,
        mesh=mesh,
        in_specs=placed,
        out_specs=P("vel", "space", None, None),
        check_vma=False,
    )
```

time: 468 us -> 325 us (0.69)
  local copies, waits for them, and re-layouts: 121 us -> 30 us
  other arithmetic: 51.5 us -> 0.65 us
  Pallas kernels: 0 us -> 20.7 us
  blocking collectives: 159 us -> 148 us
  waiting for transfers between devices: 89.6 us -> 80.1 us
    slice x6 -> x2, local copies, waits for them, and re-layouts: 54.9 us -> 0.57 us  [per_device(): hi = lax.ppermute(f[:ny], 'space', down)]
    convert_element_type x5 -> x0, other arithmetic: 51.5 us -> none  [the longest x2 40.5 us: transport(): return (center - tmask[None] * flux).astype(jnp.bfloat16)]
    all_to_all x8 -> x0, local copies, waits for them, and re-layouts: 41.1 us -> none  [the longest x6 33.2 us: per_device(): lax.all_to_all(flat, 'vel', split_axis=1, concat_axis=0, tiled=True)]
    pallas_call x0 -> x2, Pallas kernels: none -> 20.7 us  [transport(): pl.pallas_call(functools.partial(transport_kernel, ny), out_shape=jax.Sha...]
    unnamed x10 -> x20, local copies, waits for them, and re-layouts: 0.02 us -> 19.5 us
    reshape x2 -> x0, local copies, waits for them, and re-layouts: 13 us -> none  [per_device(): field = flat_new.reshape(vblock, layers, rows_y, rows_x)]
    all_to_all x3, blocking collectives: 159 us -> 148 us  [the longest x2 99.4 us: per_device(): back = lax.all_to_all(post, 'vel', 0, 0, tiled=True)]
    all_to_all x1, waiting for transfers between devices: 48.4 us -> 38 us  [per_device(): recv = lax.all_to_all(send, 'vel', 0, 0, tiled=True)]
  transfers between devices with their start and end apart: 5 -> 5, of which waited for: 5 -> 5; matrix products, arithmetic and copies ran while one was open for 0% -> 3% of each run, Pallas kernels for 0% -> 0%
where the time goes in v1:
time: 325 us; the launch traced here: 324 us
  blocking collectives  148 us (46%)
  waiting for transfers between devices  80.1 us (25%)
  local copies, waits for them, and re-layouts  30 us (9%)
  matrix products  26.8 us (8%)
  Pallas kernels  20.7 us (6%)
  starting transfers between devices  16.9 us (5%)
    all_to_all x2, blocking collectives, per_device(): back = lax.all_to_all(post, 'vel', 0, 0, tiled=True)  99.4 us
    all_to_all x1, blocking collectives, per_device(): recv = lax.all_to_all(send, 'vel', 0, 0, tiled=True)  48.9 us
    all_to_all x1, waiting for transfers between devices, per_device(): recv = lax.all_to_all(send, 'vel', 0, 0, tiled=True)  38 us
    dot_general x2, matrix products, per_device(): jnp.einsum('svk,krx->srvx', e3, delta, preferred_element_type=jnp.float32)  26.8 us
    ppermute x2, waiting for transfers between devices, per_device(): lo = lax.ppermute(f[rows - ny:], 'space', up)  22.8 us
    pallas_call x2, Pallas kernels, transport(): pl.pallas_call(functools.partial(transport_kernel, ny), out_shape=jax.Sha...  20.7 us
    unnamed x20, local copies, waits for them, and re-layouts  19.5 us
    ppermute x2, waiting for transfers between devices, per_device(): hi = lax.ppermute(f[:ny], 'space', down)  19.4 us
  transfers between devices with their start and end apart: 5, of which 5 were waited for; matrix products, arithmetic and copies ran while one was open for 3% of the time, Pallas kernels for 0%

profile of v1, /device:TPU:32, one launch (start us, length us, event | category | flops | bytes accessed | tf_op | source)
XLA Modules:
  0.0 323.6 jit_solution(58769599943253572)
XLA Ops:
  0.0 3.5 %copy.46 = bf16[448,2,16,128]{3,0,2,1:T(8,128)(2,1)S(1)} copy(bf16[448,2,16,128]{3,2,1,0:T(8,128)(2,1)} %param.6) | data formatting | bytes 7340032 | tf_op args[0]
  3.5 0.0 copy-start
  3.5 0.0 copy-start.8
  3.5 0.0 copy-start.6
  3.5 0.2 slice_bitcast_fusion
  3.7 1.6 copy-done
  5.3 1.9 collective-permute-start.1
  7.2 2.4 collective-permute-start
  9.6 0.0 copy-done.8
  9.7 0.0 copy-done.6
  9.7 0.6 compare_convert_fusion
  10.3 17.6 %collective-permute-done.1.hi_ref = bf16[16,448,128]{2,1,0:T(8,128)(2,1)S(1)} collective-permute-done((bf16[16,448,128]{2,1,0:T(8,128)(2,1)S(1)}, bf16[16,448,128]{2,1,0:T(8,128)(2,1)S(1)}, u32[]{:S(2)}, u32[]{:S(2)}) %collective-permute-start.1) | collective-permute-done | bytes 1835040 | tf_op jit(solution)/shard_map/ppermute | solution.py:100
  27.9 0.0 copy-start.2
  27.9 3.8 %collective-permute-done.lo_ref = bf16[16,448,128]{2,1,0:T(8,128)(2,1)S(1)} collective-permute-done((bf16[16,448,128]{2,1,0:T(8,128)(2,1)S(1)}, bf16[16,448,128]{2,1,0:T(8,128)(2,1)S(1)}, u32[]{:S(2)}, u32[]{:S(2)}) %collective-permute-start) | collective-permute-done | bytes 1835040 | tf_op jit(solution)/shard_map/ppermute | solution.py:99
  31.8 0.0 copy-start.3
  31.8 1.3 copy-done.3
  33.0 1.1 broadcast_in_dim.22.coef_ref
  34.1 0.0 copy-done.2
  34.1 10.4 %shard_map.64 = bf16[32,448,128]{2,1,0:T(8,128)(2,1)} custom-call(bf16[32,448,128]{2,1,0:T(8,128)(2,1)} %bitcast.85, bf16[16,448,128]{2,1,0:T(8,128)(2,1)} %copy-done.3, bf16[16,448,128]{2,1,0:T(8,128)(2,1)} %copy-done.2, f32[3,448,128]{2,1,0:T(8,128)} %broadcast_in_dim.22.coef_ref, f32[32,128]{1,0:T(8,128)} %bitcast.92), custom_call_target="tpu_custom_call" | custom-call | flops 55050240 | bytes 7340032 | tf_op jit(solution)/shard_map/pallas_call | solution.py:62
  44.5 7.1 %all-to-all-start = ((bf16[16,2,448,128]{3,2,1,0:T(8,128)(2,1)}), bf16[16,2,448,128]{3,2,1,0:T(8,128)(2,1)}, u32[]{:S(2)}, u32[]{:S(2)}) async-start(bf16[16,2,448,128]{3,2,1,0:T(8,128)(2,1)} %bitcast.88), calls=%async_computation | async-start | bytes 7340032 | tf_op jit(solution)/shard_map/all_to_all | solution.py:103
  51.6 0.0 copy-start.7
  51.6 10.4 %copy.24 = bf16[512,7168]{0,1:T(8,128)(2,1)} copy(bf16[512,7168]{1,0:T(8,128)(2,1)} %param.9) | data formatting | bytes 14680064 | tf_op args[3]
  62.0 38.0 %all-to-all-done = bf16[16,2,448,128]{3,2,1,0:T(8,128)(2,1)} async-done(((bf16[16,2,448,128]{3,2,1,0:T(8,128)(2,1)}), bf16[16,2,448,128]{3,2,1,0:T(8,128)(2,1)}, u32[]{:S(2)}, u32[]{:S(2)}) %all-to-all-start) | async-done | bytes 3670048 | tf_op jit(solution)/shard_map/all_to_all | solution.py:103
  100.0 0.0 copy-done.7
  100.0 13.4 %fusion.1 = bf16[16,2,448,128]{3,2,0,1:T(8,128)(2,1)} fusion(bf16[16,2,448,128]{3,2,1,0:T(8,128)(2,1)} %all-to-all-done, f32[2,128]{1,0:T(2,128)S(1)} %constant_dynamic-slice_fusion, bf16[16,448,512,1]{2,1,0,3:T(8,128)(2,1)} %bitcast.82, bf16[512,16,448,1]{0,2,3,1:T(8,128)(2,1)} %bitcast.80, f32[512]{0:T(512)S(1)} %copy-done.7), kind=kOutput, calls=%fused_computation.3 | convolution fusion | flops 3765698560 | bytes 22023168 | tf_op jit(solution)/shard_map/svk,krx->srvx/dot_general | solution.py:106
  113.4 2.3 copy.27
  115.7 52.9 %all_to_all.20 = bf16[16,2,448,128]{3,2,1,0:T(8,128)(2,1)S(1)} all-to-all(bf16[16,2,448,128]{3,2,1,0:T(8,128)(2,1)S(1)} %copy.27), channel_id=1, replica_groups=mesh['space'=8,'vel'=16] {'vel'}, dimensions={0} | all-to-all | bytes 7340032 | tf_op jit(solution)/shard_map/all_to_all | solution.py:108
  168.6 0.0 copy-start.1
  168.6 0.3 fusion.18
  168.9 1.5 copy-done.1
  170.4 1.9 collective-permute-start.2
  172.3 3.6 %collective-permute-start.3 = (bf16[16,448,128]{2,1,0:T(8,128)(2,1)S(1)}, bf16[16,448,128]{2,1,0:T(8,128)(2,1)S(1)}, u32[]{:S(2)}, u32[]{:S(2)}) collective-permute-start(bf16[16,448,128]{2,1,0:T(8,128)(2,1)S(1)} %bitcast.90), channel_id=1, source_target_pairs={{16,0},{32,16},{48,32},{64,48},{80,64},{96,80},{112,96},{17,1},{33... | collective-permute-start | bytes 5505032 | tf_op jit(solution)/shard_map/ppermute | solution.py:100
  176.0 19.0 %collective-permute-done.2.lo_ref = bf16[16,448,128]{2,1,0:T(8,128)(2,1)S(1)} collective-permute-done((bf16[16,448,128]{2,1,0:T(8,128)(2,1)S(1)}, bf16[16,448,128]{2,1,0:T(8,128)(2,1)S(1)}, u32[]{:S(2)}, u32[]{:S(2)}) %collective-permute-start.2) | collective-permute-done | bytes 1835040 | tf_op jit(solution)/shard_map/ppermute | solution.py:99
  194.9 0.0 copy-start.4
  194.9 1.8 collective-permute-done.3.hi_ref
  196.7 0.0 copy-start.5
  196.7 1.2 copy-done.5
  197.9 0.0 copy-done.4
  197.9 10.4 %shard_map.65 = bf16[32,448,128]{2,1,0:T(8,128)(2,1)} custom-call(bf16[32,448,128]{2,1,0:T(8,128)(2,1)} %bitcast.86, bf16[16,448,128]{2,1,0:T(8,128)(2,1)} %copy-done.4, bf16[16,448,128]{2,1,0:T(8,128)(2,1)} %copy-done.5, f32[3,448,128]{2,1,0:T(8,128)} %broadcast_in_dim.22.coef_ref, f32[32,128]{1,0:T(8,128)} %bitcast.93), custom_call_target="tpu_custom_call" | custom-call | flops 55050240 | bytes 7340032 | tf_op jit(solution)/shard_map/pallas_call | solution.py:62
  208.3 48.9 %all_to_all.21 = bf16[16,2,448,128]{3,2,1,0:T(8,128)(2,1)} all-to-all(bf16[16,2,448,128]{3,2,1,0:T(8,128)(2,1)} %bitcast.89), channel_id=1, replica_groups=mesh['space'=8,'vel'=16] {'vel'}, dimensions={0} | all-to-all | bytes 7340032 | tf_op jit(solution)/shard_map/all_to_all | solution.py:103
  257.2 13.4 %fusion = bf16[16,2,448,128]{3,2,0,1:T(8,128)(2,1)} fusion(bf16[16,2,448,128]{3,2,1,0:T(8,128)(2,1)} %all_to_all.21, f32[2,128]{1,0:T(2,128)S(1)} %constant_dynamic-slice_fusion, bf16[16,448,512,1]{2,1,0,3:T(8,128)(2,1)} %bitcast.83, bf16[512,16,448,1]{0,2,3,1:T(8,128)(2,1)} %bitcast.81, f32[512]{0:T(512)S(1)} %copy-done.7), kind=kOutput, calls=%fused_computation.1 | convolution fusion | flops 3765698560 | bytes 22023168 | tf_op jit(solution)/shard_map/svk,krx->srvx/dot_general | solution.py:106
  270.6 2.3 copy.31
  272.9 46.5 %all_to_all.22 = bf16[16,2,448,128]{3,2,1,0:T(8,128)(2,1)S(1)} all-to-all(bf16[16,2,448,128]{3,2,1,0:T(8,128)(2,1)S(1)} %copy.31), channel_id=1, replica_groups=mesh['space'=8,'vel'=16] {'vel'}, dimensions={0} | all-to-all | bytes 7340032 | tf_op jit(solution)/shard_map/all_to_all | solution.py:108
  319.4 4.2 %copy.32 = bf16[448,2,16,128]{3,2,1,0:T(8,128)(2,1)} copy(bf16[448,2,16,128]{3,0,2,1:T(8,128)(2,1)S(1)} %bitcast.87) | data formatting | bytes 7340032 | tf_op jit(solution)/shard_map/transpose | solution.py:110
  (4 shorter events, 0.1 us)
Async XLA Ops:
  3.5 1.8 copy-start
  3.5 6.2 %copy-start.8 = (s32[448]{0:T(512)S(1)}, s32[448]{0:T(512)}, u32[]{:S(2)}) copy-start(s32[448]{0:T(512)} %param.7) | copy-start | bytes 5380
  3.5 6.2 %copy-start.6 = (s32[2,16,128]{2,1,0:T(8,128)S(1)}, s32[2,16,128]{2,1,0:T(8,128)}, u32[]{:S(2)}) copy-start(s32[2,16,128]{2,1,0:T(8,128)} %param.8) | copy-start | bytes 49156
  5.3 22.6 %collective-permute-start.1 = (bf16[16,448,128]{2,1,0:T(8,128)(2,1)S(1)}, bf16[16,448,128]{2,1,0:T(8,128)(2,1)S(1)}, u32[]{:S(2)}, u32[]{:S(2)}) collective-permute-start(bf16[16,448,128]{2,1,0:T(8,128)(2,1)S(1)} %get-tuple-element.7), channel_id=1, source_target_pairs={{16,0},{32,16},{48,32},{64,48},{80,64},{96,80},{112,96},{17,1},{33... | collective-permute-start | bytes 5505032 | tf_op jit(solution)/shard_map/ppermute | solution.py:100
  7.2 24.5 %collective-permute-start = (bf16[16,448,128]{2,1,0:T(8,128)(2,1)S(1)}, bf16[16,448,128]{2,1,0:T(8,128)(2,1)S(1)}, u32[]{:S(2)}, u32[]{:S(2)}) collective-permute-start(bf16[16,448,128]{2,1,0:T(8,128)(2,1)S(1)} %get-tuple-element.8), channel_id=1, source_target_pairs={{0,16},{16,32},{32,48},{48,64},{64,80},{80,96},{96,112},{1,17},{17... | collective-permute-start | bytes 5505032 | tf_op jit(solution)/shard_map/ppermute | solution.py:99
  27.9 6.2 %copy-start.2 = (bf16[16,448,128]{2,1,0:T(8,128)(2,1)}, bf16[16,448,128]{2,1,0:T(8,128)(2,1)S(1)}, u32[]{:S(2)}) copy-start(bf16[16,448,128]{2,1,0:T(8,128)(2,1)S(1)} %collective-permute-done.1.hi_ref) | copy-start | bytes 5505028
  31.8 1.3 copy-start.3
  44.5 55.5 %all-to-all-start = ((bf16[16,2,448,128]{3,2,1,0:T(8,128)(2,1)}), bf16[16,2,448,128]{3,2,1,0:T(8,128)(2,1)}, u32[]{:S(2)}, u32[]{:S(2)}) async-start(bf16[16,2,448,128]{3,2,1,0:T(8,128)(2,1)} %bitcast.88), calls=%async_computation | async-start | bytes 7340032 | tf_op jit(solution)/shard_map/all_to_all | solution.py:103
  51.6 48.4 %copy-start.7 = (f32[512]{0:T(512)S(1)}, f32[512]{0:T(512)}, u32[]{:S(2)}) copy-start(f32[512]{0:T(512)} %param.11) | copy-start | bytes 6148
  168.6 1.8 copy-start.1
  170.4 24.5 %collective-permute-start.2 = (bf16[16,448,128]{2,1,0:T(8,128)(2,1)S(1)}, bf16[16,448,128]{2,1,0:T(8,128)(2,1)S(1)}, u32[]{:S(2)}, u32[]{:S(2)}) collective-permute-start(bf16[16,448,128]{2,1,0:T(8,128)(2,1)S(1)} %bitcast.91), channel_id=1, source_target_pairs={{0,16},{16,32},{32,48},{48,64},{64,80},{80,96},{96,112},{1,17},{17... | collective-permute-start | bytes 5505032 | tf_op jit(solution)/shard_map/ppermute | solution.py:99
  172.3 24.4 %collective-permute-start.3 = (bf16[16,448,128]{2,1,0:T(8,128)(2,1)S(1)}, bf16[16,448,128]{2,1,0:T(8,128)(2,1)S(1)}, u32[]{:S(2)}, u32[]{:S(2)}) collective-permute-start(bf16[16,448,128]{2,1,0:T(8,128)(2,1)S(1)} %bitcast.90), channel_id=1, source_target_pairs={{16,0},{32,16},{48,32},{64,48},{80,64},{96,80},{112,96},{17,1},{33... | collective-permute-start | bytes 5505032 | tf_op jit(solution)/shard_map/ppermute | solution.py:100
  194.9 3.0 copy-start.4
  196.7 1.2 copy-start.5

commit v2 on v1

--- a/solution.py
+++ b/solution.py
@@ -88,9 +88,9 @@
     coef = jnp.broadcast_to(jnp.stack([comp_x, comp_y, comp_z])[:, :, None], (3, vb, nx))
     tm = (cell_mask != 1).astype(jnp.float32).reshape(rows, nx)
     cmask = jnp.where(cell_mask == 0, 1.0, jnp.where(cell_mask == 2, 0.5, 0.0)).astype(jnp.float32)
-    cm = lax.dynamic_slice_in_dim(cmask.reshape(rows, nx), lax.axis_index("vel") * chunk, chunk, 0)
+    cm_all = cmask.reshape(rows, nx)
     w3 = w_modes.reshape(kmodes, groups, vb)
-    e3 = e_modes.reshape(groups, vb, kmodes)
+    e_local = lax.dynamic_slice_in_dim(e_modes, lax.axis_index("vel") * vb, vb, 0)
     up = [(i, i + 1) for i in range(spaces - 1)]
     down = [(i + 1, i) for i in range(spaces - 1)]
 
@@ -103,10 +103,9 @@
         recv = lax.all_to_all(send, "vel", 0, 0, tiled=True)
         moments = jnp.einsum("ksv,srvx->krx", w3, recv, preferred_element_type=jnp.float32)
         delta = (rates[:, None, None] * moments).astype(jnp.bfloat16)
-        adjustment = jnp.einsum("svk,krx->srvx", e3, delta, preferred_element_type=jnp.float32)
-        post = (recv.astype(jnp.float32) - cm[None, :, None, :] * adjustment).astype(jnp.bfloat16)
-        back = lax.all_to_all(post, "vel", 0, 0, tiled=True)
-        f = back.reshape(rows, vb, nx)
+        delta_all = lax.all_gather(delta, "vel", axis=1, tiled=True)
+        adjustment = jnp.einsum("vk,kwx->wvx", e_local, delta_all, preferred_element_type=jnp.float32)
+        f = (half.astype(jnp.float32) - cm_all[:, None, :] * adjustment).astype(jnp.bfloat16)
     return jnp.transpose(f.reshape(nzl, ny, vb, nx), (2, 0, 1, 3))
 
 

time: 325 us -> 336 us (1.034)
  waiting for transfers between devices: 80.1 us -> 184 us
  blocking collectives: 148 us -> 50.1 us
  between operations: 0.15 us -> 13.6 us
  matrix products: 26.8 us -> 22.5 us
  local copies, waits for them, and re-layouts: 30 us -> 25.8 us
    all_gather x0 -> x2, waiting for transfers between devices: none -> 103 us  [per_device(): delta_all = lax.all_gather(delta, 'vel', axis=1, tiled=True)]
    all_to_all x2 -> x0, blocking collectives: 99.4 us -> none  [per_device(): back = lax.all_to_all(post, 'vel', 0, 0, tiled=True)]
    ppermute x2, waiting for transfers between devices: 19.4 us -> 35.9 us  [per_device(): hi = lax.ppermute(f[:ny], 'space', down)]
    ppermute x2, waiting for transfers between devices: 22.8 us -> 7.75 us  [per_device(): lo = lax.ppermute(f[rows - ny:], 'space', up)]
    dot_general x2 -> x4, matrix products: 26.8 us -> 22.5 us  [the longest x2 11.4 us: per_device(): jnp.einsum('ksv,srvx->krx', w3, recv, preferred_element_type=jnp.float32)]
    reshape x0 -> x1, local copies, waits for them, and re-layouts: none -> 4.2 us  [per_device(): return jnp.transpose(f.reshape(nzl, ny, vb, nx), (2, 0, 1, 3))]
    transpose x1 -> x0, local copies, waits for them, and re-layouts: 4.2 us -> none  [per_device(): return jnp.transpose(f.reshape(nzl, ny, vb, nx), (2, 0, 1, 3))]
    unnamed x20 -> x18, local copies, waits for them, and re-layouts: 19.5 us -> 18.3 us
  transfers between devices with their start and end apart: 5 -> 7, of which waited for: 5 -> 7; matrix products, arithmetic and copies ran while one was open for 3% -> 3% of each run, Pallas kernels for 0% -> 0%
where the time goes in v2:
time: 336 us; the launch traced here: 334 us
  waiting for transfers between devices  184 us (55%)
  blocking collectives  50.1 us (15%)
  local copies, waits for them, and re-layouts  25.8 us (8%)
  matrix products  22.5 us (7%)
  Pallas kernels  20.7 us (6%)
  starting transfers between devices  15.8 us (5%)
  between operations  13.6 us (4%)
    all_gather x2, waiting for transfers between devices, per_device(): delta_all = lax.all_gather(delta, 'vel', axis=1, tiled=True)  103 us
    all_to_all x1, blocking collectives, per_device(): recv = lax.all_to_all(send, 'vel', 0, 0, tiled=True)  50.1 us
    all_to_all x1, waiting for transfers between devices, per_device(): recv = lax.all_to_all(send, 'vel', 0, 0, tiled=True)  37.9 us
    ppermute x2, waiting for transfers between devices, per_device(): hi = lax.ppermute(f[:ny], 'space', down)  35.9 us
    pallas_call x2, Pallas kernels, transport(): pl.pallas_call(functools.partial(transport_kernel, ny), out_shape=jax.Sha...  20.7 us
    unnamed x18, local copies, waits for them, and re-layouts  18.3 us
    dot_general x2, matrix products, per_device(): jnp.einsum('ksv,srvx->krx', w3, recv, preferred_element_type=jnp.float32)  11.4 us
    dot_general x2, matrix products, per_device(): jnp.einsum('vk,kwx->wvx', e_local, delta_all, preferred_element_type=jnp....  11.1 us
  transfers between devices with their start and end apart: 7, of which 7 were waited for; matrix products, arithmetic and copies ran while one was open for 3% of the time, Pallas kernels for 0%

profile of v2, /device:TPU:32, one launch (start us, length us, event | category | flops | bytes accessed | tf_op | source)
XLA Modules:
  0.0 333.6 jit_solution(6243719911642286940)
XLA Ops:
  6.5 3.5 %copy.22 = bf16[448,2,16,128]{3,0,2,1:T(8,128)(2,1)S(1)} copy(bf16[448,2,16,128]{3,2,1,0:T(8,128)(2,1)} %param.6) | data formatting | bytes 7340032 | tf_op args[0]
  10.0 0.0 copy-start
  10.0 0.0 copy-start.7
  10.0 0.0 copy-start.5
  10.0 0.2 slice_bitcast_fusion
  10.3 1.6 copy-done
  11.8 1.9 collective-permute-start.1
  13.7 2.4 collective-permute-start
  16.2 0.0 copy-done.7
  16.2 0.0 copy-done.5
  16.2 0.6 compare_convert_fusion
  16.8 17.6 %collective-permute-done.1.hi_ref = bf16[16,448,128]{2,1,0:T(8,128)(2,1)S(1)} collective-permute-done((bf16[16,448,128]{2,1,0:T(8,128)(2,1)S(1)}, bf16[16,448,128]{2,1,0:T(8,128)(2,1)S(1)}, u32[]{:S(2)}, u32[]{:S(2)}) %collective-permute-start.1) | collective-permute-done | bytes 1835040 | tf_op jit(solution)/shard_map/ppermute | solution.py:100
  34.5 0.0 copy-start.2
  34.5 3.8 %collective-permute-done.lo_ref = bf16[16,448,128]{2,1,0:T(8,128)(2,1)S(1)} collective-permute-done((bf16[16,448,128]{2,1,0:T(8,128)(2,1)S(1)}, bf16[16,448,128]{2,1,0:T(8,128)(2,1)S(1)}, u32[]{:S(2)}, u32[]{:S(2)}) %collective-permute-start) | collective-permute-done | bytes 1835040 | tf_op jit(solution)/shard_map/ppermute | solution.py:99
  38.3 0.0 copy-start.3
  38.3 1.3 copy-done.3
  39.6 1.1 broadcast_in_dim.20.coef_ref
  40.7 0.0 copy-done.2
  40.7 10.3 %shard_map.64 = bf16[32,448,128]{2,1,0:T(8,128)(2,1)} custom-call(bf16[32,448,128]{2,1,0:T(8,128)(2,1)} %bitcast.67, bf16[16,448,128]{2,1,0:T(8,128)(2,1)} %copy-done.3, bf16[16,448,128]{2,1,0:T(8,128)(2,1)} %copy-done.2, f32[3,448,128]{2,1,0:T(8,128)} %broadcast_in_dim.20.coef_ref, f32[32,128]{1,0:T(8,128)} %bitcast.71), custom_call_target="tpu_custom_call" | custom-call | flops 55050240 | bytes 7340032 | tf_op jit(solution)/shard_map/pallas_call | solution.py:62
  51.0 7.1 %all-to-all-start = ((bf16[16,2,448,128]{3,2,1,0:T(8,128)(2,1)}), bf16[16,2,448,128]{3,2,1,0:T(8,128)(2,1)}, u32[]{:S(2)}, u32[]{:S(2)}) async-start(bf16[16,2,448,128]{3,2,1,0:T(8,128)(2,1)} %bitcast.68), calls=%async_computation | async-start | bytes 7340032 | tf_op jit(solution)/shard_map/all_to_all | solution.py:103
  58.1 0.0 copy-start.6
  58.1 0.0 all-gather.3.cloned.1.call-start
  58.2 10.4 %copy.13 = bf16[512,7168]{0,1:T(8,128)(2,1)} copy(bf16[512,7168]{1,0:T(8,128)(2,1)} %param.9) | data formatting | bytes 14680064 | tf_op args[3]
  68.6 37.9 %all-to-all-done = bf16[16,2,448,128]{3,2,1,0:T(8,128)(2,1)} async-done(((bf16[16,2,448,128]{3,2,1,0:T(8,128)(2,1)}), bf16[16,2,448,128]{3,2,1,0:T(8,128)(2,1)}, u32[]{:S(2)}, u32[]{:S(2)}) %all-to-all-start) | async-done | bytes 3670048 | tf_op jit(solution)/shard_map/all_to_all | solution.py:103
  106.5 0.0 copy-done.6
  106.5 6.3 %fusion.6 = bf16[512,2,128]{0,2,1:T(8,128)(2,1)S(1)} fusion(bf16[16,2,448,128]{3,2,1,0:T(8,128)(2,1)} %all-to-all-done, bf16[512,16,448,1]{0,2,3,1:T(8,128)(2,1)} %bitcast.64, f32[512]{0:T(512)S(1)} %copy-done.6), kind=kOutput, calls=%fused_computation.13 | convolution fusion | flops 1879310336 | bytes 11274240 | tf_op jit(solution)/shard_map/ksv,srvx->krx/dot_general | solution.py:104
  112.8 0.8 copy.14
  113.6 0.0 all-gather.3.cloned.1.call-update
  113.7 0.0 all-gather.5.cloned.1.call-start
  113.7 53.7 %all-gather.3.cloned.1.call-done = bf16[512,32,128]{2,0,1:T(8,128)(2,1)} async-done(((bf16[512,2,128]{2,0,1:T(8,128)(2,1)}), bf16[512,32,128]{2,0,1:T(8,128)(2,1)}) %all-gather.3.cloned.1.call-update) | async-done | bytes 4194320 | tf_op jit(solution)/shard_map/all_gather | solution.py:106
  167.4 5.5 %fusion.1.f_ref = bf16[32,448,128]{2,1,0:T(8,128)(2,1)S(1)} fusion(bf16[32,448,128]{2,1,0:T(8,128)(2,1)} %shard_map.64, f32[32,128]{1,0:T(8,128)S(1)} %bitcast.73, bf16[512,32,128]{2,0,1:T(8,128)(2,1)} %all-gather.3.cloned.1.call-done, bf16[7168,512]{1,0:T(8,128)(2,1)} %param.10, s32[]{:T(128)S(6)} %select_n.36), kind=kOutput, calls=%fused_computation.3 | convolution fusion | flops 1886388224 | bytes 12009476 | tf_op jit(solution)/shard_map/vk,kwx->wvx/dot_general | solution.py:107
  173.0 0.0 copy-start.1
  173.0 0.2 fusion.22
  173.2 1.6 copy-done.1
  174.8 1.9 collective-permute-start.3
  176.7 2.4 collective-permute-start.2
  179.1 18.3 %collective-permute-done.3.hi_ref = bf16[16,448,128]{2,1,0:T(8,128)(2,1)S(1)} collective-permute-done((bf16[16,448,128]{2,1,0:T(8,128)(2,1)S(1)}, bf16[16,448,128]{2,1,0:T(8,128)(2,1)S(1)}, u32[]{:S(2)}, u32[]{:S(2)}) %collective-permute-start.3) | collective-permute-done | bytes 1835040 | tf_op jit(solution)/shard_map/ppermute | solution.py:100
  197.4 0.0 copy-start.4
  197.4 3.9 %collective-permute-done.2.lo_ref = bf16[16,448,128]{2,1,0:T(8,128)(2,1)} collective-permute-done((bf16[16,448,128]{2,1,0:T(8,128)(2,1)S(1)}, bf16[16,448,128]{2,1,0:T(8,128)(2,1)}, u32[]{:S(2)}, u32[]{:S(2)}) %collective-permute-start.2) | collective-permute-done | bytes 1835040 | tf_op jit(solution)/shard_map/ppermute | solution.py:99
  201.4 0.0 copy-done.4
  201.4 10.4 %shard_map.65 = bf16[32,448,128]{2,1,0:T(8,128)(2,1)} custom-call(bf16[32,448,128]{2,1,0:T(8,128)(2,1)} %copy-done.1, bf16[16,448,128]{2,1,0:T(8,128)(2,1)} %collective-permute-done.2.lo_ref, bf16[16,448,128]{2,1,0:T(8,128)(2,1)} %copy-done.4, f32[3,448,128]{2,1,0:T(8,128)} %broadcast_in_dim.20.coef_ref, f32[32,128]{1,0:T(8,128)} %bitcast.72), custom_call_target="tpu_custom_call" | custom-call | flops 55050240 | bytes 7340032 | tf_op jit(solution)/shard_map/pallas_call | solution.py:62
  211.7 50.1 %all_to_all.10 = bf16[16,2,448,128]{3,2,1,0:T(8,128)(2,1)S(1)} all-to-all(bf16[16,2,448,128]{3,2,1,0:T(8,128)(2,1)} %bitcast.69), channel_id=1, replica_groups=mesh['space'=8,'vel'=16] {'vel'}, dimensions={0} | all-to-all | bytes 7340032 | tf_op jit(solution)/shard_map/all_to_all | solution.py:103
  261.9 5.2 %fusion.7 = bf16[512,2,128]{0,2,1:T(8,128)(2,1)S(1)} fusion(bf16[16,2,448,128]{3,2,1,0:T(8,128)(2,1)S(1)} %all_to_all.10, bf16[512,16,448,1]{0,2,3,1:T(8,128)(2,1)} %bitcast.65, f32[512]{0:T(512)S(1)} %copy-done.6), kind=kOutput, calls=%fused_computation.14 | convolution fusion | flops 1879310336 | bytes 11274240 | tf_op jit(solution)/shard_map/ksv,srvx->krx/dot_general | solution.py:104
  267.0 0.8 copy.15
  267.9 0.0 all-gather.5.cloned.1.call-update
  267.9 49.1 %all-gather.5.cloned.1.call-done = bf16[512,32,128]{2,0,1:T(8,128)(2,1)} async-done(((bf16[512,2,128]{2,0,1:T(8,128)(2,1)}), bf16[512,32,128]{2,0,1:T(8,128)(2,1)}) %all-gather.5.cloned.1.call-update) | async-done | bytes 4194320 | tf_op jit(solution)/shard_map/all_gather | solution.py:106
  317.0 5.5 %fusion = bf16[32,448,128]{2,1,0:T(8,128)(2,1)S(1)} fusion(bf16[32,448,128]{2,1,0:T(8,128)(2,1)} %shard_map.65, f32[32,128]{1,0:T(8,128)S(1)} %bitcast.74, bf16[512,32,128]{2,0,1:T(8,128)(2,1)} %all-gather.5.cloned.1.call-done, bf16[7168,512]{1,0:T(8,128)(2,1)} %param.10, s32[]{:T(128)S(6)} %select_n.36), kind=kOutput, calls=%fused_computation.1 | convolution fusion | flops 1886388224 | bytes 12009476 | tf_op jit(solution)/shard_map/vk,kwx->wvx/dot_general | solution.py:107
  322.5 4.2 %copy.21 = bf16[2,16,448,128]{3,1,0,2:T(8,128)(2,1)} copy(bf16[2,16,448,128]{3,2,1,0:T(8,128)(2,1)S(1)} %bitcast.70) | data formatting | bytes 7340032 | tf_op jit(solution)/shard_map/reshape | solution.py:109
  (3 shorter events, 0.0 us)
Async XLA Ops:
  10.0 1.8 copy-start
  10.0 6.2 %copy-start.7 = (s32[448]{0:T(512)S(1)}, s32[448]{0:T(512)}, u32[]{:S(2)}) copy-start(s32[448]{0:T(512)} %param.7) | copy-start | bytes 5380
  10.0 6.2 %copy-start.5 = (s32[2,16,128]{2,1,0:T(8,128)S(1)}, s32[2,16,128]{2,1,0:T(8,128)}, u32[]{:S(2)}) copy-start(s32[2,16,128]{2,1,0:T(8,128)} %param.8) | copy-start | bytes 49156
  11.8 22.6 %collective-permute-start.1 = (bf16[16,448,128]{2,1,0:T(8,128)(2,1)S(1)}, bf16[16,448,128]{2,1,0:T(8,128)(2,1)S(1)}, u32[]{:S(2)}, u32[]{:S(2)}) collective-permute-start(bf16[16,448,128]{2,1,0:T(8,128)(2,1)S(1)} %get-tuple-element.7), channel_id=1, source_target_pairs={{16,0},{32,16},{48,32},{64,48},{80,64},{96,80},{112,96},{17,1},{33... | collective-permute-start | bytes 5505032 | tf_op jit(solution)/shard_map/ppermute | solution.py:100
  13.7 24.5 %collective-permute-start = (bf16[16,448,128]{2,1,0:T(8,128)(2,1)S(1)}, bf16[16,448,128]{2,1,0:T(8,128)(2,1)S(1)}, u32[]{:S(2)}, u32[]{:S(2)}) collective-permute-start(bf16[16,448,128]{2,1,0:T(8,128)(2,1)S(1)} %get-tuple-element.8), channel_id=1, source_target_pairs={{0,16},{16,32},{32,48},{48,64},{64,80},{80,96},{96,112},{1,17},{17... | collective-permute-start | bytes 5505032 | tf_op jit(solution)/shard_map/ppermute | solution.py:99
  34.5 6.2 %copy-start.2 = (bf16[16,448,128]{2,1,0:T(8,128)(2,1)}, bf16[16,448,128]{2,1,0:T(8,128)(2,1)S(1)}, u32[]{:S(2)}) copy-start(bf16[16,448,128]{2,1,0:T(8,128)(2,1)S(1)} %collective-permute-done.1.hi_ref) | copy-start | bytes 5505028
  38.3 1.3 copy-start.3
  51.0 55.5 %all-to-all-start = ((bf16[16,2,448,128]{3,2,1,0:T(8,128)(2,1)}), bf16[16,2,448,128]{3,2,1,0:T(8,128)(2,1)}, u32[]{:S(2)}, u32[]{:S(2)}) async-start(bf16[16,2,448,128]{3,2,1,0:T(8,128)(2,1)} %bitcast.68), calls=%async_computation | async-start | bytes 7340032 | tf_op jit(solution)/shard_map/all_to_all | solution.py:103
  58.1 48.4 %copy-start.6 = (f32[512]{0:T(512)S(1)}, f32[512]{0:T(512)}, u32[]{:S(2)}) copy-start(f32[512]{0:T(512)} %param.11) | copy-start | bytes 6148
  58.1 109.3 %all-gather.3.cloned.1.call-start = ((), (), s32[]{:S(2)}) async-start(), calls=%async_computation.2 | async-start | bytes 4456448 | tf_op jit(solution)/shard_map/all_gather | solution.py:106
  113.7 203.3 %all-gather.5.cloned.1.call-start = ((), (), s32[]{:S(2)}) async-start(), calls=%async_computation.3 | async-start | bytes 4456448 | tf_op jit(solution)/shard_map/all_gather | solution.py:106
  173.0 1.8 copy-start.1
  174.8 22.6 %collective-permute-start.3 = (bf16[16,448,128]{2,1,0:T(8,128)(2,1)S(1)}, bf16[16,448,128]{2,1,0:T(8,128)(2,1)S(1)}, u32[]{:S(2)}, u32[]{:S(2)}) collective-permute-start(bf16[16,448,128]{2,1,0:T(8,128)(2,1)S(1)} %get-tuple-element.5), channel_id=1, source_target_pairs={{16,0},{32,16},{48,32},{64,48},{80,64},{96,80},{112,96},{17,1},{33... | collective-permute-start | bytes 5505032 | tf_op jit(solution)/shard_map/ppermute | solution.py:100
  176.7 24.7 %collective-permute-start.2 = (bf16[16,448,128]{2,1,0:T(8,128)(2,1)S(1)}, bf16[16,448,128]{2,1,0:T(8,128)(2,1)}, u32[]{:S(2)}, u32[]{:S(2)}) collective-permute-start(bf16[16,448,128]{2,1,0:T(8,128)(2,1)S(1)} %get-tuple-element.6), channel_id=1, source_target_pairs={{0,16},{16,32},{32,48},{48,64},{64,80},{80,96},{96,112},{1,17},{17... | collective-permute-start | bytes 5505032 | tf_op jit(solution)/shard_map/ppermute | solution.py:99
  197.4 3.9 %copy-start.4 = (bf16[16,448,128]{2,1,0:T(8,128)(2,1)}, bf16[16,448,128]{2,1,0:T(8,128)(2,1)S(1)}, u32[]{:S(2)}) copy-start(bf16[16,448,128]{2,1,0:T(8,128)(2,1)S(1)} %collective-permute-done.3.hi_ref) | copy-start | bytes 5505028
Sparse Core Ops, SparseCore 0:
  113.8 53.5 all-gather.2
  268.0 48.9 all-gather.4

commit v3 on v1

--- a/solution.py
+++ b/solution.py
@@ -9,7 +9,8 @@
 
 VGRID = 24
 STEPS = 2
-VBLOCK = 64
+VBLOCK = 32
+PARTS = 2
 
 
 def components(vel_map):
@@ -84,6 +85,7 @@
     spaces = lax.axis_size("space")
     chunk = rows // groups
     kmodes = w_modes.shape[0]
+    part = vb // PARTS
     comp_x, comp_y, comp_z = components(vel_map)
     coef = jnp.broadcast_to(jnp.stack([comp_x, comp_y, comp_z])[:, :, None], (3, vb, nx))
     tm = (cell_mask != 1).astype(jnp.float32).reshape(rows, nx)
@@ -93,21 +95,30 @@
     e3 = e_modes.reshape(groups, vb, kmodes)
     up = [(i, i + 1) for i in range(spaces - 1)]
     down = [(i + 1, i) for i in range(spaces - 1)]
+    pieces = [slice(h * part, (h + 1) * part) for h in range(PARTS)]
 
-    f = jnp.transpose(dist, (1, 2, 0, 3)).reshape(rows, vb, nx)
+    whole = jnp.transpose(dist, (1, 2, 0, 3)).reshape(rows, vb, nx)
+    fs = [whole[:, p] for p in pieces]
     for step in range(STEPS):
-        lo = lax.ppermute(f[rows - ny :], "space", up)
-        hi = lax.ppermute(f[:ny], "space", down)
-        half = transport(f, lo, hi, coef, tm, ny)
-        send = half.reshape(groups, chunk, vb, nx)
-        recv = lax.all_to_all(send, "vel", 0, 0, tiled=True)
-        moments = jnp.einsum("ksv,srvx->krx", w3, recv, preferred_element_type=jnp.float32)
+        recvs = []
+        for h, p in enumerate(pieces):
+            f = fs[h]
+            lo = lax.ppermute(f[rows - ny :], "space", up)
+            hi = lax.ppermute(f[:ny], "space", down)
+            half = transport(f, lo, hi, coef[:, p], tm, ny)
+            recvs.append(lax.all_to_all(half.reshape(groups, chunk, part, nx), "vel", 0, 0, tiled=True))
+        moments = None
+        for h, p in enumerate(pieces):
+            term = jnp.einsum("ksv,srvx->krx", w3[:, :, p], recvs[h], preferred_element_type=jnp.float32)
+            moments = term if moments is None else moments + term
         delta = (rates[:, None, None] * moments).astype(jnp.bfloat16)
-        adjustment = jnp.einsum("svk,krx->srvx", e3, delta, preferred_element_type=jnp.float32)
-        post = (recv.astype(jnp.float32) - cm[None, :, None, :] * adjustment).astype(jnp.bfloat16)
-        back = lax.all_to_all(post, "vel", 0, 0, tiled=True)
-        f = back.reshape(rows, vb, nx)
-    return jnp.transpose(f.reshape(nzl, ny, vb, nx), (2, 0, 1, 3))
+        fs = []
+        for h, p in enumerate(pieces):
+            adjustment = jnp.einsum("svk,krx->srvx", e3[:, p], delta, preferred_element_type=jnp.float32)
+            post = (recvs[h].astype(jnp.float32) - cm[None, :, None, :] * adjustment).astype(jnp.bfloat16)
+            fs.append(lax.all_to_all(post, "vel", 0, 0, tiled=True).reshape(rows, part, nx))
+    whole = jnp.concatenate(fs, axis=1)
+    return jnp.transpose(whole.reshape(nzl, ny, vb, nx), (2, 0, 1, 3))
 
 
 def solution(mesh):

time: 325 us -> 321 us (0.988)
  blocking collectives: 148 us -> 31.7 us
  waiting for transfers between devices: 80.1 us -> 130 us
  starting transfers between devices: 16.9 us -> 57.1 us
  Pallas kernels: 20.7 us -> 29.1 us
  local copies, waits for them, and re-layouts: 30 us -> 38.1 us
  matrix products: 26.8 us -> 31 us
    all_to_all x3 -> x1, blocking collectives: 148 us -> 31.7 us  [per_device(): lax.all_to_all(post, 'vel', 0, 0, tiled=True).reshape(rows, part, nx)]
    all_to_all x1 -> x7, waiting for transfers between devices: 38 us -> 86.9 us  [the longest x3 47 us: per_device(): lax.all_to_all(post, 'vel', 0, 0, tiled=True).reshape(rows, part, nx)]
    all_to_all x1 -> x7, starting transfers between devices: 7.08 us -> 36.9 us  [the longest x4 25.3 us: per_device(): lax.all_to_all(half.reshape(groups, chunk, part, nx), 'vel', 0, 0, tiled=...]
    pallas_call x2 -> x4, Pallas kernels: 20.7 us -> 29.1 us  [transport(): pl.pallas_call(functools.partial(transport_kernel, ny), out_shape=jax.Sha...]
    ppermute x2 -> x4, starting transfers between devices: 4.31 us -> 10.6 us  [per_device(): lo = lax.ppermute(f[rows - ny:], 'space', up)]
    unnamed x20 -> x27, local copies, waits for them, and re-layouts: 19.5 us -> 14.6 us
    dot_general x2 -> x8, matrix products: 26.8 us -> 31 us  [the longest x4 17.2 us: per_device(): jnp.einsum('svk,krx->srvx', e3[:, p], delta, preferred_element_type=jnp.f...]
    convert_element_type x2 -> x4, local copies, waits for them, and re-layouts: 4.66 us -> 8.8 us  [per_device(): (recvs[h].astype(jnp.float32) - cm[None, :, None, :] * adjustment).astype...]
  transfers between devices with their start and end apart: 5 -> 15, of which waited for: 5 -> 14; matrix products, arithmetic and copies ran while one was open for 3% -> 9% of each run, Pallas kernels for 0% -> 7%
where the time goes in v3:
time: 321 us; the launch traced here: 319 us
  waiting for transfers between devices  130 us (40%)
  starting transfers between devices  57.1 us (18%)
  local copies, waits for them, and re-layouts  38.1 us (12%)
  blocking collectives  31.7 us (10%)
  matrix products  31 us (10%)
  Pallas kernels  29.1 us (9%)
    all_to_all x3, waiting for transfers between devices, per_device(): lax.all_to_all(post, 'vel', 0, 0, tiled=True).reshape(rows, part, nx)  47 us
    all_to_all x4, waiting for transfers between devices, per_device(): lax.all_to_all(half.reshape(groups, chunk, part, nx), 'vel', 0, 0, tiled=...  39.9 us
    all_to_all x1, blocking collectives, per_device(): lax.all_to_all(post, 'vel', 0, 0, tiled=True).reshape(rows, part, nx)  31.7 us
    pallas_call x4, Pallas kernels, transport(): pl.pallas_call(functools.partial(transport_kernel, ny), out_shape=jax.Sha...  29.1 us
    all_to_all x4, starting transfers between devices, per_device(): lax.all_to_all(half.reshape(groups, chunk, part, nx), 'vel', 0, 0, tiled=...  25.3 us
    ppermute x4, waiting for transfers between devices, per_device(): lo = lax.ppermute(f[rows - ny:], 'space', up)  25.2 us
    ppermute x4, waiting for transfers between devices, per_device(): hi = lax.ppermute(f[:ny], 'space', down)  18.2 us
    dot_general x4, matrix products, per_device(): jnp.einsum('svk,krx->srvx', e3[:, p], delta, preferred_element_type=jnp.f...  17.2 us
  transfers between devices with their start and end apart: 15, of which 14 were waited for; matrix products, arithmetic and copies ran while one was open for 9% of the time, Pallas kernels for 7%

profile of v3, /device:TPU:32, one launch (start us, length us, event | category | flops | bytes accessed | tf_op | source)
XLA Modules:
  0.0 318.7 jit_solution(9089114874180919903)
XLA Ops:
  0.0 3.5 %copy.42 = bf16[2,16,448,128]{3,2,1,0:T(8,128)(2,1)S(1)} copy(bf16[2,16,448,128]{3,1,0,2:T(8,128)(2,1)} %bitcast.151) | data formatting | bytes 7340032 | tf_op jit(solution)/shard_map/transpose | solution.py:100
  3.5 0.0 copy-start.11
  3.5 1.2 fusion.32
  4.7 1.9 collective-permute-start.3
  6.6 2.4 collective-permute-start.2
  9.1 0.1 fusion.36
  9.2 0.6 compare_convert_fusion
  9.8 2.1 fusion.33
  11.9 5.7 %collective-permute-done.3.hi_ref = bf16[16,224,128]{2,1,0:T(8,128)(2,1)S(1)} collective-permute-done((bf16[16,224,128]{2,1,0:T(8,128)(2,1)S(1)}, bf16[16,224,128]{2,1,0:T(8,128)(2,1)S(1)}, u32[]{:S(2)}, u32[]{:S(2)}) %collective-permute-start.3) | collective-permute-done | bytes 917536 | tf_op jit(solution)/shard_map/ppermute | solution.py:107
  17.5 3.8 %collective-permute-done.2.lo_ref = bf16[16,224,128]{2,1,0:T(8,128)(2,1)S(1)} collective-permute-done((bf16[16,224,128]{2,1,0:T(8,128)(2,1)S(1)}, bf16[16,224,128]{2,1,0:T(8,128)(2,1)S(1)}, u32[]{:S(2)}, u32[]{:S(2)}) %collective-permute-start.2) | collective-permute-done | bytes 917536 | tf_op jit(solution)/shard_map/ppermute | solution.py:106
  21.3 1.1 broadcast_in_dim.30.coef_ref
  22.4 0.0 copy-done.3
  22.4 7.3 %shard_map.65 = bf16[32,224,128]{2,1,0:T(8,128)(2,1)} custom-call(bf16[32,224,128]{2,1,0:T(8,128)(2,1)} %get-tuple-element.10.f_ref, bf16[16,224,128]{2,1,0:T(8,128)(2,1)} %copy-done.3, bf16[16,224,128]{2,1,0:T(8,128)(2,1)} %copy-done.2, f32[3,224,128]{2,1,0:T(8,128)} %broadcast_in_dim.30.coef_ref, f32[32,128]{1,0:T(8,128)} %bitcast.156), custom_call_target="tpu_custom_call" | custom-call | flops 27525120 | bytes 3670016 | tf_op jit(solution)/shard_map/pallas_call | solution.py:63
  29.7 7.0 %all-to-all-start.1 = ((bf16[16,2,224,128]{3,2,1,0:T(8,128)(2,1)}), bf16[16,2,224,128]{3,2,1,0:T(8,128)(2,1)S(1)}, u32[]{:S(2)}, u32[]{:S(2)}) async-start(bf16[16,2,224,128]{3,2,1,0:T(8,128)(2,1)} %bitcast.149), calls=%async_computation.1 | async-start | bytes 3670016 | tf_op jit(solution)/shard_map/all_to_all | solution.py:109
  36.8 1.9 collective-permute-start.1
  38.7 2.4 collective-permute-start
  41.1 8.8 %collective-permute-done.1.hi_ref = bf16[16,224,128]{2,1,0:T(8,128)(2,1)S(1)} collective-permute-done((bf16[16,224,128]{2,1,0:T(8,128)(2,1)}, bf16[16,224,128]{2,1,0:T(8,128)(2,1)S(1)}, u32[]{:S(2)}, u32[]{:S(2)}) %collective-permute-start.1) | collective-permute-done | bytes 917536 | tf_op jit(solution)/shard_map/ppermute | solution.py:107
  49.9 3.5 %collective-permute-done.lo_ref = bf16[16,224,128]{2,1,0:T(8,128)(2,1)S(1)} collective-permute-done((bf16[16,224,128]{2,1,0:T(8,128)(2,1)S(1)}, bf16[16,224,128]{2,1,0:T(8,128)(2,1)S(1)}, u32[]{:S(2)}, u32[]{:S(2)}) %collective-permute-start) | collective-permute-done | bytes 917536 | tf_op jit(solution)/shard_map/ppermute | solution.py:106
  53.4 0.9 copy-done.7
  54.3 0.9 broadcast_in_dim.26.coef_ref
  55.2 7.3 %shard_map.64 = bf16[32,224,128]{2,1,0:T(8,128)(2,1)} custom-call(bf16[32,224,128]{2,1,0:T(8,128)(2,1)} %get-tuple-element.9.f_ref, bf16[16,224,128]{2,1,0:T(8,128)(2,1)} %copy-done.7, bf16[16,224,128]{2,1,0:T(8,128)(2,1)} %copy-done.4, f32[3,224,128]{2,1,0:T(8,128)} %broadcast_in_dim.26.coef_ref, f32[32,128]{1,0:T(8,128)} %bitcast.157), custom_call_target="tpu_custom_call" | custom-call | flops 27525120 | bytes 3670016 | tf_op jit(solution)/shard_map/pallas_call | solution.py:63
  62.5 0.8 all-to-all-done.1
  63.3 6.5 %all-to-all-start = ((bf16[16,2,224,128]{3,2,1,0:T(8,128)(2,1)}), bf16[16,2,224,128]{3,2,1,0:T(8,128)(2,1)}, u32[]{:S(2)}, u32[]{:S(2)}) async-start(bf16[16,2,224,128]{3,2,1,0:T(8,128)(2,1)} %bitcast.148), calls=%async_computation | async-start | bytes 3670016 | tf_op jit(solution)/shard_map/all_to_all | solution.py:109
  69.8 10.4 %copy.44 = bf16[512,7168]{0,1:T(8,128)(2,1)} copy(bf16[512,7168]{1,0:T(8,128)(2,1)} %param.9) | data formatting | bytes 14680064 | tf_op args[3]
  80.2 3.2 fusion.12
  83.4 13.5 %all-to-all-done = bf16[16,2,224,128]{3,2,1,0:T(8,128)(2,1)} async-done(((bf16[16,2,224,128]{3,2,1,0:T(8,128)(2,1)}), bf16[16,2,224,128]{3,2,1,0:T(8,128)(2,1)}, u32[]{:S(2)}, u32[]{:S(2)}) %all-to-all-start) | async-done | bytes 1835040 | tf_op jit(solution)/shard_map/all_to_all | solution.py:109
  96.9 3.7 %fusion.23 = bf16[512,2,128,1]{0,2,3,1:T(8,128)(2,1)S(1)} fusion(f32[2,128,512]{2,1,0:T(8,128)S(1)} %fusion.12, bf16[16,2,224,128]{3,2,1,0:T(8,128)(2,1)} %all-to-all-done, bf16[512,16,448]{0,2,1:T(8,128)(2,1)} %bitcast.144, f32[512]{0:T(512)S(1)} %copy-done.12), kind=kOutput, calls=%fused_computation.32 | convolution fusion | flops 939917312 | bytes 6293504 | tf_op jit(solution)/shard_map/ksv,srvx->krx/dot_general | solution.py:112
  100.6 3.2 %fusion.11 = f32[2,128,16,224]{1,3,2,0:T(8,128)S(1)} fusion(bf16[512,2,128,1]{0,2,3,1:T(8,128)(2,1)S(1)} %fusion.23, bf16[16,448,512]{2,1,0:T(8,128)(2,1)} %bitcast.135), kind=kOutput, calls=%fused_computation.20 | convolution fusion | flops 939524096 | bytes 7602176 | tf_op jit(solution)/shard_map/svk,krx->srvx/dot_general | solution.py:117
  103.8 5.3 %fusion.3 = (bf16[16,2,224,128]{3,2,0,1:T(8,128)(2,1)}, bf16[16,2,224,128]{3,2,0,1:T(8,128)(2,1)S(1)}) fusion(bf16[16,2,224,128]{3,2,1,0:T(8,128)(2,1)} %all-to-all-done, f32[2,128]{1,0:T(2,128)S(1)} %constant_dynamic-slice_fusion, f32[2,128,16,224]{1,3,2,0:T(8,128)S(1)} %fusion.11, bf16[16,2,224,128]{3,2,1,0:T(8,128)(2,1)S(1)} %all-to-all-done.1, ...), kind=kOutput, calls=%fused_computation.12 | convolution fusion | flops 946864128 | bytes 14943232 | tf_op jit(solution)/shard_map/svk,krx->srvx/dot_general | solution.py:117
  109.2 1.5 copy.53
  110.7 3.7 %all-to-all-start.4 = ((bf16[16,2,224,128]{3,2,1,0:T(8,128)(2,1)}), bf16[16,2,224,128]{3,2,1,0:T(8,128)(2,1)S(1)}, u32[]{:S(2)}, u32[]{:S(2)}) async-start(bf16[16,2,224,128]{3,2,1,0:T(8,128)(2,1)} %copy.53), calls=%async_computation.4 | async-start | bytes 3670016 | tf_op jit(solution)/shard_map/all_to_all | solution.py:119
  114.5 2.9 copy.48
  117.4 22.0 %all-to-all-done.4 = bf16[16,2,224,128]{3,2,1,0:T(8,128)(2,1)S(1)} async-done(((bf16[16,2,224,128]{3,2,1,0:T(8,128)(2,1)}), bf16[16,2,224,128]{3,2,1,0:T(8,128)(2,1)S(1)}, u32[]{:S(2)}, u32[]{:S(2)}) %all-to-all-start.4) | async-done | bytes 1835040 | tf_op jit(solution)/shard_map/all_to_all | solution.py:119
  139.4 1.2 copy-done.1
  140.6 3.7 %all-to-all-start.2 = ((bf16[16,2,224,128]{3,2,1,0:T(8,128)(2,1)}), bf16[16,2,224,128]{3,2,1,0:T(8,128)(2,1)S(1)}, u32[]{:S(2)}, u32[]{:S(2)}) async-start(bf16[16,2,224,128]{3,2,1,0:T(8,128)(2,1)} %copy.48), calls=%async_computation.2 | async-start | bytes 3670016 | tf_op jit(solution)/shard_map/all_to_all | solution.py:119
  144.3 1.6 fusion.35
  145.9 1.9 collective-permute-start.6
  147.8 3.6 %collective-permute-start.7 = (bf16[16,224,128]{2,1,0:T(8,128)(2,1)S(1)}, bf16[16,224,128]{2,1,0:T(8,128)(2,1)S(1)}, u32[]{:S(2)}, u32[]{:S(2)}) collective-permute-start(bf16[16,224,128]{2,1,0:T(8,128)(2,1)S(1)} %bitcast.152), channel_id=1, source_target_pairs={{16,0},{32,16},{48,32},{64,48},{80,64},{96,80},{112,96},{17,1},{33... | collective-permute-start | bytes 2752520 | tf_op jit(solution)/shard_map/ppermute | solution.py:107
  151.5 9.1 %collective-permute-done.6.lo_ref = bf16[16,224,128]{2,1,0:T(8,128)(2,1)S(1)} collective-permute-done((bf16[16,224,128]{2,1,0:T(8,128)(2,1)S(1)}, bf16[16,224,128]{2,1,0:T(8,128)(2,1)S(1)}, u32[]{:S(2)}, u32[]{:S(2)}) %collective-permute-start.6) | collective-permute-done | bytes 917536 | tf_op jit(solution)/shard_map/ppermute | solution.py:106
  160.6 1.8 collective-permute-done.7.hi_ref
  162.4 1.0 copy-done.9
  163.4 7.3 %shard_map.67 = bf16[32,224,128]{2,1,0:T(8,128)(2,1)} custom-call(bf16[32,224,128]{2,1,0:T(8,128)(2,1)} %bitcast.140, bf16[16,224,128]{2,1,0:T(8,128)(2,1)} %copy-done.6, bf16[16,224,128]{2,1,0:T(8,128)(2,1)} %copy-done.9, f32[3,224,128]{2,1,0:T(8,128)} %broadcast_in_dim.30.coef_ref, f32[32,128]{1,0:T(8,128)} %bitcast.158), custom_call_target="tpu_custom_call" | custom-call | flops 27525120 | bytes 3670016 | tf_op jit(solution)/shard_map/pallas_call | solution.py:63
  170.7 7.2 %all-to-all-start.5 = ((bf16[16,2,224,128]{3,2,1,0:T(8,128)(2,1)}), bf16[16,2,224,128]{3,2,1,0:T(8,128)(2,1)}, u32[]{:S(2)}, u32[]{:S(2)}) async-start(bf16[16,2,224,128]{3,2,1,0:T(8,128)(2,1)} %bitcast.147), calls=%async_computation.5 | async-start | bytes 3670016 | tf_op jit(solution)/shard_map/all_to_all | solution.py:109
  177.9 0.1 fusion.34
  178.0 3.9 %collective-permute-start.4 = (bf16[16,224,128]{2,1,0:T(8,128)(2,1)S(1)}, bf16[16,224,128]{2,1,0:T(8,128)(2,1)S(1)}, u32[]{:S(2)}, u32[]{:S(2)}) collective-permute-start(bf16[16,224,128]{2,1,0:T(8,128)(2,1)S(1)} %bitcast.155), channel_id=1, source_target_pairs={{0,16},{16,32},{32,48},{48,64},{64,80},{80,96},{96,112},{1,17},{17... | collective-permute-start | bytes 2752520 | tf_op jit(solution)/shard_map/ppermute | solution.py:106
  181.9 2.1 collective-permute-start.5
  184.0 8.7 %collective-permute-done.4.lo_ref = bf16[16,224,128]{2,1,0:T(8,128)(2,1)S(1)} collective-permute-done((bf16[16,224,128]{2,1,0:T(8,128)(2,1)S(1)}, bf16[16,224,128]{2,1,0:T(8,128)(2,1)S(1)}, u32[]{:S(2)}, u32[]{:S(2)}) %collective-permute-start.4) | collective-permute-done | bytes 917536 | tf_op jit(solution)/shard_map/ppermute | solution.py:106
  192.7 2.0 collective-permute-done.5.hi_ref
  194.8 0.9 copy-done.8
  195.7 7.3 %shard_map.66 = bf16[32,224,128]{2,1,0:T(8,128)(2,1)} custom-call(bf16[32,224,128]{2,1,0:T(8,128)(2,1)} %bitcast.139, bf16[16,224,128]{2,1,0:T(8,128)(2,1)} %copy-done.5, bf16[16,224,128]{2,1,0:T(8,128)(2,1)} %copy-done.8, f32[3,224,128]{2,1,0:T(8,128)} %broadcast_in_dim.26.coef_ref, f32[32,128]{1,0:T(8,128)} %bitcast.159), custom_call_target="tpu_custom_call" | custom-call | flops 27525120 | bytes 3670016 | tf_op jit(solution)/shard_map/pallas_call | solution.py:63
  203.0 2.4 all-to-all-done.5
  205.4 4.5 %all-to-all-start.3 = ((bf16[16,2,224,128]{3,2,1,0:T(8,128)(2,1)}), bf16[16,2,224,128]{3,2,1,0:T(8,128)(2,1)S(1)}, u32[]{:S(2)}, u32[]{:S(2)}) async-start(bf16[16,2,224,128]{3,2,1,0:T(8,128)(2,1)} %bitcast.150), calls=%async_computation.3 | async-start | bytes 3670016 | tf_op jit(solution)/shard_map/all_to_all | solution.py:109
  209.9 3.7 %fusion.13 = f32[2,128,512]{2,1,0:T(8,128)S(1)} fusion(bf16[16,2,224,128]{3,2,1,0:T(8,128)(2,1)} %all-to-all-done.5, bf16[512,16,448]{0,2,1:T(8,128)(2,1)} %bitcast.145), kind=kOutput, calls=%fused_computation.22 | convolution fusion | flops 939524096 | bytes 6029312 | tf_op jit(solution)/shard_map/ksv,srvx->krx/dot_general | solution.py:112
  213.6 23.2 %all-to-all-done.3 = bf16[16,2,224,128]{3,2,1,0:T(8,128)(2,1)S(1)} async-done(((bf16[16,2,224,128]{3,2,1,0:T(8,128)(2,1)}), bf16[16,2,224,128]{3,2,1,0:T(8,128)(2,1)S(1)}, u32[]{:S(2)}, u32[]{:S(2)}) %all-to-all-start.3) | async-done | bytes 1835040 | tf_op jit(solution)/shard_map/all_to_all | solution.py:109
  236.9 3.2 fusion.22
  240.0 3.2 %fusion.10 = f32[2,128,16,224]{1,3,2,0:T(8,128)S(1)} fusion(bf16[512,2,128,1]{0,2,3,1:T(8,128)(2,1)S(1)} %fusion.22, bf16[16,448,512]{2,1,0:T(8,128)(2,1)} %bitcast.137), kind=kOutput, calls=%fused_computation.19 | convolution fusion | flops 939524096 | bytes 7602176 | tf_op jit(solution)/shard_map/svk,krx->srvx/dot_general | solution.py:117
  243.3 5.5 %fusion.1 = (bf16[16,2,224,128]{3,2,0,1:T(8,128)(2,1)S(1)}, bf16[16,2,224,128]{3,2,0,1:T(8,128)(2,1)}) fusion(bf16[16,2,224,128]{3,2,1,0:T(8,128)(2,1)S(1)} %all-to-all-done.3, f32[2,128]{1,0:T(2,128)S(1)} %constant_dynamic-slice_fusion, f32[2,128,16,224]{1,3,2,0:T(8,128)S(1)} %fusion.10, bf16[16,2,224,128]{3,2,1,0:T(8,128)(2,1)} %all-to-all-done.5, ...), kind=kOutput, calls=%fused_computation.8 | convolution fusion | flops 946864128 | bytes 14943232 | tf_op jit(solution)/shard_map/svk,krx->srvx/dot_general | solution.py:117
  248.8 1.4 copy.56
  250.2 4.2 %all-to-all-start.6 = ((bf16[16,2,224,128]{3,2,1,0:T(8,128)(2,1)}), bf16[16,2,224,128]{3,2,1,0:T(8,128)(2,1)S(1)}, u32[]{:S(2)}, u32[]{:S(2)}) async-start(bf16[16,2,224,128]{3,2,1,0:T(8,128)(2,1)} %copy.56), calls=%async_computation.6 | async-start | bytes 3670016 | tf_op jit(solution)/shard_map/all_to_all | solution.py:119
  254.4 2.9 copy.59
  257.3 25.0 %all-to-all-done.6 = bf16[16,2,224,128]{3,2,1,0:T(8,128)(2,1)S(1)} async-done(((bf16[16,2,224,128]{3,2,1,0:T(8,128)(2,1)}), bf16[16,2,224,128]{3,2,1,0:T(8,128)(2,1)S(1)}, u32[]{:S(2)}, u32[]{:S(2)}) %all-to-all-start.6) | async-done | bytes 1835040 | tf_op jit(solution)/shard_map/all_to_all | solution.py:119
  282.3 31.7 %all_to_all.40 = bf16[16,2,224,128]{3,2,1,0:T(8,128)(2,1)S(1)} all-to-all(bf16[16,2,224,128]{3,2,1,0:T(8,128)(2,1)} %copy.59), channel_id=1, replica_groups=mesh['space'=8,'vel'=16] {'vel'}, dimensions={0} | all-to-all | bytes 3670016 | tf_op jit(solution)/shard_map/all_to_all | solution.py:119
  314.1 0.4 maximum_bitcast_fusion
  314.5 4.2 %copy.60 = bf16[448,2,16,128]{3,2,1,0:T(8,128)(2,1)} copy(bf16[448,2,16,128]{3,0,2,1:T(8,128)(2,1)S(1)} %maximum_bitcast_fusion) | data formatting | bytes 7340032 | tf_op jit(solution)/shard_map/transpose | solution.py:121
  (25 shorter events, 0.1 us)
Async XLA Ops:
  3.5 5.6 %copy-start.11 = (s32[448]{0:T(512)S(1)}, s32[448]{0:T(512)}, u32[]{:S(2)}) copy-start(s32[448]{0:T(512)} %param.7) | copy-start | bytes 5380
  3.5 5.7 %copy-start.10 = (s32[2,16,128]{2,1,0:T(8,128)S(1)}, s32[2,16,128]{2,1,0:T(8,128)}, u32[]{:S(2)}) copy-start(s32[2,16,128]{2,1,0:T(8,128)} %param.8) | copy-start | bytes 49156
  4.7 12.8 %collective-permute-start.3 = (bf16[16,224,128]{2,1,0:T(8,128)(2,1)S(1)}, bf16[16,224,128]{2,1,0:T(8,128)(2,1)S(1)}, u32[]{:S(2)}, u32[]{:S(2)}) collective-permute-start(bf16[16,224,128]{2,1,0:T(8,128)(2,1)S(1)} %get-tuple-element.6), channel_id=1, source_target_pairs={{16,0},{32,16},{48,32},{64,48},{80,64},{96,80},{112,96},{17,1},{33... | collective-permute-start | bytes 2752520 | tf_op jit(solution)/shard_map/ppermute | solution.py:107
  6.6 14.7 %collective-permute-start.2 = (bf16[16,224,128]{2,1,0:T(8,128)(2,1)S(1)}, bf16[16,224,128]{2,1,0:T(8,128)(2,1)S(1)}, u32[]{:S(2)}, u32[]{:S(2)}) collective-permute-start(bf16[16,224,128]{2,1,0:T(8,128)(2,1)S(1)} %get-tuple-element.7), channel_id=1, source_target_pairs={{0,16},{16,32},{32,48},{48,64},{64,80},{80,96},{96,112},{1,17},{17... | collective-permute-start | bytes 2752520 | tf_op jit(solution)/shard_map/ppermute | solution.py:106
  17.5 4.9 %copy-start.2 = (bf16[16,224,128]{2,1,0:T(8,128)(2,1)}, bf16[16,224,128]{2,1,0:T(8,128)(2,1)S(1)}, u32[]{:S(2)}) copy-start(bf16[16,224,128]{2,1,0:T(8,128)(2,1)S(1)} %collective-permute-done.3.hi_ref) | copy-start | bytes 2752516
  21.3 1.1 copy-start.3
  29.7 33.6 %all-to-all-start.1 = ((bf16[16,2,224,128]{3,2,1,0:T(8,128)(2,1)}), bf16[16,2,224,128]{3,2,1,0:T(8,128)(2,1)S(1)}, u32[]{:S(2)}, u32[]{:S(2)}) async-start(bf16[16,2,224,128]{3,2,1,0:T(8,128)(2,1)} %bitcast.149), calls=%async_computation.1 | async-start | bytes 3670016 | tf_op jit(solution)/shard_map/all_to_all | solution.py:109
  36.8 13.1 %collective-permute-start.1 = (bf16[16,224,128]{2,1,0:T(8,128)(2,1)}, bf16[16,224,128]{2,1,0:T(8,128)(2,1)S(1)}, u32[]{:S(2)}, u32[]{:S(2)}) collective-permute-start(bf16[16,224,128]{2,1,0:T(8,128)(2,1)} %get-tuple-element.5), channel_id=1, source_target_pairs={{16,0},{32,16},{48,32},{64,48},{80,64},{96,80},{112,96},{17,1},{33... | collective-permute-start | bytes 2752520 | tf_op jit(solution)/shard_map/ppermute | solution.py:107
  38.7 14.7 %collective-permute-start = (bf16[16,224,128]{2,1,0:T(8,128)(2,1)S(1)}, bf16[16,224,128]{2,1,0:T(8,128)(2,1)S(1)}, u32[]{:S(2)}, u32[]{:S(2)}) collective-permute-start(bf16[16,224,128]{2,1,0:T(8,128)(2,1)S(1)} %get-tuple-element.8), channel_id=1, source_target_pairs={{0,16},{16,32},{32,48},{48,64},{64,80},{80,96},{96,112},{1,17},{17... | collective-permute-start | bytes 2752520 | tf_op jit(solution)/shard_map/ppermute | solution.py:106
  49.9 3.5 %copy-start.4 = (bf16[16,224,128]{2,1,0:T(8,128)(2,1)}, bf16[16,224,128]{2,1,0:T(8,128)(2,1)S(1)}, u32[]{:S(2)}) copy-start(bf16[16,224,128]{2,1,0:T(8,128)(2,1)S(1)} %collective-permute-done.1.hi_ref) | copy-start | bytes 2752516
  53.4 0.9 copy-start.7
  63.3 33.6 %all-to-all-start = ((bf16[16,2,224,128]{3,2,1,0:T(8,128)(2,1)}), bf16[16,2,224,128]{3,2,1,0:T(8,128)(2,1)}, u32[]{:S(2)}, u32[]{:S(2)}) async-start(bf16[16,2,224,128]{3,2,1,0:T(8,128)(2,1)} %bitcast.148), calls=%async_computation | async-start | bytes 3670016 | tf_op jit(solution)/shard_map/all_to_all | solution.py:109
  80.2 16.7 %copy-start.12 = (f32[512]{0:T(512)S(1)}, f32[512]{0:T(512)}, u32[]{:S(2)}) copy-start(f32[512]{0:T(512)} %param.11) | copy-start | bytes 6148
  110.7 28.7 %all-to-all-start.4 = ((bf16[16,2,224,128]{3,2,1,0:T(8,128)(2,1)}), bf16[16,2,224,128]{3,2,1,0:T(8,128)(2,1)S(1)}, u32[]{:S(2)}, u32[]{:S(2)}) async-start(bf16[16,2,224,128]{3,2,1,0:T(8,128)(2,1)} %copy.53), calls=%async_computation.4 | async-start | bytes 3670016 | tf_op jit(solution)/shard_map/all_to_all | solution.py:119
  139.4 1.2 copy-start.1
  140.6 30.1 %all-to-all-start.2 = ((bf16[16,2,224,128]{3,2,1,0:T(8,128)(2,1)}), bf16[16,2,224,128]{3,2,1,0:T(8,128)(2,1)S(1)}, u32[]{:S(2)}, u32[]{:S(2)}) async-start(bf16[16,2,224,128]{3,2,1,0:T(8,128)(2,1)} %copy.48), calls=%async_computation.2 | async-start | bytes 3670016 | tf_op jit(solution)/shard_map/all_to_all | solution.py:119
  145.9 14.7 %collective-permute-start.6 = (bf16[16,224,128]{2,1,0:T(8,128)(2,1)S(1)}, bf16[16,224,128]{2,1,0:T(8,128)(2,1)S(1)}, u32[]{:S(2)}, u32[]{:S(2)}) collective-permute-start(bf16[16,224,128]{2,1,0:T(8,128)(2,1)S(1)} %bitcast.154), channel_id=1, source_target_pairs={{0,16},{16,32},{32,48},{48,64},{64,80},{80,96},{96,112},{1,17},{17... | collective-permute-start | bytes 2752520 | tf_op jit(solution)/shard_map/ppermute | solution.py:106
  147.8 14.5 %collective-permute-start.7 = (bf16[16,224,128]{2,1,0:T(8,128)(2,1)S(1)}, bf16[16,224,128]{2,1,0:T(8,128)(2,1)S(1)}, u32[]{:S(2)}, u32[]{:S(2)}) collective-permute-start(bf16[16,224,128]{2,1,0:T(8,128)(2,1)S(1)} %bitcast.152), channel_id=1, source_target_pairs={{16,0},{32,16},{48,32},{64,48},{80,64},{96,80},{112,96},{17,1},{33... | collective-permute-start | bytes 2752520 | tf_op jit(solution)/shard_map/ppermute | solution.py:107
  160.6 2.7 copy-start.6
  162.4 1.0 copy-start.9
  170.6 7.4 %copy-start = (bf16[16,2,224,128]{3,2,1,0:T(8,128)(2,1)}, bf16[16,2,224,128]{3,2,1,0:T(8,128)(2,1)S(1)}, u32[]{:S(2)}) copy-start(bf16[16,2,224,128]{3,2,1,0:T(8,128)(2,1)S(1)} %all-to-all-done.2) | copy-start | bytes 5505028
  170.7 34.7 %all-to-all-start.5 = ((bf16[16,2,224,128]{3,2,1,0:T(8,128)(2,1)}), bf16[16,2,224,128]{3,2,1,0:T(8,128)(2,1)}, u32[]{:S(2)}, u32[]{:S(2)}) async-start(bf16[16,2,224,128]{3,2,1,0:T(8,128)(2,1)} %bitcast.147), calls=%async_computation.5 | async-start | bytes 3670016 | tf_op jit(solution)/shard_map/all_to_all | solution.py:109
  178.0 14.7 %collective-permute-start.4 = (bf16[16,224,128]{2,1,0:T(8,128)(2,1)S(1)}, bf16[16,224,128]{2,1,0:T(8,128)(2,1)S(1)}, u32[]{:S(2)}, u32[]{:S(2)}) collective-permute-start(bf16[16,224,128]{2,1,0:T(8,128)(2,1)S(1)} %bitcast.155), channel_id=1, source_target_pairs={{0,16},{16,32},{32,48},{48,64},{64,80},{80,96},{96,112},{1,17},{17... | collective-permute-start | bytes 2752520 | tf_op jit(solution)/shard_map/ppermute | solution.py:106
  181.9 12.8 %collective-permute-start.5 = (bf16[16,224,128]{2,1,0:T(8,128)(2,1)S(1)}, bf16[16,224,128]{2,1,0:T(8,128)(2,1)S(1)}, u32[]{:S(2)}, u32[]{:S(2)}) collective-permute-start(bf16[16,224,128]{2,1,0:T(8,128)(2,1)S(1)} %bitcast.153), channel_id=1, source_target_pairs={{16,0},{32,16},{48,32},{64,48},{80,64},{96,80},{112,96},{17,1},{33... | collective-permute-start | bytes 2752520 | tf_op jit(solution)/shard_map/ppermute | solution.py:107
  192.7 2.0 copy-start.5
  194.8 0.9 copy-start.8
  205.4 31.5 %all-to-all-start.3 = ((bf16[16,2,224,128]{3,2,1,0:T(8,128)(2,1)}), bf16[16,2,224,128]{3,2,1,0:T(8,128)(2,1)S(1)}, u32[]{:S(2)}, u32[]{:S(2)}) async-start(bf16[16,2,224,128]{3,2,1,0:T(8,128)(2,1)} %bitcast.150), calls=%async_computation.3 | async-start | bytes 3670016 | tf_op jit(solution)/shard_map/all_to_all | solution.py:109
  250.2 32.1 %all-to-all-start.6 = ((bf16[16,2,224,128]{3,2,1,0:T(8,128)(2,1)}), bf16[16,2,224,128]{3,2,1,0:T(8,128)(2,1)S(1)}, u32[]{:S(2)}, u32[]{:S(2)}) async-start(bf16[16,2,224,128]{3,2,1,0:T(8,128)(2,1)} %copy.56), calls=%async_computation.6 | async-start | bytes 3670016 | tf_op jit(solution)/shard_map/all_to_all | solution.py:119

commit v4 on v3

--- a/solution.py
+++ b/solution.py
@@ -9,7 +9,7 @@
 
 VGRID = 24
 STEPS = 2
-VBLOCK = 32
+VBLOCK = 112
 PARTS = 2
 
 
@@ -27,39 +27,37 @@
     )
 
 
-def transport_kernel(ny, f_ref, lo_ref, hi_ref, coef_ref, tm_ref, out_ref):
+def transport_kernel(ny, f_ref, lo_ref, hi_ref, coef_ref, tm_ref, out_ref, ext_ref):
     rows, tv, nx = f_ref.shape
-    nzl = rows // ny
+    ext_ref[pl.ds(0, ny)] = lo_ref[...].astype(jnp.float32)
+    ext_ref[pl.ds(ny, rows)] = f_ref[...].astype(jnp.float32)
+    ext_ref[pl.ds(ny + rows, ny)] = hi_ref[...].astype(jnp.float32)
     ax = coef_ref[0]
     ay = coef_ref[1]
     az = coef_ref[2]
+    gx, gy, gz = ax > 0.0, ay > 0.0, az > 0.0
+    wx, wy, wz = jnp.abs(ax), jnp.abs(ay), jnp.abs(az)
+    lane = lax.broadcasted_iota(jnp.int32, (tv, nx), 1)
+    edge_x = (gx & (lane == 0)) | (jnp.logical_not(gx) & (lane == nx - 1))
     zero = jnp.zeros((tv, nx), jnp.float32)
-    px, mx = jnp.maximum(ax, 0.0), jnp.minimum(ax, 0.0)
-    py, my = jnp.maximum(ay, 0.0), jnp.minimum(ay, 0.0)
-    pz, mz = jnp.maximum(az, 0.0), jnp.minimum(az, 0.0)
-    lane = lax.broadcasted_iota(jnp.int32, (tv, nx), 1)
-
-    def load(ref, i):
-        return ref[i].astype(jnp.float32)
 
     for w in range(rows):
-        z, y = divmod(w, ny)
-        c = load(f_ref, w)
-        x_low = jnp.where(lane == 0, 0.0, pltpu.roll(c, 1, 1))
-        x_high = jnp.where(lane == nx - 1, 0.0, pltpu.roll(c, nx - 1, 1))
-        y_low = load(f_ref, w - 1) if y > 0 else zero
-        y_high = load(f_ref, w + 1) if y < ny - 1 else zero
-        z_low = load(f_ref, w - ny) if z > 0 else load(lo_ref, y)
-        z_high = load(f_ref, w + ny) if z < nzl - 1 else load(hi_ref, y)
-        flux = px * (c - x_low) + mx * (x_high - c)
-        flux = flux + py * (c - y_low) + my * (y_high - c)
-        flux = flux + pz * (c - z_low) + mz * (z_high - c)
+        y = w % ny
+        e = w + ny
+        c = ext_ref[e]
+        n_x = jnp.where(edge_x, 0.0, jnp.where(gx, pltpu.roll(c, 1, 1), pltpu.roll(c, nx - 1, 1)))
+        y_low = ext_ref[e - 1] if y > 0 else zero
+        y_high = ext_ref[e + 1] if y < ny - 1 else zero
+        n_y = jnp.where(gy, y_low, y_high)
+        n_z = jnp.where(gz, ext_ref[e - ny], ext_ref[e + ny])
+        flux = wx * (c - n_x) + wy * (c - n_y)
+        flux = flux + wz * (c - n_z)
         out_ref[w] = (c - tm_ref[w : w + 1, :] * flux).astype(out_ref.dtype)
 
 
 def transport(f, lo, hi, coef, tm, ny):
     rows, vb, nx = f.shape
-    tv = VBLOCK
+    tv = min(VBLOCK, vb)
     return pl.pallas_call(
         functools.partial(transport_kernel, ny),
         out_shape=jax.ShapeDtypeStruct(f.shape, f.dtype),
@@ -72,8 +70,9 @@
             pl.BlockSpec((rows, nx), lambda i: (0, 0)),
         ],
         out_specs=pl.BlockSpec((rows, tv, nx), lambda i: (0, i, 0)),
+        scratch_shapes=[pltpu.VMEM((rows + 2 * ny, tv, nx), jnp.float32)],
         cost_estimate=pl.CostEstimate(
-            flops=30 * rows * vb * nx, transcendentals=0, bytes_accessed=4 * rows * vb * nx
+            flops=20 * rows * vb * nx, transcendentals=0, bytes_accessed=4 * rows * vb * nx
         ),
     )(f, lo, hi, coef, tm)
 

time: 321 us -> 311 us (0.969)
  Pallas kernels: 29.1 us -> 21.1 us
  waiting for transfers between devices: 130 us -> 136 us
  blocking collectives: 31.7 us -> 27.2 us
    pallas_call x4, Pallas kernels: 29.1 us -> 21.1 us  [transport(): pl.pallas_call(functools.partial(transport_kernel, ny), out_shape=jax.Sha...]
    all_to_all x4, waiting for transfers between devices: 39.9 us -> 45.1 us  [per_device(): lax.all_to_all(half.reshape(groups, chunk, part, nx), 'vel', 0, 0, tiled=...]
    all_to_all x1, blocking collectives: 31.7 us -> 27.2 us  [per_device(): lax.all_to_all(post, 'vel', 0, 0, tiled=True).reshape(rows, part, nx)]
  transfers between devices with their start and end apart: 15 -> 15, of which waited for: 14 -> 15; matrix products, arithmetic and copies ran while one was open for 9% -> 9% of each run, Pallas kernels for 7% -> 5%
where the time goes in v4:
time: 311 us; the launch traced here: 310 us
  waiting for transfers between devices  136 us (44%)
  starting transfers between devices  55.8 us (18%)
  local copies, waits for them, and re-layouts  38.1 us (12%)
  matrix products  31 us (10%)
  blocking collectives  27.2 us (9%)
  Pallas kernels  21.1 us (7%)
    all_to_all x3, waiting for transfers between devices, per_device(): lax.all_to_all(post, 'vel', 0, 0, tiled=True).reshape(rows, part, nx)  46.9 us
    all_to_all x4, waiting for transfers between devices, per_device(): lax.all_to_all(half.reshape(groups, chunk, part, nx), 'vel', 0, 0, tiled=...  45.1 us
    all_to_all x1, blocking collectives, per_device(): lax.all_to_all(post, 'vel', 0, 0, tiled=True).reshape(rows, part, nx)  27.2 us
    ppermute x4, waiting for transfers between devices, per_device(): lo = lax.ppermute(f[rows - ny:], 'space', up)  25.3 us
    all_to_all x4, starting transfers between devices, per_device(): lax.all_to_all(half.reshape(groups, chunk, part, nx), 'vel', 0, 0, tiled=...  22.4 us
    pallas_call x4, Pallas kernels, transport(): pl.pallas_call(functools.partial(transport_kernel, ny), out_shape=jax.Sha...  21.1 us
    ppermute x4, waiting for transfers between devices, per_device(): hi = lax.ppermute(f[:ny], 'space', down)  18.2 us
    dot_general x4, matrix products, per_device(): jnp.einsum('svk,krx->srvx', e3[:, p], delta, preferred_element_type=jnp.f...  17.2 us
  transfers between devices with their start and end apart: 15, of which 15 were waited for; matrix products, arithmetic and copies ran while one was open for 9% of the time, Pallas kernels for 5%

profile of v4, /device:TPU:32, one launch (start us, length us, event | category | flops | bytes accessed | tf_op | source)
XLA Modules:
  0.0 310.0 jit_solution(17167084262503623629)
XLA Ops:
  0.0 3.5 %copy.42 = bf16[2,16,448,128]{3,2,1,0:T(8,128)(2,1)S(1)} copy(bf16[2,16,448,128]{3,1,0,2:T(8,128)(2,1)} %bitcast.151) | data formatting | bytes 7340032 | tf_op jit(solution)/shard_map/transpose | solution.py:99
  3.5 1.2 fusion.32
  4.7 1.9 collective-permute-start.3
  6.6 2.4 collective-permute-start.2
  9.1 0.1 fusion.36
  9.2 0.6 compare_convert_fusion
  9.8 2.1 fusion.33
  11.9 5.7 %collective-permute-done.3.hi_ref = bf16[16,224,128]{2,1,0:T(8,128)(2,1)S(1)} collective-permute-done((bf16[16,224,128]{2,1,0:T(8,128)(2,1)S(1)}, bf16[16,224,128]{2,1,0:T(8,128)(2,1)S(1)}, u32[]{:S(2)}, u32[]{:S(2)}) %collective-permute-start.3) | collective-permute-done | bytes 917536 | tf_op jit(solution)/shard_map/ppermute | solution.py:106
  17.5 3.8 %collective-permute-done.2.lo_ref = bf16[16,224,128]{2,1,0:T(8,128)(2,1)S(1)} collective-permute-done((bf16[16,224,128]{2,1,0:T(8,128)(2,1)S(1)}, bf16[16,224,128]{2,1,0:T(8,128)(2,1)S(1)}, u32[]{:S(2)}, u32[]{:S(2)}) %collective-permute-start.2) | collective-permute-done | bytes 917536 | tf_op jit(solution)/shard_map/ppermute | solution.py:105
  21.3 1.1 broadcast_in_dim.30.coef_ref
  22.4 0.0 copy-done.3
  22.4 5.3 %shard_map.65 = bf16[32,224,128]{2,1,0:T(8,128)(2,1)} custom-call(bf16[32,224,128]{2,1,0:T(8,128)(2,1)} %get-tuple-element.10.f_ref, bf16[16,224,128]{2,1,0:T(8,128)(2,1)} %copy-done.3, bf16[16,224,128]{2,1,0:T(8,128)(2,1)} %copy-done.2, f32[3,224,128]{2,1,0:T(8,128)} %broadcast_in_dim.30.coef_ref, f32[32,128]{1,0:T(8,128)} %bitcast.156), custom_call_target="tpu_custom_call" | custom-call | flops 18350080 | bytes 3670016 | tf_op jit(solution)/shard_map/pallas_call | solution.py:61
  27.7 7.0 %all-to-all-start.1 = ((bf16[16,2,224,128]{3,2,1,0:T(8,128)(2,1)}), bf16[16,2,224,128]{3,2,1,0:T(8,128)(2,1)S(1)}, u32[]{:S(2)}, u32[]{:S(2)}) async-start(bf16[16,2,224,128]{3,2,1,0:T(8,128)(2,1)} %bitcast.149), calls=%async_computation.1 | async-start | bytes 3670016 | tf_op jit(solution)/shard_map/all_to_all | solution.py:108
  34.7 1.9 collective-permute-start.1
  36.7 2.4 collective-permute-start
  39.1 8.8 %collective-permute-done.1.hi_ref = bf16[16,224,128]{2,1,0:T(8,128)(2,1)S(1)} collective-permute-done((bf16[16,224,128]{2,1,0:T(8,128)(2,1)}, bf16[16,224,128]{2,1,0:T(8,128)(2,1)S(1)}, u32[]{:S(2)}, u32[]{:S(2)}) %collective-permute-start.1) | collective-permute-done | bytes 917536 | tf_op jit(solution)/shard_map/ppermute | solution.py:106
  47.9 3.5 %collective-permute-done.lo_ref = bf16[16,224,128]{2,1,0:T(8,128)(2,1)S(1)} collective-permute-done((bf16[16,224,128]{2,1,0:T(8,128)(2,1)S(1)}, bf16[16,224,128]{2,1,0:T(8,128)(2,1)S(1)}, u32[]{:S(2)}, u32[]{:S(2)}) %collective-permute-start) | collective-permute-done | bytes 917536 | tf_op jit(solution)/shard_map/ppermute | solution.py:105
  51.4 0.9 copy-done.7
  52.3 0.9 broadcast_in_dim.26.coef_ref
  53.2 5.3 %shard_map.64 = bf16[32,224,128]{2,1,0:T(8,128)(2,1)} custom-call(bf16[32,224,128]{2,1,0:T(8,128)(2,1)} %get-tuple-element.9.f_ref, bf16[16,224,128]{2,1,0:T(8,128)(2,1)} %copy-done.7, bf16[16,224,128]{2,1,0:T(8,128)(2,1)} %copy-done.4, f32[3,224,128]{2,1,0:T(8,128)} %broadcast_in_dim.26.coef_ref, f32[32,128]{1,0:T(8,128)} %bitcast.157), custom_call_target="tpu_custom_call" | custom-call | flops 18350080 | bytes 3670016 | tf_op jit(solution)/shard_map/pallas_call | solution.py:61
  58.5 2.8 all-to-all-done.1
  61.3 4.5 %all-to-all-start = ((bf16[16,2,224,128]{3,2,1,0:T(8,128)(2,1)}), bf16[16,2,224,128]{3,2,1,0:T(8,128)(2,1)}, u32[]{:S(2)}, u32[]{:S(2)}) async-start(bf16[16,2,224,128]{3,2,1,0:T(8,128)(2,1)} %bitcast.148), calls=%async_computation | async-start | bytes 3670016 | tf_op jit(solution)/shard_map/all_to_all | solution.py:108
  65.7 10.4 %copy.44 = bf16[512,7168]{0,1:T(8,128)(2,1)} copy(bf16[512,7168]{1,0:T(8,128)(2,1)} %param.9) | data formatting | bytes 14680064 | tf_op args[3]
  76.2 3.2 %fusion.12 = f32[2,128,512]{2,1,0:T(8,128)S(1)} fusion(bf16[16,2,224,128]{3,2,1,0:T(8,128)(2,1)S(1)} %all-to-all-done.1, bf16[512,16,448]{0,2,1:T(8,128)(2,1)} %bitcast.143), kind=kOutput, calls=%fused_computation.21 | convolution fusion | flops 939524096 | bytes 6029312 | tf_op jit(solution)/shard_map/ksv,srvx->krx/dot_general | solution.py:111
  79.4 13.5 %all-to-all-done = bf16[16,2,224,128]{3,2,1,0:T(8,128)(2,1)} async-done(((bf16[16,2,224,128]{3,2,1,0:T(8,128)(2,1)}), bf16[16,2,224,128]{3,2,1,0:T(8,128)(2,1)}, u32[]{:S(2)}, u32[]{:S(2)}) %all-to-all-start) | async-done | bytes 1835040 | tf_op jit(solution)/shard_map/all_to_all | solution.py:108
  92.9 3.7 %fusion.23 = bf16[512,2,128,1]{0,2,3,1:T(8,128)(2,1)S(1)} fusion(f32[2,128,512]{2,1,0:T(8,128)S(1)} %fusion.12, bf16[16,2,224,128]{3,2,1,0:T(8,128)(2,1)} %all-to-all-done, bf16[512,16,448]{0,2,1:T(8,128)(2,1)} %bitcast.144, f32[512]{0:T(512)S(1)} %copy-done.12), kind=kOutput, calls=%fused_computation.32 | convolution fusion | flops 939917312 | bytes 6293504 | tf_op jit(solution)/shard_map/ksv,srvx->krx/dot_general | solution.py:111
  96.6 3.2 %fusion.11 = f32[2,128,16,224]{1,3,2,0:T(8,128)S(1)} fusion(bf16[512,2,128,1]{0,2,3,1:T(8,128)(2,1)S(1)} %fusion.23, bf16[16,448,512]{2,1,0:T(8,128)(2,1)} %bitcast.135), kind=kOutput, calls=%fused_computation.20 | convolution fusion | flops 939524096 | bytes 7602176 | tf_op jit(solution)/shard_map/svk,krx->srvx/dot_general | solution.py:116
  99.8 5.3 %fusion.3 = (bf16[16,2,224,128]{3,2,0,1:T(8,128)(2,1)}, bf16[16,2,224,128]{3,2,0,1:T(8,128)(2,1)S(1)}) fusion(bf16[16,2,224,128]{3,2,1,0:T(8,128)(2,1)} %all-to-all-done, f32[2,128]{1,0:T(2,128)S(1)} %constant_dynamic-slice_fusion, f32[2,128,16,224]{1,3,2,0:T(8,128)S(1)} %fusion.11, bf16[16,2,224,128]{3,2,1,0:T(8,128)(2,1)S(1)} %all-to-all-done.1, ...), kind=kOutput, calls=%fused_computation.12 | convolution fusion | flops 946864128 | bytes 14943232 | tf_op jit(solution)/shard_map/svk,krx->srvx/dot_general | solution.py:116
  105.1 1.5 copy.53
  106.7 3.7 %all-to-all-start.4 = ((bf16[16,2,224,128]{3,2,1,0:T(8,128)(2,1)}), bf16[16,2,224,128]{3,2,1,0:T(8,128)(2,1)S(1)}, u32[]{:S(2)}, u32[]{:S(2)}) async-start(bf16[16,2,224,128]{3,2,1,0:T(8,128)(2,1)} %copy.53), calls=%async_computation.4 | async-start | bytes 3670016 | tf_op jit(solution)/shard_map/all_to_all | solution.py:118
  110.4 2.9 copy.48
  113.3 22.0 %all-to-all-done.4 = bf16[16,2,224,128]{3,2,1,0:T(8,128)(2,1)S(1)} async-done(((bf16[16,2,224,128]{3,2,1,0:T(8,128)(2,1)}), bf16[16,2,224,128]{3,2,1,0:T(8,128)(2,1)S(1)}, u32[]{:S(2)}, u32[]{:S(2)}) %all-to-all-start.4) | async-done | bytes 1835040 | tf_op jit(solution)/shard_map/all_to_all | solution.py:118
  135.3 1.2 copy-done.1
  136.5 3.7 %all-to-all-start.2 = ((bf16[16,2,224,128]{3,2,1,0:T(8,128)(2,1)}), bf16[16,2,224,128]{3,2,1,0:T(8,128)(2,1)S(1)}, u32[]{:S(2)}, u32[]{:S(2)}) async-start(bf16[16,2,224,128]{3,2,1,0:T(8,128)(2,1)} %copy.48), calls=%async_computation.2 | async-start | bytes 3670016 | tf_op jit(solution)/shard_map/all_to_all | solution.py:118
  140.3 1.6 fusion.35
  141.8 2.1 collective-permute-start.6
  144.0 3.6 %collective-permute-start.7 = (bf16[16,224,128]{2,1,0:T(8,128)(2,1)S(1)}, bf16[16,224,128]{2,1,0:T(8,128)(2,1)S(1)}, u32[]{:S(2)}, u32[]{:S(2)}) collective-permute-start(bf16[16,224,128]{2,1,0:T(8,128)(2,1)S(1)} %bitcast.152), channel_id=1, source_target_pairs={{16,0},{32,16},{48,32},{64,48},{80,64},{96,80},{112,96},{17,1},{33... | collective-permute-start | bytes 2752520 | tf_op jit(solution)/shard_map/ppermute | solution.py:106
  147.6 9.1 %collective-permute-done.6.lo_ref = bf16[16,224,128]{2,1,0:T(8,128)(2,1)S(1)} collective-permute-done((bf16[16,224,128]{2,1,0:T(8,128)(2,1)S(1)}, bf16[16,224,128]{2,1,0:T(8,128)(2,1)S(1)}, u32[]{:S(2)}, u32[]{:S(2)}) %collective-permute-start.6) | collective-permute-done | bytes 917536 | tf_op jit(solution)/shard_map/ppermute | solution.py:105
  156.7 1.8 collective-permute-done.7.hi_ref
  158.5 1.0 copy-done.9
  159.5 5.3 %shard_map.67 = bf16[32,224,128]{2,1,0:T(8,128)(2,1)} custom-call(bf16[32,224,128]{2,1,0:T(8,128)(2,1)} %bitcast.140, bf16[16,224,128]{2,1,0:T(8,128)(2,1)} %copy-done.6, bf16[16,224,128]{2,1,0:T(8,128)(2,1)} %copy-done.9, f32[3,224,128]{2,1,0:T(8,128)} %broadcast_in_dim.30.coef_ref, f32[32,128]{1,0:T(8,128)} %bitcast.158), custom_call_target="tpu_custom_call" | custom-call | flops 18350080 | bytes 3670016 | tf_op jit(solution)/shard_map/pallas_call | solution.py:61
  164.8 0.6 all-to-all-done.2
  165.3 6.7 %all-to-all-start.5 = ((bf16[16,2,224,128]{3,2,1,0:T(8,128)(2,1)}), bf16[16,2,224,128]{3,2,1,0:T(8,128)(2,1)}, u32[]{:S(2)}, u32[]{:S(2)}) async-start(bf16[16,2,224,128]{3,2,1,0:T(8,128)(2,1)} %bitcast.147), calls=%async_computation.5 | async-start | bytes 3670016 | tf_op jit(solution)/shard_map/all_to_all | solution.py:108
  172.0 0.1 fusion.34
  172.1 3.9 %collective-permute-start.4 = (bf16[16,224,128]{2,1,0:T(8,128)(2,1)S(1)}, bf16[16,224,128]{2,1,0:T(8,128)(2,1)S(1)}, u32[]{:S(2)}, u32[]{:S(2)}) collective-permute-start(bf16[16,224,128]{2,1,0:T(8,128)(2,1)S(1)} %bitcast.155), channel_id=1, source_target_pairs={{0,16},{16,32},{32,48},{48,64},{64,80},{80,96},{96,112},{1,17},{17... | collective-permute-start | bytes 2752520 | tf_op jit(solution)/shard_map/ppermute | solution.py:105
  176.0 1.9 collective-permute-start.5
  178.0 8.9 %collective-permute-done.4.lo_ref = bf16[16,224,128]{2,1,0:T(8,128)(2,1)S(1)} collective-permute-done((bf16[16,224,128]{2,1,0:T(8,128)(2,1)S(1)}, bf16[16,224,128]{2,1,0:T(8,128)(2,1)S(1)}, u32[]{:S(2)}, u32[]{:S(2)}) %collective-permute-start.4) | collective-permute-done | bytes 917536 | tf_op jit(solution)/shard_map/ppermute | solution.py:105
  186.9 2.0 collective-permute-done.5.hi_ref
  188.9 0.9 copy-done.8
  189.8 5.3 %shard_map.66 = bf16[32,224,128]{2,1,0:T(8,128)(2,1)} custom-call(bf16[32,224,128]{2,1,0:T(8,128)(2,1)} %bitcast.139, bf16[16,224,128]{2,1,0:T(8,128)(2,1)} %copy-done.5, bf16[16,224,128]{2,1,0:T(8,128)(2,1)} %copy-done.8, f32[3,224,128]{2,1,0:T(8,128)} %broadcast_in_dim.26.coef_ref, f32[32,128]{1,0:T(8,128)} %bitcast.159), custom_call_target="tpu_custom_call" | custom-call | flops 18350080 | bytes 3670016 | tf_op jit(solution)/shard_map/pallas_call | solution.py:61
  195.1 4.4 %all-to-all-done.5 = bf16[16,2,224,128]{3,2,1,0:T(8,128)(2,1)} async-done(((bf16[16,2,224,128]{3,2,1,0:T(8,128)(2,1)}), bf16[16,2,224,128]{3,2,1,0:T(8,128)(2,1)}, u32[]{:S(2)}, u32[]{:S(2)}) %all-to-all-start.5) | async-done | bytes 1835040 | tf_op jit(solution)/shard_map/all_to_all | solution.py:108
  199.5 4.2 %all-to-all-start.3 = ((bf16[16,2,224,128]{3,2,1,0:T(8,128)(2,1)}), bf16[16,2,224,128]{3,2,1,0:T(8,128)(2,1)S(1)}, u32[]{:S(2)}, u32[]{:S(2)}) async-start(bf16[16,2,224,128]{3,2,1,0:T(8,128)(2,1)} %bitcast.150), calls=%async_computation.3 | async-start | bytes 3670016 | tf_op jit(solution)/shard_map/all_to_all | solution.py:108
  203.7 3.7 %fusion.13 = f32[2,128,512]{2,1,0:T(8,128)S(1)} fusion(bf16[16,2,224,128]{3,2,1,0:T(8,128)(2,1)} %all-to-all-done.5, bf16[512,16,448]{0,2,1:T(8,128)(2,1)} %bitcast.145), kind=kOutput, calls=%fused_computation.22 | convolution fusion | flops 939524096 | bytes 6029312 | tf_op jit(solution)/shard_map/ksv,srvx->krx/dot_general | solution.py:111
  207.4 24.3 %all-to-all-done.3 = bf16[16,2,224,128]{3,2,1,0:T(8,128)(2,1)S(1)} async-done(((bf16[16,2,224,128]{3,2,1,0:T(8,128)(2,1)}), bf16[16,2,224,128]{3,2,1,0:T(8,128)(2,1)S(1)}, u32[]{:S(2)}, u32[]{:S(2)}) %all-to-all-start.3) | async-done | bytes 1835040 | tf_op jit(solution)/shard_map/all_to_all | solution.py:108
  231.8 3.2 %fusion.22 = bf16[512,2,128,1]{0,2,3,1:T(8,128)(2,1)S(1)} fusion(f32[2,128,512]{2,1,0:T(8,128)S(1)} %fusion.13, bf16[16,2,224,128]{3,2,1,0:T(8,128)(2,1)S(1)} %all-to-all-done.3, bf16[512,16,448]{0,2,1:T(8,128)(2,1)} %bitcast.146, f32[512]{0:T(512)S(1)} %copy-done.12), kind=kOutput, calls=%fused_computation.31 | convolution fusion | flops 939917312 | bytes 6293504 | tf_op jit(solution)/shard_map/ksv,srvx->krx/dot_general | solution.py:111
  234.9 3.2 %fusion.10 = f32[2,128,16,224]{1,3,2,0:T(8,128)S(1)} fusion(bf16[512,2,128,1]{0,2,3,1:T(8,128)(2,1)S(1)} %fusion.22, bf16[16,448,512]{2,1,0:T(8,128)(2,1)} %bitcast.137), kind=kOutput, calls=%fused_computation.19 | convolution fusion | flops 939524096 | bytes 7602176 | tf_op jit(solution)/shard_map/svk,krx->srvx/dot_general | solution.py:116
  238.1 5.5 %fusion.1 = (bf16[16,2,224,128]{3,2,0,1:T(8,128)(2,1)S(1)}, bf16[16,2,224,128]{3,2,0,1:T(8,128)(2,1)}) fusion(bf16[16,2,224,128]{3,2,1,0:T(8,128)(2,1)S(1)} %all-to-all-done.3, f32[2,128]{1,0:T(2,128)S(1)} %constant_dynamic-slice_fusion, f32[2,128,16,224]{1,3,2,0:T(8,128)S(1)} %fusion.10, bf16[16,2,224,128]{3,2,1,0:T(8,128)(2,1)} %all-to-all-done.5, ...), kind=kOutput, calls=%fused_computation.8 | convolution fusion | flops 946864128 | bytes 14943232 | tf_op jit(solution)/shard_map/svk,krx->srvx/dot_general | solution.py:116
  243.7 1.4 copy.56
  245.1 5.8 %all-to-all-start.6 = ((bf16[16,2,224,128]{3,2,1,0:T(8,128)(2,1)}), bf16[16,2,224,128]{3,2,1,0:T(8,128)(2,1)S(1)}, u32[]{:S(2)}, u32[]{:S(2)}) async-start(bf16[16,2,224,128]{3,2,1,0:T(8,128)(2,1)} %copy.56), calls=%async_computation.6 | async-start | bytes 3670016 | tf_op jit(solution)/shard_map/all_to_all | solution.py:118
  250.9 2.9 copy.59
  253.8 24.4 %all-to-all-done.6 = bf16[16,2,224,128]{3,2,1,0:T(8,128)(2,1)S(1)} async-done(((bf16[16,2,224,128]{3,2,1,0:T(8,128)(2,1)}), bf16[16,2,224,128]{3,2,1,0:T(8,128)(2,1)S(1)}, u32[]{:S(2)}, u32[]{:S(2)}) %all-to-all-start.6) | async-done | bytes 1835040 | tf_op jit(solution)/shard_map/all_to_all | solution.py:118
  278.2 27.2 %all_to_all.40 = bf16[16,2,224,128]{3,2,1,0:T(8,128)(2,1)S(1)} all-to-all(bf16[16,2,224,128]{3,2,1,0:T(8,128)(2,1)} %copy.59), channel_id=1, replica_groups=mesh['space'=8,'vel'=16] {'vel'}, dimensions={0} | all-to-all | bytes 3670016 | tf_op jit(solution)/shard_map/all_to_all | solution.py:118
  305.4 0.4 maximum_bitcast_fusion
  305.8 4.2 %copy.60 = bf16[448,2,16,128]{3,2,1,0:T(8,128)(2,1)} copy(bf16[448,2,16,128]{3,0,2,1:T(8,128)(2,1)S(1)} %maximum_bitcast_fusion) | data formatting | bytes 7340032 | tf_op jit(solution)/shard_map/transpose | solution.py:120
  (25 shorter events, 0.1 us)
Async XLA Ops:
  3.5 5.6 %copy-start.11 = (s32[448]{0:T(512)S(1)}, s32[448]{0:T(512)}, u32[]{:S(2)}) copy-start(s32[448]{0:T(512)} %param.7) | copy-start | bytes 5380
  3.5 5.7 %copy-start.10 = (s32[2,16,128]{2,1,0:T(8,128)S(1)}, s32[2,16,128]{2,1,0:T(8,128)}, u32[]{:S(2)}) copy-start(s32[2,16,128]{2,1,0:T(8,128)} %param.8) | copy-start | bytes 49156
  4.7 12.8 %collective-permute-start.3 = (bf16[16,224,128]{2,1,0:T(8,128)(2,1)S(1)}, bf16[16,224,128]{2,1,0:T(8,128)(2,1)S(1)}, u32[]{:S(2)}, u32[]{:S(2)}) collective-permute-start(bf16[16,224,128]{2,1,0:T(8,128)(2,1)S(1)} %get-tuple-element.6), channel_id=1, source_target_pairs={{16,0},{32,16},{48,32},{64,48},{80,64},{96,80},{112,96},{17,1},{33... | collective-permute-start | bytes 2752520 | tf_op jit(solution)/shard_map/ppermute | solution.py:106
  6.6 14.7 %collective-permute-start.2 = (bf16[16,224,128]{2,1,0:T(8,128)(2,1)S(1)}, bf16[16,224,128]{2,1,0:T(8,128)(2,1)S(1)}, u32[]{:S(2)}, u32[]{:S(2)}) collective-permute-start(bf16[16,224,128]{2,1,0:T(8,128)(2,1)S(1)} %get-tuple-element.7), channel_id=1, source_target_pairs={{0,16},{16,32},{32,48},{48,64},{64,80},{80,96},{96,112},{1,17},{17... | collective-permute-start | bytes 2752520 | tf_op jit(solution)/shard_map/ppermute | solution.py:105
  17.5 4.9 %copy-start.2 = (bf16[16,224,128]{2,1,0:T(8,128)(2,1)}, bf16[16,224,128]{2,1,0:T(8,128)(2,1)S(1)}, u32[]{:S(2)}) copy-start(bf16[16,224,128]{2,1,0:T(8,128)(2,1)S(1)} %collective-permute-done.3.hi_ref) | copy-start | bytes 2752516
  21.3 1.1 copy-start.3
  27.7 33.6 %all-to-all-start.1 = ((bf16[16,2,224,128]{3,2,1,0:T(8,128)(2,1)}), bf16[16,2,224,128]{3,2,1,0:T(8,128)(2,1)S(1)}, u32[]{:S(2)}, u32[]{:S(2)}) async-start(bf16[16,2,224,128]{3,2,1,0:T(8,128)(2,1)} %bitcast.149), calls=%async_computation.1 | async-start | bytes 3670016 | tf_op jit(solution)/shard_map/all_to_all | solution.py:108
  34.7 13.1 %collective-permute-start.1 = (bf16[16,224,128]{2,1,0:T(8,128)(2,1)}, bf16[16,224,128]{2,1,0:T(8,128)(2,1)S(1)}, u32[]{:S(2)}, u32[]{:S(2)}) collective-permute-start(bf16[16,224,128]{2,1,0:T(8,128)(2,1)} %get-tuple-element.5), channel_id=1, source_target_pairs={{16,0},{32,16},{48,32},{64,48},{80,64},{96,80},{112,96},{17,1},{33... | collective-permute-start | bytes 2752520 | tf_op jit(solution)/shard_map/ppermute | solution.py:106
  36.7 14.7 %collective-permute-start = (bf16[16,224,128]{2,1,0:T(8,128)(2,1)S(1)}, bf16[16,224,128]{2,1,0:T(8,128)(2,1)S(1)}, u32[]{:S(2)}, u32[]{:S(2)}) collective-permute-start(bf16[16,224,128]{2,1,0:T(8,128)(2,1)S(1)} %get-tuple-element.8), channel_id=1, source_target_pairs={{0,16},{16,32},{32,48},{48,64},{64,80},{80,96},{96,112},{1,17},{17... | collective-permute-start | bytes 2752520 | tf_op jit(solution)/shard_map/ppermute | solution.py:105
  47.9 3.5 %copy-start.4 = (bf16[16,224,128]{2,1,0:T(8,128)(2,1)}, bf16[16,224,128]{2,1,0:T(8,128)(2,1)S(1)}, u32[]{:S(2)}) copy-start(bf16[16,224,128]{2,1,0:T(8,128)(2,1)S(1)} %collective-permute-done.1.hi_ref) | copy-start | bytes 2752516
  51.4 0.9 copy-start.7
  61.3 31.6 %all-to-all-start = ((bf16[16,2,224,128]{3,2,1,0:T(8,128)(2,1)}), bf16[16,2,224,128]{3,2,1,0:T(8,128)(2,1)}, u32[]{:S(2)}, u32[]{:S(2)}) async-start(bf16[16,2,224,128]{3,2,1,0:T(8,128)(2,1)} %bitcast.148), calls=%async_computation | async-start | bytes 3670016 | tf_op jit(solution)/shard_map/all_to_all | solution.py:108
  76.2 16.7 %copy-start.12 = (f32[512]{0:T(512)S(1)}, f32[512]{0:T(512)}, u32[]{:S(2)}) copy-start(f32[512]{0:T(512)} %param.11) | copy-start | bytes 6148
  106.7 28.7 %all-to-all-start.4 = ((bf16[16,2,224,128]{3,2,1,0:T(8,128)(2,1)}), bf16[16,2,224,128]{3,2,1,0:T(8,128)(2,1)S(1)}, u32[]{:S(2)}, u32[]{:S(2)}) async-start(bf16[16,2,224,128]{3,2,1,0:T(8,128)(2,1)} %copy.53), calls=%async_computation.4 | async-start | bytes 3670016 | tf_op jit(solution)/shard_map/all_to_all | solution.py:118
  135.3 1.2 copy-start.1
  136.5 28.8 %all-to-all-start.2 = ((bf16[16,2,224,128]{3,2,1,0:T(8,128)(2,1)}), bf16[16,2,224,128]{3,2,1,0:T(8,128)(2,1)S(1)}, u32[]{:S(2)}, u32[]{:S(2)}) async-start(bf16[16,2,224,128]{3,2,1,0:T(8,128)(2,1)} %copy.48), calls=%async_computation.2 | async-start | bytes 3670016 | tf_op jit(solution)/shard_map/all_to_all | solution.py:118
  141.8 14.9 %collective-permute-start.6 = (bf16[16,224,128]{2,1,0:T(8,128)(2,1)S(1)}, bf16[16,224,128]{2,1,0:T(8,128)(2,1)S(1)}, u32[]{:S(2)}, u32[]{:S(2)}) collective-permute-start(bf16[16,224,128]{2,1,0:T(8,128)(2,1)S(1)} %bitcast.154), channel_id=1, source_target_pairs={{0,16},{16,32},{32,48},{48,64},{64,80},{80,96},{96,112},{1,17},{17... | collective-permute-start | bytes 2752520 | tf_op jit(solution)/shard_map/ppermute | solution.py:105
  144.0 14.5 %collective-permute-start.7 = (bf16[16,224,128]{2,1,0:T(8,128)(2,1)S(1)}, bf16[16,224,128]{2,1,0:T(8,128)(2,1)S(1)}, u32[]{:S(2)}, u32[]{:S(2)}) collective-permute-start(bf16[16,224,128]{2,1,0:T(8,128)(2,1)S(1)} %bitcast.152), channel_id=1, source_target_pairs={{16,0},{32,16},{48,32},{64,48},{80,64},{96,80},{112,96},{17,1},{33... | collective-permute-start | bytes 2752520 | tf_op jit(solution)/shard_map/ppermute | solution.py:106
  156.7 2.7 copy-start.6
  158.5 1.0 copy-start.9
  165.3 6.8 %copy-start = (bf16[16,2,224,128]{3,2,1,0:T(8,128)(2,1)}, bf16[16,2,224,128]{3,2,1,0:T(8,128)(2,1)S(1)}, u32[]{:S(2)}) copy-start(bf16[16,2,224,128]{3,2,1,0:T(8,128)(2,1)S(1)} %all-to-all-done.2) | copy-start | bytes 5505028
  165.3 34.2 %all-to-all-start.5 = ((bf16[16,2,224,128]{3,2,1,0:T(8,128)(2,1)}), bf16[16,2,224,128]{3,2,1,0:T(8,128)(2,1)}, u32[]{:S(2)}, u32[]{:S(2)}) async-start(bf16[16,2,224,128]{3,2,1,0:T(8,128)(2,1)} %bitcast.147), calls=%async_computation.5 | async-start | bytes 3670016 | tf_op jit(solution)/shard_map/all_to_all | solution.py:108
  172.1 14.7 %collective-permute-start.4 = (bf16[16,224,128]{2,1,0:T(8,128)(2,1)S(1)}, bf16[16,224,128]{2,1,0:T(8,128)(2,1)S(1)}, u32[]{:S(2)}, u32[]{:S(2)}) collective-permute-start(bf16[16,224,128]{2,1,0:T(8,128)(2,1)S(1)} %bitcast.155), channel_id=1, source_target_pairs={{0,16},{16,32},{32,48},{48,64},{64,80},{80,96},{96,112},{1,17},{17... | collective-permute-start | bytes 2752520 | tf_op jit(solution)/shard_map/ppermute | solution.py:105
  176.0 12.8 %collective-permute-start.5 = (bf16[16,224,128]{2,1,0:T(8,128)(2,1)S(1)}, bf16[16,224,128]{2,1,0:T(8,128)(2,1)S(1)}, u32[]{:S(2)}, u32[]{:S(2)}) collective-permute-start(bf16[16,224,128]{2,1,0:T(8,128)(2,1)S(1)} %bitcast.153), channel_id=1, source_target_pairs={{16,0},{32,16},{48,32},{64,48},{80,64},{96,80},{112,96},{17,1},{33... | collective-permute-start | bytes 2752520 | tf_op jit(solution)/shard_map/ppermute | solution.py:106
  186.9 2.0 copy-start.5
  188.9 0.9 copy-start.8
  199.5 32.3 %all-to-all-start.3 = ((bf16[16,2,224,128]{3,2,1,0:T(8,128)(2,1)}), bf16[16,2,224,128]{3,2,1,0:T(8,128)(2,1)S(1)}, u32[]{:S(2)}, u32[]{:S(2)}) async-start(bf16[16,2,224,128]{3,2,1,0:T(8,128)(2,1)} %bitcast.150), calls=%async_computation.3 | async-start | bytes 3670016 | tf_op jit(solution)/shard_map/all_to_all | solution.py:108
  245.1 33.1 %all-to-all-start.6 = ((bf16[16,2,224,128]{3,2,1,0:T(8,128)(2,1)}), bf16[16,2,224,128]{3,2,1,0:T(8,128)(2,1)S(1)}, u32[]{:S(2)}, u32[]{:S(2)}) async-start(bf16[16,2,224,128]{3,2,1,0:T(8,128)(2,1)} %copy.56), calls=%async_computation.6 | async-start | bytes 3670016 | tf_op jit(solution)/shard_map/all_to_all | solution.py:118

commit v5 on v4

--- a/solution.py
+++ b/solution.py
@@ -97,13 +97,18 @@
     pieces = [slice(h * part, (h + 1) * part) for h in range(PARTS)]
 
     whole = jnp.transpose(dist, (1, 2, 0, 3)).reshape(rows, vb, nx)
+    lo_all = lax.ppermute(whole[rows - ny :], "space", up)
+    hi_all = lax.ppermute(whole[:ny], "space", down)
     fs = [whole[:, p] for p in pieces]
     for step in range(STEPS):
         recvs = []
         for h, p in enumerate(pieces):
             f = fs[h]
-            lo = lax.ppermute(f[rows - ny :], "space", up)
-            hi = lax.ppermute(f[:ny], "space", down)
+            if step == 0:
+                lo, hi = lo_all[:, p], hi_all[:, p]
+            else:
+                lo = lax.ppermute(f[rows - ny :], "space", up)
+                hi = lax.ppermute(f[:ny], "space", down)
             half = transport(f, lo, hi, coef[:, p], tm, ny)
             recvs.append(lax.all_to_all(half.reshape(groups, chunk, part, nx), "vel", 0, 0, tiled=True))
         moments = None
@@ -112,10 +117,16 @@
             moments = term if moments is None else moments + term
         delta = (rates[:, None, None] * moments).astype(jnp.bfloat16)
         fs = []
+        post = None
         for h, p in enumerate(pieces):
+            recv = recvs[h]
+            if post is not None:
+                post, recv = lax.optimization_barrier((post, recv))
+                fs[-1] = lax.all_to_all(post, "vel", 0, 0, tiled=True).reshape(rows, part, nx)
             adjustment = jnp.einsum("svk,krx->srvx", e3[:, p], delta, preferred_element_type=jnp.float32)
-            post = (recvs[h].astype(jnp.float32) - cm[None, :, None, :] * adjustment).astype(jnp.bfloat16)
-            fs.append(lax.all_to_all(post, "vel", 0, 0, tiled=True).reshape(rows, part, nx))
+            post = (recv.astype(jnp.float32) - cm[None, :, None, :] * adjustment).astype(jnp.bfloat16)
+            fs.append(None)
+        fs[-1] = lax.all_to_all(post, "vel", 0, 0, tiled=True).reshape(rows, part, nx)
     whole = jnp.concatenate(fs, axis=1)
     return jnp.transpose(whole.reshape(nzl, ny, vb, nx), (2, 0, 1, 3))
 

time: 311 us -> 306 us (0.984)
  starting transfers between devices: 55.8 us -> 48.5 us
  waiting for transfers between devices: 136 us -> 141 us
    ppermute x0 -> x2, waiting for transfers between devices: none -> 18 us  [the longest x1 15.5 us: per_device(): hi_all = lax.ppermute(whole[:ny], 'space', down)]
    ppermute x4 -> x2, waiting for transfers between devices: 18.2 us -> 3.51 us  [per_device(): hi = lax.ppermute(f[:ny], 'space', down)]
    all_to_all x4, waiting for transfers between devices: 45.1 us -> 59.5 us  [per_device(): lax.all_to_all(half.reshape(groups, chunk, part, nx), 'vel', 0, 0, tiled=...]
    ppermute x4 -> x2, waiting for transfers between devices: 25.3 us -> 18.1 us  [per_device(): lo = lax.ppermute(f[rows - ny:], 'space', up)]
    ppermute x4 -> x2, starting transfers between devices: 10.8 us -> 3.84 us  [per_device(): lo = lax.ppermute(f[rows - ny:], 'space', up)]
    convert_element_type x4 -> x2, local copies, waits for them, and re-layouts: 8.8 us -> 2.84 us  [per_device(): (recv.astype(jnp.float32) - cm[None, :, None, :] * adjustment).astype(jnp...]
    all_to_all x3, waiting for transfers between devices: 46.9 us -> 41.6 us  [per_device(): lax.all_to_all(post, 'vel', 0, 0, tiled=True).reshape(rows, part, nx)]
    optimization_barrier x0 -> x2, local copies, waits for them, and re-layouts: none -> 4.36 us  [per_device(): post, recv = lax.optimization_barrier((post, recv))]
  transfers between devices with their start and end apart: 15 -> 13, of which waited for: 15 -> 13; matrix products, arithmetic and copies ran while one was open for 9% -> 11% of each run, Pallas kernels for 5% -> 5%
where the time goes in v5:
time: 306 us; the launch traced here: 304 us
  waiting for transfers between devices  141 us (46%)
  starting transfers between devices  48.5 us (16%)
  local copies, waits for them, and re-layouts  37 us (12%)
  matrix products  29 us (9%)
  blocking collectives  26.5 us (9%)
  Pallas kernels  21.1 us (7%)
    all_to_all x4, waiting for transfers between devices, per_device(): lax.all_to_all(half.reshape(groups, chunk, part, nx), 'vel', 0, 0, tiled=...  59.5 us
    all_to_all x3, waiting for transfers between devices, per_device(): lax.all_to_all(post, 'vel', 0, 0, tiled=True).reshape(rows, part, nx)  41.6 us
    all_to_all x1, blocking collectives, per_device(): lax.all_to_all(post, 'vel', 0, 0, tiled=True).reshape(rows, part, nx)  26.5 us
    all_to_all x4, starting transfers between devices, per_device(): lax.all_to_all(half.reshape(groups, chunk, part, nx), 'vel', 0, 0, tiled=...  21.7 us
    pallas_call x4, Pallas kernels, transport(): pl.pallas_call(functools.partial(transport_kernel, ny), out_shape=jax.Sha...  21.1 us
    ppermute x2, waiting for transfers between devices, per_device(): lo = lax.ppermute(f[rows - ny:], 'space', up)  18.1 us
    unnamed x20, local copies, waits for them, and re-layouts  17 us
    ppermute x1, waiting for transfers between devices, per_device(): hi_all = lax.ppermute(whole[:ny], 'space', down)  15.5 us
  transfers between devices with their start and end apart: 13, of which 13 were waited for; matrix products, arithmetic and copies ran while one was open for 11% of the time, Pallas kernels for 5%

profile of v5, /device:TPU:32, one launch (start us, length us, event | category | flops | bytes accessed | tf_op | source)
XLA Modules:
  0.0 304.3 jit_solution(2438587086777179946)
XLA Ops:
  0.0 3.5 %copy.85 = bf16[448,2,16,128]{3,0,2,1:T(8,128)(2,1)S(1)} copy(bf16[448,2,16,128]{3,2,1,0:T(8,128)(2,1)} %param.6) | data formatting | bytes 7340032 | tf_op args[0]
  3.5 0.0 copy-start.7
  3.5 0.0 copy-start.6
  3.5 0.2 slice_bitcast_fusion.12
  3.7 1.9 collective-permute-start.1
  5.7 2.4 collective-permute-start
  8.1 0.1 fusion.37
  8.2 0.6 compare_convert_fusion
  8.8 2.1 fusion.32
  10.9 15.5 %collective-permute-done.1 = bf16[16,448,128]{2,1,0:T(8,128)(2,1)S(1)} collective-permute-done((bf16[16,448,128]{2,1,0:T(8,128)(2,1)S(1)}, bf16[16,448,128]{2,1,0:T(8,128)(2,1)S(1)}, u32[]{:S(2)}, u32[]{:S(2)}) %collective-permute-start.1) | collective-permute-done | bytes 1835040 | tf_op jit(solution)/shard_map/ppermute | solution.py:101
  26.4 1.4 fusion.35
  27.7 2.5 collective-permute-done
  30.2 1.3 fusion.36
  31.6 0.9 broadcast_in_dim.30.coef_ref
  32.5 5.2 %shard_map.65 = bf16[32,224,128]{2,1,0:T(8,128)(2,1)} custom-call(bf16[32,224,128]{2,1,0:T(8,128)(2,1)} %get-tuple-element.14.f_ref, bf16[16,224,128]{2,1,0:T(8,128)(2,1)} %get-tuple-element.26.lo_ref, bf16[16,224,128]{2,1,0:T(8,128)(2,1)} %get-tuple-element.24.hi_ref, f32[3,224,128]{2,1,0:T(8,128)} %broadcast_in_dim.30.coef_ref, f32[32,128]{1,0:T(8,128)} %bitcast.162), custom_call_target="tpu_custom_call" | custom-call | flops 18350080 | bytes 3670016 | tf_op jit(solution)/shard_map/pallas_call | solution.py:61
  37.7 7.0 %all-to-all-start.1 = ((bf16[16,2,224,128]{3,2,1,0:T(8,128)(2,1)}), bf16[16,2,224,128]{3,2,1,0:T(8,128)(2,1)S(1)}, u32[]{:S(2)}, u32[]{:S(2)}) async-start(bf16[16,2,224,128]{3,2,1,0:T(8,128)(2,1)} %bitcast.156), calls=%async_computation.1 | async-start | bytes 3670016 | tf_op jit(solution)/shard_map/all_to_all | solution.py:113
  44.7 0.9 broadcast_in_dim.26.coef_ref
  45.6 5.3 %shard_map.64 = bf16[32,224,128]{2,1,0:T(8,128)(2,1)} custom-call(bf16[32,224,128]{2,1,0:T(8,128)(2,1)} %get-tuple-element.13.f_ref, bf16[16,224,128]{2,1,0:T(8,128)(2,1)} %get-tuple-element.25.lo_ref, bf16[16,224,128]{2,1,0:T(8,128)(2,1)} %get-tuple-element.23.hi_ref, f32[3,224,128]{2,1,0:T(8,128)} %broadcast_in_dim.26.coef_ref, f32[32,128]{1,0:T(8,128)} %bitcast.163), custom_call_target="tpu_custom_call" | custom-call | flops 18350080 | bytes 3670016 | tf_op jit(solution)/shard_map/pallas_call | solution.py:61
  50.9 21.3 %all-to-all-done.1 = bf16[16,2,224,128]{3,2,1,0:T(8,128)(2,1)S(1)} async-done(((bf16[16,2,224,128]{3,2,1,0:T(8,128)(2,1)}), bf16[16,2,224,128]{3,2,1,0:T(8,128)(2,1)S(1)}, u32[]{:S(2)}, u32[]{:S(2)}) %all-to-all-start.1) | async-done | bytes 1835040 | tf_op jit(solution)/shard_map/all_to_all | solution.py:113
  72.2 4.4 %all-to-all-start = ((bf16[16,2,224,128]{3,2,1,0:T(8,128)(2,1)}), bf16[16,2,224,128]{3,2,1,0:T(8,128)(2,1)}, u32[]{:S(2)}, u32[]{:S(2)}) async-start(bf16[16,2,224,128]{3,2,1,0:T(8,128)(2,1)} %bitcast.155), calls=%async_computation | async-start | bytes 3670016 | tf_op jit(solution)/shard_map/all_to_all | solution.py:113
  76.6 10.4 %copy.44 = bf16[512,7168]{0,1:T(8,128)(2,1)} copy(bf16[512,7168]{1,0:T(8,128)(2,1)} %param.9) | data formatting | bytes 14680064 | tf_op args[3]
  87.1 0.0 copy-start.8
  87.1 3.2 %fusion.12 = f32[2,128,512]{2,1,0:T(8,128)S(1)} fusion(bf16[16,2,224,128]{3,2,1,0:T(8,128)(2,1)S(1)} %all-to-all-done.1, bf16[512,16,448]{0,2,1:T(8,128)(2,1)} %bitcast.150), kind=kOutput, calls=%fused_computation.23 | convolution fusion | flops 939524096 | bytes 6029312 | tf_op jit(solution)/shard_map/ksv,srvx->krx/dot_general | solution.py:116
  90.2 11.3 %all-to-all-done = bf16[16,2,224,128]{3,2,1,0:T(8,128)(2,1)} async-done(((bf16[16,2,224,128]{3,2,1,0:T(8,128)(2,1)}), bf16[16,2,224,128]{3,2,1,0:T(8,128)(2,1)}, u32[]{:S(2)}, u32[]{:S(2)}) %all-to-all-start) | async-done | bytes 1835040 | tf_op jit(solution)/shard_map/all_to_all | solution.py:113
  101.5 3.7 %fusion.23 = bf16[512,2,128,1]{0,2,3,1:T(8,128)(2,1)S(1)} fusion(f32[2,128,512]{2,1,0:T(8,128)S(1)} %fusion.12, bf16[16,2,224,128]{3,2,1,0:T(8,128)(2,1)} %all-to-all-done, bf16[512,16,448]{0,2,1:T(8,128)(2,1)} %bitcast.151, f32[512]{0:T(512)S(1)} %copy-done.8), kind=kOutput, calls=%fused_computation.34 | convolution fusion | flops 939917312 | bytes 6293504 | tf_op jit(solution)/shard_map/ksv,srvx->krx/dot_general | solution.py:116
  105.2 5.1 %fusion.3 = bf16[16,2,224,128]{3,2,0,1:T(8,128)(2,1)} fusion(bf16[16,2,224,128]{3,2,1,0:T(8,128)(2,1)} %all-to-all-done, f32[2,128]{1,0:T(2,128)S(1)} %constant_dynamic-slice_fusion, bf16[512,2,128,1]{0,2,3,1:T(8,128)(2,1)S(1)} %fusion.23, bf16[16,448,512]{2,1,0:T(8,128)(2,1)} %bitcast.170), kind=kOutput, calls=%fused_computation.12 | convolution fusion | flops 943194112 | bytes 7603200 | tf_op jit(solution)/shard_map/svk,krx->srvx/dot_general | solution.py:126
  110.3 3.2 %fusion.2 = bf16[16,2,224,128]{3,2,0,1:T(8,128)(2,1)S(1)} fusion(bf16[16,2,224,128]{3,2,1,0:T(8,128)(2,1)S(1)} %all-to-all-done.1, f32[2,128]{1,0:T(2,128)S(1)} %constant_dynamic-slice_fusion, bf16[512,2,128,1]{0,2,3,1:T(8,128)(2,1)S(1)} %fusion.23, bf16[16,448,512]{2,1,0:T(8,128)(2,1)} %bitcast.171), kind=kOutput, calls=%fused_computation.10 | convolution fusion | flops 943194112 | bytes 7603200 | tf_op jit(solution)/shard_map/svk,krx->srvx/dot_general | solution.py:126
  113.5 1.4 copy.53
  115.0 3.7 %all-to-all-start.4 = ((bf16[16,2,224,128]{3,2,1,0:T(8,128)(2,1)}), bf16[16,2,224,128]{3,2,1,0:T(8,128)(2,1)S(1)}, u32[]{:S(2)}, u32[]{:S(2)}) async-start(bf16[16,2,224,128]{3,2,1,0:T(8,128)(2,1)} %copy.53), calls=%async_computation.4 | async-start | bytes 3670016 | tf_op jit(solution)/shard_map/all_to_all | solution.py:129
  118.7 2.9 copy.48
  121.6 21.9 %all-to-all-done.4 = bf16[16,2,224,128]{3,2,1,0:T(8,128)(2,1)S(1)} async-done(((bf16[16,2,224,128]{3,2,1,0:T(8,128)(2,1)}), bf16[16,2,224,128]{3,2,1,0:T(8,128)(2,1)S(1)}, u32[]{:S(2)}, u32[]{:S(2)}) %all-to-all-start.4) | async-done | bytes 1835040 | tf_op jit(solution)/shard_map/all_to_all | solution.py:129
  143.5 1.2 copy-done.1
  144.8 3.7 %all-to-all-start.2 = ((bf16[16,2,224,128]{3,2,1,0:T(8,128)(2,1)}), bf16[16,2,224,128]{3,2,1,0:T(8,128)(2,1)S(1)}, u32[]{:S(2)}, u32[]{:S(2)}) async-start(bf16[16,2,224,128]{3,2,1,0:T(8,128)(2,1)} %copy.48), calls=%async_computation.2 | async-start | bytes 3670016 | tf_op jit(solution)/shard_map/all_to_all | solution.py:125
  148.5 1.6 fusion.34
  150.1 1.9 collective-permute-start.4
  152.0 3.8 %collective-permute-start.5 = (bf16[16,224,128]{2,1,0:T(8,128)(2,1)S(1)}, bf16[16,224,128]{2,1,0:T(8,128)(2,1)S(1)}, u32[]{:S(2)}, u32[]{:S(2)}) collective-permute-start(bf16[16,224,128]{2,1,0:T(8,128)(2,1)S(1)} %bitcast.158), channel_id=1, source_target_pairs={{16,0},{32,16},{48,32},{64,48},{80,64},{96,80},{112,96},{17,1},{33... | collective-permute-start | bytes 2752520 | tf_op jit(solution)/shard_map/ppermute | solution.py:111
  155.8 9.0 %collective-permute-done.4.lo_ref = bf16[16,224,128]{2,1,0:T(8,128)(2,1)S(1)} collective-permute-done((bf16[16,224,128]{2,1,0:T(8,128)(2,1)S(1)}, bf16[16,224,128]{2,1,0:T(8,128)(2,1)S(1)}, u32[]{:S(2)}, u32[]{:S(2)}) %collective-permute-start.4) | collective-permute-done | bytes 917536 | tf_op jit(solution)/shard_map/ppermute | solution.py:110
  164.8 1.8 collective-permute-done.5.hi_ref
  166.5 1.0 copy-done.5
  167.5 5.3 %shard_map.67 = bf16[32,224,128]{2,1,0:T(8,128)(2,1)} custom-call(bf16[32,224,128]{2,1,0:T(8,128)(2,1)} %bitcast.147, bf16[16,224,128]{2,1,0:T(8,128)(2,1)} %copy-done.3, bf16[16,224,128]{2,1,0:T(8,128)(2,1)} %copy-done.5, f32[3,224,128]{2,1,0:T(8,128)} %broadcast_in_dim.30.coef_ref, f32[32,128]{1,0:T(8,128)} %bitcast.164), custom_call_target="tpu_custom_call" | custom-call | flops 18350080 | bytes 3670016 | tf_op jit(solution)/shard_map/pallas_call | solution.py:61
  172.8 0.7 all-to-all-done.2
  173.5 6.5 %all-to-all-start.5 = ((bf16[16,2,224,128]{3,2,1,0:T(8,128)(2,1)}), bf16[16,2,224,128]{3,2,1,0:T(8,128)(2,1)}, u32[]{:S(2)}, u32[]{:S(2)}) async-start(bf16[16,2,224,128]{3,2,1,0:T(8,128)(2,1)} %bitcast.154), calls=%async_computation.5 | async-start | bytes 3670016 | tf_op jit(solution)/shard_map/all_to_all | solution.py:113
  180.1 0.1 fusion.33
  180.2 0.0 copy-done
  180.2 1.9 collective-permute-start.2
  182.1 3.6 %collective-permute-start.3 = (bf16[16,224,128]{2,1,0:T(8,128)(2,1)S(1)}, bf16[16,224,128]{2,1,0:T(8,128)(2,1)S(1)}, u32[]{:S(2)}, u32[]{:S(2)}) collective-permute-start(bf16[16,224,128]{2,1,0:T(8,128)(2,1)S(1)} %bitcast.159), channel_id=1, source_target_pairs={{16,0},{32,16},{48,32},{64,48},{80,64},{96,80},{112,96},{17,1},{33... | collective-permute-start | bytes 2752520 | tf_op jit(solution)/shard_map/ppermute | solution.py:111
  185.8 9.1 %collective-permute-done.2.lo_ref = bf16[16,224,128]{2,1,0:T(8,128)(2,1)S(1)} collective-permute-done((bf16[16,224,128]{2,1,0:T(8,128)(2,1)S(1)}, bf16[16,224,128]{2,1,0:T(8,128)(2,1)S(1)}, u32[]{:S(2)}, u32[]{:S(2)}) %collective-permute-start.2) | collective-permute-done | bytes 917536 | tf_op jit(solution)/shard_map/ppermute | solution.py:110
  194.9 1.8 collective-permute-done.3.hi_ref
  196.7 0.9 copy-done.4
  197.6 5.3 %shard_map.66 = bf16[32,224,128]{2,1,0:T(8,128)(2,1)} custom-call(bf16[32,224,128]{2,1,0:T(8,128)(2,1)} %bitcast.146, bf16[16,224,128]{2,1,0:T(8,128)(2,1)} %copy-done.2, bf16[16,224,128]{2,1,0:T(8,128)(2,1)} %copy-done.4, f32[3,224,128]{2,1,0:T(8,128)} %broadcast_in_dim.26.coef_ref, f32[32,128]{1,0:T(8,128)} %bitcast.165), custom_call_target="tpu_custom_call" | custom-call | flops 18350080 | bytes 3670016 | tf_op jit(solution)/shard_map/pallas_call | solution.py:61
  202.9 5.1 %all-to-all-done.5 = bf16[16,2,224,128]{3,2,1,0:T(8,128)(2,1)} async-done(((bf16[16,2,224,128]{3,2,1,0:T(8,128)(2,1)}), bf16[16,2,224,128]{3,2,1,0:T(8,128)(2,1)}, u32[]{:S(2)}, u32[]{:S(2)}) %all-to-all-start.5) | async-done | bytes 1835040 | tf_op jit(solution)/shard_map/all_to_all | solution.py:113
  208.0 3.7 %all-to-all-start.3 = ((bf16[16,2,224,128]{3,2,1,0:T(8,128)(2,1)}), bf16[16,2,224,128]{3,2,1,0:T(8,128)(2,1)S(1)}, u32[]{:S(2)}, u32[]{:S(2)}) async-start(bf16[16,2,224,128]{3,2,1,0:T(8,128)(2,1)} %bitcast.157), calls=%async_computation.3 | async-start | bytes 3670016 | tf_op jit(solution)/shard_map/all_to_all | solution.py:113
  211.8 3.7 %fusion.13 = f32[2,128,512]{2,1,0:T(8,128)S(1)} fusion(bf16[16,2,224,128]{3,2,1,0:T(8,128)(2,1)} %all-to-all-done.5, bf16[512,16,448]{0,2,1:T(8,128)(2,1)} %bitcast.152), kind=kOutput, calls=%fused_computation.24 | convolution fusion | flops 939524096 | bytes 6029312 | tf_op jit(solution)/shard_map/ksv,srvx->krx/dot_general | solution.py:116
  215.5 21.9 %all-to-all-done.3 = bf16[16,2,224,128]{3,2,1,0:T(8,128)(2,1)S(1)} async-done(((bf16[16,2,224,128]{3,2,1,0:T(8,128)(2,1)}), bf16[16,2,224,128]{3,2,1,0:T(8,128)(2,1)S(1)}, u32[]{:S(2)}, u32[]{:S(2)}) %all-to-all-start.3) | async-done | bytes 1835040 | tf_op jit(solution)/shard_map/all_to_all | solution.py:113
  237.4 3.2 %fusion.22 = bf16[512,2,128,1]{0,2,3,1:T(8,128)(2,1)S(1)} fusion(f32[2,128,512]{2,1,0:T(8,128)S(1)} %fusion.13, bf16[16,2,224,128]{3,2,1,0:T(8,128)(2,1)S(1)} %all-to-all-done.3, bf16[512,16,448]{0,2,1:T(8,128)(2,1)} %bitcast.153, f32[512]{0:T(512)S(1)} %copy-done.8), kind=kOutput, calls=%fused_computation.33 | convolution fusion | flops 939917312 | bytes 6293504 | tf_op jit(solution)/shard_map/ksv,srvx->krx/dot_general | solution.py:116
  240.5 3.2 %fusion.1 = bf16[16,2,224,128]{3,2,0,1:T(8,128)(2,1)S(1)} fusion(bf16[16,2,224,128]{3,2,1,0:T(8,128)(2,1)S(1)} %all-to-all-done.3, f32[2,128]{1,0:T(2,128)S(1)} %constant_dynamic-slice_fusion, bf16[512,2,128,1]{0,2,3,1:T(8,128)(2,1)S(1)} %fusion.22, bf16[16,448,512]{2,1,0:T(8,128)(2,1)} %bitcast.172), kind=kOutput, calls=%fused_computation.8 | convolution fusion | flops 943194112 | bytes 7603200 | tf_op jit(solution)/shard_map/svk,krx->srvx/dot_general | solution.py:126
  243.7 1.4 copy.56
  245.2 3.7 %all-to-all-start.6 = ((bf16[16,2,224,128]{3,2,1,0:T(8,128)(2,1)}), bf16[16,2,224,128]{3,2,1,0:T(8,128)(2,1)S(1)}, u32[]{:S(2)}, u32[]{:S(2)}) async-start(bf16[16,2,224,128]{3,2,1,0:T(8,128)(2,1)} %copy.56), calls=%async_computation.6 | async-start | bytes 3670016 | tf_op jit(solution)/shard_map/all_to_all | solution.py:125
  248.9 3.8 %fusion = bf16[16,2,224,128]{3,2,0,1:T(8,128)(2,1)S(1)} fusion(bf16[16,2,224,128]{3,2,1,0:T(8,128)(2,1)} %all-to-all-done.5, f32[2,128]{1,0:T(2,128)S(1)} %constant_dynamic-slice_fusion, bf16[512,2,128,1]{0,2,3,1:T(8,128)(2,1)S(1)} %fusion.22, bf16[16,448,512]{2,1,0:T(8,128)(2,1)} %bitcast.173), kind=kOutput, calls=%fused_computation.6 | convolution fusion | flops 943194112 | bytes 7603200 | tf_op jit(solution)/shard_map/svk,krx->srvx/dot_general | solution.py:126
  252.7 1.4 copy.59
  254.1 19.0 %all-to-all-done.6 = bf16[16,2,224,128]{3,2,1,0:T(8,128)(2,1)S(1)} async-done(((bf16[16,2,224,128]{3,2,1,0:T(8,128)(2,1)}), bf16[16,2,224,128]{3,2,1,0:T(8,128)(2,1)S(1)}, u32[]{:S(2)}, u32[]{:S(2)}) %all-to-all-start.6) | async-done | bytes 1835040 | tf_op jit(solution)/shard_map/all_to_all | solution.py:125
  273.1 26.5 %all_to_all.40 = bf16[16,2,224,128]{3,2,1,0:T(8,128)(2,1)S(1)} all-to-all(bf16[16,2,224,128]{3,2,1,0:T(8,128)(2,1)} %copy.59), channel_id=1, replica_groups=mesh['space'=8,'vel'=16] {'vel'}, dimensions={0} | all-to-all | bytes 3670016 | tf_op jit(solution)/shard_map/all_to_all | solution.py:129
  299.6 0.4 maximum_bitcast_fusion
  300.1 4.2 %copy.60 = bf16[448,2,16,128]{3,2,1,0:T(8,128)(2,1)} copy(bf16[448,2,16,128]{3,0,2,1:T(8,128)(2,1)S(1)} %maximum_bitcast_fusion) | data formatting | bytes 7340032 | tf_op jit(solution)/shard_map/transpose | solution.py:131
  (15 shorter events, 0.1 us)
Async XLA Ops:
  3.5 4.6 %copy-start.7 = (s32[448]{0:T(512)S(1)}, s32[448]{0:T(512)}, u32[]{:S(2)}) copy-start(s32[448]{0:T(512)} %param.7) | copy-start | bytes 5380
  3.5 4.7 %copy-start.6 = (s32[2,16,128]{2,1,0:T(8,128)S(1)}, s32[2,16,128]{2,1,0:T(8,128)}, u32[]{:S(2)}) copy-start(s32[2,16,128]{2,1,0:T(8,128)} %param.8) | copy-start | bytes 49156
  3.7 22.6 %collective-permute-start.1 = (bf16[16,448,128]{2,1,0:T(8,128)(2,1)S(1)}, bf16[16,448,128]{2,1,0:T(8,128)(2,1)S(1)}, u32[]{:S(2)}, u32[]{:S(2)}) collective-permute-start(bf16[16,448,128]{2,1,0:T(8,128)(2,1)S(1)} %get-tuple-element.15), channel_id=1, source_target_pairs={{16,0},{32,16},{48,32},{64,48},{80,64},{96,80},{112,96},{17,1},{33... | collective-permute-start | bytes 5505032 | tf_op jit(solution)/shard_map/ppermute | solution.py:101
  5.7 24.5 %collective-permute-start = (bf16[16,448,128]{2,1,0:T(8,128)(2,1)S(1)}, bf16[16,448,128]{2,1,0:T(8,128)(2,1)S(1)}, u32[]{:S(2)}, u32[]{:S(2)}) collective-permute-start(bf16[16,448,128]{2,1,0:T(8,128)(2,1)S(1)} %get-tuple-element.16), channel_id=1, source_target_pairs={{0,16},{16,32},{32,48},{48,64},{64,80},{80,96},{96,112},{1,17},{17... | collective-permute-start | bytes 5505032 | tf_op jit(solution)/shard_map/ppermute | solution.py:100
  37.7 34.5 %all-to-all-start.1 = ((bf16[16,2,224,128]{3,2,1,0:T(8,128)(2,1)}), bf16[16,2,224,128]{3,2,1,0:T(8,128)(2,1)S(1)}, u32[]{:S(2)}, u32[]{:S(2)}) async-start(bf16[16,2,224,128]{3,2,1,0:T(8,128)(2,1)} %bitcast.156), calls=%async_computation.1 | async-start | bytes 3670016 | tf_op jit(solution)/shard_map/all_to_all | solution.py:113
  72.2 29.3 %all-to-all-start = ((bf16[16,2,224,128]{3,2,1,0:T(8,128)(2,1)}), bf16[16,2,224,128]{3,2,1,0:T(8,128)(2,1)}, u32[]{:S(2)}, u32[]{:S(2)}) async-start(bf16[16,2,224,128]{3,2,1,0:T(8,128)(2,1)} %bitcast.155), calls=%async_computation | async-start | bytes 3670016 | tf_op jit(solution)/shard_map/all_to_all | solution.py:113
  87.1 14.5 %copy-start.8 = (f32[512]{0:T(512)S(1)}, f32[512]{0:T(512)}, u32[]{:S(2)}) copy-start(f32[512]{0:T(512)} %param.11) | copy-start | bytes 6148
  115.0 28.6 %all-to-all-start.4 = ((bf16[16,2,224,128]{3,2,1,0:T(8,128)(2,1)}), bf16[16,2,224,128]{3,2,1,0:T(8,128)(2,1)S(1)}, u32[]{:S(2)}, u32[]{:S(2)}) async-start(bf16[16,2,224,128]{3,2,1,0:T(8,128)(2,1)} %copy.53), calls=%async_computation.4 | async-start | bytes 3670016 | tf_op jit(solution)/shard_map/all_to_all | solution.py:129
  143.5 1.2 copy-start.1
  144.8 28.8 %all-to-all-start.2 = ((bf16[16,2,224,128]{3,2,1,0:T(8,128)(2,1)}), bf16[16,2,224,128]{3,2,1,0:T(8,128)(2,1)S(1)}, u32[]{:S(2)}, u32[]{:S(2)}) async-start(bf16[16,2,224,128]{3,2,1,0:T(8,128)(2,1)} %copy.48), calls=%async_computation.2 | async-start | bytes 3670016 | tf_op jit(solution)/shard_map/all_to_all | solution.py:125
  150.1 14.7 %collective-permute-start.4 = (bf16[16,224,128]{2,1,0:T(8,128)(2,1)S(1)}, bf16[16,224,128]{2,1,0:T(8,128)(2,1)S(1)}, u32[]{:S(2)}, u32[]{:S(2)}) collective-permute-start(bf16[16,224,128]{2,1,0:T(8,128)(2,1)S(1)} %bitcast.160), channel_id=1, source_target_pairs={{0,16},{16,32},{32,48},{48,64},{64,80},{80,96},{96,112},{1,17},{17... | collective-permute-start | bytes 2752520 | tf_op jit(solution)/shard_map/ppermute | solution.py:110
  152.0 14.5 %collective-permute-start.5 = (bf16[16,224,128]{2,1,0:T(8,128)(2,1)S(1)}, bf16[16,224,128]{2,1,0:T(8,128)(2,1)S(1)}, u32[]{:S(2)}, u32[]{:S(2)}) collective-permute-start(bf16[16,224,128]{2,1,0:T(8,128)(2,1)S(1)} %bitcast.158), channel_id=1, source_target_pairs={{16,0},{32,16},{48,32},{64,48},{80,64},{96,80},{112,96},{17,1},{33... | collective-permute-start | bytes 2752520 | tf_op jit(solution)/shard_map/ppermute | solution.py:111
  164.8 2.7 copy-start.3
  166.5 1.0 copy-start.5
  173.5 6.7 %copy-start = (bf16[16,2,224,128]{3,2,1,0:T(8,128)(2,1)}, bf16[16,2,224,128]{3,2,1,0:T(8,128)(2,1)S(1)}, u32[]{:S(2)}) copy-start(bf16[16,2,224,128]{3,2,1,0:T(8,128)(2,1)S(1)} %all-to-all-done.2) | copy-start | bytes 5505028
  173.5 34.5 %all-to-all-start.5 = ((bf16[16,2,224,128]{3,2,1,0:T(8,128)(2,1)}), bf16[16,2,224,128]{3,2,1,0:T(8,128)(2,1)}, u32[]{:S(2)}, u32[]{:S(2)}) async-start(bf16[16,2,224,128]{3,2,1,0:T(8,128)(2,1)} %bitcast.154), calls=%async_computation.5 | async-start | bytes 3670016 | tf_op jit(solution)/shard_map/all_to_all | solution.py:113
  180.2 14.7 %collective-permute-start.2 = (bf16[16,224,128]{2,1,0:T(8,128)(2,1)S(1)}, bf16[16,224,128]{2,1,0:T(8,128)(2,1)S(1)}, u32[]{:S(2)}, u32[]{:S(2)}) collective-permute-start(bf16[16,224,128]{2,1,0:T(8,128)(2,1)S(1)} %bitcast.161), channel_id=1, source_target_pairs={{0,16},{16,32},{32,48},{48,64},{64,80},{80,96},{96,112},{1,17},{17... | collective-permute-start | bytes 2752520 | tf_op jit(solution)/shard_map/ppermute | solution.py:110
  182.1 14.5 %collective-permute-start.3 = (bf16[16,224,128]{2,1,0:T(8,128)(2,1)S(1)}, bf16[16,224,128]{2,1,0:T(8,128)(2,1)S(1)}, u32[]{:S(2)}, u32[]{:S(2)}) collective-permute-start(bf16[16,224,128]{2,1,0:T(8,128)(2,1)S(1)} %bitcast.159), channel_id=1, source_target_pairs={{16,0},{32,16},{48,32},{64,48},{80,64},{96,80},{112,96},{17,1},{33... | collective-permute-start | bytes 2752520 | tf_op jit(solution)/shard_map/ppermute | solution.py:111
  194.9 1.8 copy-start.2
  196.7 0.9 copy-start.4
  208.0 29.3 %all-to-all-start.3 = ((bf16[16,2,224,128]{3,2,1,0:T(8,128)(2,1)}), bf16[16,2,224,128]{3,2,1,0:T(8,128)(2,1)S(1)}, u32[]{:S(2)}, u32[]{:S(2)}) async-start(bf16[16,2,224,128]{3,2,1,0:T(8,128)(2,1)} %bitcast.157), calls=%async_computation.3 | async-start | bytes 3670016 | tf_op jit(solution)/shard_map/all_to_all | solution.py:113
  245.2 27.9 %all-to-all-start.6 = ((bf16[16,2,224,128]{3,2,1,0:T(8,128)(2,1)}), bf16[16,2,224,128]{3,2,1,0:T(8,128)(2,1)S(1)}, u32[]{:S(2)}, u32[]{:S(2)}) async-start(bf16[16,2,224,128]{3,2,1,0:T(8,128)(2,1)} %copy.56), calls=%async_computation.6 | async-start | bytes 3670016 | tf_op jit(solution)/shard_map/all_to_all | solution.py:125

commit v6 on v5

--- a/solution.py
+++ b/solution.py
@@ -6,6 +6,7 @@
 from jax.experimental import pallas as pl
 from jax.experimental.pallas import tpu as pltpu
 from jax.sharding import PartitionSpec as P
+
 
 VGRID = 24
 STEPS = 2
@@ -97,15 +98,16 @@
     pieces = [slice(h * part, (h + 1) * part) for h in range(PARTS)]
 
     whole = jnp.transpose(dist, (1, 2, 0, 3)).reshape(rows, vb, nx)
-    lo_all = lax.ppermute(whole[rows - ny :], "space", up)
-    hi_all = lax.ppermute(whole[:ny], "space", down)
     fs = [whole[:, p] for p in pieces]
+    halos = []
+    for f in fs:
+        halos.append((lax.ppermute(f[rows - ny :], "space", up), lax.ppermute(f[:ny], "space", down)))
     for step in range(STEPS):
         recvs = []
         for h, p in enumerate(pieces):
             f = fs[h]
             if step == 0:
-                lo, hi = lo_all[:, p], hi_all[:, p]
+                lo, hi = halos[h]
             else:
                 lo = lax.ppermute(f[rows - ny :], "space", up)
                 hi = lax.ppermute(f[:ny], "space", down)

time: 306 us -> 305 us (level)
  waiting for transfers between devices: 141 us -> 133 us
  starting transfers between devices: 48.5 us -> 55.4 us
    all_to_all x4, waiting for transfers between devices: 59.5 us -> 44.9 us  [per_device(): lax.all_to_all(half.reshape(groups, chunk, part, nx), 'vel', 0, 0, tiled=...]
    ppermute x2 -> x4, starting transfers between devices: 4.33 us -> 8.64 us  [the longest x2 4.81 us: per_device(): lax.ppermute(f[rows - ny:], 'space', up)]
    ppermute x2 -> x4, waiting for transfers between devices: 18 us -> 21.8 us  [the longest x2 14.5 us: per_device(): lax.ppermute(f[:ny], 'space', down)]
    transpose x0 -> x1, local copies, waits for them, and re-layouts: none -> 3.46 us  [per_device(): whole = jnp.transpose(dist, (1, 2, 0, 3)).reshape(rows, vb, nx)]
    unnamed x20 -> x27, local copies, waits for them, and re-layouts: 17 us -> 14.6 us
  transfers between devices with their start and end apart: 13 -> 15, of which waited for: 13 -> 15; matrix products, arithmetic and copies ran while one was open for 11% -> 10% of each run, Pallas kernels for 5% -> 5%
where the time goes in v6:
time: 305 us; the launch traced here: 304 us
  waiting for transfers between devices  133 us (44%)
  starting transfers between devices  55.4 us (18%)
  local copies, waits for them, and re-layouts  36.5 us (12%)
  matrix products  29 us (10%)
  blocking collectives  27.3 us (9%)
  Pallas kernels  21.2 us (7%)
    all_to_all x4, waiting for transfers between devices, per_device(): lax.all_to_all(half.reshape(groups, chunk, part, nx), 'vel', 0, 0, tiled=...  44.9 us
    all_to_all x3, waiting for transfers between devices, per_device(): lax.all_to_all(post, 'vel', 0, 0, tiled=True).reshape(rows, part, nx)  44.5 us
    all_to_all x1, blocking collectives, per_device(): lax.all_to_all(post, 'vel', 0, 0, tiled=True).reshape(rows, part, nx)  27.3 us
    all_to_all x4, starting transfers between devices, per_device(): lax.all_to_all(half.reshape(groups, chunk, part, nx), 'vel', 0, 0, tiled=...  22.4 us
    pallas_call x4, Pallas kernels, transport(): pl.pallas_call(functools.partial(transport_kernel, ny), out_shape=jax.Sha...  21.2 us
    ppermute x2, waiting for transfers between devices, per_device(): lo = lax.ppermute(f[rows - ny:], 'space', up)  17.9 us
    dot_general x4, matrix products, per_device(): jnp.einsum('svk,krx->srvx', e3[:, p], delta, preferred_element_type=jnp.f...  15.2 us
    unnamed x27, local copies, waits for them, and re-layouts  14.6 us
  transfers between devices with their start and end apart: 15, of which 15 were waited for; matrix products, arithmetic and copies ran while one was open for 10% of the time, Pallas kernels for 5%

profile of v6, /device:TPU:32, one launch (start us, length us, event | category | flops | bytes accessed | tf_op | source)
XLA Modules:
  0.0 303.6 jit_solution(6428327551162990926)
XLA Ops:
  0.0 3.5 %copy.42 = bf16[2,16,448,128]{3,2,1,0:T(8,128)(2,1)S(1)} copy(bf16[2,16,448,128]{3,1,0,2:T(8,128)(2,1)} %bitcast.151) | data formatting | bytes 7340032 | tf_op jit(solution)/shard_map/transpose | solution.py:100
  3.5 1.2 fusion.32
  4.7 1.9 collective-permute-start.3
  6.6 2.4 collective-permute-start.2
  9.1 0.1 fusion.36
  9.2 0.6 compare_convert_fusion
  9.8 2.1 fusion.33
  11.8 5.7 %collective-permute-done.3.hi_ref = bf16[16,224,128]{2,1,0:T(8,128)(2,1)S(1)} collective-permute-done((bf16[16,224,128]{2,1,0:T(8,128)(2,1)S(1)}, bf16[16,224,128]{2,1,0:T(8,128)(2,1)S(1)}, u32[]{:S(2)}, u32[]{:S(2)}) %collective-permute-start.3) | collective-permute-done | bytes 917536 | tf_op jit(solution)/shard_map/ppermute | solution.py:104
  17.5 3.8 %collective-permute-done.2.lo_ref = bf16[16,224,128]{2,1,0:T(8,128)(2,1)S(1)} collective-permute-done((bf16[16,224,128]{2,1,0:T(8,128)(2,1)S(1)}, bf16[16,224,128]{2,1,0:T(8,128)(2,1)S(1)}, u32[]{:S(2)}, u32[]{:S(2)}) %collective-permute-start.2) | collective-permute-done | bytes 917536 | tf_op jit(solution)/shard_map/ppermute | solution.py:104
  21.3 1.1 broadcast_in_dim.30.coef_ref
  22.4 0.0 copy-done.3
  22.4 5.3 %shard_map.65 = bf16[32,224,128]{2,1,0:T(8,128)(2,1)} custom-call(bf16[32,224,128]{2,1,0:T(8,128)(2,1)} %get-tuple-element.18.f_ref, bf16[16,224,128]{2,1,0:T(8,128)(2,1)} %copy-done.3, bf16[16,224,128]{2,1,0:T(8,128)(2,1)} %copy-done.2, f32[3,224,128]{2,1,0:T(8,128)} %broadcast_in_dim.30.coef_ref, f32[32,128]{1,0:T(8,128)} %bitcast.156), custom_call_target="tpu_custom_call" | custom-call | flops 18350080 | bytes 3670016 | tf_op jit(solution)/shard_map/pallas_call | solution.py:62
  27.7 7.0 %all-to-all-start.1 = ((bf16[16,2,224,128]{3,2,1,0:T(8,128)(2,1)}), bf16[16,2,224,128]{3,2,1,0:T(8,128)(2,1)S(1)}, u32[]{:S(2)}, u32[]{:S(2)}) async-start(bf16[16,2,224,128]{3,2,1,0:T(8,128)(2,1)} %bitcast.149), calls=%async_computation.1 | async-start | bytes 3670016 | tf_op jit(solution)/shard_map/all_to_all | solution.py:115
  34.7 1.9 collective-permute-start.1
  36.7 2.4 collective-permute-start
  39.1 8.8 %collective-permute-done.1.hi_ref = bf16[16,224,128]{2,1,0:T(8,128)(2,1)S(1)} collective-permute-done((bf16[16,224,128]{2,1,0:T(8,128)(2,1)}, bf16[16,224,128]{2,1,0:T(8,128)(2,1)S(1)}, u32[]{:S(2)}, u32[]{:S(2)}) %collective-permute-start.1) | collective-permute-done | bytes 917536 | tf_op jit(solution)/shard_map/ppermute | solution.py:104
  47.9 3.5 %collective-permute-done.lo_ref = bf16[16,224,128]{2,1,0:T(8,128)(2,1)S(1)} collective-permute-done((bf16[16,224,128]{2,1,0:T(8,128)(2,1)S(1)}, bf16[16,224,128]{2,1,0:T(8,128)(2,1)S(1)}, u32[]{:S(2)}, u32[]{:S(2)}) %collective-permute-start) | collective-permute-done | bytes 917536 | tf_op jit(solution)/shard_map/ppermute | solution.py:104
  51.4 0.9 copy-done.7
  52.3 0.9 broadcast_in_dim.26.coef_ref
  53.2 5.3 %shard_map.64 = bf16[32,224,128]{2,1,0:T(8,128)(2,1)} custom-call(bf16[32,224,128]{2,1,0:T(8,128)(2,1)} %get-tuple-element.17.f_ref, bf16[16,224,128]{2,1,0:T(8,128)(2,1)} %copy-done.7, bf16[16,224,128]{2,1,0:T(8,128)(2,1)} %copy-done.4, f32[3,224,128]{2,1,0:T(8,128)} %broadcast_in_dim.26.coef_ref, f32[32,128]{1,0:T(8,128)} %bitcast.157), custom_call_target="tpu_custom_call" | custom-call | flops 18350080 | bytes 3670016 | tf_op jit(solution)/shard_map/pallas_call | solution.py:62
  58.5 2.8 all-to-all-done.1
  61.3 4.5 %all-to-all-start = ((bf16[16,2,224,128]{3,2,1,0:T(8,128)(2,1)}), bf16[16,2,224,128]{3,2,1,0:T(8,128)(2,1)}, u32[]{:S(2)}, u32[]{:S(2)}) async-start(bf16[16,2,224,128]{3,2,1,0:T(8,128)(2,1)} %bitcast.148), calls=%async_computation | async-start | bytes 3670016 | tf_op jit(solution)/shard_map/all_to_all | solution.py:115
  65.8 10.4 %copy.44 = bf16[512,7168]{0,1:T(8,128)(2,1)} copy(bf16[512,7168]{1,0:T(8,128)(2,1)} %param.9) | data formatting | bytes 14680064 | tf_op args[3]
  76.2 3.2 %fusion.12 = f32[2,128,512]{2,1,0:T(8,128)S(1)} fusion(bf16[16,2,224,128]{3,2,1,0:T(8,128)(2,1)S(1)} %all-to-all-done.1, bf16[512,16,448]{0,2,1:T(8,128)(2,1)} %bitcast.143), kind=kOutput, calls=%fused_computation.21 | convolution fusion | flops 939524096 | bytes 6029312 | tf_op jit(solution)/shard_map/ksv,srvx->krx/dot_general | solution.py:118
  79.4 13.5 %all-to-all-done = bf16[16,2,224,128]{3,2,1,0:T(8,128)(2,1)} async-done(((bf16[16,2,224,128]{3,2,1,0:T(8,128)(2,1)}), bf16[16,2,224,128]{3,2,1,0:T(8,128)(2,1)}, u32[]{:S(2)}, u32[]{:S(2)}) %all-to-all-start) | async-done | bytes 1835040 | tf_op jit(solution)/shard_map/all_to_all | solution.py:115
  92.9 3.7 %fusion.23 = bf16[512,2,128,1]{0,2,3,1:T(8,128)(2,1)S(1)} fusion(f32[2,128,512]{2,1,0:T(8,128)S(1)} %fusion.12, bf16[16,2,224,128]{3,2,1,0:T(8,128)(2,1)} %all-to-all-done, bf16[512,16,448]{0,2,1:T(8,128)(2,1)} %bitcast.144, f32[512]{0:T(512)S(1)} %copy-done.12), kind=kOutput, calls=%fused_computation.32 | convolution fusion | flops 939917312 | bytes 6293504 | tf_op jit(solution)/shard_map/ksv,srvx->krx/dot_general | solution.py:118
  96.6 5.1 %fusion.3 = bf16[16,2,224,128]{3,2,0,1:T(8,128)(2,1)} fusion(bf16[16,2,224,128]{3,2,1,0:T(8,128)(2,1)} %all-to-all-done, f32[2,128]{1,0:T(2,128)S(1)} %constant_dynamic-slice_fusion, bf16[512,2,128,1]{0,2,3,1:T(8,128)(2,1)S(1)} %fusion.23, bf16[16,448,512]{2,1,0:T(8,128)(2,1)} %bitcast.164), kind=kOutput, calls=%fused_computation.12 | convolution fusion | flops 943194112 | bytes 7603200 | tf_op jit(solution)/shard_map/svk,krx->srvx/dot_general | solution.py:128
  101.7 3.2 %fusion.2 = bf16[16,2,224,128]{3,2,0,1:T(8,128)(2,1)S(1)} fusion(bf16[16,2,224,128]{3,2,1,0:T(8,128)(2,1)S(1)} %all-to-all-done.1, f32[2,128]{1,0:T(2,128)S(1)} %constant_dynamic-slice_fusion, bf16[512,2,128,1]{0,2,3,1:T(8,128)(2,1)S(1)} %fusion.23, bf16[16,448,512]{2,1,0:T(8,128)(2,1)} %bitcast.165), kind=kOutput, calls=%fused_computation.10 | convolution fusion | flops 943194112 | bytes 7603200 | tf_op jit(solution)/shard_map/svk,krx->srvx/dot_general | solution.py:128
  104.9 1.4 copy.53
  106.3 3.8 %all-to-all-start.4 = ((bf16[16,2,224,128]{3,2,1,0:T(8,128)(2,1)}), bf16[16,2,224,128]{3,2,1,0:T(8,128)(2,1)S(1)}, u32[]{:S(2)}, u32[]{:S(2)}) async-start(bf16[16,2,224,128]{3,2,1,0:T(8,128)(2,1)} %copy.53), calls=%async_computation.4 | async-start | bytes 3670016 | tf_op jit(solution)/shard_map/all_to_all | solution.py:131
  110.1 2.9 copy.48
  113.0 22.0 %all-to-all-done.4 = bf16[16,2,224,128]{3,2,1,0:T(8,128)(2,1)S(1)} async-done(((bf16[16,2,224,128]{3,2,1,0:T(8,128)(2,1)}), bf16[16,2,224,128]{3,2,1,0:T(8,128)(2,1)S(1)}, u32[]{:S(2)}, u32[]{:S(2)}) %all-to-all-start.4) | async-done | bytes 1835040 | tf_op jit(solution)/shard_map/all_to_all | solution.py:131
  135.0 1.2 copy-done.1
  136.2 3.7 %all-to-all-start.2 = ((bf16[16,2,224,128]{3,2,1,0:T(8,128)(2,1)}), bf16[16,2,224,128]{3,2,1,0:T(8,128)(2,1)S(1)}, u32[]{:S(2)}, u32[]{:S(2)}) async-start(bf16[16,2,224,128]{3,2,1,0:T(8,128)(2,1)} %copy.48), calls=%async_computation.2 | async-start | bytes 3670016 | tf_op jit(solution)/shard_map/all_to_all | solution.py:127
  139.9 1.6 fusion.35
  141.5 1.9 collective-permute-start.6
  143.5 3.8 %collective-permute-start.7 = (bf16[16,224,128]{2,1,0:T(8,128)(2,1)S(1)}, bf16[16,224,128]{2,1,0:T(8,128)(2,1)S(1)}, u32[]{:S(2)}, u32[]{:S(2)}) collective-permute-start(bf16[16,224,128]{2,1,0:T(8,128)(2,1)S(1)} %bitcast.152), channel_id=1, source_target_pairs={{16,0},{32,16},{48,32},{64,48},{80,64},{96,80},{112,96},{17,1},{33... | collective-permute-start | bytes 2752520 | tf_op jit(solution)/shard_map/ppermute | solution.py:113
  147.3 9.0 %collective-permute-done.6.lo_ref = bf16[16,224,128]{2,1,0:T(8,128)(2,1)S(1)} collective-permute-done((bf16[16,224,128]{2,1,0:T(8,128)(2,1)S(1)}, bf16[16,224,128]{2,1,0:T(8,128)(2,1)S(1)}, u32[]{:S(2)}, u32[]{:S(2)}) %collective-permute-start.6) | collective-permute-done | bytes 917536 | tf_op jit(solution)/shard_map/ppermute | solution.py:112
  156.3 1.8 collective-permute-done.7.hi_ref
  158.0 1.0 copy-done.9
  159.0 5.3 %shard_map.67 = bf16[32,224,128]{2,1,0:T(8,128)(2,1)} custom-call(bf16[32,224,128]{2,1,0:T(8,128)(2,1)} %bitcast.140, bf16[16,224,128]{2,1,0:T(8,128)(2,1)} %copy-done.6, bf16[16,224,128]{2,1,0:T(8,128)(2,1)} %copy-done.9, f32[3,224,128]{2,1,0:T(8,128)} %broadcast_in_dim.30.coef_ref, f32[32,128]{1,0:T(8,128)} %bitcast.158), custom_call_target="tpu_custom_call" | custom-call | flops 18350080 | bytes 3670016 | tf_op jit(solution)/shard_map/pallas_call | solution.py:62
  164.3 0.7 all-to-all-done.2
  165.0 6.5 %all-to-all-start.5 = ((bf16[16,2,224,128]{3,2,1,0:T(8,128)(2,1)}), bf16[16,2,224,128]{3,2,1,0:T(8,128)(2,1)}, u32[]{:S(2)}, u32[]{:S(2)}) async-start(bf16[16,2,224,128]{3,2,1,0:T(8,128)(2,1)} %bitcast.147), calls=%async_computation.5 | async-start | bytes 3670016 | tf_op jit(solution)/shard_map/all_to_all | solution.py:115
  171.6 0.1 fusion.34
  171.7 3.9 %collective-permute-start.4 = (bf16[16,224,128]{2,1,0:T(8,128)(2,1)S(1)}, bf16[16,224,128]{2,1,0:T(8,128)(2,1)S(1)}, u32[]{:S(2)}, u32[]{:S(2)}) collective-permute-start(bf16[16,224,128]{2,1,0:T(8,128)(2,1)S(1)} %bitcast.155), channel_id=1, source_target_pairs={{0,16},{16,32},{32,48},{48,64},{64,80},{80,96},{96,112},{1,17},{17... | collective-permute-start | bytes 2752520 | tf_op jit(solution)/shard_map/ppermute | solution.py:112
  175.6 1.9 collective-permute-start.5
  177.5 8.9 %collective-permute-done.4.lo_ref = bf16[16,224,128]{2,1,0:T(8,128)(2,1)S(1)} collective-permute-done((bf16[16,224,128]{2,1,0:T(8,128)(2,1)S(1)}, bf16[16,224,128]{2,1,0:T(8,128)(2,1)S(1)}, u32[]{:S(2)}, u32[]{:S(2)}) %collective-permute-start.4) | collective-permute-done | bytes 917536 | tf_op jit(solution)/shard_map/ppermute | solution.py:112
  186.4 2.0 collective-permute-done.5.hi_ref
  188.4 0.9 copy-done.8
  189.3 5.4 %shard_map.66 = bf16[32,224,128]{2,1,0:T(8,128)(2,1)} custom-call(bf16[32,224,128]{2,1,0:T(8,128)(2,1)} %bitcast.139, bf16[16,224,128]{2,1,0:T(8,128)(2,1)} %copy-done.5, bf16[16,224,128]{2,1,0:T(8,128)(2,1)} %copy-done.8, f32[3,224,128]{2,1,0:T(8,128)} %broadcast_in_dim.26.coef_ref, f32[32,128]{1,0:T(8,128)} %bitcast.159), custom_call_target="tpu_custom_call" | custom-call | flops 18350080 | bytes 3670016 | tf_op jit(solution)/shard_map/pallas_call | solution.py:62
  194.7 4.5 %all-to-all-done.5 = bf16[16,2,224,128]{3,2,1,0:T(8,128)(2,1)} async-done(((bf16[16,2,224,128]{3,2,1,0:T(8,128)(2,1)}), bf16[16,2,224,128]{3,2,1,0:T(8,128)(2,1)}, u32[]{:S(2)}, u32[]{:S(2)}) %all-to-all-start.5) | async-done | bytes 1835040 | tf_op jit(solution)/shard_map/all_to_all | solution.py:115
  199.2 4.3 %all-to-all-start.3 = ((bf16[16,2,224,128]{3,2,1,0:T(8,128)(2,1)}), bf16[16,2,224,128]{3,2,1,0:T(8,128)(2,1)S(1)}, u32[]{:S(2)}, u32[]{:S(2)}) async-start(bf16[16,2,224,128]{3,2,1,0:T(8,128)(2,1)} %bitcast.150), calls=%async_computation.3 | async-start | bytes 3670016 | tf_op jit(solution)/shard_map/all_to_all | solution.py:115
  203.4 3.7 %fusion.13 = f32[2,128,512]{2,1,0:T(8,128)S(1)} fusion(bf16[16,2,224,128]{3,2,1,0:T(8,128)(2,1)} %all-to-all-done.5, bf16[512,16,448]{0,2,1:T(8,128)(2,1)} %bitcast.145), kind=kOutput, calls=%fused_computation.22 | convolution fusion | flops 939524096 | bytes 6029312 | tf_op jit(solution)/shard_map/ksv,srvx->krx/dot_general | solution.py:118
  207.2 24.2 %all-to-all-done.3 = bf16[16,2,224,128]{3,2,1,0:T(8,128)(2,1)S(1)} async-done(((bf16[16,2,224,128]{3,2,1,0:T(8,128)(2,1)}), bf16[16,2,224,128]{3,2,1,0:T(8,128)(2,1)S(1)}, u32[]{:S(2)}, u32[]{:S(2)}) %all-to-all-start.3) | async-done | bytes 1835040 | tf_op jit(solution)/shard_map/all_to_all | solution.py:115
  231.4 3.2 %fusion.22 = bf16[512,2,128,1]{0,2,3,1:T(8,128)(2,1)S(1)} fusion(f32[2,128,512]{2,1,0:T(8,128)S(1)} %fusion.13, bf16[16,2,224,128]{3,2,1,0:T(8,128)(2,1)S(1)} %all-to-all-done.3, bf16[512,16,448]{0,2,1:T(8,128)(2,1)} %bitcast.146, f32[512]{0:T(512)S(1)} %copy-done.12), kind=kOutput, calls=%fused_computation.31 | convolution fusion | flops 939917312 | bytes 6293504 | tf_op jit(solution)/shard_map/ksv,srvx->krx/dot_general | solution.py:118
  234.6 3.2 %fusion.1 = bf16[16,2,224,128]{3,2,0,1:T(8,128)(2,1)S(1)} fusion(bf16[16,2,224,128]{3,2,1,0:T(8,128)(2,1)S(1)} %all-to-all-done.3, f32[2,128]{1,0:T(2,128)S(1)} %constant_dynamic-slice_fusion, bf16[512,2,128,1]{0,2,3,1:T(8,128)(2,1)S(1)} %fusion.22, bf16[16,448,512]{2,1,0:T(8,128)(2,1)} %bitcast.166), kind=kOutput, calls=%fused_computation.8 | convolution fusion | flops 943194112 | bytes 7603200 | tf_op jit(solution)/shard_map/svk,krx->srvx/dot_general | solution.py:128
  237.8 1.5 copy.56
  239.2 5.4 %all-to-all-start.6 = ((bf16[16,2,224,128]{3,2,1,0:T(8,128)(2,1)}), bf16[16,2,224,128]{3,2,1,0:T(8,128)(2,1)S(1)}, u32[]{:S(2)}, u32[]{:S(2)}) async-start(bf16[16,2,224,128]{3,2,1,0:T(8,128)(2,1)} %copy.56), calls=%async_computation.6 | async-start | bytes 3670016 | tf_op jit(solution)/shard_map/all_to_all | solution.py:127
  244.6 3.8 %fusion = bf16[16,2,224,128]{3,2,0,1:T(8,128)(2,1)S(1)} fusion(bf16[16,2,224,128]{3,2,1,0:T(8,128)(2,1)} %all-to-all-done.5, f32[2,128]{1,0:T(2,128)S(1)} %constant_dynamic-slice_fusion, bf16[512,2,128,1]{0,2,3,1:T(8,128)(2,1)S(1)} %fusion.22, bf16[16,448,512]{2,1,0:T(8,128)(2,1)} %bitcast.167), kind=kOutput, calls=%fused_computation.6 | convolution fusion | flops 943194112 | bytes 7603200 | tf_op jit(solution)/shard_map/svk,krx->srvx/dot_general | solution.py:128
  248.4 1.4 copy.59
  249.8 21.8 %all-to-all-done.6 = bf16[16,2,224,128]{3,2,1,0:T(8,128)(2,1)S(1)} async-done(((bf16[16,2,224,128]{3,2,1,0:T(8,128)(2,1)}), bf16[16,2,224,128]{3,2,1,0:T(8,128)(2,1)S(1)}, u32[]{:S(2)}, u32[]{:S(2)}) %all-to-all-start.6) | async-done | bytes 1835040 | tf_op jit(solution)/shard_map/all_to_all | solution.py:127
  271.7 27.3 %all_to_all.40 = bf16[16,2,224,128]{3,2,1,0:T(8,128)(2,1)S(1)} all-to-all(bf16[16,2,224,128]{3,2,1,0:T(8,128)(2,1)} %copy.59), channel_id=1, replica_groups=mesh['space'=8,'vel'=16] {'vel'}, dimensions={0} | all-to-all | bytes 3670016 | tf_op jit(solution)/shard_map/all_to_all | solution.py:131
  299.0 0.4 maximum_bitcast_fusion
  299.4 4.2 %copy.60 = bf16[448,2,16,128]{3,2,1,0:T(8,128)(2,1)} copy(bf16[448,2,16,128]{3,0,2,1:T(8,128)(2,1)S(1)} %maximum_bitcast_fusion) | data formatting | bytes 7340032 | tf_op jit(solution)/shard_map/transpose | solution.py:133
  (25 shorter events, 0.1 us)
Async XLA Ops:
  3.5 5.6 %copy-start.11 = (s32[448]{0:T(512)S(1)}, s32[448]{0:T(512)}, u32[]{:S(2)}) copy-start(s32[448]{0:T(512)} %param.7) | copy-start | bytes 5380
  3.5 5.7 %copy-start.10 = (s32[2,16,128]{2,1,0:T(8,128)S(1)}, s32[2,16,128]{2,1,0:T(8,128)}, u32[]{:S(2)}) copy-start(s32[2,16,128]{2,1,0:T(8,128)} %param.8) | copy-start | bytes 49156
  4.7 12.8 %collective-permute-start.3 = (bf16[16,224,128]{2,1,0:T(8,128)(2,1)S(1)}, bf16[16,224,128]{2,1,0:T(8,128)(2,1)S(1)}, u32[]{:S(2)}, u32[]{:S(2)}) collective-permute-start(bf16[16,224,128]{2,1,0:T(8,128)(2,1)S(1)} %get-tuple-element.14), channel_id=1, source_target_pairs={{16,0},{32,16},{48,32},{64,48},{80,64},{96,80},{112,96},{17,1},{33... | collective-permute-start | bytes 2752520 | tf_op jit(solution)/shard_map/ppermute | solution.py:104
  6.6 14.7 %collective-permute-start.2 = (bf16[16,224,128]{2,1,0:T(8,128)(2,1)S(1)}, bf16[16,224,128]{2,1,0:T(8,128)(2,1)S(1)}, u32[]{:S(2)}, u32[]{:S(2)}) collective-permute-start(bf16[16,224,128]{2,1,0:T(8,128)(2,1)S(1)} %get-tuple-element.15), channel_id=1, source_target_pairs={{0,16},{16,32},{32,48},{48,64},{64,80},{80,96},{96,112},{1,17},{17... | collective-permute-start | bytes 2752520 | tf_op jit(solution)/shard_map/ppermute | solution.py:104
  17.5 4.9 %copy-start.2 = (bf16[16,224,128]{2,1,0:T(8,128)(2,1)}, bf16[16,224,128]{2,1,0:T(8,128)(2,1)S(1)}, u32[]{:S(2)}) copy-start(bf16[16,224,128]{2,1,0:T(8,128)(2,1)S(1)} %collective-permute-done.3.hi_ref) | copy-start | bytes 2752516
  21.3 1.1 copy-start.3
  27.7 33.6 %all-to-all-start.1 = ((bf16[16,2,224,128]{3,2,1,0:T(8,128)(2,1)}), bf16[16,2,224,128]{3,2,1,0:T(8,128)(2,1)S(1)}, u32[]{:S(2)}, u32[]{:S(2)}) async-start(bf16[16,2,224,128]{3,2,1,0:T(8,128)(2,1)} %bitcast.149), calls=%async_computation.1 | async-start | bytes 3670016 | tf_op jit(solution)/shard_map/all_to_all | solution.py:115
  34.7 13.1 %collective-permute-start.1 = (bf16[16,224,128]{2,1,0:T(8,128)(2,1)}, bf16[16,224,128]{2,1,0:T(8,128)(2,1)S(1)}, u32[]{:S(2)}, u32[]{:S(2)}) collective-permute-start(bf16[16,224,128]{2,1,0:T(8,128)(2,1)} %get-tuple-element.13), channel_id=1, source_target_pairs={{16,0},{32,16},{48,32},{64,48},{80,64},{96,80},{112,96},{17,1},{33... | collective-permute-start | bytes 2752520 | tf_op jit(solution)/shard_map/ppermute | solution.py:104
  36.7 14.7 %collective-permute-start = (bf16[16,224,128]{2,1,0:T(8,128)(2,1)S(1)}, bf16[16,224,128]{2,1,0:T(8,128)(2,1)S(1)}, u32[]{:S(2)}, u32[]{:S(2)}) collective-permute-start(bf16[16,224,128]{2,1,0:T(8,128)(2,1)S(1)} %get-tuple-element.16), channel_id=1, source_target_pairs={{0,16},{16,32},{32,48},{48,64},{64,80},{80,96},{96,112},{1,17},{17... | collective-permute-start | bytes 2752520 | tf_op jit(solution)/shard_map/ppermute | solution.py:104
  47.9 3.5 %copy-start.4 = (bf16[16,224,128]{2,1,0:T(8,128)(2,1)}, bf16[16,224,128]{2,1,0:T(8,128)(2,1)S(1)}, u32[]{:S(2)}) copy-start(bf16[16,224,128]{2,1,0:T(8,128)(2,1)S(1)} %collective-permute-done.1.hi_ref) | copy-start | bytes 2752516
  51.4 0.9 copy-start.7
  61.3 31.6 %all-to-all-start = ((bf16[16,2,224,128]{3,2,1,0:T(8,128)(2,1)}), bf16[16,2,224,128]{3,2,1,0:T(8,128)(2,1)}, u32[]{:S(2)}, u32[]{:S(2)}) async-start(bf16[16,2,224,128]{3,2,1,0:T(8,128)(2,1)} %bitcast.148), calls=%async_computation | async-start | bytes 3670016 | tf_op jit(solution)/shard_map/all_to_all | solution.py:115
  76.2 16.7 %copy-start.12 = (f32[512]{0:T(512)S(1)}, f32[512]{0:T(512)}, u32[]{:S(2)}) copy-start(f32[512]{0:T(512)} %param.11) | copy-start | bytes 6148
  106.3 28.7 %all-to-all-start.4 = ((bf16[16,2,224,128]{3,2,1,0:T(8,128)(2,1)}), bf16[16,2,224,128]{3,2,1,0:T(8,128)(2,1)S(1)}, u32[]{:S(2)}, u32[]{:S(2)}) async-start(bf16[16,2,224,128]{3,2,1,0:T(8,128)(2,1)} %copy.53), calls=%async_computation.4 | async-start | bytes 3670016 | tf_op jit(solution)/shard_map/all_to_all | solution.py:131
  135.0 1.2 copy-start.1
  136.2 28.8 %all-to-all-start.2 = ((bf16[16,2,224,128]{3,2,1,0:T(8,128)(2,1)}), bf16[16,2,224,128]{3,2,1,0:T(8,128)(2,1)S(1)}, u32[]{:S(2)}, u32[]{:S(2)}) async-start(bf16[16,2,224,128]{3,2,1,0:T(8,128)(2,1)} %copy.48), calls=%async_computation.2 | async-start | bytes 3670016 | tf_op jit(solution)/shard_map/all_to_all | solution.py:127
  141.5 14.7 %collective-permute-start.6 = (bf16[16,224,128]{2,1,0:T(8,128)(2,1)S(1)}, bf16[16,224,128]{2,1,0:T(8,128)(2,1)S(1)}, u32[]{:S(2)}, u32[]{:S(2)}) collective-permute-start(bf16[16,224,128]{2,1,0:T(8,128)(2,1)S(1)} %bitcast.154), channel_id=1, source_target_pairs={{0,16},{16,32},{32,48},{48,64},{64,80},{80,96},{96,112},{1,17},{17... | collective-permute-start | bytes 2752520 | tf_op jit(solution)/shard_map/ppermute | solution.py:112
  143.5 14.5 %collective-permute-start.7 = (bf16[16,224,128]{2,1,0:T(8,128)(2,1)S(1)}, bf16[16,224,128]{2,1,0:T(8,128)(2,1)S(1)}, u32[]{:S(2)}, u32[]{:S(2)}) collective-permute-start(bf16[16,224,128]{2,1,0:T(8,128)(2,1)S(1)} %bitcast.152), channel_id=1, source_target_pairs={{16,0},{32,16},{48,32},{64,48},{80,64},{96,80},{112,96},{17,1},{33... | collective-permute-start | bytes 2752520 | tf_op jit(solution)/shard_map/ppermute | solution.py:113
  156.2 2.7 copy-start.6
  158.0 1.0 copy-start.9
  165.0 6.7 %copy-start = (bf16[16,2,224,128]{3,2,1,0:T(8,128)(2,1)}, bf16[16,2,224,128]{3,2,1,0:T(8,128)(2,1)S(1)}, u32[]{:S(2)}) copy-start(bf16[16,2,224,128]{3,2,1,0:T(8,128)(2,1)S(1)} %all-to-all-done.2) | copy-start | bytes 5505028
  165.0 34.1 %all-to-all-start.5 = ((bf16[16,2,224,128]{3,2,1,0:T(8,128)(2,1)}), bf16[16,2,224,128]{3,2,1,0:T(8,128)(2,1)}, u32[]{:S(2)}, u32[]{:S(2)}) async-start(bf16[16,2,224,128]{3,2,1,0:T(8,128)(2,1)} %bitcast.147), calls=%async_computation.5 | async-start | bytes 3670016 | tf_op jit(solution)/shard_map/all_to_all | solution.py:115
  171.7 14.7 %collective-permute-start.4 = (bf16[16,224,128]{2,1,0:T(8,128)(2,1)S(1)}, bf16[16,224,128]{2,1,0:T(8,128)(2,1)S(1)}, u32[]{:S(2)}, u32[]{:S(2)}) collective-permute-start(bf16[16,224,128]{2,1,0:T(8,128)(2,1)S(1)} %bitcast.155), channel_id=1, source_target_pairs={{0,16},{16,32},{32,48},{48,64},{64,80},{80,96},{96,112},{1,17},{17... | collective-permute-start | bytes 2752520 | tf_op jit(solution)/shard_map/ppermute | solution.py:112
  175.6 12.8 %collective-permute-start.5 = (bf16[16,224,128]{2,1,0:T(8,128)(2,1)S(1)}, bf16[16,224,128]{2,1,0:T(8,128)(2,1)S(1)}, u32[]{:S(2)}, u32[]{:S(2)}) collective-permute-start(bf16[16,224,128]{2,1,0:T(8,128)(2,1)S(1)} %bitcast.153), channel_id=1, source_target_pairs={{16,0},{32,16},{48,32},{64,48},{80,64},{96,80},{112,96},{17,1},{33... | collective-permute-start | bytes 2752520 | tf_op jit(solution)/shard_map/ppermute | solution.py:113
  186.4 2.0 copy-start.5
  188.4 0.9 copy-start.8
  199.2 32.2 %all-to-all-start.3 = ((bf16[16,2,224,128]{3,2,1,0:T(8,128)(2,1)}), bf16[16,2,224,128]{3,2,1,0:T(8,128)(2,1)S(1)}, u32[]{:S(2)}, u32[]{:S(2)}) async-start(bf16[16,2,224,128]{3,2,1,0:T(8,128)(2,1)} %bitcast.150), calls=%async_computation.3 | async-start | bytes 3670016 | tf_op jit(solution)/shard_map/all_to_all | solution.py:115
  239.2 32.4 %all-to-all-start.6 = ((bf16[16,2,224,128]{3,2,1,0:T(8,128)(2,1)}), bf16[16,2,224,128]{3,2,1,0:T(8,128)(2,1)S(1)}, u32[]{:S(2)}, u32[]{:S(2)}) async-start(bf16[16,2,224,128]{3,2,1,0:T(8,128)(2,1)} %copy.56), calls=%async_computation.6 | async-start | bytes 3670016 | tf_op jit(solution)/shard_map/all_to_all | solution.py:127

commit v7 on v4

--- a/solution.py
+++ b/solution.py
@@ -97,27 +97,34 @@
     pieces = [slice(h * part, (h + 1) * part) for h in range(PARTS)]
 
     whole = jnp.transpose(dist, (1, 2, 0, 3)).reshape(rows, vb, nx)
-    fs = [whole[:, p] for p in pieces]
-    for step in range(STEPS):
-        recvs = []
-        for h, p in enumerate(pieces):
-            f = fs[h]
-            lo = lax.ppermute(f[rows - ny :], "space", up)
-            hi = lax.ppermute(f[:ny], "space", down)
-            half = transport(f, lo, hi, coef[:, p], tm, ny)
-            recvs.append(lax.all_to_all(half.reshape(groups, chunk, part, nx), "vel", 0, 0, tiled=True))
-        moments = None
-        for h, p in enumerate(pieces):
-            term = jnp.einsum("ksv,srvx->krx", w3[:, :, p], recvs[h], preferred_element_type=jnp.float32)
-            moments = term if moments is None else moments + term
-        delta = (rates[:, None, None] * moments).astype(jnp.bfloat16)
-        fs = []
-        for h, p in enumerate(pieces):
-            adjustment = jnp.einsum("svk,krx->srvx", e3[:, p], delta, preferred_element_type=jnp.float32)
-            post = (recvs[h].astype(jnp.float32) - cm[None, :, None, :] * adjustment).astype(jnp.bfloat16)
-            fs.append(lax.all_to_all(post, "vel", 0, 0, tiled=True).reshape(rows, part, nx))
-    whole = jnp.concatenate(fs, axis=1)
-    return jnp.transpose(whole.reshape(nzl, ny, vb, nx), (2, 0, 1, 3))
+    lo = lax.ppermute(whole[rows - ny :], "space", up)
+    hi = lax.ppermute(whole[:ny], "space", down)
+    half = transport(whole, lo, hi, coef, tm, ny)
+    recv = lax.all_to_all(half.reshape(groups, chunk, vb, nx), "vel", 0, 0, tiled=True)
+    moments = jnp.einsum("ksv,srvx->krx", w3, recv, preferred_element_type=jnp.float32)
+    delta = (rates[:, None, None] * moments).astype(jnp.bfloat16)
+    fs = []
+    for p in pieces:
+        adjustment = jnp.einsum("svk,krx->srvx", e3[:, p], delta, preferred_element_type=jnp.float32)
+        post = (recv[:, :, p].astype(jnp.float32) - cm[None, :, None, :] * adjustment).astype(jnp.bfloat16)
+        fs.append(lax.all_to_all(post, "vel", 0, 0, tiled=True).reshape(rows, part, nx))
+    recvs = []
+    for h, p in enumerate(pieces):
+        f = fs[h]
+        lo = lax.ppermute(f[rows - ny :], "space", up)
+        hi = lax.ppermute(f[:ny], "space", down)
+        half = transport(f, lo, hi, coef[:, p], tm, ny)
+        recvs.append(lax.all_to_all(half.reshape(groups, chunk, part, nx), "vel", 0, 0, tiled=True))
+    moments = None
+    for h, p in enumerate(pieces):
+        term = jnp.einsum("ksv,srvx->krx", w3[:, :, p], recvs[h], preferred_element_type=jnp.float32)
+        moments = term if moments is None else moments + term
+    delta = (rates[:, None, None] * moments).astype(jnp.bfloat16)
+    recv = jnp.concatenate(recvs, axis=2)
+    adjustment = jnp.einsum("svk,krx->srvx", e3, delta, preferred_element_type=jnp.float32)
+    post = (recv.astype(jnp.float32) - cm[None, :, None, :] * adjustment).astype(jnp.bfloat16)
+    f = lax.all_to_all(post, "vel", 0, 0, tiled=True).reshape(rows, vb, nx)
+    return jnp.transpose(f.reshape(nzl, ny, vb, nx), (2, 0, 1, 3))
 
 
 def solution(mesh):

time: 311 us -> 319 us (1.026)
  blocking collectives: 27.2 us -> 46.9 us
  matrix products: 31 us -> 26.8 us
    all_to_all x0 -> x1, waiting for transfers between devices: none -> 38.1 us  [per_device(): lax.all_to_all(half.reshape(groups, chunk, vb, nx), 'vel', 0, 0, tiled=True)]
    all_to_all x3 -> x2, waiting for transfers between devices: 46.9 us -> 26.2 us  [per_device(): lax.all_to_all(post, 'vel', 0, 0, tiled=True).reshape(rows, part, nx)]
    ppermute x0 -> x2, waiting for transfers between devices: none -> 20.1 us  [the longest x1 18.3 us: per_device(): lo = lax.ppermute(whole[rows - ny:], 'space', up)]
    all_to_all x1, blocking collectives: 27.2 us -> 46.9 us  [per_device(): f = lax.all_to_all(post, 'vel', 0, 0, tiled=True).reshape(rows, vb, nx)]
    all_to_all x4 -> x2, waiting for transfers between devices: 45.1 us -> 28.6 us  [per_device(): lax.all_to_all(half.reshape(groups, chunk, part, nx), 'vel', 0, 0, tiled=...]
    ppermute x4 -> x2, waiting for transfers between devices: 18.2 us -> 3.51 us  [per_device(): hi = lax.ppermute(f[:ny], 'space', down)]
    dot_general x0 -> x2, matrix products: none -> 14 us  [the longest x1 7.58 us: per_device(): jnp.einsum('svk,krx->srvx', e3, delta, preferred_element_type=jnp.float32)]
    dot_general x4 -> x2, matrix products: 17.2 us -> 5.91 us  [per_device(): jnp.einsum('svk,krx->srvx', e3[:, p], delta, preferred_element_type=jnp.f...]
  transfers between devices with their start and end apart: 15 -> 11, of which waited for: 15 -> 11; matrix products, arithmetic and copies ran while one was open for 9% -> 7% of each run, Pallas kernels for 5% -> 3%
where the time goes in v7:
time: 319 us; the launch traced here: 318 us
  waiting for transfers between devices  135 us (42%)
  starting transfers between devices  54.4 us (17%)
  blocking collectives  46.9 us (15%)
  local copies, waits for them, and re-layouts  35.2 us (11%)
  matrix products  26.8 us (8%)
  Pallas kernels  19.2 us (6%)
    all_to_all x1, blocking collectives, per_device(): f = lax.all_to_all(post, 'vel', 0, 0, tiled=True).reshape(rows, vb, nx)  46.9 us
    all_to_all x1, waiting for transfers between devices, per_device(): lax.all_to_all(half.reshape(groups, chunk, vb, nx), 'vel', 0, 0, tiled=True)  38.1 us
    all_to_all x2, waiting for transfers between devices, per_device(): lax.all_to_all(half.reshape(groups, chunk, part, nx), 'vel', 0, 0, tiled=...  28.6 us
    all_to_all x2, waiting for transfers between devices, per_device(): lax.all_to_all(post, 'vel', 0, 0, tiled=True).reshape(rows, part, nx)  26.2 us
    pallas_call x3, Pallas kernels, transport(): pl.pallas_call(functools.partial(transport_kernel, ny), out_shape=jax.Sha...  19.2 us
    all_to_all x2, starting transfers between devices, per_device(): lax.all_to_all(post, 'vel', 0, 0, tiled=True).reshape(rows, part, nx)  18.9 us
    unnamed x30, local copies, waits for them, and re-layouts  18.9 us
    ppermute x1, waiting for transfers between devices, per_device(): lo = lax.ppermute(whole[rows - ny:], 'space', up)  18.3 us
  transfers between devices with their start and end apart: 11, of which 11 were waited for; matrix products, arithmetic and copies ran while one was open for 7% of the time, Pallas kernels for 3%

profile of v7, /device:TPU:32, one launch (start us, length us, event | category | flops | bytes accessed | tf_op | source)
XLA Modules:
  0.0 318.1 jit_solution(7999152116595059407)
XLA Ops:
  0.0 3.5 %copy.76 = bf16[448,2,16,128]{3,0,2,1:T(8,128)(2,1)S(1)} copy(bf16[448,2,16,128]{3,2,1,0:T(8,128)(2,1)} %param.6) | data formatting | bytes 7340032 | tf_op args[0]
  3.5 0.0 copy-start
  3.5 0.0 copy-start.10
  3.5 0.0 copy-start.9
  3.5 0.2 slice_bitcast_fusion.8
  3.7 1.6 copy-done
  5.3 1.9 collective-permute-start
  7.2 3.6 %collective-permute-start.1 = (bf16[16,448,128]{2,1,0:T(8,128)(2,1)S(1)}, bf16[16,448,128]{2,1,0:T(8,128)(2,1)S(1)}, u32[]{:S(2)}, u32[]{:S(2)}) collective-permute-start(bf16[16,448,128]{2,1,0:T(8,128)(2,1)S(1)} %get-tuple-element.7), channel_id=1, source_target_pairs={{16,0},{32,16},{48,32},{64,48},{80,64},{96,80},{112,96},{17,1},{33... | collective-permute-start | bytes 5505032 | tf_op jit(solution)/shard_map/ppermute | solution.py:101
  10.9 0.0 copy-done.10
  10.9 0.0 copy-done.9
  10.9 0.6 compare_convert_fusion
  11.5 18.3 %collective-permute-done.lo_ref = bf16[16,448,128]{2,1,0:T(8,128)(2,1)S(1)} collective-permute-done((bf16[16,448,128]{2,1,0:T(8,128)(2,1)S(1)}, bf16[16,448,128]{2,1,0:T(8,128)(2,1)S(1)}, u32[]{:S(2)}, u32[]{:S(2)}) %collective-permute-start) | collective-permute-done | bytes 1835040 | tf_op jit(solution)/shard_map/ppermute | solution.py:100
  29.8 1.8 collective-permute-done.1.hi_ref
  31.6 1.2 copy-done.4
  32.8 1.1 broadcast_in_dim.27.coef_ref
  33.9 0.0 copy-done.3
  33.9 8.6 %shard_map.64 = bf16[32,448,128]{2,1,0:T(8,128)(2,1)} custom-call(bf16[32,448,128]{2,1,0:T(8,128)(2,1)} %bitcast.121, bf16[16,448,128]{2,1,0:T(8,128)(2,1)} %copy-done.3, bf16[16,448,128]{2,1,0:T(8,128)(2,1)} %copy-done.4, f32[3,448,128]{2,1,0:T(8,128)} %broadcast_in_dim.27.coef_ref, f32[32,128]{1,0:T(8,128)} %bitcast.137), custom_call_target="tpu_custom_call" | custom-call | flops 36700160 | bytes 7340032 | tf_op jit(solution)/shard_map/pallas_call | solution.py:61
  42.5 7.1 %all-to-all-start = ((bf16[16,2,448,128]{3,2,1,0:T(8,128)(2,1)}), bf16[16,2,448,128]{3,2,1,0:T(8,128)(2,1)}, u32[]{:S(2)}, u32[]{:S(2)}) async-start(bf16[16,2,448,128]{3,2,1,0:T(8,128)(2,1)} %bitcast.125), calls=%async_computation | async-start | bytes 7340032 | tf_op jit(solution)/shard_map/all_to_all | solution.py:103
  49.6 0.0 copy-start.11
  49.6 10.4 %copy.39 = bf16[512,7168]{0,1:T(8,128)(2,1)} copy(bf16[512,7168]{1,0:T(8,128)(2,1)} %param.9) | data formatting | bytes 14680064 | tf_op args[3]
  60.1 38.1 %all-to-all-done = bf16[16,2,448,128]{3,2,1,0:T(8,128)(2,1)} async-done(((bf16[16,2,448,128]{3,2,1,0:T(8,128)(2,1)}), bf16[16,2,448,128]{3,2,1,0:T(8,128)(2,1)}, u32[]{:S(2)}, u32[]{:S(2)}) %all-to-all-start) | async-done | bytes 3670048 | tf_op jit(solution)/shard_map/all_to_all | solution.py:103
  98.1 0.0 copy-done.11
  98.1 6.4 %fusion.14 = bf16[512,2,128,1]{0,2,3,1:T(8,128)(2,1)S(1)} fusion(bf16[16,2,448,128]{3,2,1,0:T(8,128)(2,1)} %all-to-all-done, bf16[512,16,448,1]{0,2,3,1:T(8,128)(2,1)} %bitcast.117, f32[512]{0:T(512)S(1)} %copy-done.11), kind=kOutput, calls=%fused_computation.25 | convolution fusion | flops 1879310336 | bytes 11274240 | tf_op jit(solution)/shard_map/ksv,srvx->krx/dot_general | solution.py:104
  104.6 0.0 slice-start.1
  104.6 3.3 %fusion.3 = f32[2,128,16,224]{1,3,2,0:T(8,128)S(1)} fusion(bf16[512,2,128,1]{0,2,3,1:T(8,128)(2,1)S(1)} %fusion.14, bf16[16,448,512]{2,1,0:T(8,128)(2,1)} %bitcast.128), kind=kOutput, calls=%fused_computation.7 | convolution fusion | flops 939524096 | bytes 7602176 | tf_op jit(solution)/shard_map/svk,krx->srvx/dot_general | solution.py:108
  107.9 2.3 fusion.24
  110.2 0.0 slice-done
  110.3 0.0 slice-done.1
  110.3 2.6 fusion.6
  112.8 1.5 copy.45
  114.3 13.7 %all-to-all-start.3 = ((bf16[16,2,224,128]{3,2,1,0:T(8,128)(2,1)}), bf16[16,2,224,128]{3,2,1,0:T(8,128)(2,1)S(1)}, u32[]{:S(2)}, u32[]{:S(2)}) async-start(bf16[16,2,224,128]{3,2,1,0:T(8,128)(2,1)} %copy.45), calls=%async_computation.3 | async-start | bytes 3670016 | tf_op jit(solution)/shard_map/all_to_all | solution.py:110
  128.0 2.9 copy.42
  130.9 24.9 %all-to-all-done.3 = bf16[16,2,224,128]{3,2,1,0:T(8,128)(2,1)S(1)} async-done(((bf16[16,2,224,128]{3,2,1,0:T(8,128)(2,1)}), bf16[16,2,224,128]{3,2,1,0:T(8,128)(2,1)S(1)}, u32[]{:S(2)}, u32[]{:S(2)}) %all-to-all-start.3) | async-done | bytes 1835040 | tf_op jit(solution)/shard_map/all_to_all | solution.py:110
  155.8 1.2 copy-done.2
  157.1 5.3 %all-to-all-start.1 = ((bf16[16,2,224,128]{3,2,1,0:T(8,128)(2,1)}), bf16[16,2,224,128]{3,2,1,0:T(8,128)(2,1)S(1)}, u32[]{:S(2)}, u32[]{:S(2)}) async-start(bf16[16,2,224,128]{3,2,1,0:T(8,128)(2,1)} %copy.42), calls=%async_computation.1 | async-start | bytes 3670016 | tf_op jit(solution)/shard_map/all_to_all | solution.py:110
  162.4 1.6 fusion.26
  163.9 1.9 collective-permute-start.4
  165.9 3.6 %collective-permute-start.5 = (bf16[16,224,128]{2,1,0:T(8,128)(2,1)S(1)}, bf16[16,224,128]{2,1,0:T(8,128)(2,1)S(1)}, u32[]{:S(2)}, u32[]{:S(2)}) collective-permute-start(bf16[16,224,128]{2,1,0:T(8,128)(2,1)S(1)} %bitcast.133), channel_id=1, source_target_pairs={{16,0},{32,16},{48,32},{64,48},{80,64},{96,80},{112,96},{17,1},{33... | collective-permute-start | bytes 2752520 | tf_op jit(solution)/shard_map/ppermute | solution.py:115
  169.5 0.1 fusion.27
  169.6 9.1 %collective-permute-done.4.lo_ref = bf16[16,224,128]{2,1,0:T(8,128)(2,1)S(1)} collective-permute-done((bf16[16,224,128]{2,1,0:T(8,128)(2,1)S(1)}, bf16[16,224,128]{2,1,0:T(8,128)(2,1)S(1)}, u32[]{:S(2)}, u32[]{:S(2)}) %collective-permute-start.4) | collective-permute-done | bytes 917536 | tf_op jit(solution)/shard_map/ppermute | solution.py:114
  178.7 1.8 collective-permute-done.5.hi_ref
  180.4 1.0 copy-done.7
  181.4 0.9 broadcast_in_dim.32.coef_ref
  182.3 0.0 copy-done.5
  182.3 5.3 %shard_map.66 = bf16[32,224,128]{2,1,0:T(8,128)(2,1)} custom-call(bf16[32,224,128]{2,1,0:T(8,128)(2,1)} %bitcast.123, bf16[16,224,128]{2,1,0:T(8,128)(2,1)} %copy-done.5, bf16[16,224,128]{2,1,0:T(8,128)(2,1)} %copy-done.7, f32[3,224,128]{2,1,0:T(8,128)} %broadcast_in_dim.32.coef_ref, f32[32,128]{1,0:T(8,128)} %bitcast.138), custom_call_target="tpu_custom_call" | custom-call | flops 18350080 | bytes 3670016 | tf_op jit(solution)/shard_map/pallas_call | solution.py:61
  187.6 1.3 all-to-all-done.1
  189.0 6.0 %all-to-all-start.4 = ((bf16[16,2,224,128]{3,2,1,0:T(8,128)(2,1)}), bf16[16,2,224,128]{3,2,1,0:T(8,128)(2,1)}, u32[]{:S(2)}, u32[]{:S(2)}) async-start(bf16[16,2,224,128]{3,2,1,0:T(8,128)(2,1)} %bitcast.126), calls=%async_computation.4 | async-start | bytes 3670016 | tf_op jit(solution)/shard_map/all_to_all | solution.py:117
  194.9 0.1 fusion.25
  195.1 0.0 copy-done.1
  195.1 2.7 collective-permute-start.2
  197.7 2.9 collective-permute-start.3
  200.6 9.1 %collective-permute-done.2.lo_ref = bf16[16,224,128]{2,1,0:T(8,128)(2,1)S(1)} collective-permute-done((bf16[16,224,128]{2,1,0:T(8,128)(2,1)S(1)}, bf16[16,224,128]{2,1,0:T(8,128)(2,1)S(1)}, u32[]{:S(2)}, u32[]{:S(2)}) %collective-permute-start.2) | collective-permute-done | bytes 917536 | tf_op jit(solution)/shard_map/ppermute | solution.py:114
  209.8 1.8 collective-permute-done.3.hi_ref
  211.5 1.0 broadcast_in_dim.31.coef_ref
  212.6 5.3 %shard_map.65 = bf16[32,224,128]{2,1,0:T(8,128)(2,1)} custom-call(bf16[32,224,128]{2,1,0:T(8,128)(2,1)} %bitcast.122, bf16[16,224,128]{2,1,0:T(8,128)(2,1)} %copy-done.6, bf16[16,224,128]{2,1,0:T(8,128)(2,1)} %copy-done.8, f32[3,224,128]{2,1,0:T(8,128)} %broadcast_in_dim.31.coef_ref, f32[32,128]{1,0:T(8,128)} %bitcast.139), custom_call_target="tpu_custom_call" | custom-call | flops 18350080 | bytes 3670016 | tf_op jit(solution)/shard_map/pallas_call | solution.py:61
  217.9 5.1 %all-to-all-done.4 = bf16[16,2,224,128]{3,2,1,0:T(8,128)(2,1)} async-done(((bf16[16,2,224,128]{3,2,1,0:T(8,128)(2,1)}), bf16[16,2,224,128]{3,2,1,0:T(8,128)(2,1)}, u32[]{:S(2)}, u32[]{:S(2)}) %all-to-all-start.4) | async-done | bytes 1835040 | tf_op jit(solution)/shard_map/all_to_all | solution.py:117
  223.0 5.8 %all-to-all-start.2 = ((bf16[16,2,224,128]{3,2,1,0:T(8,128)(2,1)}), bf16[16,2,224,128]{3,2,1,0:T(8,128)(2,1)S(1)}, u32[]{:S(2)}, u32[]{:S(2)}) async-start(bf16[16,2,224,128]{3,2,1,0:T(8,128)(2,1)} %bitcast.127), calls=%async_computation.2 | async-start | bytes 3670016 | tf_op jit(solution)/shard_map/all_to_all | solution.py:117
  228.7 3.7 %fusion.8 = f32[2,128,512]{2,1,0:T(8,128)S(1)} fusion(bf16[16,2,224,128]{3,2,1,0:T(8,128)(2,1)} %all-to-all-done.4, bf16[512,16,448]{0,2,1:T(8,128)(2,1)} %bitcast.118), kind=kOutput, calls=%fused_computation.18 | convolution fusion | flops 939524096 | bytes 6029312 | tf_op jit(solution)/shard_map/ksv,srvx->krx/dot_general | solution.py:120
  232.5 23.5 %all-to-all-done.2 = bf16[16,2,224,128]{3,2,1,0:T(8,128)(2,1)S(1)} async-done(((bf16[16,2,224,128]{3,2,1,0:T(8,128)(2,1)}), bf16[16,2,224,128]{3,2,1,0:T(8,128)(2,1)S(1)}, u32[]{:S(2)}, u32[]{:S(2)}) %all-to-all-start.2) | async-done | bytes 1835040 | tf_op jit(solution)/shard_map/all_to_all | solution.py:117
  255.9 3.2 fusion.15
  259.1 7.6 %fusion = bf16[16,2,448,128]{3,2,0,1:T(8,128)(2,1)S(1)} fusion(f32[2,128]{1,0:T(2,128)S(1)} %constant_dynamic-slice_fusion, bf16[512,2,128,1]{0,2,3,1:T(8,128)(2,1)S(1)} %fusion.15, bf16[16,448,512,1]{2,1,0,3:T(8,128)(2,1)} %bitcast.129, bf16[16,2,224,128]{3,2,1,0:T(8,128)(2,1)} %all-to-all-done.4, bf16[16,2,224,128]{3,2,1,0:T(8,128)(2,1)S(1)} %all-to-all-done.2), kind=kOutput, calls=%fused_computation.1 | convolution fusion | flops 1893728256 | bytes 14943232 | tf_op jit(solution)/shard_map/svk,krx->srvx/dot_general | solution.py:124
  266.7 0.3 copy.51
  267.0 46.9 %all_to_all.30 = bf16[16,2,448,128]{3,2,1,0:T(8,128)(2,1)S(1)} all-to-all(bf16[16,2,448,128]{3,2,1,0:T(8,128)(2,1)S(1)} %copy.51), channel_id=1, replica_groups=mesh['space'=8,'vel'=16] {'vel'}, dimensions={0} | all-to-all | bytes 7340032 | tf_op jit(solution)/shard_map/all_to_all | solution.py:126
  313.9 4.2 %copy.52 = bf16[448,2,16,128]{3,2,1,0:T(8,128)(2,1)} copy(bf16[448,2,16,128]{3,0,2,1:T(8,128)(2,1)S(1)} %bitcast.124) | data formatting | bytes 7340032 | tf_op jit(solution)/shard_map/transpose | solution.py:127
  (16 shorter events, 0.1 us)
Async XLA Ops:
  3.5 1.8 copy-start
  3.5 7.4 %copy-start.10 = (s32[448]{0:T(512)S(1)}, s32[448]{0:T(512)}, u32[]{:S(2)}) copy-start(s32[448]{0:T(512)} %param.7) | copy-start | bytes 5380
  3.5 7.4 %copy-start.9 = (s32[2,16,128]{2,1,0:T(8,128)S(1)}, s32[2,16,128]{2,1,0:T(8,128)}, u32[]{:S(2)}) copy-start(s32[2,16,128]{2,1,0:T(8,128)} %param.8) | copy-start | bytes 49156
  5.3 24.5 %collective-permute-start = (bf16[16,448,128]{2,1,0:T(8,128)(2,1)S(1)}, bf16[16,448,128]{2,1,0:T(8,128)(2,1)S(1)}, u32[]{:S(2)}, u32[]{:S(2)}) collective-permute-start(bf16[16,448,128]{2,1,0:T(8,128)(2,1)S(1)} %get-tuple-element.8), channel_id=1, source_target_pairs={{0,16},{16,32},{32,48},{48,64},{64,80},{80,96},{96,112},{1,17},{17... | collective-permute-start | bytes 5505032 | tf_op jit(solution)/shard_map/ppermute | solution.py:100
  7.2 24.4 %collective-permute-start.1 = (bf16[16,448,128]{2,1,0:T(8,128)(2,1)S(1)}, bf16[16,448,128]{2,1,0:T(8,128)(2,1)S(1)}, u32[]{:S(2)}, u32[]{:S(2)}) collective-permute-start(bf16[16,448,128]{2,1,0:T(8,128)(2,1)S(1)} %get-tuple-element.7), channel_id=1, source_target_pairs={{16,0},{32,16},{48,32},{64,48},{80,64},{96,80},{112,96},{17,1},{33... | collective-permute-start | bytes 5505032 | tf_op jit(solution)/shard_map/ppermute | solution.py:101
  29.8 4.1 %copy-start.3 = (bf16[16,448,128]{2,1,0:T(8,128)(2,1)}, bf16[16,448,128]{2,1,0:T(8,128)(2,1)S(1)}, u32[]{:S(2)}) copy-start(bf16[16,448,128]{2,1,0:T(8,128)(2,1)S(1)} %collective-permute-done.lo_ref) | copy-start | bytes 5505028
  31.6 1.2 copy-start.4
  42.5 55.6 %all-to-all-start = ((bf16[16,2,448,128]{3,2,1,0:T(8,128)(2,1)}), bf16[16,2,448,128]{3,2,1,0:T(8,128)(2,1)}, u32[]{:S(2)}, u32[]{:S(2)}) async-start(bf16[16,2,448,128]{3,2,1,0:T(8,128)(2,1)} %bitcast.125), calls=%async_computation | async-start | bytes 7340032 | tf_op jit(solution)/shard_map/all_to_all | solution.py:103
  49.6 48.5 %copy-start.11 = (f32[512]{0:T(512)S(1)}, f32[512]{0:T(512)}, u32[]{:S(2)}) copy-start(f32[512]{0:T(512)} %param.11) | copy-start | bytes 6148
  98.1 12.1 %slice-start = ((s8[7340032]{0:T(1024)(128)(4,1)}), s8[4194304]{0:T(1024)(128)(4,1)S(1)}, s32[]{:S(2)}) async-start(s8[7340032]{0:T(1024)(128)(4,1)} %bitcast.130), calls=%async_computation.6 | async-start | bytes 8388608
  104.6 5.7 %slice-start.1 = ((s8[7340032]{0:T(1024)(128)(4,1)}), s8[3145728]{0:T(1024)(128)(4,1)S(1)}, s32[]{:S(2)}) async-start(s8[7340032]{0:T(1024)(128)(4,1)} %bitcast.130), calls=%async_computation.7 | async-start | bytes 6291456
  114.3 41.5 %all-to-all-start.3 = ((bf16[16,2,224,128]{3,2,1,0:T(8,128)(2,1)}), bf16[16,2,224,128]{3,2,1,0:T(8,128)(2,1)S(1)}, u32[]{:S(2)}, u32[]{:S(2)}) async-start(bf16[16,2,224,128]{3,2,1,0:T(8,128)(2,1)} %copy.45), calls=%async_computation.3 | async-start | bytes 3670016 | tf_op jit(solution)/shard_map/all_to_all | solution.py:110
  155.8 1.2 copy-start.2
  157.1 31.9 %all-to-all-start.1 = ((bf16[16,2,224,128]{3,2,1,0:T(8,128)(2,1)}), bf16[16,2,224,128]{3,2,1,0:T(8,128)(2,1)S(1)}, u32[]{:S(2)}, u32[]{:S(2)}) async-start(bf16[16,2,224,128]{3,2,1,0:T(8,128)(2,1)} %copy.42), calls=%async_computation.1 | async-start | bytes 3670016 | tf_op jit(solution)/shard_map/all_to_all | solution.py:110
  163.9 14.7 %collective-permute-start.4 = (bf16[16,224,128]{2,1,0:T(8,128)(2,1)S(1)}, bf16[16,224,128]{2,1,0:T(8,128)(2,1)S(1)}, u32[]{:S(2)}, u32[]{:S(2)}) collective-permute-start(bf16[16,224,128]{2,1,0:T(8,128)(2,1)S(1)} %bitcast.134), channel_id=1, source_target_pairs={{0,16},{16,32},{32,48},{48,64},{64,80},{80,96},{96,112},{1,17},{17... | collective-permute-start | bytes 2752520 | tf_op jit(solution)/shard_map/ppermute | solution.py:114
  165.9 14.5 %collective-permute-start.5 = (bf16[16,224,128]{2,1,0:T(8,128)(2,1)S(1)}, bf16[16,224,128]{2,1,0:T(8,128)(2,1)S(1)}, u32[]{:S(2)}, u32[]{:S(2)}) collective-permute-start(bf16[16,224,128]{2,1,0:T(8,128)(2,1)S(1)} %bitcast.133), channel_id=1, source_target_pairs={{16,0},{32,16},{48,32},{64,48},{80,64},{96,80},{112,96},{17,1},{33... | collective-permute-start | bytes 2752520 | tf_op jit(solution)/shard_map/ppermute | solution.py:115
  178.7 3.7 %copy-start.5 = (bf16[16,224,128]{2,1,0:T(8,128)(2,1)}, bf16[16,224,128]{2,1,0:T(8,128)(2,1)S(1)}, u32[]{:S(2)}) copy-start(bf16[16,224,128]{2,1,0:T(8,128)(2,1)S(1)} %collective-permute-done.4.lo_ref) | copy-start | bytes 2752516
  180.4 1.0 copy-start.7
  189.0 6.1 %copy-start.1 = (bf16[16,2,224,128]{3,2,1,0:T(8,128)(2,1)}, bf16[16,2,224,128]{3,2,1,0:T(8,128)(2,1)S(1)}, u32[]{:S(2)}) copy-start(bf16[16,2,224,128]{3,2,1,0:T(8,128)(2,1)S(1)} %all-to-all-done.1) | copy-start | bytes 5505028
  189.0 34.0 %all-to-all-start.4 = ((bf16[16,2,224,128]{3,2,1,0:T(8,128)(2,1)}), bf16[16,2,224,128]{3,2,1,0:T(8,128)(2,1)}, u32[]{:S(2)}, u32[]{:S(2)}) async-start(bf16[16,2,224,128]{3,2,1,0:T(8,128)(2,1)} %bitcast.126), calls=%async_computation.4 | async-start | bytes 3670016 | tf_op jit(solution)/shard_map/all_to_all | solution.py:117
  195.1 14.7 %collective-permute-start.2 = (bf16[16,224,128]{2,1,0:T(8,128)(2,1)S(1)}, bf16[16,224,128]{2,1,0:T(8,128)(2,1)S(1)}, u32[]{:S(2)}, u32[]{:S(2)}) collective-permute-start(bf16[16,224,128]{2,1,0:T(8,128)(2,1)S(1)} %bitcast.136), channel_id=1, source_target_pairs={{0,16},{16,32},{32,48},{48,64},{64,80},{80,96},{96,112},{1,17},{17... | collective-permute-start | bytes 2752520 | tf_op jit(solution)/shard_map/ppermute | solution.py:114
  197.7 13.8 %collective-permute-start.3 = (bf16[16,224,128]{2,1,0:T(8,128)(2,1)S(1)}, bf16[16,224,128]{2,1,0:T(8,128)(2,1)S(1)}, u32[]{:S(2)}, u32[]{:S(2)}) collective-permute-start(bf16[16,224,128]{2,1,0:T(8,128)(2,1)S(1)} %bitcast.135), channel_id=1, source_target_pairs={{16,0},{32,16},{48,32},{64,48},{80,64},{96,80},{112,96},{17,1},{33... | collective-permute-start | bytes 2752520 | tf_op jit(solution)/shard_map/ppermute | solution.py:115
  209.8 2.8 copy-start.6
  211.5 1.0 copy-start.8
  223.0 33.0 %all-to-all-start.2 = ((bf16[16,2,224,128]{3,2,1,0:T(8,128)(2,1)}), bf16[16,2,224,128]{3,2,1,0:T(8,128)(2,1)S(1)}, u32[]{:S(2)}, u32[]{:S(2)}) async-start(bf16[16,2,224,128]{3,2,1,0:T(8,128)(2,1)} %bitcast.127), calls=%async_computation.2 | async-start | bytes 3670016 | tf_op jit(solution)/shard_map/all_to_all | solution.py:117

commit v8 on v5

--- a/solution.py
+++ b/solution.py
@@ -55,24 +55,25 @@
         out_ref[w] = (c - tm_ref[w : w + 1, :] * flux).astype(out_ref.dtype)
 
 
-def transport(f, lo, hi, coef, tm, ny):
-    rows, vb, nx = f.shape
-    tv = min(VBLOCK, vb)
+def transport(f, lo, hi, coef, tm, ny, part, first):
+    rows, _, nx = f.shape
+    tv = min(VBLOCK, part)
+    base, cbase = first[0] * (part // tv), first[1] * (part // tv)
     return pl.pallas_call(
         functools.partial(transport_kernel, ny),
-        out_shape=jax.ShapeDtypeStruct(f.shape, f.dtype),
-        grid=(vb // tv,),
+        out_shape=jax.ShapeDtypeStruct((rows, part, nx), f.dtype),
+        grid=(part // tv,),
         in_specs=[
-            pl.BlockSpec((rows, tv, nx), lambda i: (0, i, 0)),
-            pl.BlockSpec((ny, tv, nx), lambda i: (0, i, 0)),
-            pl.BlockSpec((ny, tv, nx), lambda i: (0, i, 0)),
-            pl.BlockSpec((3, tv, nx), lambda i: (0, i, 0)),
+            pl.BlockSpec((rows, tv, nx), lambda i: (0, i + base, 0)),
+            pl.BlockSpec((ny, tv, nx), lambda i: (0, i + base, 0)),
+            pl.BlockSpec((ny, tv, nx), lambda i: (0, i + base, 0)),
+            pl.BlockSpec((3, tv, nx), lambda i: (0, i + cbase, 0)),
             pl.BlockSpec((rows, nx), lambda i: (0, 0)),
         ],
         out_specs=pl.BlockSpec((rows, tv, nx), lambda i: (0, i, 0)),
         scratch_shapes=[pltpu.VMEM((rows + 2 * ny, tv, nx), jnp.float32)],
         cost_estimate=pl.CostEstimate(
-            flops=20 * rows * vb * nx, transcendentals=0, bytes_accessed=4 * rows * vb * nx
+            flops=20 * rows * part * nx, transcendentals=0, bytes_accessed=4 * rows * part * nx
         ),
     )(f, lo, hi, coef, tm)
 
@@ -99,17 +100,18 @@
     whole = jnp.transpose(dist, (1, 2, 0, 3)).reshape(rows, vb, nx)
     lo_all = lax.ppermute(whole[rows - ny :], "space", up)
     hi_all = lax.ppermute(whole[:ny], "space", down)
-    fs = [whole[:, p] for p in pieces]
+    fs = [whole] * PARTS
     for step in range(STEPS):
         recvs = []
         for h, p in enumerate(pieces):
             f = fs[h]
             if step == 0:
-                lo, hi = lo_all[:, p], hi_all[:, p]
+                lo, hi, first = lo_all, hi_all, (h, h)
             else:
                 lo = lax.ppermute(f[rows - ny :], "space", up)
                 hi = lax.ppermute(f[:ny], "space", down)
-            half = transport(f, lo, hi, coef[:, p], tm, ny)
+                first = (0, h)
+            half = transport(f, lo, hi, coef, tm, ny, part, first)
             recvs.append(lax.all_to_all(half.reshape(groups, chunk, part, nx), "vel", 0, 0, tiled=True))
         moments = None
         for h, p in enumerate(pieces):

time: 306 us -> 324 us (1.059)
  waiting for transfers between devices: 141 us -> 155 us
  starting transfers between devices: 48.5 us -> 53.5 us
    ppermute x1, waiting for transfers between devices: 2.45 us -> 18.3 us  [per_device(): lo_all = lax.ppermute(whole[rows - ny:], 'space', up)]
    ppermute x1, waiting for transfers between devices: 15.5 us -> 1.75 us  [per_device(): hi_all = lax.ppermute(whole[:ny], 'space', down)]
    all_to_all x3, waiting for transfers between devices: 41.6 us -> 48.1 us  [per_device(): lax.all_to_all(post, 'vel', 0, 0, tiled=True).reshape(rows, part, nx)]
    all_to_all x4, waiting for transfers between devices: 59.5 us -> 65.3 us  [per_device(): lax.all_to_all(half.reshape(groups, chunk, part, nx), 'vel', 0, 0, tiled=...]
    slice x4 -> x0, local copies, waits for them, and re-layouts: 4.85 us -> none  [the longest x2 2.72 us: per_device(): lo, hi = (lo_all[:, p], hi_all[:, p])]
    unnamed x20 -> x24, local copies, waits for them, and re-layouts: 17 us -> 18.6 us
  transfers between devices with their start and end apart: 13 -> 13, of which waited for: 13 -> 13; matrix products, arithmetic and copies ran while one was open for 11% -> 8% of each run, Pallas kernels for 5% -> 5%
where the time goes in v8:
time: 324 us; the launch traced here: 323 us
  waiting for transfers between devices  155 us (48%)
  starting transfers between devices  53.5 us (17%)
  local copies, waits for them, and re-layouts  34.7 us (11%)
  matrix products  30.3 us (9%)
  blocking collectives  26.7 us (8%)
  Pallas kernels  21.1 us (7%)
    all_to_all x4, waiting for transfers between devices, per_device(): lax.all_to_all(half.reshape(groups, chunk, part, nx), 'vel', 0, 0, tiled=...  65.3 us
    all_to_all x3, waiting for transfers between devices, per_device(): lax.all_to_all(post, 'vel', 0, 0, tiled=True).reshape(rows, part, nx)  48.1 us
    all_to_all x1, blocking collectives, per_device(): lax.all_to_all(post, 'vel', 0, 0, tiled=True).reshape(rows, part, nx)  26.7 us
    all_to_all x4, starting transfers between devices, per_device(): lax.all_to_all(half.reshape(groups, chunk, part, nx), 'vel', 0, 0, tiled=...  23.7 us
    pallas_call x4, Pallas kernels, transport(): pl.pallas_call(functools.partial(transport_kernel, ny), out_shape=jax.Sha...  21.1 us
    unnamed x24, local copies, waits for them, and re-layouts  18.6 us
    ppermute x1, waiting for transfers between devices, per_device(): lo_all = lax.ppermute(whole[rows - ny:], 'space', up)  18.3 us
    ppermute x2, waiting for transfers between devices, per_device(): lo = lax.ppermute(f[rows - ny:], 'space', up)  18.1 us
  transfers between devices with their start and end apart: 13, of which 13 were waited for; matrix products, arithmetic and copies ran while one was open for 8% of the time, Pallas kernels for 5%

profile of v8, /device:TPU:32, one launch (start us, length us, event | category | flops | bytes accessed | tf_op | source)
XLA Modules:
  0.0 322.7 jit_solution(5446843275435170159)
XLA Ops:
  0.0 3.5 %copy.85 = bf16[448,2,16,128]{3,0,2,1:T(8,128)(2,1)S(1)} copy(bf16[448,2,16,128]{3,2,1,0:T(8,128)(2,1)} %param.6) | data formatting | bytes 7340032 | tf_op args[0]
  3.5 0.0 copy-start
  3.5 0.0 copy-start.9
  3.5 0.0 copy-start.8
  3.5 0.2 slice_bitcast_fusion.12
  3.7 1.6 copy-done
  5.3 1.9 collective-permute-start
  7.2 3.6 %collective-permute-start.1 = (bf16[16,448,128]{2,1,0:T(8,128)(2,1)S(1)}, bf16[16,448,128]{2,1,0:T(8,128)(2,1)}, u32[]{:S(2)}, u32[]{:S(2)}) collective-permute-start(bf16[16,448,128]{2,1,0:T(8,128)(2,1)S(1)} %get-tuple-element.13), channel_id=1, source_target_pairs={{16,0},{32,16},{48,32},{64,48},{80,64},{96,80},{112,96},{17,1},{33... | collective-permute-start | bytes 5505032 | tf_op jit(solution)/shard_map/ppermute | solution.py:102
  10.9 0.0 copy-done.9
  10.9 0.0 copy-done.8
  10.9 0.6 compare_convert_fusion
  11.5 18.3 %collective-permute-done.lo_ref = bf16[16,448,128]{2,1,0:T(8,128)(2,1)S(1)} collective-permute-done((bf16[16,448,128]{2,1,0:T(8,128)(2,1)S(1)}, bf16[16,448,128]{2,1,0:T(8,128)(2,1)S(1)}, u32[]{:S(2)}, u32[]{:S(2)}) %collective-permute-start) | collective-permute-done | bytes 1835040 | tf_op jit(solution)/shard_map/ppermute | solution.py:101
  29.8 1.8 collective-permute-done.1.hi_ref
  31.6 1.1 broadcast_in_dim.14.coef_ref
  32.7 0.0 copy-done.3
  32.7 5.3 %shard_map.65 = bf16[32,224,128]{2,1,0:T(8,128)(2,1)} custom-call(bf16[32,448,128]{2,1,0:T(8,128)(2,1)} %bitcast.145, bf16[16,448,128]{2,1,0:T(8,128)(2,1)} %copy-done.3, bf16[16,448,128]{2,1,0:T(8,128)(2,1)} %collective-permute-done.1.hi_ref, f32[3,448,128]{2,1,0:T(8,128)} %broadcast_in_dim.14.coef_ref, f32[32,128]{1,0:T(8,128)} %bitcast.163), custom_call_target="tpu_custom_call" | custom-call | flops 18350080 | bytes 3670016 | tf_op jit(solution)/shard_map/pallas_call | solution.py:62
  38.0 7.0 %all-to-all-start.1 = ((bf16[16,2,224,128]{3,2,1,0:T(8,128)(2,1)}), bf16[16,2,224,128]{3,2,1,0:T(8,128)(2,1)S(1)}, u32[]{:S(2)}, u32[]{:S(2)}) async-start(bf16[16,2,224,128]{3,2,1,0:T(8,128)(2,1)} %bitcast.151), calls=%async_computation.1 | async-start | bytes 3670016 | tf_op jit(solution)/shard_map/all_to_all | solution.py:115
  45.0 5.3 %shard_map.64 = bf16[32,224,128]{2,1,0:T(8,128)(2,1)} custom-call(bf16[32,448,128]{2,1,0:T(8,128)(2,1)} %bitcast.146, bf16[16,448,128]{2,1,0:T(8,128)(2,1)} %copy-done.3, bf16[16,448,128]{2,1,0:T(8,128)(2,1)} %collective-permute-done.1.hi_ref, f32[3,448,128]{2,1,0:T(8,128)} %broadcast_in_dim.14.coef_ref, f32[32,128]{1,0:T(8,128)} %bitcast.164), custom_call_target="tpu_custom_call" | custom-call | flops 18350080 | bytes 3670016 | tf_op jit(solution)/shard_map/pallas_call | solution.py:62
  50.3 22.0 %all-to-all-done.1 = bf16[16,2,224,128]{3,2,1,0:T(8,128)(2,1)S(1)} async-done(((bf16[16,2,224,128]{3,2,1,0:T(8,128)(2,1)}), bf16[16,2,224,128]{3,2,1,0:T(8,128)(2,1)S(1)}, u32[]{:S(2)}, u32[]{:S(2)}) %all-to-all-start.1) | async-done | bytes 1835040 | tf_op jit(solution)/shard_map/all_to_all | solution.py:115
  72.4 4.4 %all-to-all-start = ((bf16[16,2,224,128]{3,2,1,0:T(8,128)(2,1)}), bf16[16,2,224,128]{3,2,1,0:T(8,128)(2,1)}, u32[]{:S(2)}, u32[]{:S(2)}) async-start(bf16[16,2,224,128]{3,2,1,0:T(8,128)(2,1)} %bitcast.149), calls=%async_computation | async-start | bytes 3670016 | tf_op jit(solution)/shard_map/all_to_all | solution.py:115
  76.8 10.4 %copy.44 = bf16[512,7168]{0,1:T(8,128)(2,1)} copy(bf16[512,7168]{1,0:T(8,128)(2,1)} %param.9) | data formatting | bytes 14680064 | tf_op args[3]
  87.2 0.0 copy-start.10
  87.3 3.2 fusion.12
  90.4 14.2 %all-to-all-done = bf16[16,2,224,128]{3,2,1,0:T(8,128)(2,1)} async-done(((bf16[16,2,224,128]{3,2,1,0:T(8,128)(2,1)}), bf16[16,2,224,128]{3,2,1,0:T(8,128)(2,1)}, u32[]{:S(2)}, u32[]{:S(2)}) %all-to-all-start) | async-done | bytes 1835040 | tf_op jit(solution)/shard_map/all_to_all | solution.py:115
  104.6 0.0 copy-done.10
  104.6 3.7 %fusion.23 = bf16[512,2,128,1]{0,2,3,1:T(8,128)(2,1)S(1)} fusion(f32[2,128,512]{2,1,0:T(8,128)S(1)} %fusion.12, bf16[16,2,224,128]{3,2,1,0:T(8,128)(2,1)} %all-to-all-done, bf16[512,16,448]{0,2,1:T(8,128)(2,1)} %bitcast.154, f32[512]{0:T(512)S(1)} %copy-done.10), kind=kOutput, calls=%fused_computation.34 | convolution fusion | flops 939917312 | bytes 6293504 | tf_op jit(solution)/shard_map/ksv,srvx->krx/dot_general | solution.py:118
  108.3 5.1 %fusion.3 = bf16[16,2,224,128]{3,2,0,1:T(8,128)(2,1)} fusion(bf16[16,2,224,128]{3,2,1,0:T(8,128)(2,1)} %all-to-all-done, f32[2,128]{1,0:T(2,128)S(1)} %constant_dynamic-slice_fusion, bf16[512,2,128,1]{0,2,3,1:T(8,128)(2,1)S(1)} %fusion.23, bf16[16,448,512]{2,1,0:T(8,128)(2,1)} %bitcast.171), kind=kOutput, calls=%fused_computation.12 | convolution fusion | flops 943194112 | bytes 7603200 | tf_op jit(solution)/shard_map/svk,krx->srvx/dot_general | solution.py:128
  113.4 3.2 fusion.2
  116.6 1.4 copy.53
  118.0 5.6 %all-to-all-start.4 = ((bf16[16,2,224,128]{3,2,1,0:T(8,128)(2,1)}), bf16[16,2,224,128]{3,2,1,0:T(8,128)(2,1)S(1)}, u32[]{:S(2)}, u32[]{:S(2)}) async-start(bf16[16,2,224,128]{3,2,1,0:T(8,128)(2,1)} %copy.53), calls=%async_computation.4 | async-start | bytes 3670016 | tf_op jit(solution)/shard_map/all_to_all | solution.py:131
  123.6 3.0 copy.48
  126.6 24.8 %all-to-all-done.4 = bf16[16,2,224,128]{3,2,1,0:T(8,128)(2,1)S(1)} async-done(((bf16[16,2,224,128]{3,2,1,0:T(8,128)(2,1)}), bf16[16,2,224,128]{3,2,1,0:T(8,128)(2,1)S(1)}, u32[]{:S(2)}, u32[]{:S(2)}) %all-to-all-start.4) | async-done | bytes 1835040 | tf_op jit(solution)/shard_map/all_to_all | solution.py:131
  151.4 1.2 copy-done.2
  152.6 3.7 %all-to-all-start.2 = ((bf16[16,2,224,128]{3,2,1,0:T(8,128)(2,1)}), bf16[16,2,224,128]{3,2,1,0:T(8,128)(2,1)S(1)}, u32[]{:S(2)}, u32[]{:S(2)}) async-start(bf16[16,2,224,128]{3,2,1,0:T(8,128)(2,1)} %copy.48), calls=%async_computation.2 | async-start | bytes 3670016 | tf_op jit(solution)/shard_map/all_to_all | solution.py:127
  156.3 1.6 fusion.33
  157.9 1.9 collective-permute-start.4
  159.9 3.8 %collective-permute-start.5 = (bf16[16,224,128]{2,1,0:T(8,128)(2,1)S(1)}, bf16[16,224,128]{2,1,0:T(8,128)(2,1)S(1)}, u32[]{:S(2)}, u32[]{:S(2)}) collective-permute-start(bf16[16,224,128]{2,1,0:T(8,128)(2,1)S(1)} %bitcast.159), channel_id=1, source_target_pairs={{16,0},{32,16},{48,32},{64,48},{80,64},{96,80},{112,96},{17,1},{33... | collective-permute-start | bytes 2752520 | tf_op jit(solution)/shard_map/ppermute | solution.py:112
  163.7 9.0 %collective-permute-done.4.lo_ref = bf16[16,224,128]{2,1,0:T(8,128)(2,1)S(1)} collective-permute-done((bf16[16,224,128]{2,1,0:T(8,128)(2,1)S(1)}, bf16[16,224,128]{2,1,0:T(8,128)(2,1)S(1)}, u32[]{:S(2)}, u32[]{:S(2)}) %collective-permute-start.4) | collective-permute-done | bytes 917536 | tf_op jit(solution)/shard_map/ppermute | solution.py:111
  172.6 1.8 collective-permute-done.5.hi_ref
  174.4 1.0 copy-done.7
  175.4 5.2 %shard_map.67 = bf16[32,224,128]{2,1,0:T(8,128)(2,1)} custom-call(bf16[32,224,128]{2,1,0:T(8,128)(2,1)} %bitcast.148, bf16[16,224,128]{2,1,0:T(8,128)(2,1)} %copy-done.5, bf16[16,224,128]{2,1,0:T(8,128)(2,1)} %copy-done.7, f32[3,448,128]{2,1,0:T(8,128)} %broadcast_in_dim.14.coef_ref, f32[32,128]{1,0:T(8,128)} %bitcast.165), custom_call_target="tpu_custom_call" | custom-call | flops 18350080 | bytes 3670016 | tf_op jit(solution)/shard_map/pallas_call | solution.py:62
  180.6 1.1 all-to-all-done.2
  181.7 6.2 %all-to-all-start.5 = ((bf16[16,2,224,128]{3,2,1,0:T(8,128)(2,1)}), bf16[16,2,224,128]{3,2,1,0:T(8,128)(2,1)}, u32[]{:S(2)}, u32[]{:S(2)}) async-start(bf16[16,2,224,128]{3,2,1,0:T(8,128)(2,1)} %bitcast.157), calls=%async_computation.5 | async-start | bytes 3670016 | tf_op jit(solution)/shard_map/all_to_all | solution.py:115
  187.9 0.1 fusion.32
  188.1 3.0 collective-permute-start.2
  191.1 2.5 collective-permute-start.3
  193.6 9.1 %collective-permute-done.2.lo_ref = bf16[16,224,128]{2,1,0:T(8,128)(2,1)S(1)} collective-permute-done((bf16[16,224,128]{2,1,0:T(8,128)(2,1)S(1)}, bf16[16,224,128]{2,1,0:T(8,128)(2,1)S(1)}, u32[]{:S(2)}, u32[]{:S(2)}) %collective-permute-start.2) | collective-permute-done | bytes 917536 | tf_op jit(solution)/shard_map/ppermute | solution.py:111
  202.8 1.8 collective-permute-done.3.hi_ref
  204.5 0.9 copy-done.6
  205.5 5.3 %shard_map.66 = bf16[32,224,128]{2,1,0:T(8,128)(2,1)} custom-call(bf16[32,224,128]{2,1,0:T(8,128)(2,1)} %bitcast.147, bf16[16,224,128]{2,1,0:T(8,128)(2,1)} %copy-done.4, bf16[16,224,128]{2,1,0:T(8,128)(2,1)} %copy-done.6, f32[3,448,128]{2,1,0:T(8,128)} %broadcast_in_dim.14.coef_ref, f32[32,128]{1,0:T(8,128)} %bitcast.166), custom_call_target="tpu_custom_call" | custom-call | flops 18350080 | bytes 3670016 | tf_op jit(solution)/shard_map/pallas_call | solution.py:62
  210.7 5.2 %all-to-all-done.5 = bf16[16,2,224,128]{3,2,1,0:T(8,128)(2,1)} async-done(((bf16[16,2,224,128]{3,2,1,0:T(8,128)(2,1)}), bf16[16,2,224,128]{3,2,1,0:T(8,128)(2,1)}, u32[]{:S(2)}, u32[]{:S(2)}) %all-to-all-start.5) | async-done | bytes 1835040 | tf_op jit(solution)/shard_map/all_to_all | solution.py:115
  215.9 6.0 %all-to-all-start.3 = ((bf16[16,2,224,128]{3,2,1,0:T(8,128)(2,1)}), bf16[16,2,224,128]{3,2,1,0:T(8,128)(2,1)S(1)}, u32[]{:S(2)}, u32[]{:S(2)}) async-start(bf16[16,2,224,128]{3,2,1,0:T(8,128)(2,1)} %bitcast.158), calls=%async_computation.3 | async-start | bytes 3670016 | tf_op jit(solution)/shard_map/all_to_all | solution.py:115
  222.0 3.7 %fusion.13 = f32[2,128,512]{2,1,0:T(8,128)S(1)} fusion(bf16[16,2,224,128]{3,2,1,0:T(8,128)(2,1)} %all-to-all-done.5, bf16[512,16,448]{0,2,1:T(8,128)(2,1)} %bitcast.155), kind=kOutput, calls=%fused_computation.24 | convolution fusion | flops 939524096 | bytes 6029312 | tf_op jit(solution)/shard_map/ksv,srvx->krx/dot_general | solution.py:118
  225.7 23.9 %all-to-all-done.3 = bf16[16,2,224,128]{3,2,1,0:T(8,128)(2,1)S(1)} async-done(((bf16[16,2,224,128]{3,2,1,0:T(8,128)(2,1)}), bf16[16,2,224,128]{3,2,1,0:T(8,128)(2,1)S(1)}, u32[]{:S(2)}, u32[]{:S(2)}) %all-to-all-start.3) | async-done | bytes 1835040 | tf_op jit(solution)/shard_map/all_to_all | solution.py:115
  249.6 3.2 fusion.22
  252.8 4.5 %fusion.1 = bf16[16,2,224,128]{3,2,0,1:T(8,128)(2,1)} fusion(bf16[16,2,224,128]{3,2,1,0:T(8,128)(2,1)S(1)} %all-to-all-done.3, f32[2,128]{1,0:T(2,128)S(1)} %constant_dynamic-slice_fusion, bf16[512,2,128,1]{0,2,3,1:T(8,128)(2,1)S(1)} %fusion.22, bf16[16,448,512]{2,1,0:T(8,128)(2,1)} %bitcast.173), kind=kOutput, calls=%fused_computation.8 | convolution fusion | flops 943194112 | bytes 7603200 | tf_op jit(solution)/shard_map/svk,krx->srvx/dot_general | solution.py:128
  257.2 3.8 %fusion = bf16[16,2,224,128]{3,2,0,1:T(8,128)(2,1)S(1)} fusion(bf16[16,2,224,128]{3,2,1,0:T(8,128)(2,1)} %all-to-all-done.5, f32[2,128]{1,0:T(2,128)S(1)} %constant_dynamic-slice_fusion, bf16[512,2,128,1]{0,2,3,1:T(8,128)(2,1)S(1)} %fusion.22, bf16[16,448,512]{2,1,0:T(8,128)(2,1)} %bitcast.174), kind=kOutput, calls=%fused_computation.6 | convolution fusion | flops 943194112 | bytes 7603200 | tf_op jit(solution)/shard_map/svk,krx->srvx/dot_general | solution.py:128
  261.0 1.4 copy.59
  262.4 3.7 %all-to-all-start.7 = ((bf16[16,2,224,128]{3,2,1,0:T(8,128)(2,1)}), bf16[16,2,224,128]{3,2,1,0:T(8,128)(2,1)S(1)}, u32[]{:S(2)}, u32[]{:S(2)}) async-start(bf16[16,2,224,128]{3,2,1,0:T(8,128)(2,1)} %copy.59), calls=%async_computation.7 | async-start | bytes 3670016 | tf_op jit(solution)/shard_map/all_to_all | solution.py:131
  266.1 2.9 copy.56
  269.0 22.3 %all-to-all-done.7 = bf16[16,2,224,128]{3,2,1,0:T(8,128)(2,1)S(1)} async-done(((bf16[16,2,224,128]{3,2,1,0:T(8,128)(2,1)}), bf16[16,2,224,128]{3,2,1,0:T(8,128)(2,1)S(1)}, u32[]{:S(2)}, u32[]{:S(2)}) %all-to-all-start.7) | async-done | bytes 1835040 | tf_op jit(solution)/shard_map/all_to_all | solution.py:131
  291.3 26.7 %all_to_all.40 = bf16[16,2,224,128]{3,2,1,0:T(8,128)(2,1)S(1)} all-to-all(bf16[16,2,224,128]{3,2,1,0:T(8,128)(2,1)} %copy.56), channel_id=1, replica_groups=mesh['space'=8,'vel'=16] {'vel'}, dimensions={0} | all-to-all | bytes 3670016 | tf_op jit(solution)/shard_map/all_to_all | solution.py:127
  318.0 0.4 maximum_bitcast_fusion
  318.5 4.2 %copy.60 = bf16[448,2,16,128]{3,2,1,0:T(8,128)(2,1)} copy(bf16[448,2,16,128]{3,0,2,1:T(8,128)(2,1)S(1)} %maximum_bitcast_fusion) | data formatting | bytes 7340032 | tf_op jit(solution)/shard_map/transpose | solution.py:133
  (14 shorter events, 0.1 us)
Async XLA Ops:
  3.5 1.8 copy-start
  3.5 7.4 %copy-start.9 = (s32[448]{0:T(512)S(1)}, s32[448]{0:T(512)}, u32[]{:S(2)}) copy-start(s32[448]{0:T(512)} %param.7) | copy-start | bytes 5380
  3.5 7.4 %copy-start.8 = (s32[2,16,128]{2,1,0:T(8,128)S(1)}, s32[2,16,128]{2,1,0:T(8,128)}, u32[]{:S(2)}) copy-start(s32[2,16,128]{2,1,0:T(8,128)} %param.8) | copy-start | bytes 49156
  5.3 24.5 %collective-permute-start = (bf16[16,448,128]{2,1,0:T(8,128)(2,1)S(1)}, bf16[16,448,128]{2,1,0:T(8,128)(2,1)S(1)}, u32[]{:S(2)}, u32[]{:S(2)}) collective-permute-start(bf16[16,448,128]{2,1,0:T(8,128)(2,1)S(1)} %get-tuple-element.14), channel_id=1, source_target_pairs={{0,16},{16,32},{32,48},{48,64},{64,80},{80,96},{96,112},{1,17},{17... | collective-permute-start | bytes 5505032 | tf_op jit(solution)/shard_map/ppermute | solution.py:101
  7.2 24.4 %collective-permute-start.1 = (bf16[16,448,128]{2,1,0:T(8,128)(2,1)S(1)}, bf16[16,448,128]{2,1,0:T(8,128)(2,1)}, u32[]{:S(2)}, u32[]{:S(2)}) collective-permute-start(bf16[16,448,128]{2,1,0:T(8,128)(2,1)S(1)} %get-tuple-element.13), channel_id=1, source_target_pairs={{16,0},{32,16},{48,32},{64,48},{80,64},{96,80},{112,96},{17,1},{33... | collective-permute-start | bytes 5505032 | tf_op jit(solution)/shard_map/ppermute | solution.py:102
  29.8 2.9 copy-start.3
  38.0 34.4 %all-to-all-start.1 = ((bf16[16,2,224,128]{3,2,1,0:T(8,128)(2,1)}), bf16[16,2,224,128]{3,2,1,0:T(8,128)(2,1)S(1)}, u32[]{:S(2)}, u32[]{:S(2)}) async-start(bf16[16,2,224,128]{3,2,1,0:T(8,128)(2,1)} %bitcast.151), calls=%async_computation.1 | async-start | bytes 3670016 | tf_op jit(solution)/shard_map/all_to_all | solution.py:115
  72.4 32.2 %all-to-all-start = ((bf16[16,2,224,128]{3,2,1,0:T(8,128)(2,1)}), bf16[16,2,224,128]{3,2,1,0:T(8,128)(2,1)}, u32[]{:S(2)}, u32[]{:S(2)}) async-start(bf16[16,2,224,128]{3,2,1,0:T(8,128)(2,1)} %bitcast.149), calls=%async_computation | async-start | bytes 3670016 | tf_op jit(solution)/shard_map/all_to_all | solution.py:115
  87.2 17.4 %copy-start.10 = (f32[512]{0:T(512)S(1)}, f32[512]{0:T(512)}, u32[]{:S(2)}) copy-start(f32[512]{0:T(512)} %param.11) | copy-start | bytes 6148
  118.0 33.3 %all-to-all-start.4 = ((bf16[16,2,224,128]{3,2,1,0:T(8,128)(2,1)}), bf16[16,2,224,128]{3,2,1,0:T(8,128)(2,1)S(1)}, u32[]{:S(2)}, u32[]{:S(2)}) async-start(bf16[16,2,224,128]{3,2,1,0:T(8,128)(2,1)} %copy.53), calls=%async_computation.4 | async-start | bytes 3670016 | tf_op jit(solution)/shard_map/all_to_all | solution.py:131
  151.4 1.2 copy-start.2
  152.6 29.1 %all-to-all-start.2 = ((bf16[16,2,224,128]{3,2,1,0:T(8,128)(2,1)}), bf16[16,2,224,128]{3,2,1,0:T(8,128)(2,1)S(1)}, u32[]{:S(2)}, u32[]{:S(2)}) async-start(bf16[16,2,224,128]{3,2,1,0:T(8,128)(2,1)} %copy.48), calls=%async_computation.2 | async-start | bytes 3670016 | tf_op jit(solution)/shard_map/all_to_all | solution.py:127
  157.9 14.7 %collective-permute-start.4 = (bf16[16,224,128]{2,1,0:T(8,128)(2,1)S(1)}, bf16[16,224,128]{2,1,0:T(8,128)(2,1)S(1)}, u32[]{:S(2)}, u32[]{:S(2)}) collective-permute-start(bf16[16,224,128]{2,1,0:T(8,128)(2,1)S(1)} %bitcast.161), channel_id=1, source_target_pairs={{0,16},{16,32},{32,48},{48,64},{64,80},{80,96},{96,112},{1,17},{17... | collective-permute-start | bytes 2752520 | tf_op jit(solution)/shard_map/ppermute | solution.py:111
  159.9 14.5 %collective-permute-start.5 = (bf16[16,224,128]{2,1,0:T(8,128)(2,1)S(1)}, bf16[16,224,128]{2,1,0:T(8,128)(2,1)S(1)}, u32[]{:S(2)}, u32[]{:S(2)}) collective-permute-start(bf16[16,224,128]{2,1,0:T(8,128)(2,1)S(1)} %bitcast.159), channel_id=1, source_target_pairs={{16,0},{32,16},{48,32},{64,48},{80,64},{96,80},{112,96},{17,1},{33... | collective-permute-start | bytes 2752520 | tf_op jit(solution)/shard_map/ppermute | solution.py:112
  172.6 2.8 copy-start.5
  174.4 1.0 copy-start.7
  181.7 6.3 %copy-start.1 = (bf16[16,2,224,128]{3,2,1,0:T(8,128)(2,1)}, bf16[16,2,224,128]{3,2,1,0:T(8,128)(2,1)S(1)}, u32[]{:S(2)}) copy-start(bf16[16,2,224,128]{3,2,1,0:T(8,128)(2,1)S(1)} %all-to-all-done.2) | copy-start | bytes 5505028
  181.7 34.2 %all-to-all-start.5 = ((bf16[16,2,224,128]{3,2,1,0:T(8,128)(2,1)}), bf16[16,2,224,128]{3,2,1,0:T(8,128)(2,1)}, u32[]{:S(2)}, u32[]{:S(2)}) async-start(bf16[16,2,224,128]{3,2,1,0:T(8,128)(2,1)} %bitcast.157), calls=%async_computation.5 | async-start | bytes 3670016 | tf_op jit(solution)/shard_map/all_to_all | solution.py:115
  188.1 14.7 %collective-permute-start.2 = (bf16[16,224,128]{2,1,0:T(8,128)(2,1)S(1)}, bf16[16,224,128]{2,1,0:T(8,128)(2,1)S(1)}, u32[]{:S(2)}, u32[]{:S(2)}) collective-permute-start(bf16[16,224,128]{2,1,0:T(8,128)(2,1)S(1)} %bitcast.162), channel_id=1, source_target_pairs={{0,16},{16,32},{32,48},{48,64},{64,80},{80,96},{96,112},{1,17},{17... | collective-permute-start | bytes 2752520 | tf_op jit(solution)/shard_map/ppermute | solution.py:111
  191.1 13.4 %collective-permute-start.3 = (bf16[16,224,128]{2,1,0:T(8,128)(2,1)S(1)}, bf16[16,224,128]{2,1,0:T(8,128)(2,1)S(1)}, u32[]{:S(2)}, u32[]{:S(2)}) collective-permute-start(bf16[16,224,128]{2,1,0:T(8,128)(2,1)S(1)} %bitcast.160), channel_id=1, source_target_pairs={{16,0},{32,16},{48,32},{64,48},{80,64},{96,80},{112,96},{17,1},{33... | collective-permute-start | bytes 2752520 | tf_op jit(solution)/shard_map/ppermute | solution.py:112
  202.8 1.8 copy-start.4
  204.5 0.9 copy-start.6
  215.9 33.6 %all-to-all-start.3 = ((bf16[16,2,224,128]{3,2,1,0:T(8,128)(2,1)}), bf16[16,2,224,128]{3,2,1,0:T(8,128)(2,1)S(1)}, u32[]{:S(2)}, u32[]{:S(2)}) async-start(bf16[16,2,224,128]{3,2,1,0:T(8,128)(2,1)} %bitcast.158), calls=%async_computation.3 | async-start | bytes 3670016 | tf_op jit(solution)/shard_map/all_to_all | solution.py:115
  262.4 28.9 %all-to-all-start.7 = ((bf16[16,2,224,128]{3,2,1,0:T(8,128)(2,1)}), bf16[16,2,224,128]{3,2,1,0:T(8,128)(2,1)S(1)}, u32[]{:S(2)}, u32[]{:S(2)}) async-start(bf16[16,2,224,128]{3,2,1,0:T(8,128)(2,1)} %copy.59), calls=%async_computation.7 | async-start | bytes 3670016 | tf_op jit(solution)/shard_map/all_to_all | solution.py:131

commit v9 on v5

--- a/solution.py
+++ b/solution.py
@@ -77,6 +77,23 @@
     )(f, lo, hi, coef, tm)
 
 
+def transpose_kernel(x_ref, o_ref):
+    o_ref[...] = x_ref[...].astype(jnp.float32).T.astype(o_ref.dtype)
+
+
+def transposed(w):
+    rows, cols = w.shape
+    tile = rows
+    return pl.pallas_call(
+        transpose_kernel,
+        out_shape=jax.ShapeDtypeStruct((cols, rows), w.dtype),
+        grid=(cols // tile,),
+        in_specs=[pl.BlockSpec((rows, tile), lambda i: (0, i))],
+        out_specs=pl.BlockSpec((tile, rows), lambda i: (i, 0)),
+        cost_estimate=pl.CostEstimate(flops=0, transcendentals=0, bytes_accessed=4 * rows * cols),
+    )(w)
+
+
 def per_device(dist, vel_map, cell_mask, w_modes, e_modes, rates):
     vb, nzl, ny, nx = dist.shape
     rows = nzl * ny
@@ -90,7 +107,6 @@
     tm = (cell_mask != 1).astype(jnp.float32).reshape(rows, nx)
     cmask = jnp.where(cell_mask == 0, 1.0, jnp.where(cell_mask == 2, 0.5, 0.0)).astype(jnp.float32)
     cm = lax.dynamic_slice_in_dim(cmask.reshape(rows, nx), lax.axis_index("vel") * chunk, chunk, 0)
-    w3 = w_modes.reshape(kmodes, groups, vb)
     e3 = e_modes.reshape(groups, vb, kmodes)
     up = [(i, i + 1) for i in range(spaces - 1)]
     down = [(i + 1, i) for i in range(spaces - 1)]
@@ -99,6 +115,8 @@
     whole = jnp.transpose(dist, (1, 2, 0, 3)).reshape(rows, vb, nx)
     lo_all = lax.ppermute(whole[rows - ny :], "space", up)
     hi_all = lax.ppermute(whole[:ny], "space", down)
+    wt, lo_all, hi_all = lax.optimization_barrier((transposed(w_modes), lo_all, hi_all))
+    w3 = wt.reshape(groups, vb, kmodes)
     fs = [whole[:, p] for p in pieces]
     for step in range(STEPS):
         recvs = []
@@ -113,7 +131,7 @@
             recvs.append(lax.all_to_all(half.reshape(groups, chunk, part, nx), "vel", 0, 0, tiled=True))
         moments = None
         for h, p in enumerate(pieces):
-            term = jnp.einsum("ksv,srvx->krx", w3[:, :, p], recvs[h], preferred_element_type=jnp.float32)
+            term = jnp.einsum("svk,srvx->krx", w3[:, p], recvs[h], preferred_element_type=jnp.float32)
             moments = term if moments is None else moments + term
         delta = (rates[:, None, None] * moments).astype(jnp.bfloat16)
         fs = []

time: 306 us -> 324 us (1.059)
  Pallas kernels: 21.1 us -> 32.8 us
  waiting for transfers between devices: 141 us -> 147 us
  starting transfers between devices: 48.5 us -> 52.9 us
  local copies, waits for them, and re-layouts: 37 us -> 33.6 us
    all_to_all x4, waiting for transfers between devices: 59.5 us -> 73.6 us  [per_device(): lax.all_to_all(half.reshape(groups, chunk, part, nx), 'vel', 0, 0, tiled=...]
    ppermute x1, waiting for transfers between devices: 15.5 us -> 1.89 us  [per_device(): hi_all = lax.ppermute(whole[:ny], 'space', down)]
    pallas_call x0 -> x1, Pallas kernels: none -> 11.7 us  [transposed(): pl.pallas_call(transpose_kernel, out_shape=jax.ShapeDtypeStruct((cols, ro...]
    unnamed x20 -> x29, local copies, waits for them, and re-layouts: 17 us -> 7.44 us
    all_to_all x3, waiting for transfers between devices: 41.6 us -> 47.1 us  [per_device(): lax.all_to_all(post, 'vel', 0, 0, tiled=True).reshape(rows, part, nx)]
  transfers between devices with their start and end apart: 13 -> 13, of which waited for: 13 -> 13; matrix products, arithmetic and copies ran while one was open for 11% -> 6% of each run, Pallas kernels for 5% -> 9%
where the time goes in v9:
time: 324 us; the launch traced here: 323 us
  waiting for transfers between devices  147 us (45%)
  starting transfers between devices  52.9 us (16%)
  local copies, waits for them, and re-layouts  33.6 us (10%)
  Pallas kernels  32.8 us (10%)
  matrix products  27.8 us (9%)
  blocking collectives  27.6 us (9%)
    all_to_all x4, waiting for transfers between devices, per_device(): lax.all_to_all(half.reshape(groups, chunk, part, nx), 'vel', 0, 0, tiled=...  73.6 us
    all_to_all x3, waiting for transfers between devices, per_device(): lax.all_to_all(post, 'vel', 0, 0, tiled=True).reshape(rows, part, nx)  47.1 us
    all_to_all x1, blocking collectives, per_device(): lax.all_to_all(post, 'vel', 0, 0, tiled=True).reshape(rows, part, nx)  27.6 us
    all_to_all x4, starting transfers between devices, per_device(): lax.all_to_all(half.reshape(groups, chunk, part, nx), 'vel', 0, 0, tiled=...  22.9 us
    pallas_call x4, Pallas kernels, transport(): pl.pallas_call(functools.partial(transport_kernel, ny), out_shape=jax.Sha...  21.1 us
    ppermute x2, waiting for transfers between devices, per_device(): lo = lax.ppermute(f[rows - ny:], 'space', up)  18.3 us
    dot_general x4, matrix products, per_device(): jnp.einsum('svk,srvx->krx', w3[:, p], recvs[h], preferred_element_type=jn...  14.2 us
    dot_general x4, matrix products, per_device(): jnp.einsum('svk,krx->srvx', e3[:, p], delta, preferred_element_type=jnp.f...  13.5 us
  transfers between devices with their start and end apart: 13, of which 13 were waited for; matrix products, arithmetic and copies ran while one was open for 6% of the time, Pallas kernels for 9%

profile of v9, /device:TPU:32, one launch (start us, length us, event | category | flops | bytes accessed | tf_op | source)
XLA Modules:
  0.0 322.9 jit_solution(13052159822453504509)
XLA Ops:
  0.0 3.5 %copy.58 = bf16[448,2,16,128]{3,0,2,1:T(8,128)(2,1)S(1)} copy(bf16[448,2,16,128]{3,2,1,0:T(8,128)(2,1)} %param.6) | data formatting | bytes 7340032 | tf_op args[0]
  3.5 0.0 copy-start
  3.5 2.2 slice_bitcast_fusion.12
  5.7 0.8 copy-done
  6.5 1.9 collective-permute-start
  8.4 0.0 copy-start.8
  8.4 3.6 %collective-permute-start.1 = (bf16[16,448,128]{2,1,0:T(8,128)(2,1)}, bf16[16,448,128]{2,1,0:T(8,128)(2,1)}, u32[]{:S(2)}, u32[]{:S(2)}) collective-permute-start(bf16[16,448,128]{2,1,0:T(8,128)(2,1)} %get-tuple-element.21), channel_id=1, source_target_pairs={{16,0},{32,16},{48,32},{64,48},{80,64},{96,80},{112,96},{17,1},{33... | collective-permute-start | bytes 5505032 | tf_op jit(solution)/shard_map/ppermute | solution.py:117
  12.0 11.7 %shard_map.64 = bf16[7168,512]{1,0:T(8,128)(2,1)} custom-call(bf16[512,7168]{1,0:T(8,128)(2,1)} %x_ref.1), custom_call_target="tpu_custom_call" | custom-call | bytes 14680064 | tf_op jit(solution)/shard_map/pallas_call | solution.py:87
  23.8 0.1 fusion.37
  23.9 0.6 compare_convert_fusion
  24.5 4.2 %fusion.32 = (bf16[32,224,128]{2,1,0:T(8,128)(2,1)}, bf16[32,224,128]{2,1,0:T(8,128)(2,1)}) fusion(bf16[32,448,128]{2,1,0:T(8,128)(2,1)} %bitcast.153), kind=kLoop, calls=%fused_computation.56 | loop fusion | bytes 7340032 | tf_op jit(solution)/shard_map/slice | solution.py:120
  28.6 2.5 collective-permute-done
  31.2 1.9 collective-permute-done.1
  33.1 3.3 %fusion.35 = (bf16[16,224,128]{2,1,0:T(8,128)(2,1)}, bf16[16,224,128]{2,1,0:T(8,128)(2,1)}, bf16[16,224,128]{2,1,0:T(8,128)(2,1)}, bf16[16,224,128]{2,1,0:T(8,128)(2,1)}) fusion(bf16[16,448,128]{2,1,0:T(8,128)(2,1)} %collective-permute-done.1, bf16[16,448,128]{2,1,0:T(8,128)(2,1)S(1)} %collective-permute-done), kind=kLoop, calls=%fused_computation.59 | loop fusion | bytes 7340032 | tf_op jit(solution)/shard_map/slice | solution.py:126
  36.4 0.9 broadcast_in_dim.30.coef_ref
  37.3 5.2 %shard_map.66 = bf16[32,224,128]{2,1,0:T(8,128)(2,1)} custom-call(bf16[32,224,128]{2,1,0:T(8,128)(2,1)} %get-tuple-element.19.f_ref, bf16[16,224,128]{2,1,0:T(8,128)(2,1)} %get-tuple-element.39.lo_ref, bf16[16,224,128]{2,1,0:T(8,128)(2,1)} %get-tuple-element.29.hi_ref, f32[3,224,128]{2,1,0:T(8,128)} %broadcast_in_dim.30.coef_ref, f32[32,128]{1,0:T(8,128)} %bitcast.170), custom_call_target="tpu_custom_call" | custom-call | flops 18350080 | bytes 3670016 | tf_op jit(solution)/shard_map/pallas_call | solution.py:61
  42.5 7.0 %all-to-all-start.1 = ((bf16[16,2,224,128]{3,2,1,0:T(8,128)(2,1)}), bf16[16,2,224,128]{3,2,1,0:T(8,128)(2,1)S(1)}, u32[]{:S(2)}, u32[]{:S(2)}) async-start(bf16[16,2,224,128]{3,2,1,0:T(8,128)(2,1)} %bitcast.164), calls=%async_computation.1 | async-start | bytes 3670016 | tf_op jit(solution)/shard_map/all_to_all | solution.py:131
  49.6 0.9 broadcast_in_dim.26.coef_ref
  50.5 5.3 %shard_map.65 = bf16[32,224,128]{2,1,0:T(8,128)(2,1)} custom-call(bf16[32,224,128]{2,1,0:T(8,128)(2,1)} %get-tuple-element.20.f_ref, bf16[16,224,128]{2,1,0:T(8,128)(2,1)} %get-tuple-element.38.lo_ref, bf16[16,224,128]{2,1,0:T(8,128)(2,1)} %get-tuple-element.30.hi_ref, f32[3,224,128]{2,1,0:T(8,128)} %broadcast_in_dim.26.coef_ref, f32[32,128]{1,0:T(8,128)} %bitcast.171), custom_call_target="tpu_custom_call" | custom-call | flops 18350080 | bytes 3670016 | tf_op jit(solution)/shard_map/pallas_call | solution.py:61
  55.8 21.4 %all-to-all-done.1 = bf16[16,2,224,128]{3,2,1,0:T(8,128)(2,1)S(1)} async-done(((bf16[16,2,224,128]{3,2,1,0:T(8,128)(2,1)}), bf16[16,2,224,128]{3,2,1,0:T(8,128)(2,1)S(1)}, u32[]{:S(2)}, u32[]{:S(2)}) %all-to-all-start.1) | async-done | bytes 1835040 | tf_op jit(solution)/shard_map/all_to_all | solution.py:131
  77.1 4.4 %all-to-all-start = ((bf16[16,2,224,128]{3,2,1,0:T(8,128)(2,1)}), bf16[16,2,224,128]{3,2,1,0:T(8,128)(2,1)}, u32[]{:S(2)}, u32[]{:S(2)}) async-start(bf16[16,2,224,128]{3,2,1,0:T(8,128)(2,1)} %bitcast.163), calls=%async_computation | async-start | bytes 3670016 | tf_op jit(solution)/shard_map/all_to_all | solution.py:131
  81.6 3.2 fusion.12
  84.8 24.5 %all-to-all-done = bf16[16,2,224,128]{3,2,1,0:T(8,128)(2,1)} async-done(((bf16[16,2,224,128]{3,2,1,0:T(8,128)(2,1)}), bf16[16,2,224,128]{3,2,1,0:T(8,128)(2,1)}, u32[]{:S(2)}, u32[]{:S(2)}) %all-to-all-start) | async-done | bytes 1835040 | tf_op jit(solution)/shard_map/all_to_all | solution.py:131
  109.4 3.9 %fusion.23 = bf16[512,2,128,1]{2,0,3,1:T(8,128)(2,1)S(1)} fusion(f32[512,2,128]{2,0,1:T(8,128)S(1)} %fusion.12, bf16[16,2,224,128]{3,2,1,0:T(8,128)(2,1)} %all-to-all-done, bf16[16,448,512]{2,1,0:T(8,128)(2,1)} %bitcast.159, f32[512]{0:T(512)S(1)} %copy-done.9), kind=kOutput, calls=%fused_computation.34 | convolution fusion | flops 939917312 | bytes 6293504 | tf_op jit(solution)/shard_map/svk,srvx->krx/dot_general | solution.py:134
  113.3 0.0 slice-start.1
  113.3 5.2 %fusion.3 = bf16[16,2,224,128]{3,2,0,1:T(8,128)(2,1)} fusion(bf16[16,2,224,128]{3,2,1,0:T(8,128)(2,1)} %all-to-all-done, f32[2,128]{1,0:T(2,128)S(1)} %constant_dynamic-slice_fusion, bf16[512,2,128,1]{2,0,3,1:T(8,128)(2,1)S(1)} %fusion.23, bf16[16,448,512]{2,1,0:T(8,128)(2,1)} %bitcast.178), kind=kOutput, calls=%fused_computation.12 | convolution fusion | flops 943194112 | bytes 7603200 | tf_op jit(solution)/shard_map/svk,krx->srvx/dot_general | solution.py:144
  118.5 1.1 fusion.2
  119.7 1.4 copy.40
  121.1 5.7 %all-to-all-start.4 = ((bf16[16,2,224,128]{3,2,1,0:T(8,128)(2,1)}), bf16[16,2,224,128]{3,2,1,0:T(8,128)(2,1)S(1)}, u32[]{:S(2)}, u32[]{:S(2)}) async-start(bf16[16,2,224,128]{3,2,1,0:T(8,128)(2,1)} %copy.40), calls=%async_computation.4 | async-start | bytes 3670016 | tf_op jit(solution)/shard_map/all_to_all | solution.py:147
  126.8 2.9 copy.36
  129.7 24.8 %all-to-all-done.4 = bf16[16,2,224,128]{3,2,1,0:T(8,128)(2,1)S(1)} async-done(((bf16[16,2,224,128]{3,2,1,0:T(8,128)(2,1)}), bf16[16,2,224,128]{3,2,1,0:T(8,128)(2,1)S(1)}, u32[]{:S(2)}, u32[]{:S(2)}) %all-to-all-start.4) | async-done | bytes 1835040 | tf_op jit(solution)/shard_map/all_to_all | solution.py:147
  154.4 1.2 copy-done.2
  155.7 3.7 %all-to-all-start.2 = ((bf16[16,2,224,128]{3,2,1,0:T(8,128)(2,1)}), bf16[16,2,224,128]{3,2,1,0:T(8,128)(2,1)S(1)}, u32[]{:S(2)}, u32[]{:S(2)}) async-start(bf16[16,2,224,128]{3,2,1,0:T(8,128)(2,1)} %copy.36), calls=%async_computation.2 | async-start | bytes 3670016 | tf_op jit(solution)/shard_map/all_to_all | solution.py:143
  159.4 1.6 fusion.34
  161.0 1.9 collective-permute-start.4
  162.9 3.6 %collective-permute-start.5 = (bf16[16,224,128]{2,1,0:T(8,128)(2,1)S(1)}, bf16[16,224,128]{2,1,0:T(8,128)(2,1)S(1)}, u32[]{:S(2)}, u32[]{:S(2)}) collective-permute-start(bf16[16,224,128]{2,1,0:T(8,128)(2,1)S(1)} %bitcast.166), channel_id=1, source_target_pairs={{16,0},{32,16},{48,32},{64,48},{80,64},{96,80},{112,96},{17,1},{33... | collective-permute-start | bytes 2752520 | tf_op jit(solution)/shard_map/ppermute | solution.py:129
  166.6 9.1 %collective-permute-done.4.lo_ref = bf16[16,224,128]{2,1,0:T(8,128)(2,1)S(1)} collective-permute-done((bf16[16,224,128]{2,1,0:T(8,128)(2,1)S(1)}, bf16[16,224,128]{2,1,0:T(8,128)(2,1)S(1)}, u32[]{:S(2)}, u32[]{:S(2)}) %collective-permute-start.4) | collective-permute-done | bytes 917536 | tf_op jit(solution)/shard_map/ppermute | solution.py:128
  175.7 1.8 collective-permute-done.5.hi_ref
  177.4 1.0 copy-done.6
  178.4 5.3 %shard_map.68 = bf16[32,224,128]{2,1,0:T(8,128)(2,1)} custom-call(bf16[32,224,128]{2,1,0:T(8,128)(2,1)} %bitcast.155, bf16[16,224,128]{2,1,0:T(8,128)(2,1)} %copy-done.4, bf16[16,224,128]{2,1,0:T(8,128)(2,1)} %copy-done.6, f32[3,224,128]{2,1,0:T(8,128)} %broadcast_in_dim.30.coef_ref, f32[32,128]{1,0:T(8,128)} %bitcast.172), custom_call_target="tpu_custom_call" | custom-call | flops 18350080 | bytes 3670016 | tf_op jit(solution)/shard_map/pallas_call | solution.py:61
  183.7 0.9 all-to-all-done.2
  184.7 6.3 %all-to-all-start.5 = ((bf16[16,2,224,128]{3,2,1,0:T(8,128)(2,1)}), bf16[16,2,224,128]{3,2,1,0:T(8,128)(2,1)}, u32[]{:S(2)}, u32[]{:S(2)}) async-start(bf16[16,2,224,128]{3,2,1,0:T(8,128)(2,1)} %bitcast.162), calls=%async_computation.5 | async-start | bytes 3670016 | tf_op jit(solution)/shard_map/all_to_all | solution.py:131
  191.0 0.1 fusion.33
  191.1 2.3 collective-permute-start.2
  193.4 3.2 %collective-permute-start.3 = (bf16[16,224,128]{2,1,0:T(8,128)(2,1)S(1)}, bf16[16,224,128]{2,1,0:T(8,128)(2,1)S(1)}, u32[]{:S(2)}, u32[]{:S(2)}) collective-permute-start(bf16[16,224,128]{2,1,0:T(8,128)(2,1)S(1)} %bitcast.167), channel_id=1, source_target_pairs={{16,0},{32,16},{48,32},{64,48},{80,64},{96,80},{112,96},{17,1},{33... | collective-permute-start | bytes 2752520 | tf_op jit(solution)/shard_map/ppermute | solution.py:129
  196.7 9.1 %collective-permute-done.2.lo_ref = bf16[16,224,128]{2,1,0:T(8,128)(2,1)S(1)} collective-permute-done((bf16[16,224,128]{2,1,0:T(8,128)(2,1)S(1)}, bf16[16,224,128]{2,1,0:T(8,128)(2,1)S(1)}, u32[]{:S(2)}, u32[]{:S(2)}) %collective-permute-start.2) | collective-permute-done | bytes 917536 | tf_op jit(solution)/shard_map/ppermute | solution.py:128
  205.8 1.8 collective-permute-done.3.hi_ref
  207.6 0.9 copy-done.5
  208.5 5.3 %shard_map.67 = bf16[32,224,128]{2,1,0:T(8,128)(2,1)} custom-call(bf16[32,224,128]{2,1,0:T(8,128)(2,1)} %bitcast.154, bf16[16,224,128]{2,1,0:T(8,128)(2,1)} %copy-done.3, bf16[16,224,128]{2,1,0:T(8,128)(2,1)} %copy-done.5, f32[3,224,128]{2,1,0:T(8,128)} %broadcast_in_dim.26.coef_ref, f32[32,128]{1,0:T(8,128)} %bitcast.173), custom_call_target="tpu_custom_call" | custom-call | flops 18350080 | bytes 3670016 | tf_op jit(solution)/shard_map/pallas_call | solution.py:61
  213.8 5.0 %all-to-all-done.5 = bf16[16,2,224,128]{3,2,1,0:T(8,128)(2,1)} async-done(((bf16[16,2,224,128]{3,2,1,0:T(8,128)(2,1)}), bf16[16,2,224,128]{3,2,1,0:T(8,128)(2,1)}, u32[]{:S(2)}, u32[]{:S(2)}) %all-to-all-start.5) | async-done | bytes 1835040 | tf_op jit(solution)/shard_map/all_to_all | solution.py:131
  218.8 5.1 %all-to-all-start.3 = ((bf16[16,2,224,128]{3,2,1,0:T(8,128)(2,1)}), bf16[16,2,224,128]{3,2,1,0:T(8,128)(2,1)S(1)}, u32[]{:S(2)}, u32[]{:S(2)}) async-start(bf16[16,2,224,128]{3,2,1,0:T(8,128)(2,1)} %bitcast.165), calls=%async_computation.3 | async-start | bytes 3670016 | tf_op jit(solution)/shard_map/all_to_all | solution.py:131
  223.9 3.8 %fusion.13 = f32[512,2,128]{2,0,1:T(8,128)S(1)} fusion(bf16[16,2,224,128]{3,2,1,0:T(8,128)(2,1)} %all-to-all-done.5, bf16[16,448,512]{2,1,0:T(8,128)(2,1)} %bitcast.160), kind=kOutput, calls=%fused_computation.24 | convolution fusion | flops 939524096 | bytes 6029312 | tf_op jit(solution)/shard_map/svk,srvx->krx/dot_general | solution.py:134
  227.7 22.7 %all-to-all-done.3 = bf16[16,2,224,128]{3,2,1,0:T(8,128)(2,1)S(1)} async-done(((bf16[16,2,224,128]{3,2,1,0:T(8,128)(2,1)}), bf16[16,2,224,128]{3,2,1,0:T(8,128)(2,1)S(1)}, u32[]{:S(2)}, u32[]{:S(2)}) %all-to-all-start.3) | async-done | bytes 1835040 | tf_op jit(solution)/shard_map/all_to_all | solution.py:131
  250.4 3.4 %fusion.22 = bf16[512,2,128,1]{2,0,3,1:T(8,128)(2,1)S(1)} fusion(f32[512,2,128]{2,0,1:T(8,128)S(1)} %fusion.13, bf16[16,2,224,128]{3,2,1,0:T(8,128)(2,1)S(1)} %all-to-all-done.3, bf16[16,448,512]{2,1,0:T(8,128)(2,1)} %bitcast.161, f32[512]{0:T(512)S(1)} %copy-done.9), kind=kOutput, calls=%fused_computation.33 | convolution fusion | flops 939917312 | bytes 6293504 | tf_op jit(solution)/shard_map/svk,srvx->krx/dot_general | solution.py:134
  253.7 0.0 slice-start.3
  253.7 4.6 %fusion.1 = bf16[16,2,224,128]{3,2,0,1:T(8,128)(2,1)} fusion(bf16[16,2,224,128]{3,2,1,0:T(8,128)(2,1)S(1)} %all-to-all-done.3, f32[2,128]{1,0:T(2,128)S(1)} %constant_dynamic-slice_fusion, bf16[512,2,128,1]{2,0,3,1:T(8,128)(2,1)S(1)} %fusion.22, bf16[16,448,512]{2,1,0:T(8,128)(2,1)} %bitcast.179), kind=kOutput, calls=%fused_computation.8 | convolution fusion | flops 943194112 | bytes 7603200 | tf_op jit(solution)/shard_map/svk,krx->srvx/dot_general | solution.py:144
  258.3 2.6 fusion
  261.0 1.4 copy.44
  262.4 3.9 %all-to-all-start.7 = ((bf16[16,2,224,128]{3,2,1,0:T(8,128)(2,1)}), bf16[16,2,224,128]{3,2,1,0:T(8,128)(2,1)S(1)}, u32[]{:S(2)}, u32[]{:S(2)}) async-start(bf16[16,2,224,128]{3,2,1,0:T(8,128)(2,1)} %copy.44), calls=%async_computation.7 | async-start | bytes 3670016 | tf_op jit(solution)/shard_map/all_to_all | solution.py:147
  266.3 2.9 copy.42
  269.2 21.4 %all-to-all-done.7 = bf16[16,2,224,128]{3,2,1,0:T(8,128)(2,1)S(1)} async-done(((bf16[16,2,224,128]{3,2,1,0:T(8,128)(2,1)}), bf16[16,2,224,128]{3,2,1,0:T(8,128)(2,1)S(1)}, u32[]{:S(2)}, u32[]{:S(2)}) %all-to-all-start.7) | async-done | bytes 1835040 | tf_op jit(solution)/shard_map/all_to_all | solution.py:147
  290.7 27.6 %all_to_all.40 = bf16[16,2,224,128]{3,2,1,0:T(8,128)(2,1)S(1)} all-to-all(bf16[16,2,224,128]{3,2,1,0:T(8,128)(2,1)} %copy.42), channel_id=1, replica_groups=mesh['space'=8,'vel'=16] {'vel'}, dimensions={0} | all-to-all | bytes 3670016 | tf_op jit(solution)/shard_map/all_to_all | solution.py:143
  318.3 0.4 maximum_bitcast_fusion
  318.7 4.2 %copy.45 = bf16[448,2,16,128]{3,2,1,0:T(8,128)(2,1)} copy(bf16[448,2,16,128]{3,0,2,1:T(8,128)(2,1)S(1)} %maximum_bitcast_fusion) | data formatting | bytes 7340032 | tf_op jit(solution)/shard_map/transpose | solution.py:149
  (26 shorter events, 0.1 us)
Async XLA Ops:
  3.5 3.0 copy-start
  6.5 24.7 %collective-permute-start = (bf16[16,448,128]{2,1,0:T(8,128)(2,1)}, bf16[16,448,128]{2,1,0:T(8,128)(2,1)S(1)}, u32[]{:S(2)}, u32[]{:S(2)}) collective-permute-start(bf16[16,448,128]{2,1,0:T(8,128)(2,1)} %get-tuple-element.22), channel_id=1, source_target_pairs={{0,16},{16,32},{32,48},{48,64},{64,80},{80,96},{96,112},{1,17},{17... | collective-permute-start | bytes 5505032 | tf_op jit(solution)/shard_map/ppermute | solution.py:116
  8.4 15.4 %copy-start.8 = (s32[448]{0:T(512)S(1)}, s32[448]{0:T(512)}, u32[]{:S(2)}) copy-start(s32[448]{0:T(512)} %param.7) | copy-start | bytes 5380
  8.4 15.5 %copy-start.7 = (s32[2,16,128]{2,1,0:T(8,128)S(1)}, s32[2,16,128]{2,1,0:T(8,128)}, u32[]{:S(2)}) copy-start(s32[2,16,128]{2,1,0:T(8,128)} %param.8) | copy-start | bytes 49156
  8.4 24.7 %collective-permute-start.1 = (bf16[16,448,128]{2,1,0:T(8,128)(2,1)}, bf16[16,448,128]{2,1,0:T(8,128)(2,1)}, u32[]{:S(2)}, u32[]{:S(2)}) collective-permute-start(bf16[16,448,128]{2,1,0:T(8,128)(2,1)} %get-tuple-element.21), channel_id=1, source_target_pairs={{16,0},{32,16},{48,32},{64,48},{80,64},{96,80},{112,96},{17,1},{33... | collective-permute-start | bytes 5505032 | tf_op jit(solution)/shard_map/ppermute | solution.py:117
  42.5 34.6 %all-to-all-start.1 = ((bf16[16,2,224,128]{3,2,1,0:T(8,128)(2,1)}), bf16[16,2,224,128]{3,2,1,0:T(8,128)(2,1)S(1)}, u32[]{:S(2)}, u32[]{:S(2)}) async-start(bf16[16,2,224,128]{3,2,1,0:T(8,128)(2,1)} %bitcast.164), calls=%async_computation.1 | async-start | bytes 3670016 | tf_op jit(solution)/shard_map/all_to_all | solution.py:131
  77.1 32.2 %all-to-all-start = ((bf16[16,2,224,128]{3,2,1,0:T(8,128)(2,1)}), bf16[16,2,224,128]{3,2,1,0:T(8,128)(2,1)}, u32[]{:S(2)}, u32[]{:S(2)}) async-start(bf16[16,2,224,128]{3,2,1,0:T(8,128)(2,1)} %bitcast.163), calls=%async_computation | async-start | bytes 3670016 | tf_op jit(solution)/shard_map/all_to_all | solution.py:131
  81.6 27.7 %copy-start.9 = (f32[512]{0:T(512)S(1)}, f32[512]{0:T(512)}, u32[]{:S(2)}) copy-start(f32[512]{0:T(512)} %param.11) | copy-start | bytes 6148
  109.4 9.2 %slice-start = ((s8[7340032]{0:T(1024)(128)(4,1)}), s8[4194304]{0:T(1024)(128)(4,1)S(1)}, s32[]{:S(2)}) async-start(s8[7340032]{0:T(1024)(128)(4,1)} %bitcast.180), calls=%async_computation.8 | async-start | bytes 8388608
  113.3 5.2 %slice-start.1 = ((s8[7340032]{0:T(1024)(128)(4,1)}), s8[3145728]{0:T(1024)(128)(4,1)S(1)}, s32[]{:S(2)}) async-start(s8[7340032]{0:T(1024)(128)(4,1)} %bitcast.180), calls=%async_computation.9 | async-start | bytes 6291456
  121.1 33.4 %all-to-all-start.4 = ((bf16[16,2,224,128]{3,2,1,0:T(8,128)(2,1)}), bf16[16,2,224,128]{3,2,1,0:T(8,128)(2,1)S(1)}, u32[]{:S(2)}, u32[]{:S(2)}) async-start(bf16[16,2,224,128]{3,2,1,0:T(8,128)(2,1)} %copy.40), calls=%async_computation.4 | async-start | bytes 3670016 | tf_op jit(solution)/shard_map/all_to_all | solution.py:147
  154.4 1.2 copy-start.2
  155.7 29.0 %all-to-all-start.2 = ((bf16[16,2,224,128]{3,2,1,0:T(8,128)(2,1)}), bf16[16,2,224,128]{3,2,1,0:T(8,128)(2,1)S(1)}, u32[]{:S(2)}, u32[]{:S(2)}) async-start(bf16[16,2,224,128]{3,2,1,0:T(8,128)(2,1)} %copy.36), calls=%async_computation.2 | async-start | bytes 3670016 | tf_op jit(solution)/shard_map/all_to_all | solution.py:143
  161.0 14.7 %collective-permute-start.4 = (bf16[16,224,128]{2,1,0:T(8,128)(2,1)S(1)}, bf16[16,224,128]{2,1,0:T(8,128)(2,1)S(1)}, u32[]{:S(2)}, u32[]{:S(2)}) collective-permute-start(bf16[16,224,128]{2,1,0:T(8,128)(2,1)S(1)} %bitcast.168), channel_id=1, source_target_pairs={{0,16},{16,32},{32,48},{48,64},{64,80},{80,96},{96,112},{1,17},{17... | collective-permute-start | bytes 2752520 | tf_op jit(solution)/shard_map/ppermute | solution.py:128
  162.9 14.5 %collective-permute-start.5 = (bf16[16,224,128]{2,1,0:T(8,128)(2,1)S(1)}, bf16[16,224,128]{2,1,0:T(8,128)(2,1)S(1)}, u32[]{:S(2)}, u32[]{:S(2)}) collective-permute-start(bf16[16,224,128]{2,1,0:T(8,128)(2,1)S(1)} %bitcast.166), channel_id=1, source_target_pairs={{16,0},{32,16},{48,32},{64,48},{80,64},{96,80},{112,96},{17,1},{33... | collective-permute-start | bytes 2752520 | tf_op jit(solution)/shard_map/ppermute | solution.py:129
  175.7 2.8 copy-start.4
  177.4 1.0 copy-start.6
  184.7 6.4 %copy-start.1 = (bf16[16,2,224,128]{3,2,1,0:T(8,128)(2,1)}, bf16[16,2,224,128]{3,2,1,0:T(8,128)(2,1)S(1)}, u32[]{:S(2)}) copy-start(bf16[16,2,224,128]{3,2,1,0:T(8,128)(2,1)S(1)} %all-to-all-done.2) | copy-start | bytes 5505028
  184.7 34.1 %all-to-all-start.5 = ((bf16[16,2,224,128]{3,2,1,0:T(8,128)(2,1)}), bf16[16,2,224,128]{3,2,1,0:T(8,128)(2,1)}, u32[]{:S(2)}, u32[]{:S(2)}) async-start(bf16[16,2,224,128]{3,2,1,0:T(8,128)(2,1)} %bitcast.162), calls=%async_computation.5 | async-start | bytes 3670016 | tf_op jit(solution)/shard_map/all_to_all | solution.py:131
  191.1 14.7 %collective-permute-start.2 = (bf16[16,224,128]{2,1,0:T(8,128)(2,1)S(1)}, bf16[16,224,128]{2,1,0:T(8,128)(2,1)S(1)}, u32[]{:S(2)}, u32[]{:S(2)}) collective-permute-start(bf16[16,224,128]{2,1,0:T(8,128)(2,1)S(1)} %bitcast.169), channel_id=1, source_target_pairs={{0,16},{16,32},{32,48},{48,64},{64,80},{80,96},{96,112},{1,17},{17... | collective-permute-start | bytes 2752520 | tf_op jit(solution)/shard_map/ppermute | solution.py:128
  193.4 14.1 %collective-permute-start.3 = (bf16[16,224,128]{2,1,0:T(8,128)(2,1)S(1)}, bf16[16,224,128]{2,1,0:T(8,128)(2,1)S(1)}, u32[]{:S(2)}, u32[]{:S(2)}) collective-permute-start(bf16[16,224,128]{2,1,0:T(8,128)(2,1)S(1)} %bitcast.167), channel_id=1, source_target_pairs={{16,0},{32,16},{48,32},{64,48},{80,64},{96,80},{112,96},{17,1},{33... | collective-permute-start | bytes 2752520 | tf_op jit(solution)/shard_map/ppermute | solution.py:129
  205.8 1.8 copy-start.3
  207.6 0.9 copy-start.5
  218.8 31.6 %all-to-all-start.3 = ((bf16[16,2,224,128]{3,2,1,0:T(8,128)(2,1)}), bf16[16,2,224,128]{3,2,1,0:T(8,128)(2,1)S(1)}, u32[]{:S(2)}, u32[]{:S(2)}) async-start(bf16[16,2,224,128]{3,2,1,0:T(8,128)(2,1)} %bitcast.165), calls=%async_computation.3 | async-start | bytes 3670016 | tf_op jit(solution)/shard_map/all_to_all | solution.py:131
  250.4 8.0 %slice-start.2 = ((s8[7340032]{0:T(1024)(128)(4,1)}), s8[4194304]{0:T(1024)(128)(4,1)S(1)}, s32[]{:S(2)}) async-start(s8[7340032]{0:T(1024)(128)(4,1)} %bitcast.183), calls=%async_computation.10 | async-start | bytes 8388608
  253.7 4.6 %slice-start.3 = ((s8[7340032]{0:T(1024)(128)(4,1)}), s8[3145728]{0:T(1024)(128)(4,1)S(1)}, s32[]{:S(2)}) async-start(s8[7340032]{0:T(1024)(128)(4,1)} %bitcast.183), calls=%async_computation.11 | async-start | bytes 6291456
  262.4 28.3 %all-to-all-start.7 = ((bf16[16,2,224,128]{3,2,1,0:T(8,128)(2,1)}), bf16[16,2,224,128]{3,2,1,0:T(8,128)(2,1)S(1)}, u32[]{:S(2)}, u32[]{:S(2)}) async-start(bf16[16,2,224,128]{3,2,1,0:T(8,128)(2,1)} %copy.44), calls=%async_computation.7 | async-start | bytes 3670016 | tf_op jit(solution)/shard_map/all_to_all | solution.py:147

commit v10 on v5

--- a/solution.py
+++ b/solution.py
@@ -9,7 +9,7 @@
 
 VGRID = 24
 STEPS = 2
-VBLOCK = 112
+VBLOCK = 32
 PARTS = 2
 
 

time: 306 us -> 312 us (1.020)
  Pallas kernels: 21.1 us -> 26.8 us
    pallas_call x4, Pallas kernels: 21.1 us -> 26.8 us  [transport(): pl.pallas_call(functools.partial(transport_kernel, ny), out_shape=jax.Sha...]
  transfers between devices with their start and end apart: 13 -> 13, of which waited for: 13 -> 12; matrix products, arithmetic and copies ran while one was open for 11% -> 10% of each run, Pallas kernels for 5% -> 6%
where the time goes in v10:
time: 312 us; the launch traced here: 310 us
  waiting for transfers between devices  140 us (45%)
  starting transfers between devices  49.2 us (16%)
  local copies, waits for them, and re-layouts  37 us (12%)
  matrix products  29 us (9%)
  blocking collectives  27.3 us (9%)
  Pallas kernels  26.8 us (9%)
    all_to_all x4, waiting for transfers between devices, per_device(): lax.all_to_all(half.reshape(groups, chunk, part, nx), 'vel', 0, 0, tiled=...  58.5 us
    all_to_all x3, waiting for transfers between devices, per_device(): lax.all_to_all(post, 'vel', 0, 0, tiled=True).reshape(rows, part, nx)  41.6 us
    all_to_all x1, blocking collectives, per_device(): lax.all_to_all(post, 'vel', 0, 0, tiled=True).reshape(rows, part, nx)  27.3 us
    pallas_call x4, Pallas kernels, transport(): pl.pallas_call(functools.partial(transport_kernel, ny), out_shape=jax.Sha...  26.8 us
    all_to_all x4, starting transfers between devices, per_device(): lax.all_to_all(half.reshape(groups, chunk, part, nx), 'vel', 0, 0, tiled=...  22.6 us
    ppermute x2, waiting for transfers between devices, per_device(): lo = lax.ppermute(f[rows - ny:], 'space', up)  18.3 us
    unnamed x20, local copies, waits for them, and re-layouts  17 us
    ppermute x1, waiting for transfers between devices, per_device(): hi_all = lax.ppermute(whole[:ny], 'space', down)  15.5 us
  transfers between devices with their start and end apart: 13, of which 12 were waited for; matrix products, arithmetic and copies ran while one was open for 10% of the time, Pallas kernels for 6%

profile of v10, /device:TPU:32, one launch (start us, length us, event | category | flops | bytes accessed | tf_op | source)
XLA Modules:
  0.0 310.5 jit_solution(8740398633715904187)
XLA Ops:
  0.0 3.5 %copy.85 = bf16[448,2,16,128]{3,0,2,1:T(8,128)(2,1)S(1)} copy(bf16[448,2,16,128]{3,2,1,0:T(8,128)(2,1)} %param.6) | data formatting | bytes 7340032 | tf_op args[0]
  3.5 0.0 copy-start.7
  3.5 0.0 copy-start.6
  3.5 0.2 slice_bitcast_fusion.12
  3.7 1.9 collective-permute-start.1
  5.7 2.4 collective-permute-start
  8.1 0.1 fusion.37
  8.2 0.6 compare_convert_fusion
  8.8 2.1 fusion.32
  10.9 15.5 %collective-permute-done.1 = bf16[16,448,128]{2,1,0:T(8,128)(2,1)S(1)} collective-permute-done((bf16[16,448,128]{2,1,0:T(8,128)(2,1)S(1)}, bf16[16,448,128]{2,1,0:T(8,128)(2,1)S(1)}, u32[]{:S(2)}, u32[]{:S(2)}) %collective-permute-start.1) | collective-permute-done | bytes 1835040 | tf_op jit(solution)/shard_map/ppermute | solution.py:101
  26.4 1.4 fusion.35
  27.7 2.5 collective-permute-done
  30.2 1.3 fusion.36
  31.6 0.9 broadcast_in_dim.30.coef_ref
  32.5 6.7 %shard_map.65 = bf16[32,224,128]{2,1,0:T(8,128)(2,1)} custom-call(bf16[32,224,128]{2,1,0:T(8,128)(2,1)} %get-tuple-element.14.f_ref, bf16[16,224,128]{2,1,0:T(8,128)(2,1)} %get-tuple-element.26.lo_ref, bf16[16,224,128]{2,1,0:T(8,128)(2,1)} %get-tuple-element.24.hi_ref, f32[3,224,128]{2,1,0:T(8,128)} %broadcast_in_dim.30.coef_ref, f32[32,128]{1,0:T(8,128)} %bitcast.162), custom_call_target="tpu_custom_call" | custom-call | flops 18350080 | bytes 3670016 | tf_op jit(solution)/shard_map/pallas_call | solution.py:61
  39.2 7.0 %all-to-all-start.1 = ((bf16[16,2,224,128]{3,2,1,0:T(8,128)(2,1)}), bf16[16,2,224,128]{3,2,1,0:T(8,128)(2,1)S(1)}, u32[]{:S(2)}, u32[]{:S(2)}) async-start(bf16[16,2,224,128]{3,2,1,0:T(8,128)(2,1)} %bitcast.156), calls=%async_computation.1 | async-start | bytes 3670016 | tf_op jit(solution)/shard_map/all_to_all | solution.py:113
  46.2 0.9 broadcast_in_dim.26.coef_ref
  47.1 6.7 %shard_map.64 = bf16[32,224,128]{2,1,0:T(8,128)(2,1)} custom-call(bf16[32,224,128]{2,1,0:T(8,128)(2,1)} %get-tuple-element.13.f_ref, bf16[16,224,128]{2,1,0:T(8,128)(2,1)} %get-tuple-element.25.lo_ref, bf16[16,224,128]{2,1,0:T(8,128)(2,1)} %get-tuple-element.23.hi_ref, f32[3,224,128]{2,1,0:T(8,128)} %broadcast_in_dim.26.coef_ref, f32[32,128]{1,0:T(8,128)} %bitcast.163), custom_call_target="tpu_custom_call" | custom-call | flops 18350080 | bytes 3670016 | tf_op jit(solution)/shard_map/pallas_call | solution.py:61
  53.8 19.9 %all-to-all-done.1 = bf16[16,2,224,128]{3,2,1,0:T(8,128)(2,1)S(1)} async-done(((bf16[16,2,224,128]{3,2,1,0:T(8,128)(2,1)}), bf16[16,2,224,128]{3,2,1,0:T(8,128)(2,1)S(1)}, u32[]{:S(2)}, u32[]{:S(2)}) %all-to-all-start.1) | async-done | bytes 1835040 | tf_op jit(solution)/shard_map/all_to_all | solution.py:113
  73.7 4.4 %all-to-all-start = ((bf16[16,2,224,128]{3,2,1,0:T(8,128)(2,1)}), bf16[16,2,224,128]{3,2,1,0:T(8,128)(2,1)}, u32[]{:S(2)}, u32[]{:S(2)}) async-start(bf16[16,2,224,128]{3,2,1,0:T(8,128)(2,1)} %bitcast.155), calls=%async_computation | async-start | bytes 3670016 | tf_op jit(solution)/shard_map/all_to_all | solution.py:113
  78.1 10.4 %copy.44 = bf16[512,7168]{0,1:T(8,128)(2,1)} copy(bf16[512,7168]{1,0:T(8,128)(2,1)} %param.9) | data formatting | bytes 14680064 | tf_op args[3]
  88.5 0.0 copy-start.8
  88.5 3.2 %fusion.12 = f32[2,128,512]{2,1,0:T(8,128)S(1)} fusion(bf16[16,2,224,128]{3,2,1,0:T(8,128)(2,1)S(1)} %all-to-all-done.1, bf16[512,16,448]{0,2,1:T(8,128)(2,1)} %bitcast.150), kind=kOutput, calls=%fused_computation.23 | convolution fusion | flops 939524096 | bytes 6029312 | tf_op jit(solution)/shard_map/ksv,srvx->krx/dot_general | solution.py:116
  91.7 11.3 %all-to-all-done = bf16[16,2,224,128]{3,2,1,0:T(8,128)(2,1)} async-done(((bf16[16,2,224,128]{3,2,1,0:T(8,128)(2,1)}), bf16[16,2,224,128]{3,2,1,0:T(8,128)(2,1)}, u32[]{:S(2)}, u32[]{:S(2)}) %all-to-all-start) | async-done | bytes 1835040 | tf_op jit(solution)/shard_map/all_to_all | solution.py:113
  103.0 0.0 copy-done.8
  103.0 3.7 %fusion.23 = bf16[512,2,128,1]{0,2,3,1:T(8,128)(2,1)S(1)} fusion(f32[2,128,512]{2,1,0:T(8,128)S(1)} %fusion.12, bf16[16,2,224,128]{3,2,1,0:T(8,128)(2,1)} %all-to-all-done, bf16[512,16,448]{0,2,1:T(8,128)(2,1)} %bitcast.151, f32[512]{0:T(512)S(1)} %copy-done.8), kind=kOutput, calls=%fused_computation.34 | convolution fusion | flops 939917312 | bytes 6293504 | tf_op jit(solution)/shard_map/ksv,srvx->krx/dot_general | solution.py:116
  106.7 5.1 %fusion.3 = bf16[16,2,224,128]{3,2,0,1:T(8,128)(2,1)} fusion(bf16[16,2,224,128]{3,2,1,0:T(8,128)(2,1)} %all-to-all-done, f32[2,128]{1,0:T(2,128)S(1)} %constant_dynamic-slice_fusion, bf16[512,2,128,1]{0,2,3,1:T(8,128)(2,1)S(1)} %fusion.23, bf16[16,448,512]{2,1,0:T(8,128)(2,1)} %bitcast.170), kind=kOutput, calls=%fused_computation.12 | convolution fusion | flops 943194112 | bytes 7603200 | tf_op jit(solution)/shard_map/svk,krx->srvx/dot_general | solution.py:126
  111.8 3.2 %fusion.2 = bf16[16,2,224,128]{3,2,0,1:T(8,128)(2,1)S(1)} fusion(bf16[16,2,224,128]{3,2,1,0:T(8,128)(2,1)S(1)} %all-to-all-done.1, f32[2,128]{1,0:T(2,128)S(1)} %constant_dynamic-slice_fusion, bf16[512,2,128,1]{0,2,3,1:T(8,128)(2,1)S(1)} %fusion.23, bf16[16,448,512]{2,1,0:T(8,128)(2,1)} %bitcast.171), kind=kOutput, calls=%fused_computation.10 | convolution fusion | flops 943194112 | bytes 7603200 | tf_op jit(solution)/shard_map/svk,krx->srvx/dot_general | solution.py:126
  115.0 1.4 copy.53
  116.4 3.7 %all-to-all-start.4 = ((bf16[16,2,224,128]{3,2,1,0:T(8,128)(2,1)}), bf16[16,2,224,128]{3,2,1,0:T(8,128)(2,1)S(1)}, u32[]{:S(2)}, u32[]{:S(2)}) async-start(bf16[16,2,224,128]{3,2,1,0:T(8,128)(2,1)} %copy.53), calls=%async_computation.4 | async-start | bytes 3670016 | tf_op jit(solution)/shard_map/all_to_all | solution.py:129
  120.1 2.9 copy.48
  123.1 21.9 %all-to-all-done.4 = bf16[16,2,224,128]{3,2,1,0:T(8,128)(2,1)S(1)} async-done(((bf16[16,2,224,128]{3,2,1,0:T(8,128)(2,1)}), bf16[16,2,224,128]{3,2,1,0:T(8,128)(2,1)S(1)}, u32[]{:S(2)}, u32[]{:S(2)}) %all-to-all-start.4) | async-done | bytes 1835040 | tf_op jit(solution)/shard_map/all_to_all | solution.py:129
  145.0 1.2 copy-done.1
  146.2 3.7 %all-to-all-start.2 = ((bf16[16,2,224,128]{3,2,1,0:T(8,128)(2,1)}), bf16[16,2,224,128]{3,2,1,0:T(8,128)(2,1)S(1)}, u32[]{:S(2)}, u32[]{:S(2)}) async-start(bf16[16,2,224,128]{3,2,1,0:T(8,128)(2,1)} %copy.48), calls=%async_computation.2 | async-start | bytes 3670016 | tf_op jit(solution)/shard_map/all_to_all | solution.py:125
  149.9 1.6 fusion.34
  151.5 1.9 collective-permute-start.4
  153.5 3.6 %collective-permute-start.5 = (bf16[16,224,128]{2,1,0:T(8,128)(2,1)S(1)}, bf16[16,224,128]{2,1,0:T(8,128)(2,1)S(1)}, u32[]{:S(2)}, u32[]{:S(2)}) collective-permute-start(bf16[16,224,128]{2,1,0:T(8,128)(2,1)S(1)} %bitcast.158), channel_id=1, source_target_pairs={{16,0},{32,16},{48,32},{64,48},{80,64},{96,80},{112,96},{17,1},{33... | collective-permute-start | bytes 2752520 | tf_op jit(solution)/shard_map/ppermute | solution.py:111
  157.1 9.1 %collective-permute-done.4.lo_ref = bf16[16,224,128]{2,1,0:T(8,128)(2,1)S(1)} collective-permute-done((bf16[16,224,128]{2,1,0:T(8,128)(2,1)S(1)}, bf16[16,224,128]{2,1,0:T(8,128)(2,1)S(1)}, u32[]{:S(2)}, u32[]{:S(2)}) %collective-permute-start.4) | collective-permute-done | bytes 917536 | tf_op jit(solution)/shard_map/ppermute | solution.py:110
  166.2 1.8 collective-permute-done.5.hi_ref
  168.0 1.0 copy-done.5
  169.0 6.7 %shard_map.67 = bf16[32,224,128]{2,1,0:T(8,128)(2,1)} custom-call(bf16[32,224,128]{2,1,0:T(8,128)(2,1)} %bitcast.147, bf16[16,224,128]{2,1,0:T(8,128)(2,1)} %copy-done.3, bf16[16,224,128]{2,1,0:T(8,128)(2,1)} %copy-done.5, f32[3,224,128]{2,1,0:T(8,128)} %broadcast_in_dim.30.coef_ref, f32[32,128]{1,0:T(8,128)} %bitcast.164), custom_call_target="tpu_custom_call" | custom-call | flops 18350080 | bytes 3670016 | tf_op jit(solution)/shard_map/pallas_call | solution.py:61
  175.7 0.0 all-to-all-done.2
  175.7 7.2 %all-to-all-start.5 = ((bf16[16,2,224,128]{3,2,1,0:T(8,128)(2,1)}), bf16[16,2,224,128]{3,2,1,0:T(8,128)(2,1)}, u32[]{:S(2)}, u32[]{:S(2)}) async-start(bf16[16,2,224,128]{3,2,1,0:T(8,128)(2,1)} %bitcast.154), calls=%async_computation.5 | async-start | bytes 3670016 | tf_op jit(solution)/shard_map/all_to_all | solution.py:113
  182.9 0.1 fusion.33
  183.1 1.9 collective-permute-start.2
  185.0 3.6 %collective-permute-start.3 = (bf16[16,224,128]{2,1,0:T(8,128)(2,1)S(1)}, bf16[16,224,128]{2,1,0:T(8,128)(2,1)S(1)}, u32[]{:S(2)}, u32[]{:S(2)}) collective-permute-start(bf16[16,224,128]{2,1,0:T(8,128)(2,1)S(1)} %bitcast.159), channel_id=1, source_target_pairs={{16,0},{32,16},{48,32},{64,48},{80,64},{96,80},{112,96},{17,1},{33... | collective-permute-start | bytes 2752520 | tf_op jit(solution)/shard_map/ppermute | solution.py:111
  188.6 9.1 %collective-permute-done.2.lo_ref = bf16[16,224,128]{2,1,0:T(8,128)(2,1)S(1)} collective-permute-done((bf16[16,224,128]{2,1,0:T(8,128)(2,1)S(1)}, bf16[16,224,128]{2,1,0:T(8,128)(2,1)S(1)}, u32[]{:S(2)}, u32[]{:S(2)}) %collective-permute-start.2) | collective-permute-done | bytes 917536 | tf_op jit(solution)/shard_map/ppermute | solution.py:110
  197.8 1.8 collective-permute-done.3.hi_ref
  199.5 0.9 copy-done.4
  200.5 6.7 %shard_map.66 = bf16[32,224,128]{2,1,0:T(8,128)(2,1)} custom-call(bf16[32,224,128]{2,1,0:T(8,128)(2,1)} %bitcast.146, bf16[16,224,128]{2,1,0:T(8,128)(2,1)} %copy-done.2, bf16[16,224,128]{2,1,0:T(8,128)(2,1)} %copy-done.4, f32[3,224,128]{2,1,0:T(8,128)} %broadcast_in_dim.26.coef_ref, f32[32,128]{1,0:T(8,128)} %bitcast.165), custom_call_target="tpu_custom_call" | custom-call | flops 18350080 | bytes 3670016 | tf_op jit(solution)/shard_map/pallas_call | solution.py:61
  207.2 3.8 %all-to-all-done.5 = bf16[16,2,224,128]{3,2,1,0:T(8,128)(2,1)} async-done(((bf16[16,2,224,128]{3,2,1,0:T(8,128)(2,1)}), bf16[16,2,224,128]{3,2,1,0:T(8,128)(2,1)}, u32[]{:S(2)}, u32[]{:S(2)}) %all-to-all-start.5) | async-done | bytes 1835040 | tf_op jit(solution)/shard_map/all_to_all | solution.py:113
  210.9 3.9 %all-to-all-start.3 = ((bf16[16,2,224,128]{3,2,1,0:T(8,128)(2,1)}), bf16[16,2,224,128]{3,2,1,0:T(8,128)(2,1)S(1)}, u32[]{:S(2)}, u32[]{:S(2)}) async-start(bf16[16,2,224,128]{3,2,1,0:T(8,128)(2,1)} %bitcast.157), calls=%async_computation.3 | async-start | bytes 3670016 | tf_op jit(solution)/shard_map/all_to_all | solution.py:113
  214.8 3.7 %fusion.13 = f32[2,128,512]{2,1,0:T(8,128)S(1)} fusion(bf16[16,2,224,128]{3,2,1,0:T(8,128)(2,1)} %all-to-all-done.5, bf16[512,16,448]{0,2,1:T(8,128)(2,1)} %bitcast.152), kind=kOutput, calls=%fused_computation.24 | convolution fusion | flops 939524096 | bytes 6029312 | tf_op jit(solution)/shard_map/ksv,srvx->krx/dot_general | solution.py:116
  218.6 23.6 %all-to-all-done.3 = bf16[16,2,224,128]{3,2,1,0:T(8,128)(2,1)S(1)} async-done(((bf16[16,2,224,128]{3,2,1,0:T(8,128)(2,1)}), bf16[16,2,224,128]{3,2,1,0:T(8,128)(2,1)S(1)}, u32[]{:S(2)}, u32[]{:S(2)}) %all-to-all-start.3) | async-done | bytes 1835040 | tf_op jit(solution)/shard_map/all_to_all | solution.py:113
  242.1 3.2 %fusion.22 = bf16[512,2,128,1]{0,2,3,1:T(8,128)(2,1)S(1)} fusion(f32[2,128,512]{2,1,0:T(8,128)S(1)} %fusion.13, bf16[16,2,224,128]{3,2,1,0:T(8,128)(2,1)S(1)} %all-to-all-done.3, bf16[512,16,448]{0,2,1:T(8,128)(2,1)} %bitcast.153, f32[512]{0:T(512)S(1)} %copy-done.8), kind=kOutput, calls=%fused_computation.33 | convolution fusion | flops 939917312 | bytes 6293504 | tf_op jit(solution)/shard_map/ksv,srvx->krx/dot_general | solution.py:116
  245.3 3.2 %fusion.1 = bf16[16,2,224,128]{3,2,0,1:T(8,128)(2,1)S(1)} fusion(bf16[16,2,224,128]{3,2,1,0:T(8,128)(2,1)S(1)} %all-to-all-done.3, f32[2,128]{1,0:T(2,128)S(1)} %constant_dynamic-slice_fusion, bf16[512,2,128,1]{0,2,3,1:T(8,128)(2,1)S(1)} %fusion.22, bf16[16,448,512]{2,1,0:T(8,128)(2,1)} %bitcast.172), kind=kOutput, calls=%fused_computation.8 | convolution fusion | flops 943194112 | bytes 7603200 | tf_op jit(solution)/shard_map/svk,krx->srvx/dot_general | solution.py:126
  248.5 1.4 copy.56
  250.0 3.7 %all-to-all-start.6 = ((bf16[16,2,224,128]{3,2,1,0:T(8,128)(2,1)}), bf16[16,2,224,128]{3,2,1,0:T(8,128)(2,1)S(1)}, u32[]{:S(2)}, u32[]{:S(2)}) async-start(bf16[16,2,224,128]{3,2,1,0:T(8,128)(2,1)} %copy.56), calls=%async_computation.6 | async-start | bytes 3670016 | tf_op jit(solution)/shard_map/all_to_all | solution.py:125
  253.7 3.8 %fusion = bf16[16,2,224,128]{3,2,0,1:T(8,128)(2,1)S(1)} fusion(bf16[16,2,224,128]{3,2,1,0:T(8,128)(2,1)} %all-to-all-done.5, f32[2,128]{1,0:T(2,128)S(1)} %constant_dynamic-slice_fusion, bf16[512,2,128,1]{0,2,3,1:T(8,128)(2,1)S(1)} %fusion.22, bf16[16,448,512]{2,1,0:T(8,128)(2,1)} %bitcast.173), kind=kOutput, calls=%fused_computation.6 | convolution fusion | flops 943194112 | bytes 7603200 | tf_op jit(solution)/shard_map/svk,krx->srvx/dot_general | solution.py:126
  257.5 1.4 copy.59
  258.9 19.6 %all-to-all-done.6 = bf16[16,2,224,128]{3,2,1,0:T(8,128)(2,1)S(1)} async-done(((bf16[16,2,224,128]{3,2,1,0:T(8,128)(2,1)}), bf16[16,2,224,128]{3,2,1,0:T(8,128)(2,1)S(1)}, u32[]{:S(2)}, u32[]{:S(2)}) %all-to-all-start.6) | async-done | bytes 1835040 | tf_op jit(solution)/shard_map/all_to_all | solution.py:125
  278.5 27.3 %all_to_all.40 = bf16[16,2,224,128]{3,2,1,0:T(8,128)(2,1)S(1)} all-to-all(bf16[16,2,224,128]{3,2,1,0:T(8,128)(2,1)} %copy.59), channel_id=1, replica_groups=mesh['space'=8,'vel'=16] {'vel'}, dimensions={0} | all-to-all | bytes 3670016 | tf_op jit(solution)/shard_map/all_to_all | solution.py:129
  305.8 0.4 maximum_bitcast_fusion
  306.3 4.2 %copy.60 = bf16[448,2,16,128]{3,2,1,0:T(8,128)(2,1)} copy(bf16[448,2,16,128]{3,0,2,1:T(8,128)(2,1)S(1)} %maximum_bitcast_fusion) | data formatting | bytes 7340032 | tf_op jit(solution)/shard_map/transpose | solution.py:131
  (15 shorter events, 0.1 us)
Async XLA Ops:
  3.5 4.6 %copy-start.7 = (s32[448]{0:T(512)S(1)}, s32[448]{0:T(512)}, u32[]{:S(2)}) copy-start(s32[448]{0:T(512)} %param.7) | copy-start | bytes 5380
  3.5 4.7 %copy-start.6 = (s32[2,16,128]{2,1,0:T(8,128)S(1)}, s32[2,16,128]{2,1,0:T(8,128)}, u32[]{:S(2)}) copy-start(s32[2,16,128]{2,1,0:T(8,128)} %param.8) | copy-start | bytes 49156
  3.7 22.6 %collective-permute-start.1 = (bf16[16,448,128]{2,1,0:T(8,128)(2,1)S(1)}, bf16[16,448,128]{2,1,0:T(8,128)(2,1)S(1)}, u32[]{:S(2)}, u32[]{:S(2)}) collective-permute-start(bf16[16,448,128]{2,1,0:T(8,128)(2,1)S(1)} %get-tuple-element.15), channel_id=1, source_target_pairs={{16,0},{32,16},{48,32},{64,48},{80,64},{96,80},{112,96},{17,1},{33... | collective-permute-start | bytes 5505032 | tf_op jit(solution)/shard_map/ppermute | solution.py:101
  5.7 24.5 %collective-permute-start = (bf16[16,448,128]{2,1,0:T(8,128)(2,1)S(1)}, bf16[16,448,128]{2,1,0:T(8,128)(2,1)S(1)}, u32[]{:S(2)}, u32[]{:S(2)}) collective-permute-start(bf16[16,448,128]{2,1,0:T(8,128)(2,1)S(1)} %get-tuple-element.16), channel_id=1, source_target_pairs={{0,16},{16,32},{32,48},{48,64},{64,80},{80,96},{96,112},{1,17},{17... | collective-permute-start | bytes 5505032 | tf_op jit(solution)/shard_map/ppermute | solution.py:100
  39.2 34.5 %all-to-all-start.1 = ((bf16[16,2,224,128]{3,2,1,0:T(8,128)(2,1)}), bf16[16,2,224,128]{3,2,1,0:T(8,128)(2,1)S(1)}, u32[]{:S(2)}, u32[]{:S(2)}) async-start(bf16[16,2,224,128]{3,2,1,0:T(8,128)(2,1)} %bitcast.156), calls=%async_computation.1 | async-start | bytes 3670016 | tf_op jit(solution)/shard_map/all_to_all | solution.py:113
  73.7 29.3 %all-to-all-start = ((bf16[16,2,224,128]{3,2,1,0:T(8,128)(2,1)}), bf16[16,2,224,128]{3,2,1,0:T(8,128)(2,1)}, u32[]{:S(2)}, u32[]{:S(2)}) async-start(bf16[16,2,224,128]{3,2,1,0:T(8,128)(2,1)} %bitcast.155), calls=%async_computation | async-start | bytes 3670016 | tf_op jit(solution)/shard_map/all_to_all | solution.py:113
  88.5 14.5 %copy-start.8 = (f32[512]{0:T(512)S(1)}, f32[512]{0:T(512)}, u32[]{:S(2)}) copy-start(f32[512]{0:T(512)} %param.11) | copy-start | bytes 6148
  116.4 28.6 %all-to-all-start.4 = ((bf16[16,2,224,128]{3,2,1,0:T(8,128)(2,1)}), bf16[16,2,224,128]{3,2,1,0:T(8,128)(2,1)S(1)}, u32[]{:S(2)}, u32[]{:S(2)}) async-start(bf16[16,2,224,128]{3,2,1,0:T(8,128)(2,1)} %copy.53), calls=%async_computation.4 | async-start | bytes 3670016 | tf_op jit(solution)/shard_map/all_to_all | solution.py:129
  145.0 1.2 copy-start.1
  146.2 29.4 %all-to-all-start.2 = ((bf16[16,2,224,128]{3,2,1,0:T(8,128)(2,1)}), bf16[16,2,224,128]{3,2,1,0:T(8,128)(2,1)S(1)}, u32[]{:S(2)}, u32[]{:S(2)}) async-start(bf16[16,2,224,128]{3,2,1,0:T(8,128)(2,1)} %copy.48), calls=%async_computation.2 | async-start | bytes 3670016 | tf_op jit(solution)/shard_map/all_to_all | solution.py:125
  151.5 14.7 %collective-permute-start.4 = (bf16[16,224,128]{2,1,0:T(8,128)(2,1)S(1)}, bf16[16,224,128]{2,1,0:T(8,128)(2,1)S(1)}, u32[]{:S(2)}, u32[]{:S(2)}) collective-permute-start(bf16[16,224,128]{2,1,0:T(8,128)(2,1)S(1)} %bitcast.160), channel_id=1, source_target_pairs={{0,16},{16,32},{32,48},{48,64},{64,80},{80,96},{96,112},{1,17},{17... | collective-permute-start | bytes 2752520 | tf_op jit(solution)/shard_map/ppermute | solution.py:110
  153.5 14.5 %collective-permute-start.5 = (bf16[16,224,128]{2,1,0:T(8,128)(2,1)S(1)}, bf16[16,224,128]{2,1,0:T(8,128)(2,1)S(1)}, u32[]{:S(2)}, u32[]{:S(2)}) collective-permute-start(bf16[16,224,128]{2,1,0:T(8,128)(2,1)S(1)} %bitcast.158), channel_id=1, source_target_pairs={{16,0},{32,16},{48,32},{64,48},{80,64},{96,80},{112,96},{17,1},{33... | collective-permute-start | bytes 2752520 | tf_op jit(solution)/shard_map/ppermute | solution.py:111
  166.2 2.7 copy-start.3
  168.0 1.0 copy-start.5
  175.7 7.4 %copy-start = (bf16[16,2,224,128]{3,2,1,0:T(8,128)(2,1)}, bf16[16,2,224,128]{3,2,1,0:T(8,128)(2,1)S(1)}, u32[]{:S(2)}) copy-start(bf16[16,2,224,128]{3,2,1,0:T(8,128)(2,1)S(1)} %all-to-all-done.2) | copy-start | bytes 5505028
  175.7 35.3 %all-to-all-start.5 = ((bf16[16,2,224,128]{3,2,1,0:T(8,128)(2,1)}), bf16[16,2,224,128]{3,2,1,0:T(8,128)(2,1)}, u32[]{:S(2)}, u32[]{:S(2)}) async-start(bf16[16,2,224,128]{3,2,1,0:T(8,128)(2,1)} %bitcast.154), calls=%async_computation.5 | async-start | bytes 3670016 | tf_op jit(solution)/shard_map/all_to_all | solution.py:113
  183.1 14.7 %collective-permute-start.2 = (bf16[16,224,128]{2,1,0:T(8,128)(2,1)S(1)}, bf16[16,224,128]{2,1,0:T(8,128)(2,1)S(1)}, u32[]{:S(2)}, u32[]{:S(2)}) collective-permute-start(bf16[16,224,128]{2,1,0:T(8,128)(2,1)S(1)} %bitcast.161), channel_id=1, source_target_pairs={{0,16},{16,32},{32,48},{48,64},{64,80},{80,96},{96,112},{1,17},{17... | collective-permute-start | bytes 2752520 | tf_op jit(solution)/shard_map/ppermute | solution.py:110
  185.0 14.5 %collective-permute-start.3 = (bf16[16,224,128]{2,1,0:T(8,128)(2,1)S(1)}, bf16[16,224,128]{2,1,0:T(8,128)(2,1)S(1)}, u32[]{:S(2)}, u32[]{:S(2)}) collective-permute-start(bf16[16,224,128]{2,1,0:T(8,128)(2,1)S(1)} %bitcast.159), channel_id=1, source_target_pairs={{16,0},{32,16},{48,32},{64,48},{80,64},{96,80},{112,96},{17,1},{33... | collective-permute-start | bytes 2752520 | tf_op jit(solution)/shard_map/ppermute | solution.py:111
  197.8 1.8 copy-start.2
  199.5 0.9 copy-start.4
  210.9 31.2 %all-to-all-start.3 = ((bf16[16,2,224,128]{3,2,1,0:T(8,128)(2,1)}), bf16[16,2,224,128]{3,2,1,0:T(8,128)(2,1)S(1)}, u32[]{:S(2)}, u32[]{:S(2)}) async-start(bf16[16,2,224,128]{3,2,1,0:T(8,128)(2,1)} %bitcast.157), calls=%async_computation.3 | async-start | bytes 3670016 | tf_op jit(solution)/shard_map/all_to_all | solution.py:113
  250.0 28.6 %all-to-all-start.6 = ((bf16[16,2,224,128]{3,2,1,0:T(8,128)(2,1)}), bf16[16,2,224,128]{3,2,1,0:T(8,128)(2,1)S(1)}, u32[]{:S(2)}, u32[]{:S(2)}) async-start(bf16[16,2,224,128]{3,2,1,0:T(8,128)(2,1)} %copy.56), calls=%async_computation.6 | async-start | bytes 3670016 | tf_op jit(solution)/shard_map/all_to_all | solution.py:125

commit v11 on v5

--- a/solution.py
+++ b/solution.py
@@ -97,8 +97,8 @@
     pieces = [slice(h * part, (h + 1) * part) for h in range(PARTS)]
 
     whole = jnp.transpose(dist, (1, 2, 0, 3)).reshape(rows, vb, nx)
-    lo_all = lax.ppermute(whole[rows - ny :], "space", up)
-    hi_all = lax.ppermute(whole[:ny], "space", down)
+    lo_all = jnp.transpose(lax.ppermute(dist[:, nzl - 1], "space", up), (1, 0, 2))
+    hi_all = jnp.transpose(lax.ppermute(dist[:, 0], "space", down), (1, 0, 2))
     fs = [whole[:, p] for p in pieces]
     for step in range(STEPS):
         recvs = []

time: 306 us -> 317 us (1.036)
  starting transfers between devices: 48.5 us -> 53.2 us
  waiting for transfers between devices: 141 us -> 145 us
    all_to_all x4, waiting for transfers between devices: 59.5 us -> 63.1 us  [per_device(): lax.all_to_all(half.reshape(groups, chunk, part, nx), 'vel', 0, 0, tiled=...]
    all_to_all x3, waiting for transfers between devices: 41.6 us -> 44.9 us  [per_device(): lax.all_to_all(post, 'vel', 0, 0, tiled=True).reshape(rows, part, nx)]
    unnamed x20 -> x23, local copies, waits for them, and re-layouts: 17 us -> 14.5 us
where the time goes in v11:
time: 317 us; the launch traced here: 316 us
  waiting for transfers between devices  145 us (46%)
  starting transfers between devices  53.2 us (17%)
  local copies, waits for them, and re-layouts  38.4 us (12%)
  matrix products  29 us (9%)
  blocking collectives  27.6 us (9%)
  Pallas kernels  21 us (7%)
    all_to_all x4, waiting for transfers between devices, per_device(): lax.all_to_all(half.reshape(groups, chunk, part, nx), 'vel', 0, 0, tiled=...  63.1 us
    all_to_all x3, waiting for transfers between devices, per_device(): lax.all_to_all(post, 'vel', 0, 0, tiled=True).reshape(rows, part, nx)  44.9 us
    all_to_all x1, blocking collectives, per_device(): lax.all_to_all(post, 'vel', 0, 0, tiled=True).reshape(rows, part, nx)  27.6 us
    all_to_all x4, starting transfers between devices, per_device(): lax.all_to_all(half.reshape(groups, chunk, part, nx), 'vel', 0, 0, tiled=...  23 us
    pallas_call x4, Pallas kernels, transport(): pl.pallas_call(functools.partial(transport_kernel, ny), out_shape=jax.Sha...  21 us
    ppermute x2, waiting for transfers between devices, per_device(): lo = lax.ppermute(f[rows - ny:], 'space', up)  18.3 us
    dot_general x4, matrix products, per_device(): jnp.einsum('svk,krx->srvx', e3[:, p], delta, preferred_element_type=jnp.f...  15.3 us
    unnamed x23, local copies, waits for them, and re-layouts  14.5 us
  transfers between devices with their start and end apart: 13, of which 13 were waited for; matrix products, arithmetic and copies ran while one was open for 11% of the time, Pallas kernels for 5%

profile of v11, /device:TPU:32, one launch (start us, length us, event | category | flops | bytes accessed | tf_op | source)
XLA Modules:
  0.0 315.5 jit_solution(16248923924607291621)
XLA Ops:
  0.0 2.7 fusion.33
  2.7 0.0 copy-start.2
  2.7 0.5 copy.94
  3.2 2.1 collective-permute-start
  5.2 0.5 copy.93
  5.7 3.6 %collective-permute-start.1 = (bf16[448,16,128]{2,0,1:T(8,128)(2,1)S(1)}, bf16[448,16,128]{2,0,1:T(8,128)(2,1)S(1)}, u32[]{:S(2)}, u32[]{:S(2)}) collective-permute-start(bf16[448,16,128]{2,0,1:T(8,128)(2,1)S(1)} %bitcast.161), channel_id=1, source_target_pairs={{16,0},{32,16},{48,32},{64,48},{80,64},{96,80},{112,96},{17,1},{33... | collective-permute-start | bytes 5505032 | tf_op jit(solution)/shard_map/ppermute | solution.py:101
  9.4 0.0 copy-start.8
  9.4 1.4 copy.46
  10.9 0.1 fusion.38
  11.0 0.6 compare_convert_fusion
  11.6 2.1 fusion.32
  13.7 14.2 %collective-permute-done = bf16[448,16,128]{2,0,1:T(8,128)(2,1)S(1)} collective-permute-done((bf16[448,16,128]{2,0,1:T(8,128)(2,1)S(1)}, bf16[448,16,128]{2,0,1:T(8,128)(2,1)S(1)}, u32[]{:S(2)}, u32[]{:S(2)}) %collective-permute-start) | collective-permute-done | bytes 1835040 | tf_op jit(solution)/shard_map/ppermute | solution.py:100
  27.9 1.4 fusion.37
  29.2 0.9 collective-permute-done.1
  30.1 1.3 fusion.36
  31.4 0.9 broadcast_in_dim.30.coef_ref
  32.3 5.2 %shard_map.65 = bf16[32,224,128]{2,1,0:T(8,128)(2,1)} custom-call(bf16[32,224,128]{2,1,0:T(8,128)(2,1)} %get-tuple-element.13.f_ref, bf16[16,224,128]{2,1,0:T(8,128)(2,1)} %get-tuple-element.23.lo_ref, bf16[16,224,128]{2,1,0:T(8,128)(2,1)} %get-tuple-element.21.hi_ref, f32[3,224,128]{2,1,0:T(8,128)} %broadcast_in_dim.30.coef_ref, f32[32,128]{1,0:T(8,128)} %bitcast.167), custom_call_target="tpu_custom_call" | custom-call | flops 18350080 | bytes 3670016 | tf_op jit(solution)/shard_map/pallas_call | solution.py:61
  37.6 7.0 %all-to-all-start.1 = ((bf16[16,2,224,128]{3,2,1,0:T(8,128)(2,1)}), bf16[16,2,224,128]{3,2,1,0:T(8,128)(2,1)S(1)}, u32[]{:S(2)}, u32[]{:S(2)}) async-start(bf16[16,2,224,128]{3,2,1,0:T(8,128)(2,1)} %bitcast.157), calls=%async_computation.1 | async-start | bytes 3670016 | tf_op jit(solution)/shard_map/all_to_all | solution.py:113
  44.6 0.9 broadcast_in_dim.26.coef_ref
  45.5 5.2 %shard_map.64 = bf16[32,224,128]{2,1,0:T(8,128)(2,1)} custom-call(bf16[32,224,128]{2,1,0:T(8,128)(2,1)} %get-tuple-element.14.f_ref, bf16[16,224,128]{2,1,0:T(8,128)(2,1)} %get-tuple-element.24.lo_ref, bf16[16,224,128]{2,1,0:T(8,128)(2,1)} %get-tuple-element.22.hi_ref, f32[3,224,128]{2,1,0:T(8,128)} %broadcast_in_dim.26.coef_ref, f32[32,128]{1,0:T(8,128)} %bitcast.168), custom_call_target="tpu_custom_call" | custom-call | flops 18350080 | bytes 3670016 | tf_op jit(solution)/shard_map/pallas_call | solution.py:61
  50.8 21.4 %all-to-all-done.1 = bf16[16,2,224,128]{3,2,1,0:T(8,128)(2,1)S(1)} async-done(((bf16[16,2,224,128]{3,2,1,0:T(8,128)(2,1)}), bf16[16,2,224,128]{3,2,1,0:T(8,128)(2,1)S(1)}, u32[]{:S(2)}, u32[]{:S(2)}) %all-to-all-start.1) | async-done | bytes 1835040 | tf_op jit(solution)/shard_map/all_to_all | solution.py:113
  72.2 4.6 %all-to-all-start = ((bf16[16,2,224,128]{3,2,1,0:T(8,128)(2,1)}), bf16[16,2,224,128]{3,2,1,0:T(8,128)(2,1)}, u32[]{:S(2)}, u32[]{:S(2)}) async-start(bf16[16,2,224,128]{3,2,1,0:T(8,128)(2,1)} %bitcast.156), calls=%async_computation | async-start | bytes 3670016 | tf_op jit(solution)/shard_map/all_to_all | solution.py:113
  76.8 10.4 %copy.50 = bf16[512,7168]{0,1:T(8,128)(2,1)} copy(bf16[512,7168]{1,0:T(8,128)(2,1)} %param.9) | data formatting | bytes 14680064 | tf_op args[3]
  87.3 3.2 %fusion.12 = f32[2,128,512]{2,1,0:T(8,128)S(1)} fusion(bf16[16,2,224,128]{3,2,1,0:T(8,128)(2,1)S(1)} %all-to-all-done.1, bf16[512,16,448]{0,2,1:T(8,128)(2,1)} %bitcast.151), kind=kOutput, calls=%fused_computation.23 | convolution fusion | flops 939524096 | bytes 6029312 | tf_op jit(solution)/shard_map/ksv,srvx->krx/dot_general | solution.py:116
  90.4 14.0 %all-to-all-done = bf16[16,2,224,128]{3,2,1,0:T(8,128)(2,1)} async-done(((bf16[16,2,224,128]{3,2,1,0:T(8,128)(2,1)}), bf16[16,2,224,128]{3,2,1,0:T(8,128)(2,1)}, u32[]{:S(2)}, u32[]{:S(2)}) %all-to-all-start) | async-done | bytes 1835040 | tf_op jit(solution)/shard_map/all_to_all | solution.py:113
  104.4 3.7 %fusion.23 = bf16[512,2,128,1]{0,2,3,1:T(8,128)(2,1)S(1)} fusion(f32[2,128,512]{2,1,0:T(8,128)S(1)} %fusion.12, bf16[16,2,224,128]{3,2,1,0:T(8,128)(2,1)} %all-to-all-done, bf16[512,16,448]{0,2,1:T(8,128)(2,1)} %bitcast.152, f32[512]{0:T(512)S(1)} %copy-done.9), kind=kOutput, calls=%fused_computation.34 | convolution fusion | flops 939917312 | bytes 6293504 | tf_op jit(solution)/shard_map/ksv,srvx->krx/dot_general | solution.py:116
  108.1 5.1 %fusion.3 = bf16[16,2,224,128]{3,2,0,1:T(8,128)(2,1)} fusion(bf16[16,2,224,128]{3,2,1,0:T(8,128)(2,1)} %all-to-all-done, f32[2,128]{1,0:T(2,128)S(1)} %constant_dynamic-slice_fusion, bf16[512,2,128,1]{0,2,3,1:T(8,128)(2,1)S(1)} %fusion.23, bf16[16,448,512]{2,1,0:T(8,128)(2,1)} %bitcast.175), kind=kOutput, calls=%fused_computation.12 | convolution fusion | flops 943194112 | bytes 7603200 | tf_op jit(solution)/shard_map/svk,krx->srvx/dot_general | solution.py:126
  113.3 3.2 %fusion.2 = bf16[16,2,224,128]{3,2,0,1:T(8,128)(2,1)S(1)} fusion(bf16[16,2,224,128]{3,2,1,0:T(8,128)(2,1)S(1)} %all-to-all-done.1, f32[2,128]{1,0:T(2,128)S(1)} %constant_dynamic-slice_fusion, bf16[512,2,128,1]{0,2,3,1:T(8,128)(2,1)S(1)} %fusion.23, bf16[16,448,512]{2,1,0:T(8,128)(2,1)} %bitcast.176), kind=kOutput, calls=%fused_computation.10 | convolution fusion | flops 943194112 | bytes 7603200 | tf_op jit(solution)/shard_map/svk,krx->srvx/dot_general | solution.py:126
  116.5 1.4 copy.59
  117.9 5.7 %all-to-all-start.4 = ((bf16[16,2,224,128]{3,2,1,0:T(8,128)(2,1)}), bf16[16,2,224,128]{3,2,1,0:T(8,128)(2,1)S(1)}, u32[]{:S(2)}, u32[]{:S(2)}) async-start(bf16[16,2,224,128]{3,2,1,0:T(8,128)(2,1)} %copy.59), calls=%async_computation.4 | async-start | bytes 3670016 | tf_op jit(solution)/shard_map/all_to_all | solution.py:129
  123.5 2.9 copy.54
  126.5 24.8 %all-to-all-done.4 = bf16[16,2,224,128]{3,2,1,0:T(8,128)(2,1)S(1)} async-done(((bf16[16,2,224,128]{3,2,1,0:T(8,128)(2,1)}), bf16[16,2,224,128]{3,2,1,0:T(8,128)(2,1)S(1)}, u32[]{:S(2)}, u32[]{:S(2)}) %all-to-all-start.4) | async-done | bytes 1835040 | tf_op jit(solution)/shard_map/all_to_all | solution.py:129
  151.2 1.2 copy-done.1
  152.5 3.7 %all-to-all-start.2 = ((bf16[16,2,224,128]{3,2,1,0:T(8,128)(2,1)}), bf16[16,2,224,128]{3,2,1,0:T(8,128)(2,1)S(1)}, u32[]{:S(2)}, u32[]{:S(2)}) async-start(bf16[16,2,224,128]{3,2,1,0:T(8,128)(2,1)} %copy.54), calls=%async_computation.2 | async-start | bytes 3670016 | tf_op jit(solution)/shard_map/all_to_all | solution.py:125
  156.2 1.6 fusion.35
  157.8 1.9 collective-permute-start.4
  159.7 3.6 %collective-permute-start.5 = (bf16[16,224,128]{2,1,0:T(8,128)(2,1)S(1)}, bf16[16,224,128]{2,1,0:T(8,128)(2,1)S(1)}, u32[]{:S(2)}, u32[]{:S(2)}) collective-permute-start(bf16[16,224,128]{2,1,0:T(8,128)(2,1)S(1)} %bitcast.163), channel_id=1, source_target_pairs={{16,0},{32,16},{48,32},{64,48},{80,64},{96,80},{112,96},{17,1},{33... | collective-permute-start | bytes 2752520 | tf_op jit(solution)/shard_map/ppermute | solution.py:111
  163.4 9.1 %collective-permute-done.4.lo_ref = bf16[16,224,128]{2,1,0:T(8,128)(2,1)S(1)} collective-permute-done((bf16[16,224,128]{2,1,0:T(8,128)(2,1)S(1)}, bf16[16,224,128]{2,1,0:T(8,128)(2,1)S(1)}, u32[]{:S(2)}, u32[]{:S(2)}) %collective-permute-start.4) | collective-permute-done | bytes 917536 | tf_op jit(solution)/shard_map/ppermute | solution.py:110
  172.5 1.8 collective-permute-done.5.hi_ref
  174.2 1.0 copy-done.6
  175.2 5.3 %shard_map.67 = bf16[32,224,128]{2,1,0:T(8,128)(2,1)} custom-call(bf16[32,224,128]{2,1,0:T(8,128)(2,1)} %bitcast.146, bf16[16,224,128]{2,1,0:T(8,128)(2,1)} %copy-done.4, bf16[16,224,128]{2,1,0:T(8,128)(2,1)} %copy-done.6, f32[3,224,128]{2,1,0:T(8,128)} %broadcast_in_dim.30.coef_ref, f32[32,128]{1,0:T(8,128)} %bitcast.169), custom_call_target="tpu_custom_call" | custom-call | flops 18350080 | bytes 3670016 | tf_op jit(solution)/shard_map/pallas_call | solution.py:61
  180.5 1.0 all-to-all-done.2
  181.5 6.2 %all-to-all-start.5 = ((bf16[16,2,224,128]{3,2,1,0:T(8,128)(2,1)}), bf16[16,2,224,128]{3,2,1,0:T(8,128)(2,1)}, u32[]{:S(2)}, u32[]{:S(2)}) async-start(bf16[16,2,224,128]{3,2,1,0:T(8,128)(2,1)} %bitcast.155), calls=%async_computation.5 | async-start | bytes 3670016 | tf_op jit(solution)/shard_map/all_to_all | solution.py:113
  187.7 0.1 fusion.34
  187.9 2.3 collective-permute-start.2
  190.2 3.2 %collective-permute-start.3 = (bf16[16,224,128]{2,1,0:T(8,128)(2,1)S(1)}, bf16[16,224,128]{2,1,0:T(8,128)(2,1)S(1)}, u32[]{:S(2)}, u32[]{:S(2)}) collective-permute-start(bf16[16,224,128]{2,1,0:T(8,128)(2,1)S(1)} %bitcast.164), channel_id=1, source_target_pairs={{16,0},{32,16},{48,32},{64,48},{80,64},{96,80},{112,96},{17,1},{33... | collective-permute-start | bytes 2752520 | tf_op jit(solution)/shard_map/ppermute | solution.py:111
  193.5 9.1 %collective-permute-done.2.lo_ref = bf16[16,224,128]{2,1,0:T(8,128)(2,1)S(1)} collective-permute-done((bf16[16,224,128]{2,1,0:T(8,128)(2,1)S(1)}, bf16[16,224,128]{2,1,0:T(8,128)(2,1)S(1)}, u32[]{:S(2)}, u32[]{:S(2)}) %collective-permute-start.2) | collective-permute-done | bytes 917536 | tf_op jit(solution)/shard_map/ppermute | solution.py:110
  202.6 1.8 collective-permute-done.3.hi_ref
  204.4 0.9 copy-done.5
  205.3 5.3 %shard_map.66 = bf16[32,224,128]{2,1,0:T(8,128)(2,1)} custom-call(bf16[32,224,128]{2,1,0:T(8,128)(2,1)} %bitcast.145, bf16[16,224,128]{2,1,0:T(8,128)(2,1)} %copy-done.3, bf16[16,224,128]{2,1,0:T(8,128)(2,1)} %copy-done.5, f32[3,224,128]{2,1,0:T(8,128)} %broadcast_in_dim.26.coef_ref, f32[32,128]{1,0:T(8,128)} %bitcast.170), custom_call_target="tpu_custom_call" | custom-call | flops 18350080 | bytes 3670016 | tf_op jit(solution)/shard_map/pallas_call | solution.py:61
  210.6 5.0 %all-to-all-done.5 = bf16[16,2,224,128]{3,2,1,0:T(8,128)(2,1)} async-done(((bf16[16,2,224,128]{3,2,1,0:T(8,128)(2,1)}), bf16[16,2,224,128]{3,2,1,0:T(8,128)(2,1)}, u32[]{:S(2)}, u32[]{:S(2)}) %all-to-all-start.5) | async-done | bytes 1835040 | tf_op jit(solution)/shard_map/all_to_all | solution.py:113
  215.6 5.1 %all-to-all-start.3 = ((bf16[16,2,224,128]{3,2,1,0:T(8,128)(2,1)}), bf16[16,2,224,128]{3,2,1,0:T(8,128)(2,1)S(1)}, u32[]{:S(2)}, u32[]{:S(2)}) async-start(bf16[16,2,224,128]{3,2,1,0:T(8,128)(2,1)} %bitcast.158), calls=%async_computation.3 | async-start | bytes 3670016 | tf_op jit(solution)/shard_map/all_to_all | solution.py:113
  220.7 3.7 %fusion.13 = f32[2,128,512]{2,1,0:T(8,128)S(1)} fusion(bf16[16,2,224,128]{3,2,1,0:T(8,128)(2,1)} %all-to-all-done.5, bf16[512,16,448]{0,2,1:T(8,128)(2,1)} %bitcast.153), kind=kOutput, calls=%fused_computation.24 | convolution fusion | flops 939524096 | bytes 6029312 | tf_op jit(solution)/shard_map/ksv,srvx->krx/dot_general | solution.py:116
  224.5 22.7 %all-to-all-done.3 = bf16[16,2,224,128]{3,2,1,0:T(8,128)(2,1)S(1)} async-done(((bf16[16,2,224,128]{3,2,1,0:T(8,128)(2,1)}), bf16[16,2,224,128]{3,2,1,0:T(8,128)(2,1)S(1)}, u32[]{:S(2)}, u32[]{:S(2)}) %all-to-all-start.3) | async-done | bytes 1835040 | tf_op jit(solution)/shard_map/all_to_all | solution.py:113
  247.2 3.2 %fusion.22 = bf16[512,2,128,1]{0,2,3,1:T(8,128)(2,1)S(1)} fusion(f32[2,128,512]{2,1,0:T(8,128)S(1)} %fusion.13, bf16[16,2,224,128]{3,2,1,0:T(8,128)(2,1)S(1)} %all-to-all-done.3, bf16[512,16,448]{0,2,1:T(8,128)(2,1)} %bitcast.154, f32[512]{0:T(512)S(1)} %copy-done.9), kind=kOutput, calls=%fused_computation.33 | convolution fusion | flops 939917312 | bytes 6293504 | tf_op jit(solution)/shard_map/ksv,srvx->krx/dot_general | solution.py:116
  250.3 3.2 %fusion.1 = bf16[16,2,224,128]{3,2,0,1:T(8,128)(2,1)S(1)} fusion(bf16[16,2,224,128]{3,2,1,0:T(8,128)(2,1)S(1)} %all-to-all-done.3, f32[2,128]{1,0:T(2,128)S(1)} %constant_dynamic-slice_fusion, bf16[512,2,128,1]{0,2,3,1:T(8,128)(2,1)S(1)} %fusion.22, bf16[16,448,512]{2,1,0:T(8,128)(2,1)} %bitcast.177), kind=kOutput, calls=%fused_computation.8 | convolution fusion | flops 943194112 | bytes 7603200 | tf_op jit(solution)/shard_map/svk,krx->srvx/dot_general | solution.py:126
  253.5 1.4 copy.62
  255.0 3.9 %all-to-all-start.6 = ((bf16[16,2,224,128]{3,2,1,0:T(8,128)(2,1)}), bf16[16,2,224,128]{3,2,1,0:T(8,128)(2,1)S(1)}, u32[]{:S(2)}, u32[]{:S(2)}) async-start(bf16[16,2,224,128]{3,2,1,0:T(8,128)(2,1)} %copy.62), calls=%async_computation.6 | async-start | bytes 3670016 | tf_op jit(solution)/shard_map/all_to_all | solution.py:125
  258.9 3.8 %fusion = bf16[16,2,224,128]{3,2,0,1:T(8,128)(2,1)S(1)} fusion(bf16[16,2,224,128]{3,2,1,0:T(8,128)(2,1)} %all-to-all-done.5, f32[2,128]{1,0:T(2,128)S(1)} %constant_dynamic-slice_fusion, bf16[512,2,128,1]{0,2,3,1:T(8,128)(2,1)S(1)} %fusion.22, bf16[16,448,512]{2,1,0:T(8,128)(2,1)} %bitcast.178), kind=kOutput, calls=%fused_computation.6 | convolution fusion | flops 943194112 | bytes 7603200 | tf_op jit(solution)/shard_map/svk,krx->srvx/dot_general | solution.py:126
  262.7 1.4 copy.65
  264.1 19.2 %all-to-all-done.6 = bf16[16,2,224,128]{3,2,1,0:T(8,128)(2,1)S(1)} async-done(((bf16[16,2,224,128]{3,2,1,0:T(8,128)(2,1)}), bf16[16,2,224,128]{3,2,1,0:T(8,128)(2,1)S(1)}, u32[]{:S(2)}, u32[]{:S(2)}) %all-to-all-start.6) | async-done | bytes 1835040 | tf_op jit(solution)/shard_map/all_to_all | solution.py:125
  283.3 27.6 %all_to_all.40 = bf16[16,2,224,128]{3,2,1,0:T(8,128)(2,1)S(1)} all-to-all(bf16[16,2,224,128]{3,2,1,0:T(8,128)(2,1)} %copy.65), channel_id=1, replica_groups=mesh['space'=8,'vel'=16] {'vel'}, dimensions={0} | all-to-all | bytes 3670016 | tf_op jit(solution)/shard_map/all_to_all | solution.py:129
  310.9 0.4 maximum_bitcast_fusion
  311.3 4.2 %copy.66 = bf16[448,2,16,128]{3,2,1,0:T(8,128)(2,1)} copy(bf16[448,2,16,128]{3,0,2,1:T(8,128)(2,1)S(1)} %maximum_bitcast_fusion) | data formatting | bytes 7340032 | tf_op jit(solution)/shard_map/transpose | solution.py:131
  (19 shorter events, 0.1 us)
Async XLA Ops:
  2.7 6.7 %copy-start.2 = (bf16[448,2,16,128]{3,2,1,0:T(8,128)(2,1)S(1)}, bf16[448,2,16,128]{3,2,1,0:T(8,128)(2,1)}, u32[]{:S(2)}) copy-start(bf16[448,2,16,128]{3,2,1,0:T(8,128)(2,1)} %param.6) | copy-start | bytes 11010052
  3.2 24.7 %collective-permute-start = (bf16[448,16,128]{2,0,1:T(8,128)(2,1)S(1)}, bf16[448,16,128]{2,0,1:T(8,128)(2,1)S(1)}, u32[]{:S(2)}, u32[]{:S(2)}) collective-permute-start(bf16[448,16,128]{2,0,1:T(8,128)(2,1)S(1)} %bitcast.162), channel_id=1, source_target_pairs={{0,16},{16,32},{32,48},{48,64},{64,80},{80,96},{96,112},{1,17},{17... | collective-permute-start | bytes 5505032 | tf_op jit(solution)/shard_map/ppermute | solution.py:100
  5.7 24.4 %collective-permute-start.1 = (bf16[448,16,128]{2,0,1:T(8,128)(2,1)S(1)}, bf16[448,16,128]{2,0,1:T(8,128)(2,1)S(1)}, u32[]{:S(2)}, u32[]{:S(2)}) collective-permute-start(bf16[448,16,128]{2,0,1:T(8,128)(2,1)S(1)} %bitcast.161), channel_id=1, source_target_pairs={{16,0},{32,16},{48,32},{64,48},{80,64},{96,80},{112,96},{17,1},{33... | collective-permute-start | bytes 5505032 | tf_op jit(solution)/shard_map/ppermute | solution.py:101
  9.4 1.5 copy-start.8
  9.4 1.6 copy-start.7
  37.6 34.6 %all-to-all-start.1 = ((bf16[16,2,224,128]{3,2,1,0:T(8,128)(2,1)}), bf16[16,2,224,128]{3,2,1,0:T(8,128)(2,1)S(1)}, u32[]{:S(2)}, u32[]{:S(2)}) async-start(bf16[16,2,224,128]{3,2,1,0:T(8,128)(2,1)} %bitcast.157), calls=%async_computation.1 | async-start | bytes 3670016 | tf_op jit(solution)/shard_map/all_to_all | solution.py:113
  72.2 32.2 %all-to-all-start = ((bf16[16,2,224,128]{3,2,1,0:T(8,128)(2,1)}), bf16[16,2,224,128]{3,2,1,0:T(8,128)(2,1)}, u32[]{:S(2)}, u32[]{:S(2)}) async-start(bf16[16,2,224,128]{3,2,1,0:T(8,128)(2,1)} %bitcast.156), calls=%async_computation | async-start | bytes 3670016 | tf_op jit(solution)/shard_map/all_to_all | solution.py:113
  87.2 17.2 %copy-start.9 = (f32[512]{0:T(512)S(1)}, f32[512]{0:T(512)}, u32[]{:S(2)}) copy-start(f32[512]{0:T(512)} %param.11) | copy-start | bytes 6148
  117.9 33.4 %all-to-all-start.4 = ((bf16[16,2,224,128]{3,2,1,0:T(8,128)(2,1)}), bf16[16,2,224,128]{3,2,1,0:T(8,128)(2,1)S(1)}, u32[]{:S(2)}, u32[]{:S(2)}) async-start(bf16[16,2,224,128]{3,2,1,0:T(8,128)(2,1)} %copy.59), calls=%async_computation.4 | async-start | bytes 3670016 | tf_op jit(solution)/shard_map/all_to_all | solution.py:129
  151.2 1.2 copy-start.1
  152.5 29.0 %all-to-all-start.2 = ((bf16[16,2,224,128]{3,2,1,0:T(8,128)(2,1)}), bf16[16,2,224,128]{3,2,1,0:T(8,128)(2,1)S(1)}, u32[]{:S(2)}, u32[]{:S(2)}) async-start(bf16[16,2,224,128]{3,2,1,0:T(8,128)(2,1)} %copy.54), calls=%async_computation.2 | async-start | bytes 3670016 | tf_op jit(solution)/shard_map/all_to_all | solution.py:125
  157.8 14.7 %collective-permute-start.4 = (bf16[16,224,128]{2,1,0:T(8,128)(2,1)S(1)}, bf16[16,224,128]{2,1,0:T(8,128)(2,1)S(1)}, u32[]{:S(2)}, u32[]{:S(2)}) collective-permute-start(bf16[16,224,128]{2,1,0:T(8,128)(2,1)S(1)} %bitcast.165), channel_id=1, source_target_pairs={{0,16},{16,32},{32,48},{48,64},{64,80},{80,96},{96,112},{1,17},{17... | collective-permute-start | bytes 2752520 | tf_op jit(solution)/shard_map/ppermute | solution.py:110
  159.7 14.5 %collective-permute-start.5 = (bf16[16,224,128]{2,1,0:T(8,128)(2,1)S(1)}, bf16[16,224,128]{2,1,0:T(8,128)(2,1)S(1)}, u32[]{:S(2)}, u32[]{:S(2)}) collective-permute-start(bf16[16,224,128]{2,1,0:T(8,128)(2,1)S(1)} %bitcast.163), channel_id=1, source_target_pairs={{16,0},{32,16},{48,32},{64,48},{80,64},{96,80},{112,96},{17,1},{33... | collective-permute-start | bytes 2752520 | tf_op jit(solution)/shard_map/ppermute | solution.py:111
  172.5 2.7 copy-start.4
  174.2 1.0 copy-start.6
  181.5 6.4 %copy-start = (bf16[16,2,224,128]{3,2,1,0:T(8,128)(2,1)}, bf16[16,2,224,128]{3,2,1,0:T(8,128)(2,1)S(1)}, u32[]{:S(2)}) copy-start(bf16[16,2,224,128]{3,2,1,0:T(8,128)(2,1)S(1)} %all-to-all-done.2) | copy-start | bytes 5505028
  181.5 34.1 %all-to-all-start.5 = ((bf16[16,2,224,128]{3,2,1,0:T(8,128)(2,1)}), bf16[16,2,224,128]{3,2,1,0:T(8,128)(2,1)}, u32[]{:S(2)}, u32[]{:S(2)}) async-start(bf16[16,2,224,128]{3,2,1,0:T(8,128)(2,1)} %bitcast.155), calls=%async_computation.5 | async-start | bytes 3670016 | tf_op jit(solution)/shard_map/all_to_all | solution.py:113
  187.9 14.7 %collective-permute-start.2 = (bf16[16,224,128]{2,1,0:T(8,128)(2,1)S(1)}, bf16[16,224,128]{2,1,0:T(8,128)(2,1)S(1)}, u32[]{:S(2)}, u32[]{:S(2)}) collective-permute-start(bf16[16,224,128]{2,1,0:T(8,128)(2,1)S(1)} %bitcast.166), channel_id=1, source_target_pairs={{0,16},{16,32},{32,48},{48,64},{64,80},{80,96},{96,112},{1,17},{17... | collective-permute-start | bytes 2752520 | tf_op jit(solution)/shard_map/ppermute | solution.py:110
  190.2 14.1 %collective-permute-start.3 = (bf16[16,224,128]{2,1,0:T(8,128)(2,1)S(1)}, bf16[16,224,128]{2,1,0:T(8,128)(2,1)S(1)}, u32[]{:S(2)}, u32[]{:S(2)}) collective-permute-start(bf16[16,224,128]{2,1,0:T(8,128)(2,1)S(1)} %bitcast.164), channel_id=1, source_target_pairs={{16,0},{32,16},{48,32},{64,48},{80,64},{96,80},{112,96},{17,1},{33... | collective-permute-start | bytes 2752520 | tf_op jit(solution)/shard_map/ppermute | solution.py:111
  202.6 1.8 copy-start.3
  204.3 0.9 copy-start.5
  215.6 31.6 %all-to-all-start.3 = ((bf16[16,2,224,128]{3,2,1,0:T(8,128)(2,1)}), bf16[16,2,224,128]{3,2,1,0:T(8,128)(2,1)S(1)}, u32[]{:S(2)}, u32[]{:S(2)}) async-start(bf16[16,2,224,128]{3,2,1,0:T(8,128)(2,1)} %bitcast.158), calls=%async_computation.3 | async-start | bytes 3670016 | tf_op jit(solution)/shard_map/all_to_all | solution.py:113
  255.0 28.3 %all-to-all-start.6 = ((bf16[16,2,224,128]{3,2,1,0:T(8,128)(2,1)}), bf16[16,2,224,128]{3,2,1,0:T(8,128)(2,1)S(1)}, u32[]{:S(2)}, u32[]{:S(2)}) async-start(bf16[16,2,224,128]{3,2,1,0:T(8,128)(2,1)} %copy.62), calls=%async_computation.6 | async-start | bytes 3670016 | tf_op jit(solution)/shard_map/all_to_all | solution.py:125

commit v12 on v5

--- a/solution.py
+++ b/solution.py
@@ -116,17 +116,19 @@
             term = jnp.einsum("ksv,srvx->krx", w3[:, :, p], recvs[h], preferred_element_type=jnp.float32)
             moments = term if moments is None else moments + term
         delta = (rates[:, None, None] * moments).astype(jnp.bfloat16)
-        fs = []
+        fs = [None] * PARTS
         post = None
-        for h, p in enumerate(pieces):
+        last = None
+        for h in (reversed(range(PARTS)) if step == 0 else range(PARTS)):
+            p = pieces[h]
             recv = recvs[h]
             if post is not None:
                 post, recv = lax.optimization_barrier((post, recv))
-                fs[-1] = lax.all_to_all(post, "vel", 0, 0, tiled=True).reshape(rows, part, nx)
+                fs[last] = lax.all_to_all(post, "vel", 0, 0, tiled=True).reshape(rows, part, nx)
             adjustment = jnp.einsum("svk,krx->srvx", e3[:, p], delta, preferred_element_type=jnp.float32)
             post = (recv.astype(jnp.float32) - cm[None, :, None, :] * adjustment).astype(jnp.bfloat16)
-            fs.append(None)
-        fs[-1] = lax.all_to_all(post, "vel", 0, 0, tiled=True).reshape(rows, part, nx)
+            last = h
+        fs[last] = lax.all_to_all(post, "vel", 0, 0, tiled=True).reshape(rows, part, nx)
     whole = jnp.concatenate(fs, axis=1)
     return jnp.transpose(whole.reshape(nzl, ny, vb, nx), (2, 0, 1, 3))
 

time: 306 us -> 307 us (level)
  the two profiles are of different devices: /device:TPU:32 before, /device:TPU:64 now
where the time goes in v12:
time: 307 us; the launch traced here: 306 us
  waiting for transfers between devices  137 us (45%)
  starting transfers between devices  52.3 us (17%)
  local copies, waits for them, and re-layouts  35.5 us (12%)
  blocking collectives  31.5 us (10%)
  matrix products  27.7 us (9%)
  Pallas kernels  21.1 us (7%)
    all_to_all x4, waiting for transfers between devices, per_device(): lax.all_to_all(half.reshape(groups, chunk, part, nx), 'vel', 0, 0, tiled=...  55.7 us
    all_to_all x3, waiting for transfers between devices, per_device(): lax.all_to_all(post, 'vel', 0, 0, tiled=True).reshape(rows, part, nx)  41.3 us
    all_to_all x1, blocking collectives, per_device(): lax.all_to_all(post, 'vel', 0, 0, tiled=True).reshape(rows, part, nx)  31.5 us
    all_to_all x4, starting transfers between devices, per_device(): lax.all_to_all(half.reshape(groups, chunk, part, nx), 'vel', 0, 0, tiled=...  23.4 us
    pallas_call x4, Pallas kernels, transport(): pl.pallas_call(functools.partial(transport_kernel, ny), out_shape=jax.Sha...  21.1 us
    ppermute x2, waiting for transfers between devices, per_device(): lo = lax.ppermute(f[rows - ny:], 'space', up)  17.5 us
    unnamed x20, local copies, waits for them, and re-layouts  17 us
    ppermute x1, waiting for transfers between devices, per_device(): hi_all = lax.ppermute(whole[:ny], 'space', down)  15.5 us
  transfers between devices with their start and end apart: 13, of which 13 were waited for; matrix products, arithmetic and copies ran while one was open for 11% of the time, Pallas kernels for 5%

profile of v12, /device:TPU:64, one launch (start us, length us, event | category | flops | bytes accessed | tf_op | source)
XLA Modules:
  0.0 306.0 jit_solution(17644101527951344626)
XLA Ops:
  0.0 3.5 %copy.85 = bf16[448,2,16,128]{3,0,2,1:T(8,128)(2,1)S(1)} copy(bf16[448,2,16,128]{3,2,1,0:T(8,128)(2,1)} %param.6) | data formatting | bytes 7340032 | tf_op args[0]
  3.5 0.0 copy-start.7
  3.5 0.0 copy-start.6
  3.5 0.2 slice_bitcast_fusion.12
  3.7 1.9 collective-permute-start.1
  5.7 2.4 collective-permute-start
  8.1 0.1 fusion.37
  8.2 0.0 copy-done.6
  8.2 0.6 compare_convert_fusion
  8.8 2.1 fusion.32
  10.9 15.5 %collective-permute-done.1 = bf16[16,448,128]{2,1,0:T(8,128)(2,1)S(1)} collective-permute-done((bf16[16,448,128]{2,1,0:T(8,128)(2,1)S(1)}, bf16[16,448,128]{2,1,0:T(8,128)(2,1)S(1)}, u32[]{:S(2)}, u32[]{:S(2)}) %collective-permute-start.1) | collective-permute-done | bytes 1835040 | tf_op jit(solution)/shard_map/ppermute | solution.py:101
  26.4 1.4 fusion.35
  27.7 2.5 collective-permute-done
  30.2 1.3 fusion.36
  31.6 0.9 broadcast_in_dim.26.coef_ref
  32.5 5.2 %shard_map.64 = bf16[32,224,128]{2,1,0:T(8,128)(2,1)} custom-call(bf16[32,224,128]{2,1,0:T(8,128)(2,1)} %get-tuple-element.14.f_ref, bf16[16,224,128]{2,1,0:T(8,128)(2,1)} %get-tuple-element.26.lo_ref, bf16[16,224,128]{2,1,0:T(8,128)(2,1)} %get-tuple-element.24.hi_ref, f32[3,224,128]{2,1,0:T(8,128)} %broadcast_in_dim.26.coef_ref, f32[32,128]{1,0:T(8,128)} %bitcast.162), custom_call_target="tpu_custom_call" | custom-call | flops 18350080 | bytes 3670016 | tf_op jit(solution)/shard_map/pallas_call | solution.py:61
  37.7 7.0 %all-to-all-start = ((bf16[16,2,224,128]{3,2,1,0:T(8,128)(2,1)}), bf16[16,2,224,128]{3,2,1,0:T(8,128)(2,1)S(1)}, u32[]{:S(2)}, u32[]{:S(2)}) async-start(bf16[16,2,224,128]{3,2,1,0:T(8,128)(2,1)} %bitcast.156), calls=%async_computation | async-start | bytes 3670016 | tf_op jit(solution)/shard_map/all_to_all | solution.py:113
  44.7 0.9 broadcast_in_dim.30.coef_ref
  45.6 5.3 %shard_map.65 = bf16[32,224,128]{2,1,0:T(8,128)(2,1)} custom-call(bf16[32,224,128]{2,1,0:T(8,128)(2,1)} %get-tuple-element.13.f_ref, bf16[16,224,128]{2,1,0:T(8,128)(2,1)} %get-tuple-element.25.lo_ref, bf16[16,224,128]{2,1,0:T(8,128)(2,1)} %get-tuple-element.23.hi_ref, f32[3,224,128]{2,1,0:T(8,128)} %broadcast_in_dim.30.coef_ref, f32[32,128]{1,0:T(8,128)} %bitcast.163), custom_call_target="tpu_custom_call" | custom-call | flops 18350080 | bytes 3670016 | tf_op jit(solution)/shard_map/pallas_call | solution.py:61
  50.9 20.7 %all-to-all-done = bf16[16,2,224,128]{3,2,1,0:T(8,128)(2,1)S(1)} async-done(((bf16[16,2,224,128]{3,2,1,0:T(8,128)(2,1)}), bf16[16,2,224,128]{3,2,1,0:T(8,128)(2,1)S(1)}, u32[]{:S(2)}, u32[]{:S(2)}) %all-to-all-start) | async-done | bytes 1835040 | tf_op jit(solution)/shard_map/all_to_all | solution.py:113
  71.7 4.4 %all-to-all-start.1 = ((bf16[16,2,224,128]{3,2,1,0:T(8,128)(2,1)}), bf16[16,2,224,128]{3,2,1,0:T(8,128)(2,1)}, u32[]{:S(2)}, u32[]{:S(2)}) async-start(bf16[16,2,224,128]{3,2,1,0:T(8,128)(2,1)} %bitcast.155), calls=%async_computation.1 | async-start | bytes 3670016 | tf_op jit(solution)/shard_map/all_to_all | solution.py:113
  76.1 10.4 %copy.44 = bf16[512,7168]{0,1:T(8,128)(2,1)} copy(bf16[512,7168]{1,0:T(8,128)(2,1)} %param.9) | data formatting | bytes 14680064 | tf_op args[3]
  86.5 0.0 copy-start.8
  86.5 3.2 %fusion.12 = f32[2,128,512]{2,1,0:T(8,128)S(1)} fusion(bf16[16,2,224,128]{3,2,1,0:T(8,128)(2,1)S(1)} %all-to-all-done, bf16[512,16,448]{0,2,1:T(8,128)(2,1)} %bitcast.150), kind=kOutput, calls=%fused_computation.23 | convolution fusion | flops 939524096 | bytes 6029312 | tf_op jit(solution)/shard_map/ksv,srvx->krx/dot_general | solution.py:116
  89.7 10.6 %all-to-all-done.1 = bf16[16,2,224,128]{3,2,1,0:T(8,128)(2,1)} async-done(((bf16[16,2,224,128]{3,2,1,0:T(8,128)(2,1)}), bf16[16,2,224,128]{3,2,1,0:T(8,128)(2,1)}, u32[]{:S(2)}, u32[]{:S(2)}) %all-to-all-start.1) | async-done | bytes 1835040 | tf_op jit(solution)/shard_map/all_to_all | solution.py:113
  100.3 3.7 %fusion.23 = bf16[512,2,128,1]{0,2,3,1:T(8,128)(2,1)S(1)} fusion(f32[2,128,512]{2,1,0:T(8,128)S(1)} %fusion.12, bf16[16,2,224,128]{3,2,1,0:T(8,128)(2,1)} %all-to-all-done.1, bf16[512,16,448]{0,2,1:T(8,128)(2,1)} %bitcast.151, f32[512]{0:T(512)S(1)} %copy-done.8), kind=kOutput, calls=%fused_computation.34 | convolution fusion | flops 939917312 | bytes 6293504 | tf_op jit(solution)/shard_map/ksv,srvx->krx/dot_general | solution.py:116
  104.0 3.2 %fusion.3 = bf16[16,2,224,128]{3,2,0,1:T(8,128)(2,1)S(1)} fusion(bf16[16,2,224,128]{3,2,1,0:T(8,128)(2,1)S(1)} %all-to-all-done, f32[2,128]{1,0:T(2,128)S(1)} %constant_dynamic-slice_fusion, bf16[512,2,128,1]{0,2,3,1:T(8,128)(2,1)S(1)} %fusion.23, bf16[16,448,512]{2,1,0:T(8,128)(2,1)} %bitcast.170), kind=kOutput, calls=%fused_computation.12 | convolution fusion | flops 943194112 | bytes 7603200 | tf_op jit(solution)/shard_map/svk,krx->srvx/dot_general | solution.py:128
  107.2 1.4 copy.53
  108.6 4.6 %all-to-all-start.4 = ((bf16[16,2,224,128]{3,2,1,0:T(8,128)(2,1)}), bf16[16,2,224,128]{3,2,1,0:T(8,128)(2,1)S(1)}, u32[]{:S(2)}, u32[]{:S(2)}) async-start(bf16[16,2,224,128]{3,2,1,0:T(8,128)(2,1)} %copy.53), calls=%async_computation.4 | async-start | bytes 3670016 | tf_op jit(solution)/shard_map/all_to_all | solution.py:127
  113.2 3.8 %fusion.2 = bf16[16,2,224,128]{3,2,0,1:T(8,128)(2,1)S(1)} fusion(bf16[16,2,224,128]{3,2,1,0:T(8,128)(2,1)} %all-to-all-done.1, f32[2,128]{1,0:T(2,128)S(1)} %constant_dynamic-slice_fusion, bf16[512,2,128,1]{0,2,3,1:T(8,128)(2,1)S(1)} %fusion.23, bf16[16,448,512]{2,1,0:T(8,128)(2,1)} %bitcast.171), kind=kOutput, calls=%fused_computation.10 | convolution fusion | flops 943194112 | bytes 7603200 | tf_op jit(solution)/shard_map/svk,krx->srvx/dot_general | solution.py:128
  117.0 1.4 copy.50
  118.4 17.7 %all-to-all-done.4 = bf16[16,2,224,128]{3,2,1,0:T(8,128)(2,1)S(1)} async-done(((bf16[16,2,224,128]{3,2,1,0:T(8,128)(2,1)}), bf16[16,2,224,128]{3,2,1,0:T(8,128)(2,1)S(1)}, u32[]{:S(2)}, u32[]{:S(2)}) %all-to-all-start.4) | async-done | bytes 1835040 | tf_op jit(solution)/shard_map/all_to_all | solution.py:127
  136.1 1.2 copy-done.1
  137.4 3.7 %all-to-all-start.2 = ((bf16[16,2,224,128]{3,2,1,0:T(8,128)(2,1)}), bf16[16,2,224,128]{3,2,1,0:T(8,128)(2,1)S(1)}, u32[]{:S(2)}, u32[]{:S(2)}) async-start(bf16[16,2,224,128]{3,2,1,0:T(8,128)(2,1)} %copy.50), calls=%async_computation.2 | async-start | bytes 3670016 | tf_op jit(solution)/shard_map/all_to_all | solution.py:131
  141.1 1.6 fusion.34
  142.7 1.9 collective-permute-start.4
  144.6 3.8 %collective-permute-start.5 = (bf16[16,224,128]{2,1,0:T(8,128)(2,1)S(1)}, bf16[16,224,128]{2,1,0:T(8,128)(2,1)S(1)}, u32[]{:S(2)}, u32[]{:S(2)}) collective-permute-start(bf16[16,224,128]{2,1,0:T(8,128)(2,1)S(1)} %bitcast.158), channel_id=1, source_target_pairs={{16,0},{32,16},{48,32},{64,48},{80,64},{96,80},{112,96},{17,1},{33... | collective-permute-start | bytes 2752520 | tf_op jit(solution)/shard_map/ppermute | solution.py:111
  148.5 9.0 %collective-permute-done.4.lo_ref = bf16[16,224,128]{2,1,0:T(8,128)(2,1)S(1)} collective-permute-done((bf16[16,224,128]{2,1,0:T(8,128)(2,1)S(1)}, bf16[16,224,128]{2,1,0:T(8,128)(2,1)S(1)}, u32[]{:S(2)}, u32[]{:S(2)}) %collective-permute-start.4) | collective-permute-done | bytes 917536 | tf_op jit(solution)/shard_map/ppermute | solution.py:110
  157.4 1.8 collective-permute-done.5.hi_ref
  159.2 1.0 copy-done.5
  160.1 5.3 %shard_map.67 = bf16[32,224,128]{2,1,0:T(8,128)(2,1)} custom-call(bf16[32,224,128]{2,1,0:T(8,128)(2,1)} %bitcast.147, bf16[16,224,128]{2,1,0:T(8,128)(2,1)} %copy-done.3, bf16[16,224,128]{2,1,0:T(8,128)(2,1)} %copy-done.5, f32[3,224,128]{2,1,0:T(8,128)} %broadcast_in_dim.26.coef_ref, f32[32,128]{1,0:T(8,128)} %bitcast.164), custom_call_target="tpu_custom_call" | custom-call | flops 18350080 | bytes 3670016 | tf_op jit(solution)/shard_map/pallas_call | solution.py:61
  165.4 0.9 all-to-all-done.2
  166.3 6.4 %all-to-all-start.5 = ((bf16[16,2,224,128]{3,2,1,0:T(8,128)(2,1)}), bf16[16,2,224,128]{3,2,1,0:T(8,128)(2,1)}, u32[]{:S(2)}, u32[]{:S(2)}) async-start(bf16[16,2,224,128]{3,2,1,0:T(8,128)(2,1)} %bitcast.154), calls=%async_computation.5 | async-start | bytes 3670016 | tf_op jit(solution)/shard_map/all_to_all | solution.py:113
  172.7 0.1 fusion.33
  172.9 4.4 %collective-permute-start.2 = (bf16[16,224,128]{2,1,0:T(8,128)(2,1)S(1)}, bf16[16,224,128]{2,1,0:T(8,128)(2,1)S(1)}, u32[]{:S(2)}, u32[]{:S(2)}) collective-permute-start(bf16[16,224,128]{2,1,0:T(8,128)(2,1)S(1)} %bitcast.161), channel_id=1, source_target_pairs={{0,16},{16,32},{32,48},{48,64},{64,80},{80,96},{96,112},{1,17},{17... | collective-permute-start | bytes 2752520 | tf_op jit(solution)/shard_map/ppermute | solution.py:110
  177.3 1.9 collective-permute-start.3
  179.2 8.6 %collective-permute-done.2.lo_ref = bf16[16,224,128]{2,1,0:T(8,128)(2,1)S(1)} collective-permute-done((bf16[16,224,128]{2,1,0:T(8,128)(2,1)S(1)}, bf16[16,224,128]{2,1,0:T(8,128)(2,1)S(1)}, u32[]{:S(2)}, u32[]{:S(2)}) %collective-permute-start.2) | collective-permute-done | bytes 917536 | tf_op jit(solution)/shard_map/ppermute | solution.py:110
  187.8 2.3 collective-permute-done.3.hi_ref
  190.1 0.9 copy-done.4
  191.0 5.3 %shard_map.66 = bf16[32,224,128]{2,1,0:T(8,128)(2,1)} custom-call(bf16[32,224,128]{2,1,0:T(8,128)(2,1)} %bitcast.146, bf16[16,224,128]{2,1,0:T(8,128)(2,1)} %copy-done.2, bf16[16,224,128]{2,1,0:T(8,128)(2,1)} %copy-done.4, f32[3,224,128]{2,1,0:T(8,128)} %broadcast_in_dim.30.coef_ref, f32[32,128]{1,0:T(8,128)} %bitcast.165), custom_call_target="tpu_custom_call" | custom-call | flops 18350080 | bytes 3670016 | tf_op jit(solution)/shard_map/pallas_call | solution.py:61
  196.3 1.3 all-to-all-done.5
  197.6 5.6 %all-to-all-start.3 = ((bf16[16,2,224,128]{3,2,1,0:T(8,128)(2,1)}), bf16[16,2,224,128]{3,2,1,0:T(8,128)(2,1)S(1)}, u32[]{:S(2)}, u32[]{:S(2)}) async-start(bf16[16,2,224,128]{3,2,1,0:T(8,128)(2,1)} %bitcast.157), calls=%async_computation.3 | async-start | bytes 3670016 | tf_op jit(solution)/shard_map/all_to_all | solution.py:113
  203.2 3.7 %fusion.13 = f32[2,128,512]{2,1,0:T(8,128)S(1)} fusion(bf16[16,2,224,128]{3,2,1,0:T(8,128)(2,1)} %all-to-all-done.5, bf16[512,16,448]{0,2,1:T(8,128)(2,1)} %bitcast.152), kind=kOutput, calls=%fused_computation.24 | convolution fusion | flops 939524096 | bytes 6029312 | tf_op jit(solution)/shard_map/ksv,srvx->krx/dot_general | solution.py:116
  206.9 23.1 %all-to-all-done.3 = bf16[16,2,224,128]{3,2,1,0:T(8,128)(2,1)S(1)} async-done(((bf16[16,2,224,128]{3,2,1,0:T(8,128)(2,1)}), bf16[16,2,224,128]{3,2,1,0:T(8,128)(2,1)S(1)}, u32[]{:S(2)}, u32[]{:S(2)}) %all-to-all-start.3) | async-done | bytes 1835040 | tf_op jit(solution)/shard_map/all_to_all | solution.py:113
  230.1 3.2 %fusion.22 = bf16[512,2,128,1]{0,2,3,1:T(8,128)(2,1)S(1)} fusion(f32[2,128,512]{2,1,0:T(8,128)S(1)} %fusion.13, bf16[16,2,224,128]{3,2,1,0:T(8,128)(2,1)S(1)} %all-to-all-done.3, bf16[512,16,448]{0,2,1:T(8,128)(2,1)} %bitcast.153, f32[512]{0:T(512)S(1)} %copy-done.8), kind=kOutput, calls=%fused_computation.33 | convolution fusion | flops 939917312 | bytes 6293504 | tf_op jit(solution)/shard_map/ksv,srvx->krx/dot_general | solution.py:116
  233.2 3.2 %fusion.1 = bf16[16,2,224,128]{3,2,0,1:T(8,128)(2,1)S(1)} fusion(bf16[16,2,224,128]{3,2,1,0:T(8,128)(2,1)S(1)} %all-to-all-done.3, f32[2,128]{1,0:T(2,128)S(1)} %constant_dynamic-slice_fusion, bf16[512,2,128,1]{0,2,3,1:T(8,128)(2,1)S(1)} %fusion.22, bf16[16,448,512]{2,1,0:T(8,128)(2,1)} %bitcast.172), kind=kOutput, calls=%fused_computation.8 | convolution fusion | flops 943194112 | bytes 7603200 | tf_op jit(solution)/shard_map/svk,krx->srvx/dot_general | solution.py:128
  236.4 1.4 copy.56
  237.9 4.1 %all-to-all-start.6 = ((bf16[16,2,224,128]{3,2,1,0:T(8,128)(2,1)}), bf16[16,2,224,128]{3,2,1,0:T(8,128)(2,1)S(1)}, u32[]{:S(2)}, u32[]{:S(2)}) async-start(bf16[16,2,224,128]{3,2,1,0:T(8,128)(2,1)} %copy.56), calls=%async_computation.6 | async-start | bytes 3670016 | tf_op jit(solution)/shard_map/all_to_all | solution.py:127
  242.0 3.8 %fusion = bf16[16,2,224,128]{3,2,0,1:T(8,128)(2,1)S(1)} fusion(bf16[16,2,224,128]{3,2,1,0:T(8,128)(2,1)} %all-to-all-done.5, f32[2,128]{1,0:T(2,128)S(1)} %constant_dynamic-slice_fusion, bf16[512,2,128,1]{0,2,3,1:T(8,128)(2,1)S(1)} %fusion.22, bf16[16,448,512]{2,1,0:T(8,128)(2,1)} %bitcast.173), kind=kOutput, calls=%fused_computation.6 | convolution fusion | flops 943194112 | bytes 7603200 | tf_op jit(solution)/shard_map/svk,krx->srvx/dot_general | solution.py:128
  245.8 1.4 copy.59
  247.2 22.6 %all-to-all-done.6 = bf16[16,2,224,128]{3,2,1,0:T(8,128)(2,1)S(1)} async-done(((bf16[16,2,224,128]{3,2,1,0:T(8,128)(2,1)}), bf16[16,2,224,128]{3,2,1,0:T(8,128)(2,1)S(1)}, u32[]{:S(2)}, u32[]{:S(2)}) %all-to-all-start.6) | async-done | bytes 1835040 | tf_op jit(solution)/shard_map/all_to_all | solution.py:127
  269.9 31.5 %all_to_all.40 = bf16[16,2,224,128]{3,2,1,0:T(8,128)(2,1)S(1)} all-to-all(bf16[16,2,224,128]{3,2,1,0:T(8,128)(2,1)} %copy.59), channel_id=1, replica_groups=mesh['space'=8,'vel'=16] {'vel'}, dimensions={0} | all-to-all | bytes 3670016 | tf_op jit(solution)/shard_map/all_to_all | solution.py:131
  301.4 0.4 maximum_bitcast_fusion
  301.8 4.2 %copy.60 = bf16[448,2,16,128]{3,2,1,0:T(8,128)(2,1)} copy(bf16[448,2,16,128]{3,0,2,1:T(8,128)(2,1)S(1)} %maximum_bitcast_fusion) | data formatting | bytes 7340032 | tf_op jit(solution)/shard_map/transpose | solution.py:133
  (15 shorter events, 0.1 us)
Async XLA Ops:
  3.5 4.6 %copy-start.7 = (s32[448]{0:T(512)S(1)}, s32[448]{0:T(512)}, u32[]{:S(2)}) copy-start(s32[448]{0:T(512)} %param.7) | copy-start | bytes 5380
  3.5 4.7 %copy-start.6 = (s32[2,16,128]{2,1,0:T(8,128)S(1)}, s32[2,16,128]{2,1,0:T(8,128)}, u32[]{:S(2)}) copy-start(s32[2,16,128]{2,1,0:T(8,128)} %param.8) | copy-start | bytes 49156
  3.7 22.6 %collective-permute-start.1 = (bf16[16,448,128]{2,1,0:T(8,128)(2,1)S(1)}, bf16[16,448,128]{2,1,0:T(8,128)(2,1)S(1)}, u32[]{:S(2)}, u32[]{:S(2)}) collective-permute-start(bf16[16,448,128]{2,1,0:T(8,128)(2,1)S(1)} %get-tuple-element.15), channel_id=1, source_target_pairs={{16,0},{32,16},{48,32},{64,48},{80,64},{96,80},{112,96},{17,1},{33... | collective-permute-start | bytes 5505032 | tf_op jit(solution)/shard_map/ppermute | solution.py:101
  5.7 24.5 %collective-permute-start = (bf16[16,448,128]{2,1,0:T(8,128)(2,1)S(1)}, bf16[16,448,128]{2,1,0:T(8,128)(2,1)S(1)}, u32[]{:S(2)}, u32[]{:S(2)}) collective-permute-start(bf16[16,448,128]{2,1,0:T(8,128)(2,1)S(1)} %get-tuple-element.16), channel_id=1, source_target_pairs={{0,16},{16,32},{32,48},{48,64},{64,80},{80,96},{96,112},{1,17},{17... | collective-permute-start | bytes 5505032 | tf_op jit(solution)/shard_map/ppermute | solution.py:100
  37.7 34.0 %all-to-all-start = ((bf16[16,2,224,128]{3,2,1,0:T(8,128)(2,1)}), bf16[16,2,224,128]{3,2,1,0:T(8,128)(2,1)S(1)}, u32[]{:S(2)}, u32[]{:S(2)}) async-start(bf16[16,2,224,128]{3,2,1,0:T(8,128)(2,1)} %bitcast.156), calls=%async_computation | async-start | bytes 3670016 | tf_op jit(solution)/shard_map/all_to_all | solution.py:113
  71.7 28.6 %all-to-all-start.1 = ((bf16[16,2,224,128]{3,2,1,0:T(8,128)(2,1)}), bf16[16,2,224,128]{3,2,1,0:T(8,128)(2,1)}, u32[]{:S(2)}, u32[]{:S(2)}) async-start(bf16[16,2,224,128]{3,2,1,0:T(8,128)(2,1)} %bitcast.155), calls=%async_computation.1 | async-start | bytes 3670016 | tf_op jit(solution)/shard_map/all_to_all | solution.py:113
  86.5 13.8 %copy-start.8 = (f32[512]{0:T(512)S(1)}, f32[512]{0:T(512)}, u32[]{:S(2)}) copy-start(f32[512]{0:T(512)} %param.11) | copy-start | bytes 6148
  108.6 27.5 %all-to-all-start.4 = ((bf16[16,2,224,128]{3,2,1,0:T(8,128)(2,1)}), bf16[16,2,224,128]{3,2,1,0:T(8,128)(2,1)S(1)}, u32[]{:S(2)}, u32[]{:S(2)}) async-start(bf16[16,2,224,128]{3,2,1,0:T(8,128)(2,1)} %copy.53), calls=%async_computation.4 | async-start | bytes 3670016 | tf_op jit(solution)/shard_map/all_to_all | solution.py:127
  136.1 1.2 copy-start.1
  137.4 29.0 %all-to-all-start.2 = ((bf16[16,2,224,128]{3,2,1,0:T(8,128)(2,1)}), bf16[16,2,224,128]{3,2,1,0:T(8,128)(2,1)S(1)}, u32[]{:S(2)}, u32[]{:S(2)}) async-start(bf16[16,2,224,128]{3,2,1,0:T(8,128)(2,1)} %copy.50), calls=%async_computation.2 | async-start | bytes 3670016 | tf_op jit(solution)/shard_map/all_to_all | solution.py:131
  142.7 14.7 %collective-permute-start.4 = (bf16[16,224,128]{2,1,0:T(8,128)(2,1)S(1)}, bf16[16,224,128]{2,1,0:T(8,128)(2,1)S(1)}, u32[]{:S(2)}, u32[]{:S(2)}) collective-permute-start(bf16[16,224,128]{2,1,0:T(8,128)(2,1)S(1)} %bitcast.160), channel_id=1, source_target_pairs={{0,16},{16,32},{32,48},{48,64},{64,80},{80,96},{96,112},{1,17},{17... | collective-permute-start | bytes 2752520 | tf_op jit(solution)/shard_map/ppermute | solution.py:110
  144.6 14.5 %collective-permute-start.5 = (bf16[16,224,128]{2,1,0:T(8,128)(2,1)S(1)}, bf16[16,224,128]{2,1,0:T(8,128)(2,1)S(1)}, u32[]{:S(2)}, u32[]{:S(2)}) collective-permute-start(bf16[16,224,128]{2,1,0:T(8,128)(2,1)S(1)} %bitcast.158), channel_id=1, source_target_pairs={{16,0},{32,16},{48,32},{64,48},{80,64},{96,80},{112,96},{17,1},{33... | collective-permute-start | bytes 2752520 | tf_op jit(solution)/shard_map/ppermute | solution.py:111
  157.4 2.7 copy-start.3
  159.2 1.0 copy-start.5
  166.3 6.5 %copy-start = (bf16[16,2,224,128]{3,2,1,0:T(8,128)(2,1)}, bf16[16,2,224,128]{3,2,1,0:T(8,128)(2,1)S(1)}, u32[]{:S(2)}) copy-start(bf16[16,2,224,128]{3,2,1,0:T(8,128)(2,1)S(1)} %all-to-all-done.2) | copy-start | bytes 5505028
  166.3 31.3 %all-to-all-start.5 = ((bf16[16,2,224,128]{3,2,1,0:T(8,128)(2,1)}), bf16[16,2,224,128]{3,2,1,0:T(8,128)(2,1)}, u32[]{:S(2)}, u32[]{:S(2)}) async-start(bf16[16,2,224,128]{3,2,1,0:T(8,128)(2,1)} %bitcast.154), calls=%async_computation.5 | async-start | bytes 3670016 | tf_op jit(solution)/shard_map/all_to_all | solution.py:113
  172.9 14.9 %collective-permute-start.2 = (bf16[16,224,128]{2,1,0:T(8,128)(2,1)S(1)}, bf16[16,224,128]{2,1,0:T(8,128)(2,1)S(1)}, u32[]{:S(2)}, u32[]{:S(2)}) collective-permute-start(bf16[16,224,128]{2,1,0:T(8,128)(2,1)S(1)} %bitcast.161), channel_id=1, source_target_pairs={{0,16},{16,32},{32,48},{48,64},{64,80},{80,96},{96,112},{1,17},{17... | collective-permute-start | bytes 2752520 | tf_op jit(solution)/shard_map/ppermute | solution.py:110
  177.3 12.8 %collective-permute-start.3 = (bf16[16,224,128]{2,1,0:T(8,128)(2,1)S(1)}, bf16[16,224,128]{2,1,0:T(8,128)(2,1)S(1)}, u32[]{:S(2)}, u32[]{:S(2)}) collective-permute-start(bf16[16,224,128]{2,1,0:T(8,128)(2,1)S(1)} %bitcast.159), channel_id=1, source_target_pairs={{16,0},{32,16},{48,32},{64,48},{80,64},{96,80},{112,96},{17,1},{33... | collective-permute-start | bytes 2752520 | tf_op jit(solution)/shard_map/ppermute | solution.py:111
  187.8 2.3 copy-start.2
  190.1 0.9 copy-start.4
  197.6 32.5 %all-to-all-start.3 = ((bf16[16,2,224,128]{3,2,1,0:T(8,128)(2,1)}), bf16[16,2,224,128]{3,2,1,0:T(8,128)(2,1)S(1)}, u32[]{:S(2)}, u32[]{:S(2)}) async-start(bf16[16,2,224,128]{3,2,1,0:T(8,128)(2,1)} %bitcast.157), calls=%async_computation.3 | async-start | bytes 3670016 | tf_op jit(solution)/shard_map/all_to_all | solution.py:113
  237.9 32.0 %all-to-all-start.6 = ((bf16[16,2,224,128]{3,2,1,0:T(8,128)(2,1)}), bf16[16,2,224,128]{3,2,1,0:T(8,128)(2,1)S(1)}, u32[]{:S(2)}, u32[]{:S(2)}) async-start(bf16[16,2,224,128]{3,2,1,0:T(8,128)(2,1)} %copy.56), calls=%async_computation.6 | async-start | bytes 3670016 | tf_op jit(solution)/shard_map/all_to_all | solution.py:127

commit v13 on v5

--- a/solution.py
+++ b/solution.py
@@ -55,17 +55,18 @@
         out_ref[w] = (c - tm_ref[w : w + 1, :] * flux).astype(out_ref.dtype)
 
 
-def transport(f, lo, hi, coef, tm, ny):
+def transport(f, lo, hi, coef, tm, ny, halo_part=0):
     rows, vb, nx = f.shape
     tv = min(VBLOCK, vb)
+    hb = halo_part * (vb // tv)
     return pl.pallas_call(
         functools.partial(transport_kernel, ny),
         out_shape=jax.ShapeDtypeStruct(f.shape, f.dtype),
         grid=(vb // tv,),
         in_specs=[
             pl.BlockSpec((rows, tv, nx), lambda i: (0, i, 0)),
-            pl.BlockSpec((ny, tv, nx), lambda i: (0, i, 0)),
-            pl.BlockSpec((ny, tv, nx), lambda i: (0, i, 0)),
+            pl.BlockSpec((ny, tv, nx), lambda i: (0, i + hb, 0)),
+            pl.BlockSpec((ny, tv, nx), lambda i: (0, i + hb, 0)),
             pl.BlockSpec((3, tv, nx), lambda i: (0, i, 0)),
             pl.BlockSpec((rows, nx), lambda i: (0, 0)),
         ],
@@ -105,11 +106,12 @@
         for h, p in enumerate(pieces):
             f = fs[h]
             if step == 0:
-                lo, hi = lo_all[:, p], hi_all[:, p]
+                lo, hi, hp = lo_all, hi_all, h
             else:
                 lo = lax.ppermute(f[rows - ny :], "space", up)
                 hi = lax.ppermute(f[:ny], "space", down)
-            half = transport(f, lo, hi, coef[:, p], tm, ny)
+                hp = 0
+            half = transport(f, lo, hi, coef[:, p], tm, ny, hp)
             recvs.append(lax.all_to_all(half.reshape(groups, chunk, part, nx), "vel", 0, 0, tiled=True))
         moments = None
         for h, p in enumerate(pieces):

time: 306 us -> 310 us (1.013)
  blocking collectives: 26.5 us -> 31.5 us
  starting transfers between devices: 48.5 us -> 52.9 us
    all_to_all x4, waiting for transfers between devices: 59.5 us -> 54.3 us  [per_device(): lax.all_to_all(half.reshape(groups, chunk, part, nx), 'vel', 0, 0, tiled=...]
    all_to_all x1, blocking collectives: 26.5 us -> 31.5 us  [per_device(): lax.all_to_all(post, 'vel', 0, 0, tiled=True).reshape(rows, part, nx)]
    unnamed x20 -> x22, local copies, waits for them, and re-layouts: 17 us -> 17 us
  transfers between devices with their start and end apart: 13 -> 13, of which waited for: 13 -> 13; matrix products, arithmetic and copies ran while one was open for 11% -> 10% of each run, Pallas kernels for 5% -> 5%
where the time goes in v13:
time: 310 us; the launch traced here: 309 us
  waiting for transfers between devices  139 us (45%)
  starting transfers between devices  52.9 us (17%)
  local copies, waits for them, and re-layouts  34.4 us (11%)
  blocking collectives  31.5 us (10%)
  matrix products  29 us (9%)
  Pallas kernels  21.1 us (7%)
    all_to_all x4, waiting for transfers between devices, per_device(): lax.all_to_all(half.reshape(groups, chunk, part, nx), 'vel', 0, 0, tiled=...  54.3 us
    all_to_all x3, waiting for transfers between devices, per_device(): lax.all_to_all(post, 'vel', 0, 0, tiled=True).reshape(rows, part, nx)  43.5 us
    all_to_all x1, blocking collectives, per_device(): lax.all_to_all(post, 'vel', 0, 0, tiled=True).reshape(rows, part, nx)  31.5 us
    all_to_all x4, starting transfers between devices, per_device(): lax.all_to_all(half.reshape(groups, chunk, part, nx), 'vel', 0, 0, tiled=...  24.4 us
    pallas_call x4, Pallas kernels, transport(): pl.pallas_call(functools.partial(transport_kernel, ny), out_shape=jax.Sha...  21.1 us
    ppermute x2, waiting for transfers between devices, per_device(): lo = lax.ppermute(f[rows - ny:], 'space', up)  17.1 us
    unnamed x22, local copies, waits for them, and re-layouts  17 us
    ppermute x1, waiting for transfers between devices, per_device(): hi_all = lax.ppermute(whole[:ny], 'space', down)  15.5 us
  transfers between devices with their start and end apart: 13, of which 13 were waited for; matrix products, arithmetic and copies ran while one was open for 10% of the time, Pallas kernels for 5%

profile of v13, /device:TPU:32, one launch (start us, length us, event | category | flops | bytes accessed | tf_op | source)
XLA Modules:
  0.0 309.0 jit_solution(15549453498954326186)
XLA Ops:
  0.0 3.5 %copy.85 = bf16[448,2,16,128]{3,0,2,1:T(8,128)(2,1)S(1)} copy(bf16[448,2,16,128]{3,2,1,0:T(8,128)(2,1)} %param.6) | data formatting | bytes 7340032 | tf_op args[0]
  3.5 0.0 copy-start.8
  3.5 0.0 copy-start.7
  3.5 0.2 slice_bitcast_fusion.12
  3.7 1.9 collective-permute-start.1
  5.7 2.4 collective-permute-start
  8.1 0.0 copy-done.8
  8.1 0.1 fusion.35
  8.2 0.0 copy-done.7
  8.2 0.6 compare_convert_fusion
  8.8 2.1 fusion.32
  10.9 15.5 %collective-permute-done.1.hi_ref = bf16[16,448,128]{2,1,0:T(8,128)(2,1)S(1)} collective-permute-done((bf16[16,448,128]{2,1,0:T(8,128)(2,1)S(1)}, bf16[16,448,128]{2,1,0:T(8,128)(2,1)S(1)}, u32[]{:S(2)}, u32[]{:S(2)}) %collective-permute-start.1) | collective-permute-done | bytes 1835040 | tf_op jit(solution)/shard_map/ppermute | solution.py:102
  26.4 3.9 %collective-permute-done.lo_ref = bf16[16,448,128]{2,1,0:T(8,128)(2,1)} collective-permute-done((bf16[16,448,128]{2,1,0:T(8,128)(2,1)S(1)}, bf16[16,448,128]{2,1,0:T(8,128)(2,1)}, u32[]{:S(2)}, u32[]{:S(2)}) %collective-permute-start) | collective-permute-done | bytes 1835040 | tf_op jit(solution)/shard_map/ppermute | solution.py:101
  30.3 0.9 broadcast_in_dim.30.coef_ref
  31.2 5.3 %shard_map.65 = bf16[32,224,128]{2,1,0:T(8,128)(2,1)} custom-call(bf16[32,224,128]{2,1,0:T(8,128)(2,1)} %get-tuple-element.14.f_ref, bf16[16,448,128]{2,1,0:T(8,128)(2,1)} %collective-permute-done.lo_ref, bf16[16,448,128]{2,1,0:T(8,128)(2,1)} %copy-done.2, f32[3,224,128]{2,1,0:T(8,128)} %broadcast_in_dim.30.coef_ref, f32[32,128]{1,0:T(8,128)} %bitcast.162), custom_call_target="tpu_custom_call" | custom-call | flops 18350080 | bytes 3670016 | tf_op jit(solution)/shard_map/pallas_call | solution.py:62
  36.5 7.0 %all-to-all-start.1 = ((bf16[16,2,224,128]{3,2,1,0:T(8,128)(2,1)}), bf16[16,2,224,128]{3,2,1,0:T(8,128)(2,1)S(1)}, u32[]{:S(2)}, u32[]{:S(2)}) async-start(bf16[16,2,224,128]{3,2,1,0:T(8,128)(2,1)} %bitcast.157), calls=%async_computation.1 | async-start | bytes 3670016 | tf_op jit(solution)/shard_map/all_to_all | solution.py:115
  43.5 0.9 broadcast_in_dim.26.coef_ref
  44.4 5.3 %shard_map.64 = bf16[32,224,128]{2,1,0:T(8,128)(2,1)} custom-call(bf16[32,224,128]{2,1,0:T(8,128)(2,1)} %get-tuple-element.13.f_ref, bf16[16,448,128]{2,1,0:T(8,128)(2,1)} %collective-permute-done.lo_ref, bf16[16,448,128]{2,1,0:T(8,128)(2,1)} %copy-done.2, f32[3,224,128]{2,1,0:T(8,128)} %broadcast_in_dim.26.coef_ref, f32[32,128]{1,0:T(8,128)} %bitcast.163), custom_call_target="tpu_custom_call" | custom-call | flops 18350080 | bytes 3670016 | tf_op jit(solution)/shard_map/pallas_call | solution.py:62
  49.7 20.2 %all-to-all-done.1 = bf16[16,2,224,128]{3,2,1,0:T(8,128)(2,1)S(1)} async-done(((bf16[16,2,224,128]{3,2,1,0:T(8,128)(2,1)}), bf16[16,2,224,128]{3,2,1,0:T(8,128)(2,1)S(1)}, u32[]{:S(2)}, u32[]{:S(2)}) %all-to-all-start.1) | async-done | bytes 1835040 | tf_op jit(solution)/shard_map/all_to_all | solution.py:115
  69.9 4.4 %all-to-all-start = ((bf16[16,2,224,128]{3,2,1,0:T(8,128)(2,1)}), bf16[16,2,224,128]{3,2,1,0:T(8,128)(2,1)}, u32[]{:S(2)}, u32[]{:S(2)}) async-start(bf16[16,2,224,128]{3,2,1,0:T(8,128)(2,1)} %bitcast.156), calls=%async_computation | async-start | bytes 3670016 | tf_op jit(solution)/shard_map/all_to_all | solution.py:115
  74.3 10.4 %copy.44 = bf16[512,7168]{0,1:T(8,128)(2,1)} copy(bf16[512,7168]{1,0:T(8,128)(2,1)} %param.9) | data formatting | bytes 14680064 | tf_op args[3]
  84.8 0.0 copy-start.9
  84.8 3.2 %fusion.12 = f32[2,128,512]{2,1,0:T(8,128)S(1)} fusion(bf16[16,2,224,128]{3,2,1,0:T(8,128)(2,1)S(1)} %all-to-all-done.1, bf16[512,16,448]{0,2,1:T(8,128)(2,1)} %bitcast.150), kind=kOutput, calls=%fused_computation.23 | convolution fusion | flops 939524096 | bytes 6029312 | tf_op jit(solution)/shard_map/ksv,srvx->krx/dot_general | solution.py:118
  87.9 10.4 %all-to-all-done = bf16[16,2,224,128]{3,2,1,0:T(8,128)(2,1)} async-done(((bf16[16,2,224,128]{3,2,1,0:T(8,128)(2,1)}), bf16[16,2,224,128]{3,2,1,0:T(8,128)(2,1)}, u32[]{:S(2)}, u32[]{:S(2)}) %all-to-all-start) | async-done | bytes 1835040 | tf_op jit(solution)/shard_map/all_to_all | solution.py:115
  98.4 3.7 %fusion.23 = bf16[512,2,128,1]{0,2,3,1:T(8,128)(2,1)S(1)} fusion(f32[2,128,512]{2,1,0:T(8,128)S(1)} %fusion.12, bf16[16,2,224,128]{3,2,1,0:T(8,128)(2,1)} %all-to-all-done, bf16[512,16,448]{0,2,1:T(8,128)(2,1)} %bitcast.151, f32[512]{0:T(512)S(1)} %copy-done.9), kind=kOutput, calls=%fused_computation.34 | convolution fusion | flops 939917312 | bytes 6293504 | tf_op jit(solution)/shard_map/ksv,srvx->krx/dot_general | solution.py:118
  102.1 5.1 %fusion.3 = bf16[16,2,224,128]{3,2,0,1:T(8,128)(2,1)} fusion(bf16[16,2,224,128]{3,2,1,0:T(8,128)(2,1)} %all-to-all-done, f32[2,128]{1,0:T(2,128)S(1)} %constant_dynamic-slice_fusion, bf16[512,2,128,1]{0,2,3,1:T(8,128)(2,1)S(1)} %fusion.23, bf16[16,448,512]{2,1,0:T(8,128)(2,1)} %bitcast.170), kind=kOutput, calls=%fused_computation.12 | convolution fusion | flops 943194112 | bytes 7603200 | tf_op jit(solution)/shard_map/svk,krx->srvx/dot_general | solution.py:128
  107.2 3.2 %fusion.2 = bf16[16,2,224,128]{3,2,0,1:T(8,128)(2,1)S(1)} fusion(bf16[16,2,224,128]{3,2,1,0:T(8,128)(2,1)S(1)} %all-to-all-done.1, f32[2,128]{1,0:T(2,128)S(1)} %constant_dynamic-slice_fusion, bf16[512,2,128,1]{0,2,3,1:T(8,128)(2,1)S(1)} %fusion.23, bf16[16,448,512]{2,1,0:T(8,128)(2,1)} %bitcast.171), kind=kOutput, calls=%fused_computation.10 | convolution fusion | flops 943194112 | bytes 7603200 | tf_op jit(solution)/shard_map/svk,krx->srvx/dot_general | solution.py:128
  110.4 1.4 copy.53
  111.8 4.1 %all-to-all-start.4 = ((bf16[16,2,224,128]{3,2,1,0:T(8,128)(2,1)}), bf16[16,2,224,128]{3,2,1,0:T(8,128)(2,1)S(1)}, u32[]{:S(2)}, u32[]{:S(2)}) async-start(bf16[16,2,224,128]{3,2,1,0:T(8,128)(2,1)} %copy.53), calls=%async_computation.4 | async-start | bytes 3670016 | tf_op jit(solution)/shard_map/all_to_all | solution.py:131
  115.9 2.9 copy.48
  118.8 20.2 %all-to-all-done.4 = bf16[16,2,224,128]{3,2,1,0:T(8,128)(2,1)S(1)} async-done(((bf16[16,2,224,128]{3,2,1,0:T(8,128)(2,1)}), bf16[16,2,224,128]{3,2,1,0:T(8,128)(2,1)S(1)}, u32[]{:S(2)}, u32[]{:S(2)}) %all-to-all-start.4) | async-done | bytes 1835040 | tf_op jit(solution)/shard_map/all_to_all | solution.py:131
  139.0 1.2 copy-done.1
  140.2 3.7 %all-to-all-start.2 = ((bf16[16,2,224,128]{3,2,1,0:T(8,128)(2,1)}), bf16[16,2,224,128]{3,2,1,0:T(8,128)(2,1)S(1)}, u32[]{:S(2)}, u32[]{:S(2)}) async-start(bf16[16,2,224,128]{3,2,1,0:T(8,128)(2,1)} %copy.48), calls=%async_computation.2 | async-start | bytes 3670016 | tf_op jit(solution)/shard_map/all_to_all | solution.py:127
  143.9 1.6 fusion.34
  145.5 1.9 collective-permute-start.4
  147.5 3.8 %collective-permute-start.5 = (bf16[16,224,128]{2,1,0:T(8,128)(2,1)S(1)}, bf16[16,224,128]{2,1,0:T(8,128)(2,1)S(1)}, u32[]{:S(2)}, u32[]{:S(2)}) collective-permute-start(bf16[16,224,128]{2,1,0:T(8,128)(2,1)S(1)} %bitcast.158), channel_id=1, source_target_pairs={{16,0},{32,16},{48,32},{64,48},{80,64},{96,80},{112,96},{17,1},{33... | collective-permute-start | bytes 2752520 | tf_op jit(solution)/shard_map/ppermute | solution.py:112
  151.3 9.0 %collective-permute-done.4.lo_ref = bf16[16,224,128]{2,1,0:T(8,128)(2,1)S(1)} collective-permute-done((bf16[16,224,128]{2,1,0:T(8,128)(2,1)S(1)}, bf16[16,224,128]{2,1,0:T(8,128)(2,1)S(1)}, u32[]{:S(2)}, u32[]{:S(2)}) %collective-permute-start.4) | collective-permute-done | bytes 917536 | tf_op jit(solution)/shard_map/ppermute | solution.py:111
  160.3 1.8 collective-permute-done.5.hi_ref
  162.0 1.0 copy-done.6
  163.0 0.0 copy-done.4
  163.0 5.3 %shard_map.67 = bf16[32,224,128]{2,1,0:T(8,128)(2,1)} custom-call(bf16[32,224,128]{2,1,0:T(8,128)(2,1)} %bitcast.147, bf16[16,224,128]{2,1,0:T(8,128)(2,1)} %copy-done.4, bf16[16,224,128]{2,1,0:T(8,128)(2,1)} %copy-done.6, f32[3,224,128]{2,1,0:T(8,128)} %broadcast_in_dim.30.coef_ref, f32[32,128]{1,0:T(8,128)} %bitcast.164), custom_call_target="tpu_custom_call" | custom-call | flops 18350080 | bytes 3670016 | tf_op jit(solution)/shard_map/pallas_call | solution.py:62
  168.3 0.6 all-to-all-done.2
  168.9 6.6 %all-to-all-start.5 = ((bf16[16,2,224,128]{3,2,1,0:T(8,128)(2,1)}), bf16[16,2,224,128]{3,2,1,0:T(8,128)(2,1)}, u32[]{:S(2)}, u32[]{:S(2)}) async-start(bf16[16,2,224,128]{3,2,1,0:T(8,128)(2,1)} %bitcast.154), calls=%async_computation.5 | async-start | bytes 3670016 | tf_op jit(solution)/shard_map/all_to_all | solution.py:115
  175.5 0.1 fusion.33
  175.7 4.6 %collective-permute-start.2 = (bf16[16,224,128]{2,1,0:T(8,128)(2,1)S(1)}, bf16[16,224,128]{2,1,0:T(8,128)(2,1)S(1)}, u32[]{:S(2)}, u32[]{:S(2)}) collective-permute-start(bf16[16,224,128]{2,1,0:T(8,128)(2,1)S(1)} %bitcast.161), channel_id=1, source_target_pairs={{0,16},{16,32},{32,48},{48,64},{64,80},{80,96},{96,112},{1,17},{17... | collective-permute-start | bytes 2752520 | tf_op jit(solution)/shard_map/ppermute | solution.py:111
  180.3 1.9 collective-permute-start.3
  182.2 8.2 %collective-permute-done.2.lo_ref = bf16[16,224,128]{2,1,0:T(8,128)(2,1)S(1)} collective-permute-done((bf16[16,224,128]{2,1,0:T(8,128)(2,1)S(1)}, bf16[16,224,128]{2,1,0:T(8,128)(2,1)S(1)}, u32[]{:S(2)}, u32[]{:S(2)}) %collective-permute-start.2) | collective-permute-done | bytes 917536 | tf_op jit(solution)/shard_map/ppermute | solution.py:111
  190.4 2.7 collective-permute-done.3.hi_ref
  193.1 0.9 copy-done.5
  194.0 5.3 %shard_map.66 = bf16[32,224,128]{2,1,0:T(8,128)(2,1)} custom-call(bf16[32,224,128]{2,1,0:T(8,128)(2,1)} %bitcast.146, bf16[16,224,128]{2,1,0:T(8,128)(2,1)} %copy-done.3, bf16[16,224,128]{2,1,0:T(8,128)(2,1)} %copy-done.5, f32[3,224,128]{2,1,0:T(8,128)} %broadcast_in_dim.26.coef_ref, f32[32,128]{1,0:T(8,128)} %bitcast.165), custom_call_target="tpu_custom_call" | custom-call | flops 18350080 | bytes 3670016 | tf_op jit(solution)/shard_map/pallas_call | solution.py:62
  199.3 0.6 all-to-all-done.5
  199.9 6.3 %all-to-all-start.3 = ((bf16[16,2,224,128]{3,2,1,0:T(8,128)(2,1)}), bf16[16,2,224,128]{3,2,1,0:T(8,128)(2,1)S(1)}, u32[]{:S(2)}, u32[]{:S(2)}) async-start(bf16[16,2,224,128]{3,2,1,0:T(8,128)(2,1)} %bitcast.155), calls=%async_computation.3 | async-start | bytes 3670016 | tf_op jit(solution)/shard_map/all_to_all | solution.py:115
  206.2 3.7 %fusion.13 = f32[2,128,512]{2,1,0:T(8,128)S(1)} fusion(bf16[16,2,224,128]{3,2,1,0:T(8,128)(2,1)} %all-to-all-done.5, bf16[512,16,448]{0,2,1:T(8,128)(2,1)} %bitcast.152), kind=kOutput, calls=%fused_computation.24 | convolution fusion | flops 939524096 | bytes 6029312 | tf_op jit(solution)/shard_map/ksv,srvx->krx/dot_general | solution.py:118
  209.9 23.1 %all-to-all-done.3 = bf16[16,2,224,128]{3,2,1,0:T(8,128)(2,1)S(1)} async-done(((bf16[16,2,224,128]{3,2,1,0:T(8,128)(2,1)}), bf16[16,2,224,128]{3,2,1,0:T(8,128)(2,1)S(1)}, u32[]{:S(2)}, u32[]{:S(2)}) %all-to-all-start.3) | async-done | bytes 1835040 | tf_op jit(solution)/shard_map/all_to_all | solution.py:115
  233.1 3.2 %fusion.22 = bf16[512,2,128,1]{0,2,3,1:T(8,128)(2,1)S(1)} fusion(f32[2,128,512]{2,1,0:T(8,128)S(1)} %fusion.13, bf16[16,2,224,128]{3,2,1,0:T(8,128)(2,1)S(1)} %all-to-all-done.3, bf16[512,16,448]{0,2,1:T(8,128)(2,1)} %bitcast.153, f32[512]{0:T(512)S(1)} %copy-done.9), kind=kOutput, calls=%fused_computation.33 | convolution fusion | flops 939917312 | bytes 6293504 | tf_op jit(solution)/shard_map/ksv,srvx->krx/dot_general | solution.py:118
  236.3 3.2 %fusion.1 = bf16[16,2,224,128]{3,2,0,1:T(8,128)(2,1)S(1)} fusion(bf16[16,2,224,128]{3,2,1,0:T(8,128)(2,1)S(1)} %all-to-all-done.3, f32[2,128]{1,0:T(2,128)S(1)} %constant_dynamic-slice_fusion, bf16[512,2,128,1]{0,2,3,1:T(8,128)(2,1)S(1)} %fusion.22, bf16[16,448,512]{2,1,0:T(8,128)(2,1)} %bitcast.172), kind=kOutput, calls=%fused_computation.8 | convolution fusion | flops 943194112 | bytes 7603200 | tf_op jit(solution)/shard_map/svk,krx->srvx/dot_general | solution.py:128
  239.4 1.4 copy.56
  240.9 4.1 %all-to-all-start.6 = ((bf16[16,2,224,128]{3,2,1,0:T(8,128)(2,1)}), bf16[16,2,224,128]{3,2,1,0:T(8,128)(2,1)S(1)}, u32[]{:S(2)}, u32[]{:S(2)}) async-start(bf16[16,2,224,128]{3,2,1,0:T(8,128)(2,1)} %copy.56), calls=%async_computation.6 | async-start | bytes 3670016 | tf_op jit(solution)/shard_map/all_to_all | solution.py:127
  245.0 3.8 %fusion = bf16[16,2,224,128]{3,2,0,1:T(8,128)(2,1)S(1)} fusion(bf16[16,2,224,128]{3,2,1,0:T(8,128)(2,1)} %all-to-all-done.5, f32[2,128]{1,0:T(2,128)S(1)} %constant_dynamic-slice_fusion, bf16[512,2,128,1]{0,2,3,1:T(8,128)(2,1)S(1)} %fusion.22, bf16[16,448,512]{2,1,0:T(8,128)(2,1)} %bitcast.173), kind=kOutput, calls=%fused_computation.6 | convolution fusion | flops 943194112 | bytes 7603200 | tf_op jit(solution)/shard_map/svk,krx->srvx/dot_general | solution.py:128
  248.8 1.4 copy.59
  250.2 22.6 %all-to-all-done.6 = bf16[16,2,224,128]{3,2,1,0:T(8,128)(2,1)S(1)} async-done(((bf16[16,2,224,128]{3,2,1,0:T(8,128)(2,1)}), bf16[16,2,224,128]{3,2,1,0:T(8,128)(2,1)S(1)}, u32[]{:S(2)}, u32[]{:S(2)}) %all-to-all-start.6) | async-done | bytes 1835040 | tf_op jit(solution)/shard_map/all_to_all | solution.py:127
  272.9 31.5 %all_to_all.40 = bf16[16,2,224,128]{3,2,1,0:T(8,128)(2,1)S(1)} all-to-all(bf16[16,2,224,128]{3,2,1,0:T(8,128)(2,1)} %copy.59), channel_id=1, replica_groups=mesh['space'=8,'vel'=16] {'vel'}, dimensions={0} | all-to-all | bytes 3670016 | tf_op jit(solution)/shard_map/all_to_all | solution.py:131
  304.4 0.4 maximum_bitcast_fusion
  304.8 4.2 %copy.60 = bf16[448,2,16,128]{3,2,1,0:T(8,128)(2,1)} copy(bf16[448,2,16,128]{3,0,2,1:T(8,128)(2,1)S(1)} %maximum_bitcast_fusion) | data formatting | bytes 7340032 | tf_op jit(solution)/shard_map/transpose | solution.py:133
  (15 shorter events, 0.1 us)
Async XLA Ops:
  3.5 4.6 %copy-start.8 = (s32[448]{0:T(512)S(1)}, s32[448]{0:T(512)}, u32[]{:S(2)}) copy-start(s32[448]{0:T(512)} %param.7) | copy-start | bytes 5380
  3.5 4.7 %copy-start.7 = (s32[2,16,128]{2,1,0:T(8,128)S(1)}, s32[2,16,128]{2,1,0:T(8,128)}, u32[]{:S(2)}) copy-start(s32[2,16,128]{2,1,0:T(8,128)} %param.8) | copy-start | bytes 49156
  3.7 22.6 %collective-permute-start.1 = (bf16[16,448,128]{2,1,0:T(8,128)(2,1)S(1)}, bf16[16,448,128]{2,1,0:T(8,128)(2,1)S(1)}, u32[]{:S(2)}, u32[]{:S(2)}) collective-permute-start(bf16[16,448,128]{2,1,0:T(8,128)(2,1)S(1)} %get-tuple-element.15), channel_id=1, source_target_pairs={{16,0},{32,16},{48,32},{64,48},{80,64},{96,80},{112,96},{17,1},{33... | collective-permute-start | bytes 5505032 | tf_op jit(solution)/shard_map/ppermute | solution.py:102
  5.7 24.7 %collective-permute-start = (bf16[16,448,128]{2,1,0:T(8,128)(2,1)S(1)}, bf16[16,448,128]{2,1,0:T(8,128)(2,1)}, u32[]{:S(2)}, u32[]{:S(2)}) collective-permute-start(bf16[16,448,128]{2,1,0:T(8,128)(2,1)S(1)} %get-tuple-element.16), channel_id=1, source_target_pairs={{0,16},{16,32},{32,48},{48,64},{64,80},{80,96},{96,112},{1,17},{17... | collective-permute-start | bytes 5505032 | tf_op jit(solution)/shard_map/ppermute | solution.py:101
  26.4 4.8 %copy-start.2 = (bf16[16,448,128]{2,1,0:T(8,128)(2,1)}, bf16[16,448,128]{2,1,0:T(8,128)(2,1)S(1)}, u32[]{:S(2)}) copy-start(bf16[16,448,128]{2,1,0:T(8,128)(2,1)S(1)} %collective-permute-done.1.hi_ref) | copy-start | bytes 5505028
  36.5 33.4 %all-to-all-start.1 = ((bf16[16,2,224,128]{3,2,1,0:T(8,128)(2,1)}), bf16[16,2,224,128]{3,2,1,0:T(8,128)(2,1)S(1)}, u32[]{:S(2)}, u32[]{:S(2)}) async-start(bf16[16,2,224,128]{3,2,1,0:T(8,128)(2,1)} %bitcast.157), calls=%async_computation.1 | async-start | bytes 3670016 | tf_op jit(solution)/shard_map/all_to_all | solution.py:115
  69.9 28.5 %all-to-all-start = ((bf16[16,2,224,128]{3,2,1,0:T(8,128)(2,1)}), bf16[16,2,224,128]{3,2,1,0:T(8,128)(2,1)}, u32[]{:S(2)}, u32[]{:S(2)}) async-start(bf16[16,2,224,128]{3,2,1,0:T(8,128)(2,1)} %bitcast.156), calls=%async_computation | async-start | bytes 3670016 | tf_op jit(solution)/shard_map/all_to_all | solution.py:115
  84.8 13.6 %copy-start.9 = (f32[512]{0:T(512)S(1)}, f32[512]{0:T(512)}, u32[]{:S(2)}) copy-start(f32[512]{0:T(512)} %param.11) | copy-start | bytes 6148
  111.8 27.2 %all-to-all-start.4 = ((bf16[16,2,224,128]{3,2,1,0:T(8,128)(2,1)}), bf16[16,2,224,128]{3,2,1,0:T(8,128)(2,1)S(1)}, u32[]{:S(2)}, u32[]{:S(2)}) async-start(bf16[16,2,224,128]{3,2,1,0:T(8,128)(2,1)} %copy.53), calls=%async_computation.4 | async-start | bytes 3670016 | tf_op jit(solution)/shard_map/all_to_all | solution.py:131
  139.0 1.2 copy-start.1
  140.2 28.7 %all-to-all-start.2 = ((bf16[16,2,224,128]{3,2,1,0:T(8,128)(2,1)}), bf16[16,2,224,128]{3,2,1,0:T(8,128)(2,1)S(1)}, u32[]{:S(2)}, u32[]{:S(2)}) async-start(bf16[16,2,224,128]{3,2,1,0:T(8,128)(2,1)} %copy.48), calls=%async_computation.2 | async-start | bytes 3670016 | tf_op jit(solution)/shard_map/all_to_all | solution.py:127
  145.5 14.7 %collective-permute-start.4 = (bf16[16,224,128]{2,1,0:T(8,128)(2,1)S(1)}, bf16[16,224,128]{2,1,0:T(8,128)(2,1)S(1)}, u32[]{:S(2)}, u32[]{:S(2)}) collective-permute-start(bf16[16,224,128]{2,1,0:T(8,128)(2,1)S(1)} %bitcast.160), channel_id=1, source_target_pairs={{0,16},{16,32},{32,48},{48,64},{64,80},{80,96},{96,112},{1,17},{17... | collective-permute-start | bytes 2752520 | tf_op jit(solution)/shard_map/ppermute | solution.py:111
  147.5 14.5 %collective-permute-start.5 = (bf16[16,224,128]{2,1,0:T(8,128)(2,1)S(1)}, bf16[16,224,128]{2,1,0:T(8,128)(2,1)S(1)}, u32[]{:S(2)}, u32[]{:S(2)}) collective-permute-start(bf16[16,224,128]{2,1,0:T(8,128)(2,1)S(1)} %bitcast.158), channel_id=1, source_target_pairs={{16,0},{32,16},{48,32},{64,48},{80,64},{96,80},{112,96},{17,1},{33... | collective-permute-start | bytes 2752520 | tf_op jit(solution)/shard_map/ppermute | solution.py:112
  160.3 2.7 copy-start.4
  162.0 1.0 copy-start.6
  168.9 6.7 %copy-start = (bf16[16,2,224,128]{3,2,1,0:T(8,128)(2,1)}, bf16[16,2,224,128]{3,2,1,0:T(8,128)(2,1)S(1)}, u32[]{:S(2)}) copy-start(bf16[16,2,224,128]{3,2,1,0:T(8,128)(2,1)S(1)} %all-to-all-done.2) | copy-start | bytes 5505028
  168.9 31.0 %all-to-all-start.5 = ((bf16[16,2,224,128]{3,2,1,0:T(8,128)(2,1)}), bf16[16,2,224,128]{3,2,1,0:T(8,128)(2,1)}, u32[]{:S(2)}, u32[]{:S(2)}) async-start(bf16[16,2,224,128]{3,2,1,0:T(8,128)(2,1)} %bitcast.154), calls=%async_computation.5 | async-start | bytes 3670016 | tf_op jit(solution)/shard_map/all_to_all | solution.py:115
  175.7 14.7 %collective-permute-start.2 = (bf16[16,224,128]{2,1,0:T(8,128)(2,1)S(1)}, bf16[16,224,128]{2,1,0:T(8,128)(2,1)S(1)}, u32[]{:S(2)}, u32[]{:S(2)}) collective-permute-start(bf16[16,224,128]{2,1,0:T(8,128)(2,1)S(1)} %bitcast.161), channel_id=1, source_target_pairs={{0,16},{16,32},{32,48},{48,64},{64,80},{80,96},{96,112},{1,17},{17... | collective-permute-start | bytes 2752520 | tf_op jit(solution)/shard_map/ppermute | solution.py:111
  180.3 12.8 %collective-permute-start.3 = (bf16[16,224,128]{2,1,0:T(8,128)(2,1)S(1)}, bf16[16,224,128]{2,1,0:T(8,128)(2,1)S(1)}, u32[]{:S(2)}, u32[]{:S(2)}) collective-permute-start(bf16[16,224,128]{2,1,0:T(8,128)(2,1)S(1)} %bitcast.159), channel_id=1, source_target_pairs={{16,0},{32,16},{48,32},{64,48},{80,64},{96,80},{112,96},{17,1},{33... | collective-permute-start | bytes 2752520 | tf_op jit(solution)/shard_map/ppermute | solution.py:112
  190.4 2.7 copy-start.3
  193.1 0.9 copy-start.5
  199.9 33.2 %all-to-all-start.3 = ((bf16[16,2,224,128]{3,2,1,0:T(8,128)(2,1)}), bf16[16,2,224,128]{3,2,1,0:T(8,128)(2,1)S(1)}, u32[]{:S(2)}, u32[]{:S(2)}) async-start(bf16[16,2,224,128]{3,2,1,0:T(8,128)(2,1)} %bitcast.155), calls=%async_computation.3 | async-start | bytes 3670016 | tf_op jit(solution)/shard_map/all_to_all | solution.py:115
  240.9 32.0 %all-to-all-start.6 = ((bf16[16,2,224,128]{3,2,1,0:T(8,128)(2,1)}), bf16[16,2,224,128]{3,2,1,0:T(8,128)(2,1)S(1)}, u32[]{:S(2)}, u32[]{:S(2)}) async-start(bf16[16,2,224,128]{3,2,1,0:T(8,128)(2,1)} %copy.56), calls=%async_computation.6 | async-start | bytes 3670016 | tf_op jit(solution)/shard_map/all_to_all | solution.py:127
